TPU v7x, 32 devices: a whole 2x2x4 slice. The times are simulated.
32 devices in a mesh: req: 2 (over x), tile: 16 (over z, y, core).
Axes of the slice: x: 2, y: 2, z: 4, core: 2. Of those that a mesh axis runs over, the one named last changes fastest.
Arguments:
- queries: bfloat16 [32, 512, 384], P(('req', 'tile')), parts along dimension 0, may hold values from -12 to 12
- keys: bfloat16 [32, 512, 384], P(('req', 'tile')), parts along dimension 0, may hold values from -5 to 5
- values: bfloat16 [32, 512, 384], P(('req', 'tile')), parts along dimension 0, may hold values from -6 to 6
- text_keys: bfloat16 [512, 1536], P(('req', 'tile')), parts along dimension 0, may hold values from -6 to 6
- text_values: bfloat16 [512, 1536], P(('req', 'tile')), parts along dimension 0, may hold values from -6 to 6
- text_mask: int32 [512], P(('req', 'tile')), parts along dimension 0, may hold values 0 or 1
Outputs:
- attended: bfloat16 [32, 512, 384], P(('req', 'tile')), parts along dimension 0
There are 2 independent parts, one for each index of `req`. A program takes and returns all parts, laid end to end along the dimension named above; each array names one. Nothing has to cross between parts.
All inputs are finite; a program needn't handle non-finite values. No bound on the sum of `text_mask` on one device may be relied on, other than what follows from the above.
Results may differ from a plain program's by a relative error of at most 0.004.
Values may be sent and summed in bfloat16 or wider, within the bound.
No kernel may reach another device: no remote copies, remote signals or barrier semaphores. Data moves between devices by JAX's collectives and lax.ppermute only.
A program may use at most 192 MiB of HBM per device.

v0:
```python
import math

import jax
import jax.numpy as jnp
from jax import lax
from jax.sharding import PartitionSpec as P

TS = 8
HEAD_DIM = 128
HEAD_GROUPS = 4


MASKED = -1e30


def passed_along(value, axis, steps):
    count = lax.axis_size(axis)
    first, last = (max(0, -steps), min(count, count - steps))
    return lax.ppermute(value, axis, [(source, source + steps) for source in range(first, last)])


def shortened(value):
    return jax.tree.map(lambda a: a.astype(jnp.bfloat16) if a.dtype == jnp.float32 else a, value)


def fold_block(running, query_heads, key_block, value_block, key_keep):
    row_top, row_total, summed = running
    head_count = query_heads.shape[1]
    key_heads = key_block.reshape(key_block.shape[0], head_count, HEAD_DIM)
    value_heads = value_block.reshape(value_block.shape[0], head_count, HEAD_DIM)
    scores = jnp.einsum("qhd,khd->hqk", query_heads, key_heads, preferred_element_type=jnp.float32)
    scores = scores * (1.0 / math.sqrt(HEAD_DIM))
    scores = jnp.where(key_keep[None, None, :], scores, MASKED)
    new_top = jnp.maximum(row_top, jnp.max(scores, axis=-1))
    scale_down = jnp.exp(row_top - new_top)
    exp_terms = jnp.where(key_keep[None, None, :], jnp.exp(scores - new_top[:, :, None]), 0.0)
    row_total = row_total * scale_down + jnp.sum(exp_terms, axis=-1)
    weights = exp_terms.astype(jnp.bfloat16)
    summed = summed * scale_down[:, :, None] + jnp.einsum(
        "hqk,khd->hqd", weights, value_heads, preferred_element_type=jnp.float32
    )
    return (new_top, row_total, summed)


def shards(queries, keys, values, text_keys, text_values, text_mask):
    tokens = queries.shape[1]
    lane_width = queries.shape[2]
    head_count = lane_width // HEAD_DIM
    query_heads = queries[0].reshape(tokens, head_count, HEAD_DIM)
    own_pair = jnp.stack([keys[0], values[0]])
    group_count = HEAD_GROUPS
    tiles_all = lax.axis_size("tile") // group_count
    grid_w = min(4, tiles_all)
    grid_h = min(4, tiles_all // grid_w)
    grid_f = tiles_all // (grid_w * grid_h)
    frames_valid = grid_f * TS - TS // 4
    my_index = lax.axis_index("tile")
    tile_id = my_index // group_count
    head_group = my_index % group_count
    w_pos = tile_id % grid_w
    h_pos = tile_id // grid_w % grid_h
    f_pos = tile_id // (grid_w * grid_h)
    local_frame = jnp.arange(tokens, dtype=jnp.int32) // (TS * TS)

    def keep_mask(off_frame, off_height, off_width):
        inside = (
            (f_pos + off_frame >= 0)
            & (f_pos + off_frame < grid_f)
            & (h_pos + off_height >= 0)
            & (h_pos + off_height < grid_h)
            & (w_pos + off_width >= 0)
            & (w_pos + off_width < grid_w)
        )
        return inside & ((f_pos + off_frame) * TS + local_frame < frames_valid)

    running = (
        jnp.full((head_count, tokens), MASKED, jnp.float32),
        jnp.zeros((head_count, tokens), jnp.float32),
        jnp.zeros((head_count, tokens, HEAD_DIM), jnp.float32),
    )
    text_flags = text_mask.astype(jnp.bfloat16)
    piece_keys = lax.dynamic_slice_in_dim(
        lax.all_gather(text_keys, "tile", axis=0, tiled=True),
        head_group * lane_width,
        lane_width,
        1,
    )
    piece_values = lax.dynamic_slice_in_dim(
        lax.all_gather(text_values, "tile", axis=0, tiled=True),
        head_group * lane_width,
        lane_width,
        1,
    )
    running = fold_block(
        running,
        query_heads,
        piece_keys,
        piece_values,
        lax.all_gather(text_flags, "tile", axis=0, tiled=True) > 0.5,
    )
    running = fold_block(running, query_heads, own_pair[0], own_pair[1], keep_mask(0, 0, 0))
    width_set = {0: own_pair}
    for off_width in (-1, 1):
        width_set[off_width] = passed_along(own_pair, "tile", -off_width * group_count)
    width_offsets = sorted(width_set)
    row_stack = jnp.stack([width_set[spot] for spot in width_offsets])
    height_set = {0: row_stack}
    if grid_h > 1:
        for off_height in (-1, 1):
            height_set[off_height] = passed_along(
                shortened(row_stack), "tile", -off_height * grid_w * group_count
            ).astype(row_stack.dtype)
    height_offsets = sorted(height_set)
    slab_stack = jnp.stack([height_set[spot] for spot in height_offsets])

    def fold_slab(state_now, slab_pairs, off_frame):
        for h_slot, off_height in enumerate(height_offsets):
            for w_slot, off_width in enumerate(width_offsets):
                if off_frame == 0 and off_height == 0 and (off_width == 0):
                    continue
                state_now = fold_block(
                    state_now,
                    query_heads,
                    slab_pairs[h_slot, w_slot, 0],
                    slab_pairs[h_slot, w_slot, 1],
                    keep_mask(off_frame, off_height, off_width),
                )
        return state_now

    running = fold_slab(running, slab_stack, 0)
    if grid_f > 1:
        for off_frame in (-1, 1):
            got_slab = passed_along(
                shortened(slab_stack), "tile", -off_frame * grid_h * grid_w * group_count
            ).astype(slab_stack.dtype)
            running = fold_slab(running, got_slab, off_frame)
    row_top, row_total, summed = running
    result = summed / row_total[:, :, None]
    result = jnp.transpose(result, (1, 0, 2)).reshape(tokens, lane_width)
    return result.astype(jnp.bfloat16)[None]


def solution(mesh):
    return jax.shard_map(
        shards,
        mesh=mesh,
        in_specs=(
            P(("req", "tile"), None, None),
            P(("req", "tile"), None, None),
            P(("req", "tile"), None, None),
            P(("req", "tile"), None),
            P(("req", "tile"), None),
            P(("req", "tile")),
        ),
        out_specs=P(("req", "tile"), None, None),
        check_vma=False,
    )
```

profile of v0, /device:TPU:0, one launch (start us, length us, event | category | flops | bytes accessed | tf_op | source)
XLA Modules:
  0.0 110.9 jit_solution(2474602428731131896)
XLA Ops:
  0.0 0.0 copy-start.3
  0.0 0.0 copy-start.2
  0.0 0.0 copy-start
  0.0 0.0 copy-start.1
  0.0 1.2 %copy.51 = bf16[1,512,384]{1,2,0:T(8,128)(2,1)S(1)} copy(bf16[1,512,384]{2,1,0:T(8,128)(2,1)} %param.7) | data formatting | bytes 786432 | tf_op args[1]
  1.2 1.2 %copy.56 = bf16[1,512,384]{1,2,0:T(8,128)(2,1)S(1)} copy(bf16[1,512,384]{2,1,0:T(8,128)(2,1)} %param.8) | data formatting | bytes 786432 | tf_op args[2]
  2.4 1.0 fusion.71
  3.4 1.3 %collective-permute-start.1 = (bf16[2,512,384]{1,2,0:T(8,128)(2,1)}, bf16[2,512,384]{1,2,0:T(8,128)(2,1)}, u32[]{:S(2)}, u32[]{:S(2)}) collective-permute-start(bf16[2,512,384]{1,2,0:T(8,128)(2,1)} %get-tuple-element.16), channel_id=1, source_target_pairs={{4,0},{5,1},{6,2},{7,3},{8,4},{9,5},{10,6},{11,7},{12,8},{13,9},{1... | collective-permute-start | bytes 2359304 | tf_op jit(solution)/shard_map/ppermute | solution.py:19
  4.7 6.5 %collective-permute-start = (bf16[2,512,384]{1,2,0:T(8,128)(2,1)}, bf16[2,512,384]{1,2,0:T(8,128)(2,1)}, u32[]{:S(2)}, u32[]{:S(2)}) collective-permute-start(bf16[2,512,384]{1,2,0:T(8,128)(2,1)} %get-tuple-element.16), channel_id=1, source_target_pairs={{0,4},{1,5},{2,6},{3,7},{4,8},{5,9},{6,10},{7,11},{8,12},{9,13},{1... | collective-permute-start | bytes 2359304 | tf_op jit(solution)/shard_map/ppermute | solution.py:19
  11.1 0.0 copy-done.2
  11.2 0.0 copy-done.3
  11.2 0.6 dynamic-slice
  12.4 0.2 dynamic-update-slice
  12.7 41.9 %all-reduce = bf16[256]{0:T(256)(128)(2,1)S(1)} all-reduce(bf16[256]{0:T(256)(128)(2,1)S(1)} %dynamic-update-slice), channel_id=1, replica_groups=mesh['req'=2,'tile'=16] {'tile'}, use_global_device_ids=true, to_apply=%add | all-reduce | flops 256 | bytes 1024
  54.6 0.0 copy-done
  54.6 0.2 copy.46
  54.8 0.0 copy-done.1
  54.8 19.6 %all_gather.10 = bf16[256,1536]{1,0:T(8,128)(2,1)S(1)} all-gather(bf16[16,1536]{1,0:T(8,128)(2,1)S(1)} %copy-done.1), channel_id=1, replica_groups=mesh['req'=2,'tile'=16] {'tile'}, dimensions={0}, use_global_device_ids=true | all-gather | bytes 835584 | tf_op jit(solution)/shard_map/all_gather | solution.py:83
  74.4 21.4 %all_gather.11 = bf16[256,1536]{1,0:T(8,128)(2,1)S(1)} all-gather(bf16[16,1536]{1,0:T(8,128)(2,1)} %param.10), channel_id=1, replica_groups=mesh['req'=2,'tile'=16] {'tile'}, dimensions={0}, use_global_device_ids=true | all-gather | bytes 835584 | tf_op jit(solution)/shard_map/all_gather | solution.py:89
  95.8 0.8 constant_dynamic-slice_fusion
  96.6 1.1 copy.49
  97.6 1.1 copy.79
  98.8 0.4 bitcast_reduce_fusion.2
  99.2 0.8 fusion.4
  100.0 0.0 collective-permute-done.1
  100.0 0.0 collective-permute-done
  100.0 1.6 %maximum_bitcast_fusion = bf16[1,3,2,512,384]{3,4,2,1,0:T(8,128)(2,1)S(1)} fusion(bf16[1,2,512,384]{2,3,1,0:T(8,128)(2,1)} %bitcast.13, bf16[1,2,512,384]{2,3,1,0:T(8,128)(2,1)S(1)} %get-tuple-element.15, bf16[1,2,512,384]{2,3,1,0:T(8,128)(2,1)} %bitcast.11), kind=kLoop, calls=%fused_computation.13 | loop fusion | flops 2359296 | bytes 4718592 | tf_op jit(solution)/shard_map/stack | solution.py:114
  101.7 0.1 fusion.75
  101.8 0.8 bitcast_reduce_fusion
  102.6 0.8 bitcast_reduce_fusion.1
  103.5 0.9 fusion.9
  104.3 1.0 fusion.38
  105.3 0.9 fusion.7
  106.2 1.0 fusion.35
  107.2 0.9 fusion.5
  108.1 1.0 fusion.24
  109.1 0.3 fusion.41
  109.4 0.6 fusion.43
  110.0 0.9 copy.66
  (7 shorter events, 0.1 us)
Async XLA Ops:
  0.0 11.2 %copy-start.3 = (u32[32]{0:T(128)S(1)}, u32[32]{0:T(128)}, u32[]{:S(2)}) copy-start(u32[32]{0:T(128)} %constant.104) | copy-start | bytes 388
  0.0 11.1 %copy-start.2 = (s32[16]{0:T(128)S(1)}, s32[16]{0:T(128)}, u32[]{:S(2)}) copy-start(s32[16]{0:T(128)} %param.11) | copy-start | bytes 196
  0.0 54.6 %copy-start = (bf16[1,512,384]{2,1,0:T(8,128)(2,1)S(1)}, bf16[1,512,384]{2,1,0:T(8,128)(2,1)}, u32[]{:S(2)}) copy-start(bf16[1,512,384]{2,1,0:T(8,128)(2,1)} %param.6) | copy-start | bytes 1179652
  0.0 54.8 %copy-start.1 = (bf16[16,1536]{1,0:T(8,128)(2,1)S(1)}, bf16[16,1536]{1,0:T(8,128)(2,1)}, u32[]{:S(2)}) copy-start(bf16[16,1536]{1,0:T(8,128)(2,1)} %param.9) | copy-start | bytes 147460
  3.4 96.6 %collective-permute-start.1 = (bf16[2,512,384]{1,2,0:T(8,128)(2,1)}, bf16[2,512,384]{1,2,0:T(8,128)(2,1)}, u32[]{:S(2)}, u32[]{:S(2)}) collective-permute-start(bf16[2,512,384]{1,2,0:T(8,128)(2,1)} %get-tuple-element.16), channel_id=1, source_target_pairs={{4,0},{5,1},{6,2},{7,3},{8,4},{9,5},{10,6},{11,7},{12,8},{13,9},{1... | collective-permute-start | bytes 2359304 | tf_op jit(solution)/shard_map/ppermute | solution.py:19
  4.7 95.4 %collective-permute-start = (bf16[2,512,384]{1,2,0:T(8,128)(2,1)}, bf16[2,512,384]{1,2,0:T(8,128)(2,1)}, u32[]{:S(2)}, u32[]{:S(2)}) collective-permute-start(bf16[2,512,384]{1,2,0:T(8,128)(2,1)} %get-tuple-element.16), channel_id=1, source_target_pairs={{0,4},{1,5},{2,6},{3,7},{4,8},{5,9},{6,10},{7,11},{8,12},{9,13},{1... | collective-permute-start | bytes 2359304 | tf_op jit(solution)/shard_map/ppermute | solution.py:19
where the time goes:
time: 111 us
  blocking collectives  82.9 us (75%)
  starting transfers between devices  7.75 us (7%)
  local copies, waits for them, and re-layouts  7.34 us (7%)
  matrix products  6.38 us (6%)
  other arithmetic  5.66 us (5%)
    unnamed x1, blocking collectives  41.9 us
    all_gather x1, blocking collectives, shards(): lax.all_gather(text_values, 'tile', axis=0, tiled=True)  21.4 us
    all_gather x1, blocking collectives, shards(): lax.all_gather(text_keys, 'tile', axis=0, tiled=True)  19.6 us
    ppermute x2, starting transfers between devices, passed_along(): lax.ppermute(value, axis, [(source, source + steps) for source in range(f...  7.75 us
    unnamed x15, local copies, waits for them, and re-layouts  4.48 us
    dot_general x4, matrix products, fold_block(): jnp.einsum('hqk,khd->hqd', weights, value_heads, preferred_element_type=j...  3.48 us
    reduce_sum x4, other arithmetic, fold_block(): row_total = row_total * scale_down + jnp.sum(exp_terms, axis=-1)  2.97 us
    dot_general x4, matrix products, fold_block(): jnp.einsum('qhd,khd->hqk', query_heads, key_heads, preferred_element_type...  2.9 us
  transfers between devices with their start and end apart: 2, of which 0 were waited for; matrix products, arithmetic and copies ran while one was open for 5% of the time, Pallas kernels for 0%

commit v1 on v0

--- a/solution.py
+++ b/solution.py
@@ -42,12 +42,33 @@
     return (new_top, row_total, summed)
 
 
+def text_pieces(text_keys, text_values, text_mask, group_count, lane_width):
+    count = lax.axis_size("tile")
+    rows = text_keys.shape[0]
+    flags = jnp.broadcast_to(text_mask.astype(jnp.bfloat16)[:, None], (rows, 128))
+    per_group = jnp.stack(
+        [
+            jnp.concatenate(
+                [
+                    text_keys[:, g * lane_width : (g + 1) * lane_width],
+                    text_values[:, g * lane_width : (g + 1) * lane_width],
+                    flags,
+                ],
+                axis=1,
+            )
+            for g in range(group_count)
+        ]
+    )
+    outgoing = jnp.tile(per_group, (count // group_count, 1, 1)).reshape(count * rows, 2 * lane_width + 128)
+    got = lax.all_to_all(outgoing, "tile", 0, 0, tiled=True)
+    return got[:, :lane_width], got[:, lane_width : 2 * lane_width], got[:, 2 * lane_width] > 0.5
+
+
 def shards(queries, keys, values, text_keys, text_values, text_mask):
     tokens = queries.shape[1]
     lane_width = queries.shape[2]
     head_count = lane_width // HEAD_DIM
     query_heads = queries[0].reshape(tokens, head_count, HEAD_DIM)
-    own_pair = jnp.stack([keys[0], values[0]])
     group_count = HEAD_GROUPS
     tiles_all = lax.axis_size("tile") // group_count
     grid_w = min(4, tiles_all)
@@ -60,7 +81,11 @@
     w_pos = tile_id % grid_w
     h_pos = tile_id // grid_w % grid_h
     f_pos = tile_id // (grid_w * grid_h)
-    local_frame = jnp.arange(tokens, dtype=jnp.int32) // (TS * TS)
+    key_rows = tokens
+    if grid_f == 1:
+        key_rows = min(tokens, frames_valid * TS * TS)
+    own_pair = jnp.stack([keys[0, :key_rows], values[0, :key_rows]])
+    local_frame = jnp.arange(key_rows, dtype=jnp.int32) // (TS * TS)
 
     def keep_mask(off_frame, off_height, off_width):
         inside = (
@@ -78,26 +103,8 @@
         jnp.zeros((head_count, tokens), jnp.float32),
         jnp.zeros((head_count, tokens, HEAD_DIM), jnp.float32),
     )
-    text_flags = text_mask.astype(jnp.bfloat16)
-    piece_keys = lax.dynamic_slice_in_dim(
-        lax.all_gather(text_keys, "tile", axis=0, tiled=True),
-        head_group * lane_width,
-        lane_width,
-        1,
-    )
-    piece_values = lax.dynamic_slice_in_dim(
-        lax.all_gather(text_values, "tile", axis=0, tiled=True),
-        head_group * lane_width,
-        lane_width,
-        1,
-    )
-    running = fold_block(
-        running,
-        query_heads,
-        piece_keys,
-        piece_values,
-        lax.all_gather(text_flags, "tile", axis=0, tiled=True) > 0.5,
-    )
+    piece_keys, piece_values, text_keep = text_pieces(text_keys, text_values, text_mask, group_count, lane_width)
+    running = fold_block(running, query_heads, piece_keys, piece_values, text_keep)
     running = fold_block(running, query_heads, own_pair[0], own_pair[1], keep_mask(0, 0, 0))
     width_set = {0: own_pair}
     for off_width in (-1, 1):

time: 111 us -> 45.6 us (0.41)
  the two profiles are of different devices: /device:TPU:0 before, /device:TPU:18 now
where the time goes in v1:
time: 45.6 us; the launch traced here: 45.1 us
  starting transfers between devices  11 us (24%)
  local copies, waits for them, and re-layouts  10.3 us (23%)
  waiting for transfers between devices  9.76 us (21%)
  matrix products  7.83 us (17%)
  other arithmetic  5.85 us (13%)
    ppermute x2, waiting for transfers between devices, passed_along(): lax.ppermute(value, axis, [(source, source + steps) for source in range(f...  6.67 us
    ppermute x2, starting transfers between devices, passed_along(): lax.ppermute(value, axis, [(source, source + steps) for source in range(f...  5.88 us
    all_to_all x1, starting transfers between devices, text_pieces(): got = lax.all_to_all(outgoing, 'tile', 0, 0, tiled=True)  5.17 us
    dot_general x4, matrix products, fold_block(): jnp.einsum('qhd,khd->hqk', query_heads, key_heads, preferred_element_type...  4.97 us
    reduce_sum x4, other arithmetic, fold_block(): row_total = row_total * scale_down + jnp.sum(exp_terms, axis=-1)  4.23 us
    all_to_all x1, waiting for transfers between devices, text_pieces(): got = lax.all_to_all(outgoing, 'tile', 0, 0, tiled=True)  3.09 us
    dot_general x4, matrix products, fold_block(): jnp.einsum('hqk,khd->hqd', weights, value_heads, preferred_element_type=j...  2.86 us
    unnamed x17, local copies, waits for them, and re-layouts  2.62 us
  transfers between devices with their start and end apart: 3, of which 3 were waited for; matrix products, arithmetic and copies ran while one was open for 20% of the time, Pallas kernels for 0%

profile of v1, /device:TPU:18, one launch (start us, length us, event | category | flops | bytes accessed | tf_op | source)
XLA Modules:
  0.0 45.1 jit_solution(307559780185493664)
XLA Ops:
  0.0 0.0 copy-start.6
  0.0 0.0 copy-start.5
  0.0 0.0 copy-start.4
  0.0 1.0 %slice.62 = bf16[1,384,384]{2,1,0:T(8,128)(2,1)S(1)} slice(bf16[1,512,384]{2,1,0:T(8,128)(2,1)} %param.7), slice={[0:1], [0:384], [0:384]} | slice | bytes 589824 | tf_op jit(solution)/shard_map/slice | solution.py:87
  1.0 0.2 copy.68
  1.2 1.0 %slice.63 = bf16[1,384,384]{2,1,0:T(8,128)(2,1)S(1)} slice(bf16[1,512,384]{2,1,0:T(8,128)(2,1)} %param.8), slice={[0:1], [0:384], [0:384]} | slice | bytes 589824 | tf_op jit(solution)/shard_map/slice | solution.py:87
  2.2 0.2 copy.69
  2.5 0.1 fusion.72
  2.6 2.4 %collective-permute-start.1 = (bf16[2,384,384]{1,2,0:T(8,128)(2,1)S(1)}, bf16[2,384,384]{1,2,0:T(8,128)(2,1)S(1)}, u32[]{:S(2)}, u32[]{:S(2)}) collective-permute-start(bf16[2,384,384]{1,2,0:T(8,128)(2,1)S(1)} %get-tuple-element.16), channel_id=1, source_target_pairs={{4,0},{5,1},{6,2},{7,3},{8,4},{9,5},{10,6},{11,7},{12,8},{13,9},{1... | collective-permute-start | bytes 1769480 | tf_op jit(solution)/shard_map/ppermute | solution.py:19
  4.9 3.5 %collective-permute-start = (bf16[2,384,384]{1,2,0:T(8,128)(2,1)S(1)}, bf16[2,384,384]{1,2,0:T(8,128)(2,1)}, u32[]{:S(2)}, u32[]{:S(2)}) collective-permute-start(bf16[2,384,384]{1,2,0:T(8,128)(2,1)S(1)} %get-tuple-element.16), channel_id=1, source_target_pairs={{0,4},{1,5},{2,6},{3,7},{4,8},{5,9},{6,10},{7,11},{8,12},{9,13},{1... | collective-permute-start | bytes 1769480 | tf_op jit(solution)/shard_map/ppermute | solution.py:19
  8.5 0.0 copy-done.6
  8.5 0.0 copy-done.5
  8.5 0.0 copy-done.4
  8.5 0.1 broadcast_in_dim.98
  8.7 0.8 %tile.8 = bf16[4,4,16,896]{3,2,1,0:T(8,128)(2,1)} broadcast(bf16[4,16,896]{2,1,0:T(8,128)(2,1)S(1)} %pad_maximum_fusion.1), dimensions={1,2,3} | broadcast | bytes 573440 | tf_op jit(solution)/shard_map/tile | solution.py:62
  9.5 5.2 %all-to-all-start = ((bf16[16,16,896]{2,1,0:T(8,128)(2,1)}), bf16[16,16,896]{2,1,0:T(8,128)(2,1)S(1)}, u32[]{:S(2)}, u32[]{:S(2)}) async-start(bf16[16,16,896]{2,1,0:T(8,128)(2,1)} %bitcast.4), calls=%async_computation | async-start | bytes 917504 | tf_op jit(solution)/shard_map/all_to_all | solution.py:63
  14.6 1.2 %copy.39 = bf16[1,512,384]{1,2,0:T(8,128)(2,1)S(1)} copy(bf16[1,512,384]{2,1,0:T(8,128)(2,1)} %param.6) | data formatting | bytes 786432 | tf_op args[0]
  15.9 2.0 %fusion.4 = (f32[3,512]{1,0:T(4,128)S(1)}, f32[3,512,384]{1,2,0:T(8,128)}) fusion(pred[384]{0:T(512)(128)(4,1)S(1)} %get-tuple-element.43, bf16[512,3,128]{0,2,1:T(8,128)(2,1)S(1)} %bitcast.165, bf16[384,3,128]{0,2,1:T(8,128)(2,1)S(1)} %bitcast.169), kind=kOutput, calls=%fused_computation.12 | convolution fusion | flops 152762880 | bytes 3053952 | tf_op jit(solution)/shard_map/qhd,khd->hqk/dot_general | solution.py:31
  17.9 2.8 %collective-permute-done.1 = bf16[2,384,384]{1,2,0:T(8,128)(2,1)S(1)} collective-permute-done((bf16[2,384,384]{1,2,0:T(8,128)(2,1)S(1)}, bf16[2,384,384]{1,2,0:T(8,128)(2,1)S(1)}, u32[]{:S(2)}, u32[]{:S(2)}) %collective-permute-start.1) | collective-permute-done | bytes 589856 | tf_op jit(solution)/shard_map/ppermute | solution.py:19
  20.7 3.8 %collective-permute-done = bf16[2,384,384]{1,2,0:T(8,128)(2,1)} collective-permute-done((bf16[2,384,384]{1,2,0:T(8,128)(2,1)S(1)}, bf16[2,384,384]{1,2,0:T(8,128)(2,1)}, u32[]{:S(2)}, u32[]{:S(2)}) %collective-permute-start) | collective-permute-done | bytes 589856 | tf_op jit(solution)/shard_map/ppermute | solution.py:19
  24.5 1.3 %maximum_bitcast_fusion = bf16[1,3,2,384,384]{3,4,2,1,0:T(8,128)(2,1)S(1)} fusion(bf16[1,2,384,384]{2,3,1,0:T(8,128)(2,1)S(1)} %bitcast.177, bf16[1,2,384,384]{2,3,1,0:T(8,128)(2,1)S(1)} %get-tuple-element.15, bf16[1,2,384,384]{2,3,1,0:T(8,128)(2,1)} %bitcast.16), kind=kLoop, calls=%fused_computation.13 | loop fusion | flops 1769472 | bytes 3538944 | tf_op jit(solution)/shard_map/stack | solution.py:121
  25.8 0.9 %fusion.76 = (bf16[1,1,1,384,384]{3,4,2,1,0:T(8,128)(2,1)}, bf16[1,1,1,384,384]{3,4,2,1,0:T(8,128)(2,1)}, bf16[1,1,1,384,384]{3,4,2,1,0:T(8,128)(2,1)S(1)}, bf16[1,1,1,384,384]{3,4,2,1,0:T(8,128)(2,1)S(1)}) fusion(bf16[1,3,2,384,384]{3,4,2,1,0:T(8,128)(2,1)S(1)} %maximum_bitcast_fusion), kind=kLoop, calls=%fused_computation.111 | loop fusion | bytes 2359296 | tf_op jit(solution)/shard_map/slice | solution.py:132
  26.8 2.0 %bitcast_reduce_fusion = (f32[3,512]{1,0:T(4,128)S(1)}, f32[3,384,512]{2,1,0:T(8,128)}) fusion(pred[384]{0:T(512)(128)(4,1)S(1)} %get-tuple-element.42, bf16[384,3,128]{0,2,1:T(8,128)(2,1)S(1)} %bitcast.173, bf16[512,3,128]{0,2,1:T(8,128)(2,1)S(1)} %bitcast.166), kind=kOutput, calls=%fused_computation.1 | convolution fusion | flops 152762880 | bytes 3053952 | tf_op jit(solution)/shard_map/qhd,khd->hqk/dot_general | solution.py:31
  28.7 0.6 %bitcast_reduce_fusion.1 = (f32[3,512]{1,0:T(4,128)S(1)}, f32[3,384,512]{2,1,0:T(8,128)S(1)}) fusion(pred[384]{0:T(512)(128)(4,1)S(1)} %broadcast_and_fusion.1, bf16[384,3,128]{0,2,1:T(8,128)(2,1)S(1)} %bitcast.172, bf16[512,3,128]{0,2,1:T(8,128)(2,1)S(1)} %bitcast.167), kind=kOutput, calls=%fused_computation.5 | convolution fusion | flops 152762880 | bytes 3053952 | tf_op jit(solution)/shard_map/qhd,khd->hqk/dot_general | solution.py:31
  29.3 3.1 %all-to-all-done = bf16[16,16,896]{2,1,0:T(8,128)(2,1)S(1)} async-done(((bf16[16,16,896]{2,1,0:T(8,128)(2,1)}), bf16[16,16,896]{2,1,0:T(8,128)(2,1)S(1)}, u32[]{:S(2)}, u32[]{:S(2)}) %all-to-all-start) | async-done | bytes 458784 | tf_op jit(solution)/shard_map/all_to_all | solution.py:63
  32.4 0.1 compare_reduce_fusion
  32.5 0.8 %fusion.77 = (bf16[256,384]{1,0:T(8,128)(2,1)}, bf16[256,384]{1,0:T(8,128)(2,1)}) fusion(bf16[256,896]{1,0:T(8,128)(2,1)S(1)} %bitcast.171), kind=kLoop, calls=%fused_computation.112 | loop fusion | bytes 786432 | tf_op jit(solution)/shard_map/slice | solution.py:64
  33.3 1.1 %copy.42 = bf16[256,384]{0,1:T(8,128)(2,1)S(1)} copy(bf16[256,384]{1,0:T(8,128)(2,1)} %get-tuple-element.17) | data formatting | bytes 393216 | tf_op jit(solution)/shard_map/slice | solution.py:64
  34.4 1.1 %copy.38 = bf16[256,384]{0,1:T(8,128)(2,1)S(1)} copy(bf16[256,384]{1,0:T(8,128)(2,1)} %get-tuple-element.18) | data formatting | bytes 393216 | tf_op jit(solution)/shard_map/slice | solution.py:64
  35.5 0.0 copy-start.1
  35.5 0.0 copy-start.3
  35.5 0.4 bitcast_reduce_fusion.2
  35.9 2.6 %fusion.9 = f32[3,512]{1,0:T(4,128)S(1)} fusion(f32[3,384,512]{2,1,0:T(8,128)} %get-tuple-element.35, f32[3,512]{1,0:T(4,128)S(1)} %get-tuple-element.8, pred[384]{0:T(512)(128)(4,1)S(1)} %get-tuple-element.42), kind=kLoop, calls=%fused_computation.18 | loop fusion | flops 2947584 | bytes 2371968 | tf_op jit(solution)/shard_map/reduce_sum | solution.py:37
  38.5 0.0 copy-start
  38.5 0.0 copy-done.1
  38.5 0.0 copy-done.3
  38.5 0.8 %convolution_bitcast_fusion = f32[512,3,128]{0,2,1:T(8,128)S(1)} fusion(bf16[384,3,128]{0,2,1:T(8,128)(2,1)S(1)} %bitcast.180, f32[3,384,512]{2,1,0:T(8,128)S(1)} %copy-done.1, f32[3,512]{1,0:T(4,128)S(1)} %get-tuple-element.8, pred[384]{0:T(512)(128)(4,1)S(1)} %get-tuple-element.42), kind=kOutput, calls=%fused_computation.25 | convolution fusion | flops 153944064 | bytes 3447168 | tf_op jit(solution)/shard_map/hqk,khd->hqd/dot_general | solution.py:39
  39.3 0.8 %copy-done = f32[3,512,384]{1,2,0:T(8,128)S(1)} copy-done((f32[3,512,384]{1,2,0:T(8,128)S(1)}, f32[3,512,384]{1,2,0:T(8,128)}, u32[]{:S(2)}) %copy-start) | copy-done | bytes 2359320
  40.2 0.7 %fusion.5 = f32[3,512]{1,0:T(4,128)S(1)} fusion(f32[3,512,384]{1,2,0:T(8,128)S(1)} %copy-done, f32[3,512]{1,0:T(4,128)S(1)} %get-tuple-element.10, pred[384]{0:T(512)(128)(4,1)S(1)} %get-tuple-element.43), kind=kLoop, calls=%fused_computation.14 | loop fusion | flops 2947584 | bytes 2371968 | tf_op jit(solution)/shard_map/reduce_sum | solution.py:37
  40.8 0.8 %convolution_bitcast_fusion.2 = f32[512,3,128]{0,2,1:T(8,128)S(1)} fusion(bf16[384,3,128]{0,2,1:T(8,128)(2,1)S(1)} %bitcast.174, f32[3,512,384]{1,2,0:T(8,128)S(1)} %copy-done, f32[3,512]{1,0:T(4,128)S(1)} %get-tuple-element.10, pred[384]{0:T(512)(128)(4,1)S(1)} %get-tuple-element.43), kind=kOutput, calls=%fused_computation.27 | convolution fusion | flops 153944064 | bytes 3447168 | tf_op jit(solution)/shard_map/hqk,khd->hqd/dot_general | solution.py:39
  41.7 0.7 %fusion.7 = f32[3,512]{1,0:T(4,128)S(1)} fusion(f32[3,384,512]{2,1,0:T(8,128)S(1)} %get-tuple-element.37, f32[3,512]{1,0:T(4,128)S(1)} %get-tuple-element.9, pred[384]{0:T(512)(128)(4,1)S(1)} %broadcast_and_fusion.1), kind=kLoop, calls=%fused_computation.16 | loop fusion | flops 2947584 | bytes 2371968 | tf_op jit(solution)/shard_map/reduce_sum | solution.py:37
  42.3 0.0 copy-start.2
  42.4 0.3 fusion.21
  42.7 0.4 fusion.16
  43.1 0.2 copy-done.2
  43.3 0.8 %fusion.23 = bf16[512,3,128]{0,2,1:T(8,128)(2,1)S(1)} fusion(f32[512,3,128]{0,2,1:T(8,128)S(1)} %convolution_bitcast_fusion, f32[512,3,128]{0,2,1:T(8,128)S(1)} %fusion.16, bf16[384,3,128]{0,2,1:T(8,128)(2,1)S(1)} %bitcast.179, f32[3,384,512]{2,1,0:T(8,128)S(1)} %get-tuple-element.37, f32[3,512]{1,0:T(4,128)S(1)} %get-tuple-element.9, ...), kind=kOutput, calls=%fused_computation.39 | convolution fusion | flops 154927104 | bytes 4639104 | tf_op jit(solution)/shard_map/hqk,khd->hqd/dot_general | solution.py:39
  44.1 0.9 %copy.55 = bf16[1,512,384]{2,1,0:T(8,128)(2,1)} copy(bf16[1,512,384]{1,2,0:T(8,128)(2,1)S(1)} %bitcast.178) | data formatting | bytes 786432 | tf_op jit(solution)/shard_map/convert_element_type | solution.py:147
  (8 shorter events, 0.1 us)
Async XLA Ops:
  0.0 8.5 %copy-start.6 = (s32[16]{0:T(128)S(1)}, s32[16]{0:T(128)}, u32[]{:S(2)}) copy-start(s32[16]{0:T(128)} %param.11) | copy-start | bytes 196
  0.0 8.5 %copy-start.5 = (bf16[16,1536]{1,0:T(8,128)(2,1)S(1)}, bf16[16,1536]{1,0:T(8,128)(2,1)}, u32[]{:S(2)}) copy-start(bf16[16,1536]{1,0:T(8,128)(2,1)} %param.10) | copy-start | bytes 147460
  0.0 8.5 %copy-start.4 = (bf16[16,1536]{1,0:T(8,128)(2,1)S(1)}, bf16[16,1536]{1,0:T(8,128)(2,1)}, u32[]{:S(2)}) copy-start(bf16[16,1536]{1,0:T(8,128)(2,1)} %param.9) | copy-start | bytes 147460
  2.6 18.1 %collective-permute-start.1 = (bf16[2,384,384]{1,2,0:T(8,128)(2,1)S(1)}, bf16[2,384,384]{1,2,0:T(8,128)(2,1)S(1)}, u32[]{:S(2)}, u32[]{:S(2)}) collective-permute-start(bf16[2,384,384]{1,2,0:T(8,128)(2,1)S(1)} %get-tuple-element.16), channel_id=1, source_target_pairs={{4,0},{5,1},{6,2},{7,3},{8,4},{9,5},{10,6},{11,7},{12,8},{13,9},{1... | collective-permute-start | bytes 1769480 | tf_op jit(solution)/shard_map/ppermute | solution.py:19
  4.9 19.6 %collective-permute-start = (bf16[2,384,384]{1,2,0:T(8,128)(2,1)S(1)}, bf16[2,384,384]{1,2,0:T(8,128)(2,1)}, u32[]{:S(2)}, u32[]{:S(2)}) collective-permute-start(bf16[2,384,384]{1,2,0:T(8,128)(2,1)S(1)} %get-tuple-element.16), channel_id=1, source_target_pairs={{0,4},{1,5},{2,6},{3,7},{4,8},{5,9},{6,10},{7,11},{8,12},{9,13},{1... | collective-permute-start | bytes 1769480 | tf_op jit(solution)/shard_map/ppermute | solution.py:19
  9.5 22.9 %all-to-all-start = ((bf16[16,16,896]{2,1,0:T(8,128)(2,1)}), bf16[16,16,896]{2,1,0:T(8,128)(2,1)S(1)}, u32[]{:S(2)}, u32[]{:S(2)}) async-start(bf16[16,16,896]{2,1,0:T(8,128)(2,1)} %bitcast.4), calls=%async_computation | async-start | bytes 917504 | tf_op jit(solution)/shard_map/all_to_all | solution.py:63
  35.5 3.1 %copy-start.1 = (f32[3,384,512]{2,1,0:T(8,128)S(1)}, f32[3,384,512]{2,1,0:T(8,128)}, u32[]{:S(2)}) copy-start(f32[3,384,512]{2,1,0:T(8,128)} %get-tuple-element.35) | copy-start | bytes 7077892
  35.5 3.1 %copy-start.3 = (bf16[1,1,1,384,384]{3,4,2,1,0:T(8,128)(2,1)S(1)}, bf16[1,1,1,384,384]{3,4,2,1,0:T(8,128)(2,1)}, u32[]{:S(2)}) copy-start(bf16[1,1,1,384,384]{3,4,2,1,0:T(8,128)(2,1)} %get-tuple-element.12) | copy-start | bytes 884740
  38.5 1.7 %copy-start = (f32[3,512,384]{1,2,0:T(8,128)S(1)}, f32[3,512,384]{1,2,0:T(8,128)}, u32[]{:S(2)}) copy-start(f32[3,512,384]{1,2,0:T(8,128)} %get-tuple-element.39) | copy-start | bytes 7077892
  42.3 1.0 %copy-start.2 = (bf16[1,1,1,384,384]{3,4,2,1,0:T(8,128)(2,1)S(1)}, bf16[1,1,1,384,384]{3,4,2,1,0:T(8,128)(2,1)}, u32[]{:S(2)}) copy-start(bf16[1,1,1,384,384]{3,4,2,1,0:T(8,128)(2,1)} %get-tuple-element.11) | copy-start | bytes 884740

commit v2 on v1

--- a/solution.py
+++ b/solution.py
@@ -1,8 +1,11 @@
+import functools
 import math
 
 import jax
 import jax.numpy as jnp
 from jax import lax
+from jax.experimental import pallas as pl
+from jax.experimental.pallas import tpu as pltpu
 from jax.sharding import PartitionSpec as P
 
 TS = 8
@@ -40,6 +43,67 @@
         "hqk,khd->hqd", weights, value_heads, preferred_element_type=jnp.float32
     )
     return (new_top, row_total, summed)
+
+
+def window_kernel(block_count, q_ref, *refs):
+    key_refs = refs[:block_count]
+    value_refs = refs[block_count : 2 * block_count]
+    keep_refs = refs[2 * block_count : 3 * block_count]
+    out_ref = refs[3 * block_count]
+    query = q_ref[...]
+    scores = []
+    for b in range(block_count):
+        s = lax.dot_general(
+            query, key_refs[b][...], (((1,), (1,)), ((), ())), preferred_element_type=jnp.float32
+        )
+        s = s * (1.0 / math.sqrt(HEAD_DIM))
+        scores.append(jnp.where(keep_refs[b][...] > 0.5, s, MASKED))
+    top = scores[0].max(axis=1, keepdims=True)
+    for s in scores[1:]:
+        top = jnp.maximum(top, s.max(axis=1, keepdims=True))
+    total = jnp.zeros_like(top)
+    summed = jnp.zeros(out_ref.shape, jnp.float32)
+    for b in range(block_count):
+        terms = jnp.where(keep_refs[b][...] > 0.5, jnp.exp(scores[b] - top), 0.0)
+        total = total + terms.sum(axis=1, keepdims=True)
+        summed = summed + jnp.dot(
+            terms.astype(jnp.bfloat16), value_refs[b][...], preferred_element_type=jnp.float32
+        )
+    out_ref[...] = (summed / total).astype(out_ref.dtype)
+
+
+def window_attention(query_rows, blocks):
+    tokens, lane_width = query_rows.shape
+    head_count = lane_width // HEAD_DIM
+    q_chunk = 256 if tokens % 256 == 0 else tokens
+    chunks = tokens // q_chunk
+    key_specs, value_specs, keep_specs, key_args, value_args, keep_args = [], [], [], [], [], []
+    key_total = 0
+    for source, key_at, value_at, keep in blocks:
+        rows = keep.shape[1]
+        key_total += rows
+        if source.ndim == 3:
+            key_specs.append(pl.BlockSpec((pl.Squeezed(), rows, HEAD_DIM), lambda h, i, s=key_at: (s, 0, h)))
+            value_specs.append(pl.BlockSpec((pl.Squeezed(), rows, HEAD_DIM), lambda h, i, s=value_at: (s, 0, h)))
+        else:
+            key_specs.append(pl.BlockSpec((rows, HEAD_DIM), lambda h, i, s=key_at: (0, s + h)))
+            value_specs.append(pl.BlockSpec((rows, HEAD_DIM), lambda h, i, s=value_at: (0, s + h)))
+        keep_specs.append(pl.BlockSpec((1, rows), lambda h, i: (0, 0)))
+        key_args.append(source)
+        value_args.append(source)
+        keep_args.append(keep)
+    flops = 4 * tokens * key_total * lane_width
+    moved = 2 * (2 * tokens * lane_width + 2 * key_total * lane_width)
+    return pl.pallas_call(
+        functools.partial(window_kernel, len(blocks)),
+        out_shape=jax.ShapeDtypeStruct((tokens, lane_width), jnp.bfloat16),
+        grid=(head_count, chunks),
+        in_specs=[pl.BlockSpec((q_chunk, HEAD_DIM), lambda h, i: (i, h))] + key_specs + value_specs + keep_specs,
+        out_specs=pl.BlockSpec((q_chunk, HEAD_DIM), lambda h, i: (i, h)),
+        cost_estimate=pl.CostEstimate(
+            flops=flops, transcendentals=tokens * key_total * head_count, bytes_accessed=moved
+        ),
+    )(query_rows, *key_args, *value_args, *keep_args)
 
 
 def text_pieces(text_keys, text_values, text_mask, group_count, lane_width):
@@ -61,7 +125,7 @@
     )
     outgoing = jnp.tile(per_group, (count // group_count, 1, 1)).reshape(count * rows, 2 * lane_width + 128)
     got = lax.all_to_all(outgoing, "tile", 0, 0, tiled=True)
-    return got[:, :lane_width], got[:, lane_width : 2 * lane_width], got[:, 2 * lane_width] > 0.5
+    return got, got[:, 2 * lane_width] > 0.5
 
 
 def shards(queries, keys, values, text_keys, text_values, text_mask):
@@ -103,12 +167,20 @@
         jnp.zeros((head_count, tokens), jnp.float32),
         jnp.zeros((head_count, tokens, HEAD_DIM), jnp.float32),
     )
-    piece_keys, piece_values, text_keep = text_pieces(text_keys, text_values, text_mask, group_count, lane_width)
-    running = fold_block(running, query_heads, piece_keys, piece_values, text_keep)
-    running = fold_block(running, query_heads, own_pair[0], own_pair[1], keep_mask(0, 0, 0))
+    text_got, text_keep = text_pieces(text_keys, text_values, text_mask, group_count, lane_width)
     width_set = {0: own_pair}
     for off_width in (-1, 1):
         width_set[off_width] = passed_along(own_pair, "tile", -off_width * group_count)
+    if grid_h == 1 and grid_f == 1:
+        as_row = lambda keep: keep.astype(jnp.float32)[None, :]
+        blocks = [(text_got, 0, head_count, as_row(text_keep))]
+        for off_width in (-1, 0, 1):
+            blocks.append((width_set[off_width], 0, 1, as_row(keep_mask(0, 0, off_width))))
+        return window_attention(queries[0], blocks)[None]
+    piece_keys = text_got[:, :lane_width]
+    piece_values = text_got[:, lane_width : 2 * lane_width]
+    running = fold_block(running, query_heads, piece_keys, piece_values, text_keep)
+    running = fold_block(running, query_heads, own_pair[0], own_pair[1], keep_mask(0, 0, 0))
     width_offsets = sorted(width_set)
     row_stack = jnp.stack([width_set[spot] for spot in width_offsets])
     height_set = {0: row_stack}

time: 45.6 us -> 43.2 us (0.947)
  the two profiles are of different devices: /device:TPU:18 before, /device:TPU:10 now
where the time goes in v2:
time: 43.2 us; the launch traced here: 42.8 us
  waiting for transfers between devices  16.1 us (37%)
  starting transfers between devices  12.1 us (28%)
  Pallas kernels  7.89 us (18%)
  local copies, waits for them, and re-layouts  3.75 us (9%)
  other arithmetic  2.7 us (6%)
    ppermute x2, waiting for transfers between devices, passed_along(): lax.ppermute(value, axis, [(source, source + steps) for source in range(f...  12.2 us
    pallas_call x1, Pallas kernels, window_attention(): pl.pallas_call(functools.partial(window_kernel, len(blocks)), out_shape=j...  7.89 us
    all_to_all x1, starting transfers between devices, text_pieces(): got = lax.all_to_all(outgoing, 'tile', 0, 0, tiled=True)  6.3 us
    ppermute x2, starting transfers between devices, passed_along(): lax.ppermute(value, axis, [(source, source + steps) for source in range(f...  5.84 us
    all_to_all x1, waiting for transfers between devices, text_pieces(): got = lax.all_to_all(outgoing, 'tile', 0, 0, tiled=True)  3.99 us
    convert_element_type x3, other arithmetic, shards(): as_row = lambda keep: keep.astype(jnp.float32)[None, :]  1.94 us
    slice x4, local copies, waits for them, and re-layouts, shards(): own_pair = jnp.stack([keys[0, :key_rows], values[0, :key_rows]])  1.04 us
    unnamed x8, local copies, waits for them, and re-layouts  0.99 us
  transfers between devices with their start and end apart: 3, of which 2 were waited for; matrix products, arithmetic and copies ran while one was open for 5% of the time, Pallas kernels for 0%

profile of v2, /device:TPU:10, one launch (start us, length us, event | category | flops | bytes accessed | tf_op | source)
XLA Modules:
  0.0 42.8 jit_solution(12615515960487552931)
XLA Ops:
  0.0 0.7 %convert_element_type.46 = bf16[16]{0:T(256)(128)(2,1)S(1)} convert(s32[16]{0:T(128)} %param.11) | non-fusion elementwise | flops 16 | bytes 96 | tf_op jit(solution)/shard_map/convert_element_type | solution.py:112
  0.7 0.8 %fusion.6 = (bf16[16,384]{1,0:T(8,128)(2,1)S(1)}, bf16[16,384]{1,0:T(8,128)(2,1)S(1)}, bf16[16,384]{1,0:T(8,128)(2,1)S(1)}, bf16[16,384]{1,0:T(8,128)(2,1)S(1)},...) fusion(bf16[16,1536]{1,0:T(8,128)(2,1)} %param.9, ...), kind=kLoop, calls=%fused_computation.20 | loop fusion | bytes 196608 | tf_op jit(solution)/shard_map/slice | solution.py:117
  1.5 0.1 broadcast_in_dim.4
  1.6 0.8 %tile.8 = bf16[4,4,16,896]{3,2,1,0:T(8,128)(2,1)} broadcast(bf16[4,16,896]{2,1,0:T(8,128)(2,1)S(1)} %pad_maximum_fusion.1), dimensions={1,2,3} | broadcast | bytes 573440 | tf_op jit(solution)/shard_map/tile | solution.py:126
  2.4 6.3 %all-to-all-start = ((bf16[16,16,896]{2,1,0:T(8,128)(2,1)}), bf16[16,16,896]{2,1,0:T(8,128)(2,1)S(1)}, u32[]{:S(2)}, u32[]{:S(2)}) async-start(bf16[16,16,896]{2,1,0:T(8,128)(2,1)} %bitcast.5), calls=%async_computation | async-start | bytes 917504 | tf_op jit(solution)/shard_map/all_to_all | solution.py:127
  8.7 0.0 slice-start
  8.7 0.0 slice-start.1
  8.8 0.9 %slice-done = bf16[1,384,384]{2,1,0:T(8,128)(2,1)S(1)} async-done(((bf16[1,512,384]{2,1,0:T(8,128)(2,1)}), bf16[1,384,384]{2,1,0:T(8,128)(2,1)S(1)}, s32[]{:S(2)}) %slice-start) | async-done | bytes 294936 | tf_op jit(solution)/shard_map/slice | solution.py:151
  9.7 0.1 slice-done.1
  9.8 0.1 pad_maximum_fusion.refs_2_.refs_6_
  9.9 0.0 copy-start
  9.9 2.0 %collective-permute-start.1 = (bf16[2,384,384]{2,1,0:T(8,128)(2,1)S(1)}, bf16[2,384,384]{2,1,0:T(8,128)(2,1)S(1)}, u32[]{:S(2)}, u32[]{:S(2)}) collective-permute-start(bf16[2,384,384]{2,1,0:T(8,128)(2,1)S(1)} %pad_maximum_fusion.refs_2_.refs_6_), channel_id=1, source_target_pairs={{4,0},{5,1},{6,2},{7,3},{8,4},{9,5},{10,6},{11,7},{12,8},{13,9},{1... | collective-permute-start | bytes 1769480 | tf_op jit(solution)/shard_map/ppermute | solution.py:22
  11.9 3.8 %collective-permute-start = (bf16[2,384,384]{2,1,0:T(8,128)(2,1)S(1)}, bf16[2,384,384]{2,1,0:T(8,128)(2,1)S(1)}, u32[]{:S(2)}, u32[]{:S(2)}) collective-permute-start(bf16[2,384,384]{2,1,0:T(8,128)(2,1)S(1)} %pad_maximum_fusion.refs_2_.refs_6_), channel_id=1, source_target_pairs={{0,4},{1,5},{2,6},{3,7},{4,8},{5,9},{6,10},{7,11},{8,12},{9,13},{1... | collective-permute-start | bytes 1769480 | tf_op jit(solution)/shard_map/ppermute | solution.py:22
  15.8 0.6 %and_convert_fusion.2.refs_9_ = f32[1,384]{1,0:T(1,128)} fusion(pred[]{:T(512)S(6)} %and.126, s32[]{:T(128)S(6)} %mul.2), kind=kLoop, calls=%fused_computation.13 | loop fusion | flops 4608 | bytes 1541 | tf_op jit(solution)/shard_map/convert_element_type | solution.py:175
  16.4 0.6 %and_convert_fusion = (f32[1,384]{1,0:T(1,128)}, f32[1,384]{1,0:T(1,128)}) fusion(pred[]{:T(512)S(6)} %and.135, s32[]{:T(128)S(6)} %mul.2, pred[]{:T(512)S(6)} %and.131), kind=kLoop, calls=%fused_computation.11 | loop fusion | flops 5376 | bytes 3078 | tf_op jit(solution)/shard_map/convert_element_type | solution.py:175
  17.0 4.0 %all-to-all-done = bf16[16,16,896]{2,1,0:T(8,128)(2,1)S(1)} async-done(((bf16[16,16,896]{2,1,0:T(8,128)(2,1)}), bf16[16,16,896]{2,1,0:T(8,128)(2,1)S(1)}, u32[]{:S(2)}, u32[]{:S(2)}) %all-to-all-start) | async-done | bytes 458784 | tf_op jit(solution)/shard_map/all_to_all | solution.py:127
  21.0 0.0 copy-start.1
  21.0 0.7 %convert_reduce_fusion = f32[256]{0:T(256)} fusion(bf16[256,896]{1,0:T(8,128)(2,1)S(1)} %bitcast.13), kind=kLoop, calls=%fused_computation.1 | loop fusion | flops 512 | bytes 1536 | tf_op jit(solution)/shard_map/convert_element_type | solution.py:175
  21.7 12.1 %collective-permute-done.1.refs_3_.refs_7_ = bf16[2,384,384]{2,1,0:T(8,128)(2,1)S(1)} collective-permute-done((bf16[2,384,384]{2,1,0:T(8,128)(2,1)S(1)}, bf16[2,384,384]{2,1,0:T(8,128)(2,1)S(1)}, u32[]{:S(2)}, u32[]{:S(2)}) %collective-permute-start.1) | collective-permute-done | bytes 589856 | tf_op jit(solution)/shard_map/ppermute | solution.py:22
  33.9 0.0 copy-start.2
  33.9 0.0 collective-permute-done.refs_1_.refs_5_
  33.9 0.0 copy-start.3
  33.9 0.0 copy-done
  33.9 0.0 copy-done.1
  33.9 0.8 %copy-done.2 = bf16[2,384,384]{2,1,0:T(8,128)(2,1)} copy-done((bf16[2,384,384]{2,1,0:T(8,128)(2,1)}, bf16[2,384,384]{2,1,0:T(8,128)(2,1)S(1)}, u32[]{:S(2)}) %copy-start.2) | copy-done | bytes 589848
  34.7 0.2 copy-done.3
  34.9 7.9 %shard_map.64 = bf16[512,384]{1,0:T(8,128)(2,1)} custom-call(bf16[512,384]{1,0:T(8,128)(2,1)} %bitcast.16, bf16[256,896]{1,0:T(8,128)(2,1)} %bitcast.14, bf16[2,384,384]{2,1,0:T(8,128)(2,1)} %copy-done.3, bf16[2,384,384]{2,1,0:T(8,128)(2,1)} %copy-done, bf16[2,384,384]{2,1,0:T(8,128)(2,1)} %copy-done.2, bf16[256,896]{1,0:T(8,128)(2,1)} %bitcast.15, ...), custom_call_target="tpu_custom_call" | custom-call | flops 1107296256 | bytes 2949120 | tf_op jit(solution)/shard_map/pallas_call | solution.py:97
  (2 shorter events, 0.0 us)
Async XLA Ops:
  2.4 18.5 %all-to-all-start = ((bf16[16,16,896]{2,1,0:T(8,128)(2,1)}), bf16[16,16,896]{2,1,0:T(8,128)(2,1)S(1)}, u32[]{:S(2)}, u32[]{:S(2)}) async-start(bf16[16,16,896]{2,1,0:T(8,128)(2,1)} %bitcast.5), calls=%async_computation | async-start | bytes 917504 | tf_op jit(solution)/shard_map/all_to_all | solution.py:127
  8.7 1.0 %slice-start = ((bf16[1,512,384]{2,1,0:T(8,128)(2,1)}), bf16[1,384,384]{2,1,0:T(8,128)(2,1)S(1)}, s32[]{:S(2)}) async-start(bf16[1,512,384]{2,1,0:T(8,128)(2,1)} %param.7), calls=%async_computation.1 | async-start | bytes 589824 | tf_op jit(solution)/shard_map/slice | solution.py:151
  8.7 1.0 %slice-start.1 = ((bf16[1,512,384]{2,1,0:T(8,128)(2,1)}), bf16[1,384,384]{2,1,0:T(8,128)(2,1)S(1)}, s32[]{:S(2)}) async-start(bf16[1,512,384]{2,1,0:T(8,128)(2,1)} %param.8), calls=%async_computation.2 | async-start | bytes 589824 | tf_op jit(solution)/shard_map/slice | solution.py:151
  9.9 24.0 %copy-start = (bf16[2,384,384]{2,1,0:T(8,128)(2,1)}, bf16[2,384,384]{2,1,0:T(8,128)(2,1)S(1)}, u32[]{:S(2)}) copy-start(bf16[2,384,384]{2,1,0:T(8,128)(2,1)S(1)} %pad_maximum_fusion.refs_2_.refs_6_) | copy-start | bytes 1769476
  9.9 24.0 %collective-permute-start.1 = (bf16[2,384,384]{2,1,0:T(8,128)(2,1)S(1)}, bf16[2,384,384]{2,1,0:T(8,128)(2,1)S(1)}, u32[]{:S(2)}, u32[]{:S(2)}) collective-permute-start(bf16[2,384,384]{2,1,0:T(8,128)(2,1)S(1)} %pad_maximum_fusion.refs_2_.refs_6_), channel_id=1, source_target_pairs={{4,0},{5,1},{6,2},{7,3},{8,4},{9,5},{10,6},{11,7},{12,8},{13,9},{1... | collective-permute-start | bytes 1769480 | tf_op jit(solution)/shard_map/ppermute | solution.py:22
  11.9 22.0 %collective-permute-start = (bf16[2,384,384]{2,1,0:T(8,128)(2,1)S(1)}, bf16[2,384,384]{2,1,0:T(8,128)(2,1)S(1)}, u32[]{:S(2)}, u32[]{:S(2)}) collective-permute-start(bf16[2,384,384]{2,1,0:T(8,128)(2,1)S(1)} %pad_maximum_fusion.refs_2_.refs_6_), channel_id=1, source_target_pairs={{0,4},{1,5},{2,6},{3,7},{4,8},{5,9},{6,10},{7,11},{8,12},{9,13},{1... | collective-permute-start | bytes 1769480 | tf_op jit(solution)/shard_map/ppermute | solution.py:22
  21.0 12.9 %copy-start.1 = (bf16[16,16,896]{2,1,0:T(8,128)(2,1)}, bf16[16,16,896]{2,1,0:T(8,128)(2,1)S(1)}, u32[]{:S(2)}) copy-start(bf16[16,16,896]{2,1,0:T(8,128)(2,1)S(1)} %all-to-all-done) | copy-start | bytes 1376260
  33.9 0.8 %copy-start.2 = (bf16[2,384,384]{2,1,0:T(8,128)(2,1)}, bf16[2,384,384]{2,1,0:T(8,128)(2,1)S(1)}, u32[]{:S(2)}) copy-start(bf16[2,384,384]{2,1,0:T(8,128)(2,1)S(1)} %collective-permute-done.1.refs_3_.refs_7_) | copy-start | bytes 1769476
  33.9 1.0 %copy-start.3 = (bf16[2,384,384]{2,1,0:T(8,128)(2,1)}, bf16[2,384,384]{2,1,0:T(8,128)(2,1)S(1)}, u32[]{:S(2)}) copy-start(bf16[2,384,384]{2,1,0:T(8,128)(2,1)S(1)} %collective-permute-done.refs_1_.refs_5_) | copy-start | bytes 1769476

commit v3 on v2

--- a/solution.py
+++ b/solution.py
@@ -45,11 +45,11 @@
     return (new_top, row_total, summed)
 
 
-def window_kernel(block_count, q_ref, *refs):
+def window_kernel(block_count, carry_in, finish, q_ref, *refs):
     key_refs = refs[:block_count]
     value_refs = refs[block_count : 2 * block_count]
     keep_refs = refs[2 * block_count : 3 * block_count]
-    out_ref = refs[3 * block_count]
+    rest = refs[3 * block_count :]
     query = q_ref[...]
     scores = []
     for b in range(block_count):
@@ -61,18 +61,30 @@
     top = scores[0].max(axis=1, keepdims=True)
     for s in scores[1:]:
         top = jnp.maximum(top, s.max(axis=1, keepdims=True))
-    total = jnp.zeros_like(top)
-    summed = jnp.zeros(out_ref.shape, jnp.float32)
+    if carry_in:
+        top_in, total_in, summed_in = rest[0][...], rest[1][...], rest[2][...]
+        rest = rest[3:]
+        top = jnp.maximum(top, top_in)
+        scale_down = jnp.exp(top_in - top)
+        total = total_in * scale_down
+        summed = summed_in * scale_down
+    else:
+        total = jnp.zeros_like(top)
+        summed = None
     for b in range(block_count):
-        terms = jnp.where(keep_refs[b][...] > 0.5, jnp.exp(scores[b] - top), 0.0)
+        terms = jnp.exp(scores[b] - top)
         total = total + terms.sum(axis=1, keepdims=True)
-        summed = summed + jnp.dot(
-            terms.astype(jnp.bfloat16), value_refs[b][...], preferred_element_type=jnp.float32
-        )
-    out_ref[...] = (summed / total).astype(out_ref.dtype)
-
-
-def window_attention(query_rows, blocks):
+        part = jnp.dot(terms.astype(jnp.bfloat16), value_refs[b][...], preferred_element_type=jnp.float32)
+        summed = part if summed is None else summed + part
+    if finish:
+        rest[0][...] = (summed / total).astype(rest[0].dtype)
+    else:
+        rest[0][...] = top
+        rest[1][...] = total
+        rest[2][...] = summed
+
+
+def window_attention(query_rows, blocks, carry=None, finish=True):
     tokens, lane_width = query_rows.shape
     head_count = lane_width // HEAD_DIM
     q_chunk = 256 if tokens % 256 == 0 else tokens
@@ -92,18 +104,28 @@
         key_args.append(source)
         value_args.append(source)
         keep_args.append(keep)
+    stat_spec = pl.BlockSpec((pl.Squeezed(), q_chunk, 1), lambda h, i: (h, i, 0))
+    lane_spec = pl.BlockSpec((q_chunk, HEAD_DIM), lambda h, i: (i, h))
+    stat_shape = jax.ShapeDtypeStruct((head_count, tokens, 1), jnp.float32)
+    carry_specs = [] if carry is None else [stat_spec, stat_spec, lane_spec]
+    if finish:
+        out_shape = jax.ShapeDtypeStruct((tokens, lane_width), jnp.bfloat16)
+        out_specs = lane_spec
+    else:
+        out_shape = (stat_shape, stat_shape, jax.ShapeDtypeStruct((tokens, lane_width), jnp.float32))
+        out_specs = (stat_spec, stat_spec, lane_spec)
     flops = 4 * tokens * key_total * lane_width
-    moved = 2 * (2 * tokens * lane_width + 2 * key_total * lane_width)
+    moved = 2 * (2 * tokens * lane_width + 2 * key_total * lane_width) + 4 * 6 * tokens * lane_width
     return pl.pallas_call(
-        functools.partial(window_kernel, len(blocks)),
-        out_shape=jax.ShapeDtypeStruct((tokens, lane_width), jnp.bfloat16),
+        functools.partial(window_kernel, len(blocks), carry is not None, finish),
+        out_shape=out_shape,
         grid=(head_count, chunks),
-        in_specs=[pl.BlockSpec((q_chunk, HEAD_DIM), lambda h, i: (i, h))] + key_specs + value_specs + keep_specs,
-        out_specs=pl.BlockSpec((q_chunk, HEAD_DIM), lambda h, i: (i, h)),
+        in_specs=[lane_spec] + key_specs + value_specs + keep_specs + carry_specs,
+        out_specs=out_specs,
         cost_estimate=pl.CostEstimate(
             flops=flops, transcendentals=tokens * key_total * head_count, bytes_accessed=moved
         ),
-    )(query_rows, *key_args, *value_args, *keep_args)
+    )(query_rows, *key_args, *value_args, *keep_args, *(() if carry is None else carry))
 
 
 def text_pieces(text_keys, text_values, text_mask, group_count, lane_width):
@@ -173,10 +195,12 @@
         width_set[off_width] = passed_along(own_pair, "tile", -off_width * group_count)
     if grid_h == 1 and grid_f == 1:
         as_row = lambda keep: keep.astype(jnp.float32)[None, :]
-        blocks = [(text_got, 0, head_count, as_row(text_keep))]
-        for off_width in (-1, 0, 1):
-            blocks.append((width_set[off_width], 0, 1, as_row(keep_mask(0, 0, off_width))))
-        return window_attention(queries[0], blocks)[None]
+        carry = window_attention(queries[0], [(own_pair, 0, 1, as_row(keep_mask(0, 0, 0)))], finish=False)
+        carry = window_attention(
+            queries[0], [(text_got, 0, head_count, as_row(text_keep))], carry=carry, finish=False
+        )
+        blocks = [(width_set[off_width], 0, 1, as_row(keep_mask(0, 0, off_width))) for off_width in (-1, 1)]
+        return window_attention(queries[0], blocks, carry=carry)[None]
     piece_keys = text_got[:, :lane_width]
     piece_values = text_got[:, lane_width : 2 * lane_width]
     running = fold_block(running, query_heads, piece_keys, piece_values, text_keep)

time: 43.2 us -> 42.8 us (level)
  waiting for transfers between devices: 16.1 us -> 4.07 us
  Pallas kernels: 7.89 us -> 19.4 us
    pallas_call x1 -> x3, Pallas kernels: 7.89 us -> 19.4 us  [window_attention(): pl.pallas_call(functools.partial(window_kernel, len(blocks), carry is not...]
    ppermute x2, waiting for transfers between devices: 12.2 us -> 4.06 us  [passed_along(): lax.ppermute(value, axis, [(source, source + steps) for source in range(f...]
    all_to_all x1, waiting for transfers between devices: 3.99 us -> 0.01 us  [text_pieces(): got = lax.all_to_all(outgoing, 'tile', 0, 0, tiled=True)]
  transfers between devices with their start and end apart: 3 -> 3, of which waited for: 2 -> 2; matrix products, arithmetic and copies ran while one was open for 5% -> 5% of each run, Pallas kernels for 0% -> 29%
where the time goes in v3:
time: 42.8 us; the launch traced here: 42.1 us
  Pallas kernels  19.4 us (45%)
  starting transfers between devices  12.2 us (29%)
  waiting for transfers between devices  4.07 us (10%)
  local copies, waits for them, and re-layouts  3.63 us (8%)
  other arithmetic  2.64 us (6%)
    pallas_call x3, Pallas kernels, window_attention(): pl.pallas_call(functools.partial(window_kernel, len(blocks), carry is not...  19.4 us
    all_to_all x1, starting transfers between devices, text_pieces(): got = lax.all_to_all(outgoing, 'tile', 0, 0, tiled=True)  6.3 us
    ppermute x2, starting transfers between devices, passed_along(): lax.ppermute(value, axis, [(source, source + steps) for source in range(f...  5.88 us
    ppermute x2, waiting for transfers between devices, passed_along(): lax.ppermute(value, axis, [(source, source + steps) for source in range(f...  4.06 us
    convert_element_type x3, other arithmetic, shards(): as_row = lambda keep: keep.astype(jnp.float32)[None, :]  1.88 us
    slice x4, local copies, waits for them, and re-layouts, shards(): own_pair = jnp.stack([keys[0, :key_rows], values[0, :key_rows]])  1.04 us
    unnamed x8, local copies, waits for them, and re-layouts  0.89 us
  transfers between devices with their start and end apart: 3, of which 2 were waited for; matrix products, arithmetic and copies ran while one was open for 5% of the time, Pallas kernels for 29%

profile of v3, /device:TPU:10, one launch (start us, length us, event | category | flops | bytes accessed | tf_op | source)
XLA Modules:
  0.0 42.1 jit_solution(13130166912045145954)
XLA Ops:
  0.0 0.7 %convert_element_type.48 = bf16[16]{0:T(256)(128)(2,1)S(1)} convert(s32[16]{0:T(128)} %param.11) | non-fusion elementwise | flops 16 | bytes 96 | tf_op jit(solution)/shard_map/convert_element_type | solution.py:134
  0.7 0.8 %fusion.6 = (bf16[16,384]{1,0:T(8,128)(2,1)S(1)}, bf16[16,384]{1,0:T(8,128)(2,1)S(1)}, bf16[16,384]{1,0:T(8,128)(2,1)S(1)}, bf16[16,384]{1,0:T(8,128)(2,1)S(1)},...) fusion(bf16[16,1536]{1,0:T(8,128)(2,1)} %param.9, ...), kind=kLoop, calls=%fused_computation.20 | loop fusion | bytes 196608 | tf_op jit(solution)/shard_map/slice | solution.py:139
  1.5 0.1 broadcast_in_dim.4
  1.6 0.8 %tile.8 = bf16[4,4,16,896]{3,2,1,0:T(8,128)(2,1)} broadcast(bf16[4,16,896]{2,1,0:T(8,128)(2,1)S(1)} %pad_maximum_fusion.1), dimensions={1,2,3} | broadcast | bytes 573440 | tf_op jit(solution)/shard_map/tile | solution.py:148
  2.4 6.3 %all-to-all-start = ((bf16[16,16,896]{2,1,0:T(8,128)(2,1)}), bf16[16,16,896]{2,1,0:T(8,128)(2,1)S(1)}, u32[]{:S(2)}, u32[]{:S(2)}) async-start(bf16[16,16,896]{2,1,0:T(8,128)(2,1)} %bitcast.5), calls=%async_computation | async-start | bytes 917504 | tf_op jit(solution)/shard_map/all_to_all | solution.py:149
  8.7 0.0 slice-start
  8.7 0.0 slice-start.1
  8.7 0.9 %slice-done = bf16[1,384,384]{2,1,0:T(8,128)(2,1)S(1)} async-done(((bf16[1,512,384]{2,1,0:T(8,128)(2,1)}), bf16[1,384,384]{2,1,0:T(8,128)(2,1)S(1)}, s32[]{:S(2)}) %slice-start) | async-done | bytes 294936 | tf_op jit(solution)/shard_map/slice | solution.py:173
  9.7 0.1 slice-done.1
  9.8 0.1 pad_maximum_fusion.refs_0_.refs_1_
  9.8 0.0 copy-start
  9.8 3.4 %collective-permute-start = (bf16[2,384,384]{2,1,0:T(8,128)(2,1)S(1)}, bf16[2,384,384]{2,1,0:T(8,128)(2,1)S(1)}, u32[]{:S(2)}, u32[]{:S(2)}) collective-permute-start(bf16[2,384,384]{2,1,0:T(8,128)(2,1)S(1)} %pad_maximum_fusion.refs_0_.refs_1_), channel_id=1, source_target_pairs={{0,4},{1,5},{2,6},{3,7},{4,8},{5,9},{6,10},{7,11},{8,12},{9,13},{1... | collective-permute-start | bytes 1769480 | tf_op jit(solution)/shard_map/ppermute | solution.py:22
  13.2 2.5 %collective-permute-start.1 = (bf16[2,384,384]{2,1,0:T(8,128)(2,1)S(1)}, bf16[2,384,384]{2,1,0:T(8,128)(2,1)S(1)}, u32[]{:S(2)}, u32[]{:S(2)}) collective-permute-start(bf16[2,384,384]{2,1,0:T(8,128)(2,1)S(1)} %pad_maximum_fusion.refs_0_.refs_1_), channel_id=1, source_target_pairs={{4,0},{5,1},{6,2},{7,3},{8,4},{9,5},{10,6},{11,7},{12,8},{13,9},{1... | collective-permute-start | bytes 1769480 | tf_op jit(solution)/shard_map/ppermute | solution.py:22
  15.8 0.6 %and_convert_fusion.refs_2_ = f32[1,384]{1,0:T(1,128)} fusion(pred[]{:T(512)S(6)} %and.135, s32[]{:T(128)S(6)} %mul.2), kind=kLoop, calls=%fused_computation.11 | loop fusion | flops 4608 | bytes 1541 | tf_op jit(solution)/shard_map/convert_element_type | solution.py:197
  16.4 0.0 copy-done
  16.4 5.6 %shard_map.64 = (f32[3,512,1]{2,1,0:T(8,128)}, f32[3,512,1]{2,1,0:T(8,128)}, f32[512,384]{1,0:T(8,128)}) custom-call(bf16[512,384]{1,0:T(8,128)(2,1)} %bitcast.16, bf16[2,384,384]{2,1,0:T(8,128)(2,1)} %copy-done, bf16[2,384,384]{2,1,0:T(8,128)(2,1)} %copy-done, f32[1,384]{1,0:T(1,128)} %and_convert_fusion.refs_2_), custom_call_target="tpu_custom_call" | custom-call | flops 301989888 | bytes 6094848 | tf_op jit(solution)/shard_map/pallas_call | solution.py:119
  22.0 0.6 %and_convert_fusion.1 = (f32[1,384]{1,0:T(1,128)}, f32[1,384]{1,0:T(1,128)}) fusion(pred[]{:T(512)S(6)} %and.131, s32[]{:T(128)S(6)} %mul.2, pred[]{:T(512)S(6)} %and.126), kind=kLoop, calls=%fused_computation.12 | loop fusion | flops 5376 | bytes 3078 | tf_op jit(solution)/shard_map/convert_element_type | solution.py:197
  22.6 0.0 all-to-all-done
  22.6 0.0 copy-start.1
  22.6 0.7 %convert_reduce_fusion = f32[256]{0:T(256)} fusion(bf16[256,896]{1,0:T(8,128)(2,1)S(1)} %bitcast.13), kind=kLoop, calls=%fused_computation.1 | loop fusion | flops 512 | bytes 1536 | tf_op jit(solution)/shard_map/convert_element_type | solution.py:197
  23.3 0.1 copy-done.1
  23.3 6.5 %shard_map.65 = (f32[3,512,1]{2,1,0:T(8,128)}, f32[3,512,1]{2,1,0:T(8,128)}, f32[512,384]{1,0:T(8,128)}) custom-call(bf16[512,384]{1,0:T(8,128)(2,1)} %bitcast.17, bf16[256,896]{1,0:T(8,128)(2,1)} %bitcast.14, bf16[256,896]{1,0:T(8,128)(2,1)} %bitcast.15, f32[1,256]{1,0:T(1,128)} %bitcast.19, f32[3,512,1]{2,1,0:T(8,128)} %get-tuple-element.11.refs_3_, ...), custom_call_target="tpu_custom_call" | custom-call | flops 201326592 | bytes 5898240 | tf_op jit(solution)/shard_map/pallas_call | solution.py:119
  29.8 2.2 %collective-permute-done.refs_0_.refs_2_ = bf16[2,384,384]{2,1,0:T(8,128)(2,1)S(1)} collective-permute-done((bf16[2,384,384]{2,1,0:T(8,128)(2,1)S(1)}, bf16[2,384,384]{2,1,0:T(8,128)(2,1)S(1)}, u32[]{:S(2)}, u32[]{:S(2)}) %collective-permute-start) | collective-permute-done | bytes 589856 | tf_op jit(solution)/shard_map/ppermute | solution.py:22
  32.0 0.0 copy-start.2
  32.0 1.9 %collective-permute-done.1.refs_1_.refs_3_ = bf16[2,384,384]{2,1,0:T(8,128)(2,1)S(1)} collective-permute-done((bf16[2,384,384]{2,1,0:T(8,128)(2,1)S(1)}, bf16[2,384,384]{2,1,0:T(8,128)(2,1)S(1)}, u32[]{:S(2)}, u32[]{:S(2)}) %collective-permute-start.1) | collective-permute-done | bytes 589856 | tf_op jit(solution)/shard_map/ppermute | solution.py:22
  33.8 0.0 copy-start.3
  33.8 0.0 copy-done.2
  33.9 0.8 %copy-done.3 = bf16[2,384,384]{2,1,0:T(8,128)(2,1)} copy-done((bf16[2,384,384]{2,1,0:T(8,128)(2,1)}, bf16[2,384,384]{2,1,0:T(8,128)(2,1)S(1)}, u32[]{:S(2)}) %copy-start.3) | copy-done | bytes 589848
  34.7 7.4 %shard_map.66 = bf16[512,384]{1,0:T(8,128)(2,1)} custom-call(bf16[512,384]{1,0:T(8,128)(2,1)} %bitcast.18, bf16[2,384,384]{2,1,0:T(8,128)(2,1)} %copy-done.2, bf16[2,384,384]{2,1,0:T(8,128)(2,1)} %copy-done.3, bf16[2,384,384]{2,1,0:T(8,128)(2,1)} %copy-done.2, bf16[2,384,384]{2,1,0:T(8,128)(2,1)} %copy-done.3, f32[1,384]{1,0:T(1,128)} %get-tuple-element.30.refs_4_, ...), custom_call_target="tpu_custom_call" | custom-call | flops 603979776 | bytes 6684672 | tf_op jit(solution)/shard_map/pallas_call | solution.py:119
  (2 shorter events, 0.0 us)
Async XLA Ops:
  2.4 20.1 %all-to-all-start = ((bf16[16,16,896]{2,1,0:T(8,128)(2,1)}), bf16[16,16,896]{2,1,0:T(8,128)(2,1)S(1)}, u32[]{:S(2)}, u32[]{:S(2)}) async-start(bf16[16,16,896]{2,1,0:T(8,128)(2,1)} %bitcast.5), calls=%async_computation | async-start | bytes 917504 | tf_op jit(solution)/shard_map/all_to_all | solution.py:149
  8.7 1.0 %slice-start = ((bf16[1,512,384]{2,1,0:T(8,128)(2,1)}), bf16[1,384,384]{2,1,0:T(8,128)(2,1)S(1)}, s32[]{:S(2)}) async-start(bf16[1,512,384]{2,1,0:T(8,128)(2,1)} %param.7), calls=%async_computation.1 | async-start | bytes 589824 | tf_op jit(solution)/shard_map/slice | solution.py:173
  8.7 1.0 %slice-start.1 = ((bf16[1,512,384]{2,1,0:T(8,128)(2,1)}), bf16[1,384,384]{2,1,0:T(8,128)(2,1)S(1)}, s32[]{:S(2)}) async-start(bf16[1,512,384]{2,1,0:T(8,128)(2,1)} %param.8), calls=%async_computation.2 | async-start | bytes 589824 | tf_op jit(solution)/shard_map/slice | solution.py:173
  9.8 6.5 %copy-start = (bf16[2,384,384]{2,1,0:T(8,128)(2,1)}, bf16[2,384,384]{2,1,0:T(8,128)(2,1)S(1)}, u32[]{:S(2)}) copy-start(bf16[2,384,384]{2,1,0:T(8,128)(2,1)S(1)} %pad_maximum_fusion.refs_0_.refs_1_) | copy-start | bytes 1769476
  9.8 22.1 %collective-permute-start = (bf16[2,384,384]{2,1,0:T(8,128)(2,1)S(1)}, bf16[2,384,384]{2,1,0:T(8,128)(2,1)S(1)}, u32[]{:S(2)}, u32[]{:S(2)}) collective-permute-start(bf16[2,384,384]{2,1,0:T(8,128)(2,1)S(1)} %pad_maximum_fusion.refs_0_.refs_1_), channel_id=1, source_target_pairs={{0,4},{1,5},{2,6},{3,7},{4,8},{5,9},{6,10},{7,11},{8,12},{9,13},{1... | collective-permute-start | bytes 1769480 | tf_op jit(solution)/shard_map/ppermute | solution.py:22
  13.2 20.6 %collective-permute-start.1 = (bf16[2,384,384]{2,1,0:T(8,128)(2,1)S(1)}, bf16[2,384,384]{2,1,0:T(8,128)(2,1)S(1)}, u32[]{:S(2)}, u32[]{:S(2)}) collective-permute-start(bf16[2,384,384]{2,1,0:T(8,128)(2,1)S(1)} %pad_maximum_fusion.refs_0_.refs_1_), channel_id=1, source_target_pairs={{4,0},{5,1},{6,2},{7,3},{8,4},{9,5},{10,6},{11,7},{12,8},{13,9},{1... | collective-permute-start | bytes 1769480 | tf_op jit(solution)/shard_map/ppermute | solution.py:22
  22.6 0.8 %copy-start.1 = (bf16[16,16,896]{2,1,0:T(8,128)(2,1)}, bf16[16,16,896]{2,1,0:T(8,128)(2,1)S(1)}, u32[]{:S(2)}) copy-start(bf16[16,16,896]{2,1,0:T(8,128)(2,1)S(1)} %all-to-all-done) | copy-start | bytes 1376260
  32.0 1.9 %copy-start.2 = (bf16[2,384,384]{2,1,0:T(8,128)(2,1)}, bf16[2,384,384]{2,1,0:T(8,128)(2,1)S(1)}, u32[]{:S(2)}) copy-start(bf16[2,384,384]{2,1,0:T(8,128)(2,1)S(1)} %collective-permute-done.refs_0_.refs_2_) | copy-start | bytes 1769476
  33.8 0.8 %copy-start.3 = (bf16[2,384,384]{2,1,0:T(8,128)(2,1)}, bf16[2,384,384]{2,1,0:T(8,128)(2,1)S(1)}, u32[]{:S(2)}) copy-start(bf16[2,384,384]{2,1,0:T(8,128)(2,1)S(1)} %collective-permute-done.1.refs_1_.refs_3_) | copy-start | bytes 1769476

commit v4 on v1

--- a/solution.py
+++ b/solution.py
@@ -1,8 +1,11 @@
+import functools
 import math
 
 import jax
 import jax.numpy as jnp
 from jax import lax
+from jax.experimental import pallas as pl
+from jax.experimental.pallas import tpu as pltpu
 from jax.sharding import PartitionSpec as P
 
 TS = 8
@@ -40,6 +43,92 @@
         "hqk,khd->hqd", weights, value_heads, preferred_element_type=jnp.float32
     )
     return (new_top, row_total, summed)
+
+
+def window_kernel(blocks, carry_in, finish, q_chunk, q_ref, *refs):
+    block_count = len(blocks)
+    source_refs = refs[:block_count]
+    keep_refs = refs[block_count : 2 * block_count]
+    rest = refs[2 * block_count :]
+    tokens, lane_width = q_ref.shape
+    head_count = lane_width // HEAD_DIM
+    keeps = [keep_refs[b][...] > 0.5 for b in range(block_count)]
+    for h in range(head_count):
+        lanes = slice(h * HEAD_DIM, (h + 1) * HEAD_DIM)
+        for c in range(tokens // q_chunk):
+            rows = slice(c * q_chunk, (c + 1) * q_chunk)
+            query = q_ref[rows, lanes]
+            scores, value_tiles = [], []
+            for b, (pair_form, key_at, value_at) in enumerate(blocks):
+                if pair_form:
+                    key_tile = source_refs[b][key_at, :, lanes]
+                    value_tile = source_refs[b][value_at, :, lanes]
+                else:
+                    key_tile = source_refs[b][:, (key_at + h) * HEAD_DIM : (key_at + h + 1) * HEAD_DIM]
+                    value_tile = source_refs[b][:, (value_at + h) * HEAD_DIM : (value_at + h + 1) * HEAD_DIM]
+                s = lax.dot_general(
+                    query, key_tile, (((1,), (1,)), ((), ())), preferred_element_type=jnp.float32
+                )
+                s = s * (1.0 / math.sqrt(HEAD_DIM))
+                scores.append(jnp.where(keeps[b], s, MASKED))
+                value_tiles.append(value_tile)
+            top = scores[0].max(axis=1, keepdims=True)
+            for s in scores[1:]:
+                top = jnp.maximum(top, s.max(axis=1, keepdims=True))
+            if carry_in:
+                top_in = rest[0][h, rows, :]
+                top = jnp.maximum(top, top_in)
+                scale_down = jnp.exp(top_in - top)
+                total = rest[1][h, rows, :] * scale_down
+                summed = rest[2][rows, lanes] * scale_down
+            else:
+                total = jnp.zeros_like(top)
+                summed = None
+            for b in range(block_count):
+                terms = jnp.exp(scores[b] - top)
+                total = total + terms.sum(axis=1, keepdims=True)
+                part = jnp.dot(terms.astype(jnp.bfloat16), value_tiles[b], preferred_element_type=jnp.float32)
+                summed = part if summed is None else summed + part
+            outs = rest[3:] if carry_in else rest
+            if finish:
+                outs[0][rows, lanes] = (summed / total).astype(outs[0].dtype)
+            else:
+                outs[0][h, rows, :] = top
+                outs[1][h, rows, :] = total
+                outs[2][rows, lanes] = summed
+
+
+def window_attention(query_rows, blocks, carry=None, finish=True):
+    tokens, lane_width = query_rows.shape
+    head_count = lane_width // HEAD_DIM
+    q_chunk = 256 if tokens % 256 == 0 else tokens
+    layout, sources, keeps = [], [], []
+    key_total = 0
+    for source, key_at, value_at, keep in blocks:
+        key_total += keep.shape[1]
+        layout.append((source.ndim == 3, key_at, value_at))
+        sources.append(source)
+        keeps.append(keep)
+    stat_shape = jax.ShapeDtypeStruct((head_count, tokens, 1), jnp.float32)
+    if finish:
+        out_shape = jax.ShapeDtypeStruct((tokens, lane_width), jnp.bfloat16)
+        out_specs = pl.BlockSpec(memory_space=pltpu.VMEM)
+    else:
+        out_shape = (stat_shape, stat_shape, jax.ShapeDtypeStruct((tokens, lane_width), jnp.float32))
+        out_specs = tuple(pl.BlockSpec(memory_space=pltpu.VMEM) for _ in range(3))
+    carry_args = () if carry is None else tuple(carry)
+    operand_count = 1 + 2 * len(blocks) + len(carry_args)
+    flops = 4 * tokens * key_total * lane_width
+    moved = 2 * (2 * tokens * lane_width + 2 * key_total * lane_width) + 4 * 6 * tokens * lane_width
+    return pl.pallas_call(
+        functools.partial(window_kernel, tuple(layout), carry is not None, finish, q_chunk),
+        out_shape=out_shape,
+        in_specs=[pl.BlockSpec(memory_space=pltpu.VMEM)] * operand_count,
+        out_specs=out_specs,
+        cost_estimate=pl.CostEstimate(
+            flops=flops, transcendentals=tokens * key_total * head_count, bytes_accessed=moved
+        ),
+    )(query_rows, *sources, *keeps, *carry_args)
 
 
 def text_pieces(text_keys, text_values, text_mask, group_count, lane_width):
@@ -61,7 +150,7 @@
     )
     outgoing = jnp.tile(per_group, (count // group_count, 1, 1)).reshape(count * rows, 2 * lane_width + 128)
     got = lax.all_to_all(outgoing, "tile", 0, 0, tiled=True)
-    return got[:, :lane_width], got[:, lane_width : 2 * lane_width], got[:, 2 * lane_width] > 0.5
+    return got, got[:, 2 * lane_width] > 0.5
 
 
 def shards(queries, keys, values, text_keys, text_values, text_mask):
@@ -103,12 +192,22 @@
         jnp.zeros((head_count, tokens), jnp.float32),
         jnp.zeros((head_count, tokens, HEAD_DIM), jnp.float32),
     )
-    piece_keys, piece_values, text_keep = text_pieces(text_keys, text_values, text_mask, group_count, lane_width)
-    running = fold_block(running, query_heads, piece_keys, piece_values, text_keep)
-    running = fold_block(running, query_heads, own_pair[0], own_pair[1], keep_mask(0, 0, 0))
+    text_got, text_keep = text_pieces(text_keys, text_values, text_mask, group_count, lane_width)
     width_set = {0: own_pair}
     for off_width in (-1, 1):
         width_set[off_width] = passed_along(own_pair, "tile", -off_width * group_count)
+    if grid_h == 1 and grid_f == 1:
+        as_row = lambda keep: keep.astype(jnp.float32)[None, :]
+        carry = window_attention(queries[0], [(own_pair, 0, 1, as_row(keep_mask(0, 0, 0)))], finish=False)
+        carry = window_attention(
+            queries[0], [(text_got, 0, head_count, as_row(text_keep))], carry=carry, finish=False
+        )
+        blocks = [(width_set[off_width], 0, 1, as_row(keep_mask(0, 0, off_width))) for off_width in (-1, 1)]
+        return window_attention(queries[0], blocks, carry=carry)[None]
+    piece_keys = text_got[:, :lane_width]
+    piece_values = text_got[:, lane_width : 2 * lane_width]
+    running = fold_block(running, query_heads, piece_keys, piece_values, text_keep)
+    running = fold_block(running, query_heads, own_pair[0], own_pair[1], keep_mask(0, 0, 0))
     width_offsets = sorted(width_set)
     row_stack = jnp.stack([width_set[spot] for spot in width_offsets])
     height_set = {0: row_stack}

time: 45.6 us -> 41.1 us (0.901)
  the two profiles are of different devices: /device:TPU:18 before, /device:TPU:10 now
where the time goes in v4:
time: 41.1 us; the launch traced here: 40.7 us
  Pallas kernels  16.6 us (40%)
  starting transfers between devices  12.2 us (30%)
  waiting for transfers between devices  5.57 us (14%)
  local copies, waits for them, and re-layouts  3.63 us (9%)
  other arithmetic  2.64 us (6%)
    pallas_call x3, Pallas kernels, window_attention(): pl.pallas_call(functools.partial(window_kernel, tuple(layout), carry is n...  16.6 us
    all_to_all x1, starting transfers between devices, text_pieces(): got = lax.all_to_all(outgoing, 'tile', 0, 0, tiled=True)  6.3 us
    ppermute x2, starting transfers between devices, passed_along(): lax.ppermute(value, axis, [(source, source + steps) for source in range(f...  5.88 us
    ppermute x2, waiting for transfers between devices, passed_along(): lax.ppermute(value, axis, [(source, source + steps) for source in range(f...  5.57 us
    convert_element_type x3, other arithmetic, shards(): as_row = lambda keep: keep.astype(jnp.float32)[None, :]  1.88 us
    slice x4, local copies, waits for them, and re-layouts, shards(): own_pair = jnp.stack([keys[0, :key_rows], values[0, :key_rows]])  1.04 us
    unnamed x8, local copies, waits for them, and re-layouts  0.89 us
    slice x1, local copies, waits for them, and re-layouts, text_pieces(): text_keys[:, g * lane_width:(g + 1) * lane_width]  0.84 us
  transfers between devices with their start and end apart: 3, of which 2 were waited for; matrix products, arithmetic and copies ran while one was open for 5% of the time, Pallas kernels for 26%

profile of v4, /device:TPU:10, one launch (start us, length us, event | category | flops | bytes accessed | tf_op | source)
XLA Modules:
  0.0 40.7 jit_solution(7226759107556365650)
XLA Ops:
  0.0 0.7 %convert_element_type.48 = bf16[16]{0:T(256)(128)(2,1)S(1)} convert(s32[16]{0:T(128)} %param.11) | non-fusion elementwise | flops 16 | bytes 96 | tf_op jit(solution)/shard_map/convert_element_type | solution.py:137
  0.7 0.8 %fusion.6 = (bf16[16,384]{1,0:T(8,128)(2,1)S(1)}, bf16[16,384]{1,0:T(8,128)(2,1)S(1)}, bf16[16,384]{1,0:T(8,128)(2,1)S(1)}, bf16[16,384]{1,0:T(8,128)(2,1)S(1)},...) fusion(bf16[16,1536]{1,0:T(8,128)(2,1)} %param.9, ...), kind=kLoop, calls=%fused_computation.20 | loop fusion | bytes 196608 | tf_op jit(solution)/shard_map/slice | solution.py:142
  1.5 0.1 broadcast_in_dim.4
  1.6 0.8 %tile.8 = bf16[4,4,16,896]{3,2,1,0:T(8,128)(2,1)} broadcast(bf16[4,16,896]{2,1,0:T(8,128)(2,1)S(1)} %pad_maximum_fusion.1), dimensions={1,2,3} | broadcast | bytes 573440 | tf_op jit(solution)/shard_map/tile | solution.py:151
  2.4 6.3 %all-to-all-start = ((bf16[16,16,896]{2,1,0:T(8,128)(2,1)}), bf16[16,16,896]{2,1,0:T(8,128)(2,1)S(1)}, u32[]{:S(2)}, u32[]{:S(2)}) async-start(bf16[16,16,896]{2,1,0:T(8,128)(2,1)} %bitcast.5), calls=%async_computation | async-start | bytes 917504 | tf_op jit(solution)/shard_map/all_to_all | solution.py:152
  8.7 0.0 slice-start
  8.7 0.0 slice-start.1
  8.7 0.9 %slice-done = bf16[1,384,384]{2,1,0:T(8,128)(2,1)S(1)} async-done(((bf16[1,512,384]{2,1,0:T(8,128)(2,1)}), bf16[1,384,384]{2,1,0:T(8,128)(2,1)S(1)}, s32[]{:S(2)}) %slice-start) | async-done | bytes 294936 | tf_op jit(solution)/shard_map/slice | solution.py:176
  9.7 0.1 slice-done.1
  9.8 0.1 pad_maximum_fusion.refs_0_
  9.8 0.0 copy-start.3
  9.8 3.4 %collective-permute-start = (bf16[2,384,384]{2,1,0:T(8,128)(2,1)S(1)}, bf16[2,384,384]{2,1,0:T(8,128)(2,1)S(1)}, u32[]{:S(2)}, u32[]{:S(2)}) collective-permute-start(bf16[2,384,384]{2,1,0:T(8,128)(2,1)S(1)} %pad_maximum_fusion.refs_0_), channel_id=1, source_target_pairs={{0,4},{1,5},{2,6},{3,7},{4,8},{5,9},{6,10},{7,11},{8,12},{9,13},{1... | collective-permute-start | bytes 1769480 | tf_op jit(solution)/shard_map/ppermute | solution.py:22
  13.2 2.5 %collective-permute-start.1 = (bf16[2,384,384]{2,1,0:T(8,128)(2,1)S(1)}, bf16[2,384,384]{2,1,0:T(8,128)(2,1)S(1)}, u32[]{:S(2)}, u32[]{:S(2)}) collective-permute-start(bf16[2,384,384]{2,1,0:T(8,128)(2,1)S(1)} %pad_maximum_fusion.refs_0_), channel_id=1, source_target_pairs={{4,0},{5,1},{6,2},{7,3},{8,4},{9,5},{10,6},{11,7},{12,8},{13,9},{1... | collective-permute-start | bytes 1769480 | tf_op jit(solution)/shard_map/ppermute | solution.py:22
  15.8 0.6 %and_convert_fusion.refs_1_ = f32[1,384]{1,0:T(1,128)} fusion(pred[]{:T(512)S(6)} %and.135, s32[]{:T(128)S(6)} %mul.2), kind=kLoop, calls=%fused_computation.11 | loop fusion | flops 4608 | bytes 1541 | tf_op jit(solution)/shard_map/convert_element_type | solution.py:200
  16.4 0.0 copy-done.3
  16.4 4.4 %shard_map.64 = (f32[3,512,1]{2,1,0:T(8,128)}, f32[3,512,1]{2,1,0:T(8,128)}, f32[512,384]{1,0:T(8,128)}) custom-call(bf16[512,384]{1,0:T(8,128)(2,1)} %bitcast.15, bf16[2,384,384]{2,1,0:T(8,128)(2,1)} %copy-done.3, f32[1,384]{1,0:T(1,128)} %and_convert_fusion.refs_1_), custom_call_target="tpu_custom_call" | custom-call | flops 301989888 | bytes 6094848 | tf_op jit(solution)/shard_map/pallas_call | solution.py:123
  20.8 0.6 %and_convert_fusion.1 = (f32[1,384]{1,0:T(1,128)}, f32[1,384]{1,0:T(1,128)}) fusion(pred[]{:T(512)S(6)} %and.131, s32[]{:T(128)S(6)} %mul.2, pred[]{:T(512)S(6)} %and.126), kind=kLoop, calls=%fused_computation.12 | loop fusion | flops 5376 | bytes 3078 | tf_op jit(solution)/shard_map/convert_element_type | solution.py:200
  21.3 0.0 all-to-all-done
  21.3 0.0 copy-start
  21.4 0.7 %convert_reduce_fusion = f32[256]{0:T(256)} fusion(bf16[256,896]{1,0:T(8,128)(2,1)S(1)} %bitcast.13), kind=kLoop, calls=%fused_computation.1 | loop fusion | flops 512 | bytes 1536 | tf_op jit(solution)/shard_map/convert_element_type | solution.py:200
  22.1 0.1 copy-done
  22.1 6.2 %shard_map.65 = (f32[3,512,1]{2,1,0:T(8,128)}, f32[3,512,1]{2,1,0:T(8,128)}, f32[512,384]{1,0:T(8,128)}) custom-call(bf16[512,384]{1,0:T(8,128)(2,1)} %bitcast.16, bf16[256,896]{1,0:T(8,128)(2,1)} %bitcast.14, f32[1,256]{1,0:T(1,128)} %bitcast.18, f32[3,512,1]{2,1,0:T(8,128)} %get-tuple-element.11.refs_2_, f32[3,512,1]{2,1,0:T(8,128)} %get-tuple-element.12.refs_3_, ...), custom_call_target="tpu_custom_call" | custom-call | flops 201326592 | bytes 5898240 | tf_op jit(solution)/shard_map/pallas_call | solution.py:123
  28.3 3.7 %collective-permute-done.refs_0_ = bf16[2,384,384]{2,1,0:T(8,128)(2,1)S(1)} collective-permute-done((bf16[2,384,384]{2,1,0:T(8,128)(2,1)S(1)}, bf16[2,384,384]{2,1,0:T(8,128)(2,1)S(1)}, u32[]{:S(2)}, u32[]{:S(2)}) %collective-permute-start) | collective-permute-done | bytes 589856 | tf_op jit(solution)/shard_map/ppermute | solution.py:22
  32.0 0.0 copy-start.1
  32.0 1.9 %collective-permute-done.1.refs_1_ = bf16[2,384,384]{2,1,0:T(8,128)(2,1)S(1)} collective-permute-done((bf16[2,384,384]{2,1,0:T(8,128)(2,1)S(1)}, bf16[2,384,384]{2,1,0:T(8,128)(2,1)S(1)}, u32[]{:S(2)}, u32[]{:S(2)}) %collective-permute-start.1) | collective-permute-done | bytes 589856 | tf_op jit(solution)/shard_map/ppermute | solution.py:22
  33.8 0.0 copy-start.2
  33.8 0.0 copy-done.1
  33.9 0.8 %copy-done.2 = bf16[2,384,384]{2,1,0:T(8,128)(2,1)} copy-done((bf16[2,384,384]{2,1,0:T(8,128)(2,1)}, bf16[2,384,384]{2,1,0:T(8,128)(2,1)S(1)}, u32[]{:S(2)}) %copy-start.2) | copy-done | bytes 589848
  34.7 6.1 %shard_map.66 = bf16[512,384]{1,0:T(8,128)(2,1)} custom-call(bf16[512,384]{1,0:T(8,128)(2,1)} %bitcast.17, bf16[2,384,384]{2,1,0:T(8,128)(2,1)} %copy-done.1, bf16[2,384,384]{2,1,0:T(8,128)(2,1)} %copy-done.2, f32[1,384]{1,0:T(1,128)} %get-tuple-element.30.refs_2_, f32[1,384]{1,0:T(1,128)} %get-tuple-element.29.refs_3_, ...), custom_call_target="tpu_custom_call" | custom-call | flops 603979776 | bytes 6684672 | tf_op jit(solution)/shard_map/pallas_call | solution.py:123
  (2 shorter events, 0.0 us)
Async XLA Ops:
  2.4 18.9 %all-to-all-start = ((bf16[16,16,896]{2,1,0:T(8,128)(2,1)}), bf16[16,16,896]{2,1,0:T(8,128)(2,1)S(1)}, u32[]{:S(2)}, u32[]{:S(2)}) async-start(bf16[16,16,896]{2,1,0:T(8,128)(2,1)} %bitcast.5), calls=%async_computation | async-start | bytes 917504 | tf_op jit(solution)/shard_map/all_to_all | solution.py:152
  8.7 1.0 %slice-start = ((bf16[1,512,384]{2,1,0:T(8,128)(2,1)}), bf16[1,384,384]{2,1,0:T(8,128)(2,1)S(1)}, s32[]{:S(2)}) async-start(bf16[1,512,384]{2,1,0:T(8,128)(2,1)} %param.7), calls=%async_computation.1 | async-start | bytes 589824 | tf_op jit(solution)/shard_map/slice | solution.py:176
  8.7 1.0 %slice-start.1 = ((bf16[1,512,384]{2,1,0:T(8,128)(2,1)}), bf16[1,384,384]{2,1,0:T(8,128)(2,1)S(1)}, s32[]{:S(2)}) async-start(bf16[1,512,384]{2,1,0:T(8,128)(2,1)} %param.8), calls=%async_computation.2 | async-start | bytes 589824 | tf_op jit(solution)/shard_map/slice | solution.py:176
  9.8 6.5 %copy-start.3 = (bf16[2,384,384]{2,1,0:T(8,128)(2,1)}, bf16[2,384,384]{2,1,0:T(8,128)(2,1)S(1)}, u32[]{:S(2)}) copy-start(bf16[2,384,384]{2,1,0:T(8,128)(2,1)S(1)} %pad_maximum_fusion.refs_0_) | copy-start | bytes 1769476
  9.8 22.1 %collective-permute-start = (bf16[2,384,384]{2,1,0:T(8,128)(2,1)S(1)}, bf16[2,384,384]{2,1,0:T(8,128)(2,1)S(1)}, u32[]{:S(2)}, u32[]{:S(2)}) collective-permute-start(bf16[2,384,384]{2,1,0:T(8,128)(2,1)S(1)} %pad_maximum_fusion.refs_0_), channel_id=1, source_target_pairs={{0,4},{1,5},{2,6},{3,7},{4,8},{5,9},{6,10},{7,11},{8,12},{9,13},{1... | collective-permute-start | bytes 1769480 | tf_op jit(solution)/shard_map/ppermute | solution.py:22
  13.2 20.6 %collective-permute-start.1 = (bf16[2,384,384]{2,1,0:T(8,128)(2,1)S(1)}, bf16[2,384,384]{2,1,0:T(8,128)(2,1)S(1)}, u32[]{:S(2)}, u32[]{:S(2)}) collective-permute-start(bf16[2,384,384]{2,1,0:T(8,128)(2,1)S(1)} %pad_maximum_fusion.refs_0_), channel_id=1, source_target_pairs={{4,0},{5,1},{6,2},{7,3},{8,4},{9,5},{10,6},{11,7},{12,8},{13,9},{1... | collective-permute-start | bytes 1769480 | tf_op jit(solution)/shard_map/ppermute | solution.py:22
  21.3 0.8 %copy-start = (bf16[16,16,896]{2,1,0:T(8,128)(2,1)}, bf16[16,16,896]{2,1,0:T(8,128)(2,1)S(1)}, u32[]{:S(2)}) copy-start(bf16[16,16,896]{2,1,0:T(8,128)(2,1)S(1)} %all-to-all-done) | copy-start | bytes 1376260
  32.0 1.9 %copy-start.1 = (bf16[2,384,384]{2,1,0:T(8,128)(2,1)}, bf16[2,384,384]{2,1,0:T(8,128)(2,1)S(1)}, u32[]{:S(2)}) copy-start(bf16[2,384,384]{2,1,0:T(8,128)(2,1)S(1)} %collective-permute-done.refs_0_) | copy-start | bytes 1769476
  33.8 0.8 %copy-start.2 = (bf16[2,384,384]{2,1,0:T(8,128)(2,1)}, bf16[2,384,384]{2,1,0:T(8,128)(2,1)S(1)}, u32[]{:S(2)}) copy-start(bf16[2,384,384]{2,1,0:T(8,128)(2,1)S(1)} %collective-permute-done.1.refs_1_) | copy-start | bytes 1769476

commit v5 on v4

--- a/solution.py
+++ b/solution.py
@@ -101,7 +101,7 @@
 def window_attention(query_rows, blocks, carry=None, finish=True):
     tokens, lane_width = query_rows.shape
     head_count = lane_width // HEAD_DIM
-    q_chunk = 256 if tokens % 256 == 0 else tokens
+    q_chunk = 512 if tokens % 512 == 0 else tokens
     layout, sources, keeps = [], [], []
     key_total = 0
     for source, key_at, value_at, keep in blocks:

time: 41.1 us -> 40.4 us (0.983)
  Pallas kernels: 16.6 us -> 14.8 us
  waiting for transfers between devices: 5.57 us -> 6.62 us
    pallas_call x3, Pallas kernels: 16.6 us -> 14.8 us  [window_attention(): pl.pallas_call(functools.partial(window_kernel, tuple(layout), carry is n...]
    ppermute x2, waiting for transfers between devices: 5.57 us -> 6.38 us  [passed_along(): lax.ppermute(value, axis, [(source, source + steps) for source in range(f...]
  transfers between devices with their start and end apart: 3 -> 3, of which waited for: 2 -> 3; matrix products, arithmetic and copies ran while one was open for 5% -> 5% of each run, Pallas kernels for 26% -> 24%
where the time goes in v5:
time: 40.4 us; the launch traced here: 40 us
  Pallas kernels  14.8 us (37%)
  starting transfers between devices  12.2 us (30%)
  waiting for transfers between devices  6.62 us (16%)
  local copies, waits for them, and re-layouts  3.63 us (9%)
  other arithmetic  2.64 us (7%)
    pallas_call x3, Pallas kernels, window_attention(): pl.pallas_call(functools.partial(window_kernel, tuple(layout), carry is n...  14.8 us
    ppermute x2, waiting for transfers between devices, passed_along(): lax.ppermute(value, axis, [(source, source + steps) for source in range(f...  6.38 us
    all_to_all x1, starting transfers between devices, text_pieces(): got = lax.all_to_all(outgoing, 'tile', 0, 0, tiled=True)  6.3 us
    ppermute x2, starting transfers between devices, passed_along(): lax.ppermute(value, axis, [(source, source + steps) for source in range(f...  5.88 us
    convert_element_type x3, other arithmetic, shards(): as_row = lambda keep: keep.astype(jnp.float32)[None, :]  1.88 us
    slice x4, local copies, waits for them, and re-layouts, shards(): own_pair = jnp.stack([keys[0, :key_rows], values[0, :key_rows]])  1.04 us
    unnamed x8, local copies, waits for them, and re-layouts  0.89 us
    slice x1, local copies, waits for them, and re-layouts, text_pieces(): text_keys[:, g * lane_width:(g + 1) * lane_width]  0.84 us
  transfers between devices with their start and end apart: 3, of which 3 were waited for; matrix products, arithmetic and copies ran while one was open for 5% of the time, Pallas kernels for 24%

profile of v5, /device:TPU:10, one launch (start us, length us, event | category | flops | bytes accessed | tf_op | source)
XLA Modules:
  0.0 40.0 jit_solution(2019824804895246540)
XLA Ops:
  0.0 0.7 %convert_element_type.48 = bf16[16]{0:T(256)(128)(2,1)S(1)} convert(s32[16]{0:T(128)} %param.11) | non-fusion elementwise | flops 16 | bytes 96 | tf_op jit(solution)/shard_map/convert_element_type | solution.py:137
  0.7 0.8 %fusion.6 = (bf16[16,384]{1,0:T(8,128)(2,1)S(1)}, bf16[16,384]{1,0:T(8,128)(2,1)S(1)}, bf16[16,384]{1,0:T(8,128)(2,1)S(1)}, bf16[16,384]{1,0:T(8,128)(2,1)S(1)},...) fusion(bf16[16,1536]{1,0:T(8,128)(2,1)} %param.9, ...), kind=kLoop, calls=%fused_computation.20 | loop fusion | bytes 196608 | tf_op jit(solution)/shard_map/slice | solution.py:142
  1.5 0.1 broadcast_in_dim.4
  1.6 0.8 %tile.8 = bf16[4,4,16,896]{3,2,1,0:T(8,128)(2,1)} broadcast(bf16[4,16,896]{2,1,0:T(8,128)(2,1)S(1)} %pad_maximum_fusion.1), dimensions={1,2,3} | broadcast | bytes 573440 | tf_op jit(solution)/shard_map/tile | solution.py:151
  2.4 6.3 %all-to-all-start = ((bf16[16,16,896]{2,1,0:T(8,128)(2,1)}), bf16[16,16,896]{2,1,0:T(8,128)(2,1)S(1)}, u32[]{:S(2)}, u32[]{:S(2)}) async-start(bf16[16,16,896]{2,1,0:T(8,128)(2,1)} %bitcast.5), calls=%async_computation | async-start | bytes 917504 | tf_op jit(solution)/shard_map/all_to_all | solution.py:152
  8.7 0.0 slice-start
  8.7 0.0 slice-start.1
  8.7 0.9 %slice-done = bf16[1,384,384]{2,1,0:T(8,128)(2,1)S(1)} async-done(((bf16[1,512,384]{2,1,0:T(8,128)(2,1)}), bf16[1,384,384]{2,1,0:T(8,128)(2,1)S(1)}, s32[]{:S(2)}) %slice-start) | async-done | bytes 294936 | tf_op jit(solution)/shard_map/slice | solution.py:176
  9.7 0.1 slice-done.1
  9.8 0.1 pad_maximum_fusion.refs_0_
  9.8 0.0 copy-start.3
  9.8 3.4 %collective-permute-start = (bf16[2,384,384]{2,1,0:T(8,128)(2,1)S(1)}, bf16[2,384,384]{2,1,0:T(8,128)(2,1)S(1)}, u32[]{:S(2)}, u32[]{:S(2)}) collective-permute-start(bf16[2,384,384]{2,1,0:T(8,128)(2,1)S(1)} %pad_maximum_fusion.refs_0_), channel_id=1, source_target_pairs={{0,4},{1,5},{2,6},{3,7},{4,8},{5,9},{6,10},{7,11},{8,12},{9,13},{1... | collective-permute-start | bytes 1769480 | tf_op jit(solution)/shard_map/ppermute | solution.py:22
  13.2 2.5 %collective-permute-start.1 = (bf16[2,384,384]{2,1,0:T(8,128)(2,1)S(1)}, bf16[2,384,384]{2,1,0:T(8,128)(2,1)S(1)}, u32[]{:S(2)}, u32[]{:S(2)}) collective-permute-start(bf16[2,384,384]{2,1,0:T(8,128)(2,1)S(1)} %pad_maximum_fusion.refs_0_), channel_id=1, source_target_pairs={{4,0},{5,1},{6,2},{7,3},{8,4},{9,5},{10,6},{11,7},{12,8},{13,9},{1... | collective-permute-start | bytes 1769480 | tf_op jit(solution)/shard_map/ppermute | solution.py:22
  15.8 0.6 %and_convert_fusion.refs_1_ = f32[1,384]{1,0:T(1,128)} fusion(pred[]{:T(512)S(6)} %and.135, s32[]{:T(128)S(6)} %mul.2), kind=kLoop, calls=%fused_computation.11 | loop fusion | flops 4608 | bytes 1541 | tf_op jit(solution)/shard_map/convert_element_type | solution.py:200
  16.4 0.0 copy-done.3
  16.4 3.7 %shard_map.64 = (f32[3,512,1]{2,1,0:T(8,128)}, f32[3,512,1]{2,1,0:T(8,128)}, f32[512,384]{1,0:T(8,128)}) custom-call(bf16[512,384]{1,0:T(8,128)(2,1)} %bitcast.15, bf16[2,384,384]{2,1,0:T(8,128)(2,1)} %copy-done.3, f32[1,384]{1,0:T(1,128)} %and_convert_fusion.refs_1_), custom_call_target="tpu_custom_call" | custom-call | flops 301989888 | bytes 6094848 | tf_op jit(solution)/shard_map/pallas_call | solution.py:123
  20.1 0.6 %and_convert_fusion.1 = (f32[1,384]{1,0:T(1,128)}, f32[1,384]{1,0:T(1,128)}) fusion(pred[]{:T(512)S(6)} %and.131, s32[]{:T(128)S(6)} %mul.2, pred[]{:T(512)S(6)} %and.126), kind=kLoop, calls=%fused_computation.12 | loop fusion | flops 5376 | bytes 3078 | tf_op jit(solution)/shard_map/convert_element_type | solution.py:200
  20.7 0.2 all-to-all-done
  21.0 0.0 copy-start
  21.0 0.7 %convert_reduce_fusion = f32[256]{0:T(256)} fusion(bf16[256,896]{1,0:T(8,128)(2,1)S(1)} %bitcast.13), kind=kLoop, calls=%fused_computation.1 | loop fusion | flops 512 | bytes 1536 | tf_op jit(solution)/shard_map/convert_element_type | solution.py:200
  21.7 0.1 copy-done
  21.7 5.7 %shard_map.65 = (f32[3,512,1]{2,1,0:T(8,128)}, f32[3,512,1]{2,1,0:T(8,128)}, f32[512,384]{1,0:T(8,128)}) custom-call(bf16[512,384]{1,0:T(8,128)(2,1)} %bitcast.16, bf16[256,896]{1,0:T(8,128)(2,1)} %bitcast.14, f32[1,256]{1,0:T(1,128)} %bitcast.18, f32[3,512,1]{2,1,0:T(8,128)} %get-tuple-element.11.refs_2_, f32[3,512,1]{2,1,0:T(8,128)} %get-tuple-element.12.refs_3_, ...), custom_call_target="tpu_custom_call" | custom-call | flops 201326592 | bytes 5898240 | tf_op jit(solution)/shard_map/pallas_call | solution.py:123
  27.5 4.5 %collective-permute-done.refs_0_ = bf16[2,384,384]{2,1,0:T(8,128)(2,1)S(1)} collective-permute-done((bf16[2,384,384]{2,1,0:T(8,128)(2,1)S(1)}, bf16[2,384,384]{2,1,0:T(8,128)(2,1)S(1)}, u32[]{:S(2)}, u32[]{:S(2)}) %collective-permute-start) | collective-permute-done | bytes 589856 | tf_op jit(solution)/shard_map/ppermute | solution.py:22
  32.0 0.0 copy-start.1
  32.0 1.9 %collective-permute-done.1.refs_1_ = bf16[2,384,384]{2,1,0:T(8,128)(2,1)S(1)} collective-permute-done((bf16[2,384,384]{2,1,0:T(8,128)(2,1)S(1)}, bf16[2,384,384]{2,1,0:T(8,128)(2,1)S(1)}, u32[]{:S(2)}, u32[]{:S(2)}) %collective-permute-start.1) | collective-permute-done | bytes 589856 | tf_op jit(solution)/shard_map/ppermute | solution.py:22
  33.8 0.0 copy-start.2
  33.8 0.0 copy-done.1
  33.9 0.8 %copy-done.2 = bf16[2,384,384]{2,1,0:T(8,128)(2,1)} copy-done((bf16[2,384,384]{2,1,0:T(8,128)(2,1)}, bf16[2,384,384]{2,1,0:T(8,128)(2,1)S(1)}, u32[]{:S(2)}) %copy-start.2) | copy-done | bytes 589848
  34.7 5.3 %shard_map.66 = bf16[512,384]{1,0:T(8,128)(2,1)} custom-call(bf16[512,384]{1,0:T(8,128)(2,1)} %bitcast.17, bf16[2,384,384]{2,1,0:T(8,128)(2,1)} %copy-done.1, bf16[2,384,384]{2,1,0:T(8,128)(2,1)} %copy-done.2, f32[1,384]{1,0:T(1,128)} %get-tuple-element.30.refs_2_, f32[1,384]{1,0:T(1,128)} %get-tuple-element.29.refs_3_, ...), custom_call_target="tpu_custom_call" | custom-call | flops 603979776 | bytes 6684672 | tf_op jit(solution)/shard_map/pallas_call | solution.py:123
  (2 shorter events, 0.0 us)
Async XLA Ops:
  2.4 18.5 %all-to-all-start = ((bf16[16,16,896]{2,1,0:T(8,128)(2,1)}), bf16[16,16,896]{2,1,0:T(8,128)(2,1)S(1)}, u32[]{:S(2)}, u32[]{:S(2)}) async-start(bf16[16,16,896]{2,1,0:T(8,128)(2,1)} %bitcast.5), calls=%async_computation | async-start | bytes 917504 | tf_op jit(solution)/shard_map/all_to_all | solution.py:152
  8.7 1.0 %slice-start = ((bf16[1,512,384]{2,1,0:T(8,128)(2,1)}), bf16[1,384,384]{2,1,0:T(8,128)(2,1)S(1)}, s32[]{:S(2)}) async-start(bf16[1,512,384]{2,1,0:T(8,128)(2,1)} %param.7), calls=%async_computation.1 | async-start | bytes 589824 | tf_op jit(solution)/shard_map/slice | solution.py:176
  8.7 1.0 %slice-start.1 = ((bf16[1,512,384]{2,1,0:T(8,128)(2,1)}), bf16[1,384,384]{2,1,0:T(8,128)(2,1)S(1)}, s32[]{:S(2)}) async-start(bf16[1,512,384]{2,1,0:T(8,128)(2,1)} %param.8), calls=%async_computation.2 | async-start | bytes 589824 | tf_op jit(solution)/shard_map/slice | solution.py:176
  9.8 6.5 %copy-start.3 = (bf16[2,384,384]{2,1,0:T(8,128)(2,1)}, bf16[2,384,384]{2,1,0:T(8,128)(2,1)S(1)}, u32[]{:S(2)}) copy-start(bf16[2,384,384]{2,1,0:T(8,128)(2,1)S(1)} %pad_maximum_fusion.refs_0_) | copy-start | bytes 1769476
  9.8 22.1 %collective-permute-start = (bf16[2,384,384]{2,1,0:T(8,128)(2,1)S(1)}, bf16[2,384,384]{2,1,0:T(8,128)(2,1)S(1)}, u32[]{:S(2)}, u32[]{:S(2)}) collective-permute-start(bf16[2,384,384]{2,1,0:T(8,128)(2,1)S(1)} %pad_maximum_fusion.refs_0_), channel_id=1, source_target_pairs={{0,4},{1,5},{2,6},{3,7},{4,8},{5,9},{6,10},{7,11},{8,12},{9,13},{1... | collective-permute-start | bytes 1769480 | tf_op jit(solution)/shard_map/ppermute | solution.py:22
  13.2 20.6 %collective-permute-start.1 = (bf16[2,384,384]{2,1,0:T(8,128)(2,1)S(1)}, bf16[2,384,384]{2,1,0:T(8,128)(2,1)S(1)}, u32[]{:S(2)}, u32[]{:S(2)}) collective-permute-start(bf16[2,384,384]{2,1,0:T(8,128)(2,1)S(1)} %pad_maximum_fusion.refs_0_), channel_id=1, source_target_pairs={{4,0},{5,1},{6,2},{7,3},{8,4},{9,5},{10,6},{11,7},{12,8},{13,9},{1... | collective-permute-start | bytes 1769480 | tf_op jit(solution)/shard_map/ppermute | solution.py:22
  21.0 0.8 %copy-start = (bf16[16,16,896]{2,1,0:T(8,128)(2,1)}, bf16[16,16,896]{2,1,0:T(8,128)(2,1)S(1)}, u32[]{:S(2)}) copy-start(bf16[16,16,896]{2,1,0:T(8,128)(2,1)S(1)} %all-to-all-done) | copy-start | bytes 1376260
  32.0 1.9 %copy-start.1 = (bf16[2,384,384]{2,1,0:T(8,128)(2,1)}, bf16[2,384,384]{2,1,0:T(8,128)(2,1)S(1)}, u32[]{:S(2)}) copy-start(bf16[2,384,384]{2,1,0:T(8,128)(2,1)S(1)} %collective-permute-done.refs_0_) | copy-start | bytes 1769476
  33.8 0.8 %copy-start.2 = (bf16[2,384,384]{2,1,0:T(8,128)(2,1)}, bf16[2,384,384]{2,1,0:T(8,128)(2,1)S(1)}, u32[]{:S(2)}) copy-start(bf16[2,384,384]{2,1,0:T(8,128)(2,1)S(1)} %collective-permute-done.1.refs_1_) | copy-start | bytes 1769476

commit v6 on v5

--- a/solution.py
+++ b/solution.py
@@ -202,7 +202,10 @@
         carry = window_attention(
             queries[0], [(text_got, 0, head_count, as_row(text_keep))], carry=carry, finish=False
         )
-        blocks = [(width_set[off_width], 0, 1, as_row(keep_mask(0, 0, off_width))) for off_width in (-1, 1)]
+        for off_width in (-1,):
+            blocks = [(width_set[off_width], 0, 1, as_row(keep_mask(0, 0, off_width)))]
+            carry = window_attention(queries[0], blocks, carry=carry, finish=False)
+        blocks = [(width_set[1], 0, 1, as_row(keep_mask(0, 0, 1)))]
         return window_attention(queries[0], blocks, carry=carry)[None]
     piece_keys = text_got[:, :lane_width]
     piece_values = text_got[:, lane_width : 2 * lane_width]

time: 40.4 us -> 48.7 us (1.21)
  the two profiles are of different devices: /device:TPU:10 before, /device:TPU:16 now
where the time goes in v6:
time: 48.7 us; the launch traced here: 48.3 us
  Pallas kernels  23.2 us (48%)
  starting transfers between devices  12 us (25%)
  waiting for transfers between devices  5.26 us (11%)
  local copies, waits for them, and re-layouts  4.44 us (9%)
  other arithmetic  3.24 us (7%)
    pallas_call x4, Pallas kernels, window_attention(): pl.pallas_call(functools.partial(window_kernel, tuple(layout), carry is n...  23.2 us
    all_to_all x1, starting transfers between devices, text_pieces(): got = lax.all_to_all(outgoing, 'tile', 0, 0, tiled=True)  6.18 us
    ppermute x2, starting transfers between devices, passed_along(): lax.ppermute(value, axis, [(source, source + steps) for source in range(f...  5.84 us
    ppermute x2, waiting for transfers between devices, passed_along(): lax.ppermute(value, axis, [(source, source + steps) for source in range(f...  4.93 us
    convert_element_type x4, other arithmetic, shards(): as_row = lambda keep: keep.astype(jnp.float32)[None, :]  2.47 us
    unnamed x8, local copies, waits for them, and re-layouts  1.67 us
    slice x4, local copies, waits for them, and re-layouts, shards(): own_pair = jnp.stack([keys[0, :key_rows], values[0, :key_rows]])  1.04 us
  transfers between devices with their start and end apart: 3, of which 2 were waited for; matrix products, arithmetic and copies ran while one was open for 5% of the time, Pallas kernels for 33%

profile of v6, /device:TPU:16, one launch (start us, length us, event | category | flops | bytes accessed | tf_op | source)
XLA Modules:
  0.0 48.3 jit_solution(5047049447767631274)
XLA Ops:
  0.0 0.7 %convert_element_type.48 = bf16[16]{0:T(256)(128)(2,1)S(1)} convert(s32[16]{0:T(128)} %param.11) | non-fusion elementwise | flops 16 | bytes 96 | tf_op jit(solution)/shard_map/convert_element_type | solution.py:137
  0.7 0.8 %fusion.6 = (bf16[16,384]{1,0:T(8,128)(2,1)S(1)}, bf16[16,384]{1,0:T(8,128)(2,1)S(1)}, bf16[16,384]{1,0:T(8,128)(2,1)S(1)}, bf16[16,384]{1,0:T(8,128)(2,1)S(1)},...) fusion(bf16[16,1536]{1,0:T(8,128)(2,1)} %param.9, ...), kind=kLoop, calls=%fused_computation.20 | loop fusion | bytes 196608 | tf_op jit(solution)/shard_map/slice | solution.py:142
  1.5 0.1 broadcast_in_dim.4
  1.6 0.8 %tile.8 = bf16[4,4,16,896]{3,2,1,0:T(8,128)(2,1)} broadcast(bf16[4,16,896]{2,1,0:T(8,128)(2,1)S(1)} %pad_maximum_fusion.1), dimensions={1,2,3} | broadcast | bytes 573440 | tf_op jit(solution)/shard_map/tile | solution.py:151
  2.4 6.2 %all-to-all-start = ((bf16[16,16,896]{2,1,0:T(8,128)(2,1)}), bf16[16,16,896]{2,1,0:T(8,128)(2,1)S(1)}, u32[]{:S(2)}, u32[]{:S(2)}) async-start(bf16[16,16,896]{2,1,0:T(8,128)(2,1)} %bitcast.5), calls=%async_computation | async-start | bytes 917504 | tf_op jit(solution)/shard_map/all_to_all | solution.py:152
  8.6 0.0 slice-start
  8.6 0.0 slice-start.1
  8.6 0.9 %slice-done = bf16[1,384,384]{2,1,0:T(8,128)(2,1)S(1)} async-done(((bf16[1,512,384]{2,1,0:T(8,128)(2,1)}), bf16[1,384,384]{2,1,0:T(8,128)(2,1)S(1)}, s32[]{:S(2)}) %slice-start) | async-done | bytes 294936 | tf_op jit(solution)/shard_map/slice | solution.py:176
  9.6 0.1 slice-done.1
  9.7 0.1 pad_maximum_fusion.refs_0_
  9.8 0.0 copy-start.1
  9.8 3.4 %collective-permute-start.1 = (bf16[2,384,384]{2,1,0:T(8,128)(2,1)S(1)}, bf16[2,384,384]{2,1,0:T(8,128)(2,1)S(1)}, u32[]{:S(2)}, u32[]{:S(2)}) collective-permute-start(bf16[2,384,384]{2,1,0:T(8,128)(2,1)S(1)} %pad_maximum_fusion.refs_0_), channel_id=1, source_target_pairs={{0,4},{1,5},{2,6},{3,7},{4,8},{5,9},{6,10},{7,11},{8,12},{9,13},{1... | collective-permute-start | bytes 1769480 | tf_op jit(solution)/shard_map/ppermute | solution.py:22
  13.1 2.5 %collective-permute-start = (bf16[2,384,384]{2,1,0:T(8,128)(2,1)S(1)}, bf16[2,384,384]{2,1,0:T(8,128)(2,1)S(1)}, u32[]{:S(2)}, u32[]{:S(2)}) collective-permute-start(bf16[2,384,384]{2,1,0:T(8,128)(2,1)S(1)} %pad_maximum_fusion.refs_0_), channel_id=1, source_target_pairs={{4,0},{5,1},{6,2},{7,3},{8,4},{9,5},{10,6},{11,7},{12,8},{13,9},{1... | collective-permute-start | bytes 1769480 | tf_op jit(solution)/shard_map/ppermute | solution.py:22
  15.7 0.6 %and_convert_fusion.refs_1_ = f32[1,384]{1,0:T(1,128)} fusion(pred[]{:T(512)S(6)} %and.135, s32[]{:T(128)S(6)} %mul.2), kind=kLoop, calls=%fused_computation.11 | loop fusion | flops 4608 | bytes 1541 | tf_op jit(solution)/shard_map/convert_element_type | solution.py:200
  16.3 0.0 copy-done.1
  16.3 3.7 %shard_map.64 = (f32[3,512,1]{2,1,0:T(8,128)}, f32[3,512,1]{2,1,0:T(8,128)}, f32[512,384]{1,0:T(8,128)}) custom-call(bf16[512,384]{1,0:T(8,128)(2,1)} %bitcast.13, bf16[2,384,384]{2,1,0:T(8,128)(2,1)} %copy-done.1, f32[1,384]{1,0:T(1,128)} %and_convert_fusion.refs_1_), custom_call_target="tpu_custom_call" | custom-call | flops 301989888 | bytes 6094848 | tf_op jit(solution)/shard_map/pallas_call | solution.py:123
  20.0 0.6 %and_convert_fusion.1.refs_1_ = f32[1,384]{1,0:T(1,128)} fusion(pred[]{:T(512)S(6)} %and.131, s32[]{:T(128)S(6)} %mul.2), kind=kLoop, calls=%fused_computation.12 | loop fusion | flops 4608 | bytes 1541 | tf_op jit(solution)/shard_map/convert_element_type | solution.py:200
  20.6 0.6 %and_convert_fusion.2.refs_1_ = f32[1,384]{1,0:T(1,128)} fusion(pred[]{:T(512)S(6)} %and.126, s32[]{:T(128)S(6)} %mul.2), kind=kLoop, calls=%fused_computation.13 | loop fusion | flops 4608 | bytes 1541 | tf_op jit(solution)/shard_map/convert_element_type | solution.py:200
  21.1 0.3 all-to-all-done
  21.5 0.0 copy-start
  21.5 0.7 %convert_reduce_fusion = f32[256]{0:T(256)} fusion(bf16[256,896]{1,0:T(8,128)(2,1)S(1)} %bitcast.17), kind=kLoop, calls=%fused_computation.1 | loop fusion | flops 512 | bytes 1536 | tf_op jit(solution)/shard_map/convert_element_type | solution.py:200
  22.2 0.0 copy-done
  22.2 5.7 %shard_map.65 = (f32[3,512,1]{2,1,0:T(8,128)}, f32[3,512,1]{2,1,0:T(8,128)}, f32[512,384]{1,0:T(8,128)}) custom-call(bf16[512,384]{1,0:T(8,128)(2,1)} %bitcast.14, bf16[256,896]{1,0:T(8,128)(2,1)} %bitcast.18, f32[1,256]{1,0:T(1,128)} %bitcast.19, f32[3,512,1]{2,1,0:T(8,128)} %get-tuple-element.14.refs_2_, f32[3,512,1]{2,1,0:T(8,128)} %get-tuple-element.15.refs_3_, ...), custom_call_target="tpu_custom_call" | custom-call | flops 201326592 | bytes 5898240 | tf_op jit(solution)/shard_map/pallas_call | solution.py:123
  28.0 4.9 %collective-permute-done.1.refs_0_ = bf16[2,384,384]{2,1,0:T(8,128)(2,1)S(1)} collective-permute-done((bf16[2,384,384]{2,1,0:T(8,128)(2,1)S(1)}, bf16[2,384,384]{2,1,0:T(8,128)(2,1)S(1)}, u32[]{:S(2)}, u32[]{:S(2)}) %collective-permute-start.1) | collective-permute-done | bytes 589856 | tf_op jit(solution)/shard_map/ppermute | solution.py:22
  32.9 0.0 copy-start.3
  32.9 0.8 %copy-done.3 = bf16[2,384,384]{2,1,0:T(8,128)(2,1)} copy-done((bf16[2,384,384]{2,1,0:T(8,128)(2,1)}, bf16[2,384,384]{2,1,0:T(8,128)(2,1)S(1)}, u32[]{:S(2)}) %copy-start.3) | copy-done | bytes 589848
  33.7 6.4 %shard_map.66 = (f32[3,512,1]{2,1,0:T(8,128)}, f32[3,512,1]{2,1,0:T(8,128)}, f32[512,384]{1,0:T(8,128)}) custom-call(bf16[512,384]{1,0:T(8,128)(2,1)} %bitcast.15, bf16[2,384,384]{2,1,0:T(8,128)(2,1)} %copy-done.3, f32[1,384]{1,0:T(1,128)} %and_convert_fusion.1.refs_1_, f32[3,512,1]{2,1,0:T(8,128)} %get-tuple-element.17.refs_2_, ...), custom_call_target="tpu_custom_call" | custom-call | flops 301989888 | bytes 6094848 | tf_op jit(solution)/shard_map/pallas_call | solution.py:123
  40.2 0.0 collective-permute-done.refs_0_
  40.2 0.0 copy-start.2
  40.2 0.8 %copy-done.2 = bf16[2,384,384]{2,1,0:T(8,128)(2,1)} copy-done((bf16[2,384,384]{2,1,0:T(8,128)(2,1)}, bf16[2,384,384]{2,1,0:T(8,128)(2,1)S(1)}, u32[]{:S(2)}) %copy-start.2) | copy-done | bytes 589848
  41.0 7.3 %shard_map.67 = bf16[512,384]{1,0:T(8,128)(2,1)} custom-call(bf16[512,384]{1,0:T(8,128)(2,1)} %bitcast.16, bf16[2,384,384]{2,1,0:T(8,128)(2,1)} %copy-done.2, f32[1,384]{1,0:T(1,128)} %and_convert_fusion.2.refs_1_, f32[3,512,1]{2,1,0:T(8,128)} %get-tuple-element.20.refs_2_, f32[3,512,1]{2,1,0:T(8,128)} %get-tuple-element.21.refs_3_, ...), custom_call_target="tpu_custom_call" | custom-call | flops 301989888 | bytes 6094848 | tf_op jit(solution)/shard_map/pallas_call | solution.py:123
  (2 shorter events, 0.0 us)
Async XLA Ops:
  2.4 19.0 %all-to-all-start = ((bf16[16,16,896]{2,1,0:T(8,128)(2,1)}), bf16[16,16,896]{2,1,0:T(8,128)(2,1)S(1)}, u32[]{:S(2)}, u32[]{:S(2)}) async-start(bf16[16,16,896]{2,1,0:T(8,128)(2,1)} %bitcast.5), calls=%async_computation | async-start | bytes 917504 | tf_op jit(solution)/shard_map/all_to_all | solution.py:152
  8.6 1.0 %slice-start = ((bf16[1,512,384]{2,1,0:T(8,128)(2,1)}), bf16[1,384,384]{2,1,0:T(8,128)(2,1)S(1)}, s32[]{:S(2)}) async-start(bf16[1,512,384]{2,1,0:T(8,128)(2,1)} %param.7), calls=%async_computation.1 | async-start | bytes 589824 | tf_op jit(solution)/shard_map/slice | solution.py:176
  8.6 1.0 %slice-start.1 = ((bf16[1,512,384]{2,1,0:T(8,128)(2,1)}), bf16[1,384,384]{2,1,0:T(8,128)(2,1)S(1)}, s32[]{:S(2)}) async-start(bf16[1,512,384]{2,1,0:T(8,128)(2,1)} %param.8), calls=%async_computation.2 | async-start | bytes 589824 | tf_op jit(solution)/shard_map/slice | solution.py:176
  9.8 6.5 %copy-start.1 = (bf16[2,384,384]{2,1,0:T(8,128)(2,1)}, bf16[2,384,384]{2,1,0:T(8,128)(2,1)S(1)}, u32[]{:S(2)}) copy-start(bf16[2,384,384]{2,1,0:T(8,128)(2,1)S(1)} %pad_maximum_fusion.refs_0_) | copy-start | bytes 1769476
  9.8 23.1 %collective-permute-start.1 = (bf16[2,384,384]{2,1,0:T(8,128)(2,1)S(1)}, bf16[2,384,384]{2,1,0:T(8,128)(2,1)S(1)}, u32[]{:S(2)}, u32[]{:S(2)}) collective-permute-start(bf16[2,384,384]{2,1,0:T(8,128)(2,1)S(1)} %pad_maximum_fusion.refs_0_), channel_id=1, source_target_pairs={{0,4},{1,5},{2,6},{3,7},{4,8},{5,9},{6,10},{7,11},{8,12},{9,13},{1... | collective-permute-start | bytes 1769480 | tf_op jit(solution)/shard_map/ppermute | solution.py:22
  13.1 27.0 %collective-permute-start = (bf16[2,384,384]{2,1,0:T(8,128)(2,1)S(1)}, bf16[2,384,384]{2,1,0:T(8,128)(2,1)S(1)}, u32[]{:S(2)}, u32[]{:S(2)}) collective-permute-start(bf16[2,384,384]{2,1,0:T(8,128)(2,1)S(1)} %pad_maximum_fusion.refs_0_), channel_id=1, source_target_pairs={{4,0},{5,1},{6,2},{7,3},{8,4},{9,5},{10,6},{11,7},{12,8},{13,9},{1... | collective-permute-start | bytes 1769480 | tf_op jit(solution)/shard_map/ppermute | solution.py:22
  21.5 0.8 %copy-start = (bf16[16,16,896]{2,1,0:T(8,128)(2,1)}, bf16[16,16,896]{2,1,0:T(8,128)(2,1)S(1)}, u32[]{:S(2)}) copy-start(bf16[16,16,896]{2,1,0:T(8,128)(2,1)S(1)} %all-to-all-done) | copy-start | bytes 1376260
  32.9 0.8 %copy-start.3 = (bf16[2,384,384]{2,1,0:T(8,128)(2,1)}, bf16[2,384,384]{2,1,0:T(8,128)(2,1)S(1)}, u32[]{:S(2)}) copy-start(bf16[2,384,384]{2,1,0:T(8,128)(2,1)S(1)} %collective-permute-done.1.refs_0_) | copy-start | bytes 1769476
  40.2 0.8 %copy-start.2 = (bf16[2,384,384]{2,1,0:T(8,128)(2,1)}, bf16[2,384,384]{2,1,0:T(8,128)(2,1)S(1)}, u32[]{:S(2)}) copy-start(bf16[2,384,384]{2,1,0:T(8,128)(2,1)S(1)} %collective-permute-done.refs_0_) | copy-start | bytes 1769476

commit v7 on v5

--- a/solution.py
+++ b/solution.py
@@ -76,11 +76,11 @@
             for s in scores[1:]:
                 top = jnp.maximum(top, s.max(axis=1, keepdims=True))
             if carry_in:
-                top_in = rest[0][h, rows, :]
+                top_in = rest[0][rows, h : h + 1]
                 top = jnp.maximum(top, top_in)
                 scale_down = jnp.exp(top_in - top)
-                total = rest[1][h, rows, :] * scale_down
-                summed = rest[2][rows, lanes] * scale_down
+                total = rest[0][rows, head_count + h : head_count + h + 1] * scale_down
+                summed = rest[1][rows, lanes] * scale_down
             else:
                 total = jnp.zeros_like(top)
                 summed = None
@@ -89,13 +89,13 @@
                 total = total + terms.sum(axis=1, keepdims=True)
                 part = jnp.dot(terms.astype(jnp.bfloat16), value_tiles[b], preferred_element_type=jnp.float32)
                 summed = part if summed is None else summed + part
-            outs = rest[3:] if carry_in else rest
+            outs = rest[2:] if carry_in else rest
             if finish:
                 outs[0][rows, lanes] = (summed / total).astype(outs[0].dtype)
             else:
-                outs[0][h, rows, :] = top
-                outs[1][h, rows, :] = total
-                outs[2][rows, lanes] = summed
+                outs[0][rows, h : h + 1] = top
+                outs[0][rows, head_count + h : head_count + h + 1] = total
+                outs[1][rows, lanes] = summed
 
 
 def window_attention(query_rows, blocks, carry=None, finish=True):
@@ -109,17 +109,17 @@
         layout.append((source.ndim == 3, key_at, value_at))
         sources.append(source)
         keeps.append(keep)
-    stat_shape = jax.ShapeDtypeStruct((head_count, tokens, 1), jnp.float32)
+    stat_shape = jax.ShapeDtypeStruct((tokens, 128), jnp.float32)
     if finish:
         out_shape = jax.ShapeDtypeStruct((tokens, lane_width), jnp.bfloat16)
         out_specs = pl.BlockSpec(memory_space=pltpu.VMEM)
     else:
-        out_shape = (stat_shape, stat_shape, jax.ShapeDtypeStruct((tokens, lane_width), jnp.float32))
-        out_specs = tuple(pl.BlockSpec(memory_space=pltpu.VMEM) for _ in range(3))
+        out_shape = (stat_shape, jax.ShapeDtypeStruct((tokens, lane_width), jnp.float32))
+        out_specs = tuple(pl.BlockSpec(memory_space=pltpu.VMEM) for _ in range(2))
     carry_args = () if carry is None else tuple(carry)
     operand_count = 1 + 2 * len(blocks) + len(carry_args)
     flops = 4 * tokens * key_total * lane_width
-    moved = 2 * (2 * tokens * lane_width + 2 * key_total * lane_width) + 4 * 6 * tokens * lane_width
+    moved = 2 * (2 * tokens * lane_width + 2 * key_total * lane_width) + 4 * 2 * tokens * (lane_width + 128)
     return pl.pallas_call(
         functools.partial(window_kernel, tuple(layout), carry is not None, finish, q_chunk),
         out_shape=out_shape,

time: 40.4 us -> 40.3 us (level)
  Pallas kernels: 14.8 us -> 13.6 us
  waiting for transfers between devices: 6.62 us -> 7.59 us
    pallas_call x3, Pallas kernels: 14.8 us -> 13.6 us  [window_attention(): pl.pallas_call(functools.partial(window_kernel, tuple(layout), carry is n...]
    ppermute x2, waiting for transfers between devices: 6.38 us -> 7.04 us  [passed_along(): lax.ppermute(value, axis, [(source, source + steps) for source in range(f...]
  transfers between devices with their start and end apart: 3 -> 3, of which waited for: 3 -> 3; matrix products, arithmetic and copies ran while one was open for 5% -> 5% of each run, Pallas kernels for 24% -> 21%
where the time goes in v7:
time: 40.3 us; the launch traced here: 39.9 us
  Pallas kernels  13.6 us (34%)
  starting transfers between devices  12.2 us (30%)
  waiting for transfers between devices  7.59 us (19%)
  local copies, waits for them, and re-layouts  3.67 us (9%)
  other arithmetic  2.71 us (7%)
    pallas_call x3, Pallas kernels, window_attention(): pl.pallas_call(functools.partial(window_kernel, tuple(layout), carry is n...  13.6 us
    ppermute x2, waiting for transfers between devices, passed_along(): lax.ppermute(value, axis, [(source, source + steps) for source in range(f...  7.04 us
    all_to_all x1, starting transfers between devices, text_pieces(): got = lax.all_to_all(outgoing, 'tile', 0, 0, tiled=True)  6.3 us
    ppermute x2, starting transfers between devices, passed_along(): lax.ppermute(value, axis, [(source, source + steps) for source in range(f...  5.88 us
    convert_element_type x3, other arithmetic, shards(): as_row = lambda keep: keep.astype(jnp.float32)[None, :]  1.94 us
    slice x4, local copies, waits for them, and re-layouts, shards(): own_pair = jnp.stack([keys[0, :key_rows], values[0, :key_rows]])  1.04 us
    unnamed x8, local copies, waits for them, and re-layouts  0.88 us
    slice x1, local copies, waits for them, and re-layouts, text_pieces(): text_keys[:, g * lane_width:(g + 1) * lane_width]  0.84 us
  transfers between devices with their start and end apart: 3, of which 3 were waited for; matrix products, arithmetic and copies ran while one was open for 5% of the time, Pallas kernels for 21%

profile of v7, /device:TPU:10, one launch (start us, length us, event | category | flops | bytes accessed | tf_op | source)
XLA Modules:
  0.0 39.9 jit_solution(18279334700242728926)
XLA Ops:
  0.0 0.7 %convert_element_type.48 = bf16[16]{0:T(256)(128)(2,1)S(1)} convert(s32[16]{0:T(128)} %param.11) | non-fusion elementwise | flops 16 | bytes 96 | tf_op jit(solution)/shard_map/convert_element_type | solution.py:137
  0.7 0.8 %fusion.6 = (bf16[16,384]{1,0:T(8,128)(2,1)S(1)}, bf16[16,384]{1,0:T(8,128)(2,1)S(1)}, bf16[16,384]{1,0:T(8,128)(2,1)S(1)}, bf16[16,384]{1,0:T(8,128)(2,1)S(1)},...) fusion(bf16[16,1536]{1,0:T(8,128)(2,1)} %param.9, ...), kind=kLoop, calls=%fused_computation.20 | loop fusion | bytes 196608 | tf_op jit(solution)/shard_map/slice | solution.py:142
  1.5 0.1 broadcast_in_dim.4
  1.6 0.8 %tile.8 = bf16[4,4,16,896]{3,2,1,0:T(8,128)(2,1)} broadcast(bf16[4,16,896]{2,1,0:T(8,128)(2,1)S(1)} %pad_maximum_fusion.1), dimensions={1,2,3} | broadcast | bytes 573440 | tf_op jit(solution)/shard_map/tile | solution.py:151
  2.5 6.3 %all-to-all-start = ((bf16[16,16,896]{2,1,0:T(8,128)(2,1)}), bf16[16,16,896]{2,1,0:T(8,128)(2,1)S(1)}, u32[]{:S(2)}, u32[]{:S(2)}) async-start(bf16[16,16,896]{2,1,0:T(8,128)(2,1)} %bitcast.5), calls=%async_computation | async-start | bytes 917504 | tf_op jit(solution)/shard_map/all_to_all | solution.py:152
  8.8 0.0 slice-start
  8.8 0.0 slice-start.1
  8.8 0.9 %slice-done = bf16[1,384,384]{2,1,0:T(8,128)(2,1)S(1)} async-done(((bf16[1,512,384]{2,1,0:T(8,128)(2,1)}), bf16[1,384,384]{2,1,0:T(8,128)(2,1)S(1)}, s32[]{:S(2)}) %slice-start) | async-done | bytes 294936 | tf_op jit(solution)/shard_map/slice | solution.py:176
  9.7 0.1 slice-done.1
  9.8 0.1 pad_maximum_fusion.refs_0_
  9.9 0.0 copy-start.1
  9.9 3.4 %collective-permute-start = (bf16[2,384,384]{2,1,0:T(8,128)(2,1)S(1)}, bf16[2,384,384]{2,1,0:T(8,128)(2,1)S(1)}, u32[]{:S(2)}, u32[]{:S(2)}) collective-permute-start(bf16[2,384,384]{2,1,0:T(8,128)(2,1)S(1)} %pad_maximum_fusion.refs_0_), channel_id=1, source_target_pairs={{0,4},{1,5},{2,6},{3,7},{4,8},{5,9},{6,10},{7,11},{8,12},{9,13},{1... | collective-permute-start | bytes 1769480 | tf_op jit(solution)/shard_map/ppermute | solution.py:22
  13.3 2.5 %collective-permute-start.1 = (bf16[2,384,384]{2,1,0:T(8,128)(2,1)S(1)}, bf16[2,384,384]{2,1,0:T(8,128)(2,1)S(1)}, u32[]{:S(2)}, u32[]{:S(2)}) collective-permute-start(bf16[2,384,384]{2,1,0:T(8,128)(2,1)S(1)} %pad_maximum_fusion.refs_0_), channel_id=1, source_target_pairs={{4,0},{5,1},{6,2},{7,3},{8,4},{9,5},{10,6},{11,7},{12,8},{13,9},{1... | collective-permute-start | bytes 1769480 | tf_op jit(solution)/shard_map/ppermute | solution.py:22
  15.8 0.6 %and_convert_fusion.refs_1_ = f32[1,384]{1,0:T(1,128)} fusion(pred[]{:T(512)S(6)} %and.135, s32[]{:T(128)S(6)} %mul.2), kind=kLoop, calls=%fused_computation.11 | loop fusion | flops 4608 | bytes 1541 | tf_op jit(solution)/shard_map/convert_element_type | solution.py:200
  16.4 0.0 copy-done.1
  16.5 3.4 %shard_map.64 = (f32[512,128]{1,0:T(8,128)}, f32[512,384]{1,0:T(8,128)}) custom-call(bf16[512,384]{1,0:T(8,128)(2,1)} %bitcast.15, bf16[2,384,384]{2,1,0:T(8,128)(2,1)} %copy-done.1, f32[1,384]{1,0:T(1,128)} %and_convert_fusion.refs_1_), custom_call_target="tpu_custom_call" | custom-call | flops 301989888 | bytes 3473408 | tf_op jit(solution)/shard_map/pallas_call | solution.py:123
  19.9 0.6 %and_convert_fusion.1 = (f32[1,384]{1,0:T(1,128)}, f32[1,384]{1,0:T(1,128)}) fusion(pred[]{:T(512)S(6)} %and.131, s32[]{:T(128)S(6)} %mul.2, pred[]{:T(512)S(6)} %and.126), kind=kLoop, calls=%fused_computation.12 | loop fusion | flops 5376 | bytes 3078 | tf_op jit(solution)/shard_map/convert_element_type | solution.py:200
  20.5 0.5 %all-to-all-done = bf16[16,16,896]{2,1,0:T(8,128)(2,1)S(1)} async-done(((bf16[16,16,896]{2,1,0:T(8,128)(2,1)}), bf16[16,16,896]{2,1,0:T(8,128)(2,1)S(1)}, u32[]{:S(2)}, u32[]{:S(2)}) %all-to-all-start) | async-done | bytes 458784 | tf_op jit(solution)/shard_map/all_to_all | solution.py:152
  21.0 0.0 copy-start
  21.0 0.7 %convert_reduce_fusion = f32[256]{0:T(256)} fusion(bf16[256,896]{1,0:T(8,128)(2,1)S(1)} %bitcast.13), kind=kLoop, calls=%fused_computation.1 | loop fusion | flops 512 | bytes 1536 | tf_op jit(solution)/shard_map/convert_element_type | solution.py:200
  21.7 0.0 copy-done
  21.8 5.1 %shard_map.65 = (f32[512,128]{1,0:T(8,128)}, f32[512,384]{1,0:T(8,128)}) custom-call(bf16[512,384]{1,0:T(8,128)(2,1)} %bitcast.16, bf16[256,896]{1,0:T(8,128)(2,1)} %bitcast.14, f32[1,256]{1,0:T(1,128)} %bitcast.18, f32[512,128]{1,0:T(8,128)} %get-tuple-element.9.refs_2_, f32[512,384]{1,0:T(8,128)} %get-tuple-element.10.refs_3_), custom_call_target="tpu_custom_call" | custom-call | flops 201326592 | bytes 3276800 | tf_op jit(solution)/shard_map/pallas_call | solution.py:123
  26.8 5.2 %collective-permute-done.refs_0_ = bf16[2,384,384]{2,1,0:T(8,128)(2,1)S(1)} collective-permute-done((bf16[2,384,384]{2,1,0:T(8,128)(2,1)S(1)}, bf16[2,384,384]{2,1,0:T(8,128)(2,1)S(1)}, u32[]{:S(2)}, u32[]{:S(2)}) %collective-permute-start) | collective-permute-done | bytes 589856 | tf_op jit(solution)/shard_map/ppermute | solution.py:22
  32.0 0.0 copy-start.2
  32.0 1.9 %collective-permute-done.1.refs_1_ = bf16[2,384,384]{2,1,0:T(8,128)(2,1)S(1)} collective-permute-done((bf16[2,384,384]{2,1,0:T(8,128)(2,1)S(1)}, bf16[2,384,384]{2,1,0:T(8,128)(2,1)S(1)}, u32[]{:S(2)}, u32[]{:S(2)}) %collective-permute-start.1) | collective-permute-done | bytes 589856 | tf_op jit(solution)/shard_map/ppermute | solution.py:22
  33.9 0.0 copy-start.3
  33.9 0.0 copy-done.2
  33.9 0.8 %copy-done.3 = bf16[2,384,384]{2,1,0:T(8,128)(2,1)} copy-done((bf16[2,384,384]{2,1,0:T(8,128)(2,1)}, bf16[2,384,384]{2,1,0:T(8,128)(2,1)S(1)}, u32[]{:S(2)}) %copy-start.3) | copy-done | bytes 589848
  34.7 5.2 %shard_map.66 = bf16[512,384]{1,0:T(8,128)(2,1)} custom-call(bf16[512,384]{1,0:T(8,128)(2,1)} %bitcast.17, bf16[2,384,384]{2,1,0:T(8,128)(2,1)} %copy-done.2, bf16[2,384,384]{2,1,0:T(8,128)(2,1)} %copy-done.3, f32[1,384]{1,0:T(1,128)} %get-tuple-element.26.refs_2_, f32[1,384]{1,0:T(1,128)} %get-tuple-element.25.refs_3_, ...), custom_call_target="tpu_custom_call" | custom-call | flops 603979776 | bytes 4063232 | tf_op jit(solution)/shard_map/pallas_call | solution.py:123
  (2 shorter events, 0.0 us)
Async XLA Ops:
  2.5 18.5 %all-to-all-start = ((bf16[16,16,896]{2,1,0:T(8,128)(2,1)}), bf16[16,16,896]{2,1,0:T(8,128)(2,1)S(1)}, u32[]{:S(2)}, u32[]{:S(2)}) async-start(bf16[16,16,896]{2,1,0:T(8,128)(2,1)} %bitcast.5), calls=%async_computation | async-start | bytes 917504 | tf_op jit(solution)/shard_map/all_to_all | solution.py:152
  8.8 1.0 %slice-start = ((bf16[1,512,384]{2,1,0:T(8,128)(2,1)}), bf16[1,384,384]{2,1,0:T(8,128)(2,1)S(1)}, s32[]{:S(2)}) async-start(bf16[1,512,384]{2,1,0:T(8,128)(2,1)} %param.7), calls=%async_computation.1 | async-start | bytes 589824 | tf_op jit(solution)/shard_map/slice | solution.py:176
  8.8 1.0 %slice-start.1 = ((bf16[1,512,384]{2,1,0:T(8,128)(2,1)}), bf16[1,384,384]{2,1,0:T(8,128)(2,1)S(1)}, s32[]{:S(2)}) async-start(bf16[1,512,384]{2,1,0:T(8,128)(2,1)} %param.8), calls=%async_computation.2 | async-start | bytes 589824 | tf_op jit(solution)/shard_map/slice | solution.py:176
  9.9 6.6 %copy-start.1 = (bf16[2,384,384]{2,1,0:T(8,128)(2,1)}, bf16[2,384,384]{2,1,0:T(8,128)(2,1)S(1)}, u32[]{:S(2)}) copy-start(bf16[2,384,384]{2,1,0:T(8,128)(2,1)S(1)} %pad_maximum_fusion.refs_0_) | copy-start | bytes 1769476
  9.9 22.1 %collective-permute-start = (bf16[2,384,384]{2,1,0:T(8,128)(2,1)S(1)}, bf16[2,384,384]{2,1,0:T(8,128)(2,1)S(1)}, u32[]{:S(2)}, u32[]{:S(2)}) collective-permute-start(bf16[2,384,384]{2,1,0:T(8,128)(2,1)S(1)} %pad_maximum_fusion.refs_0_), channel_id=1, source_target_pairs={{0,4},{1,5},{2,6},{3,7},{4,8},{5,9},{6,10},{7,11},{8,12},{9,13},{1... | collective-permute-start | bytes 1769480 | tf_op jit(solution)/shard_map/ppermute | solution.py:22
  13.3 20.6 %collective-permute-start.1 = (bf16[2,384,384]{2,1,0:T(8,128)(2,1)S(1)}, bf16[2,384,384]{2,1,0:T(8,128)(2,1)S(1)}, u32[]{:S(2)}, u32[]{:S(2)}) collective-permute-start(bf16[2,384,384]{2,1,0:T(8,128)(2,1)S(1)} %pad_maximum_fusion.refs_0_), channel_id=1, source_target_pairs={{4,0},{5,1},{6,2},{7,3},{8,4},{9,5},{10,6},{11,7},{12,8},{13,9},{1... | collective-permute-start | bytes 1769480 | tf_op jit(solution)/shard_map/ppermute | solution.py:22
  21.0 0.8 %copy-start = (bf16[16,16,896]{2,1,0:T(8,128)(2,1)}, bf16[16,16,896]{2,1,0:T(8,128)(2,1)S(1)}, u32[]{:S(2)}) copy-start(bf16[16,16,896]{2,1,0:T(8,128)(2,1)S(1)} %all-to-all-done) | copy-start | bytes 1376260
  32.0 1.9 %copy-start.2 = (bf16[2,384,384]{2,1,0:T(8,128)(2,1)}, bf16[2,384,384]{2,1,0:T(8,128)(2,1)S(1)}, u32[]{:S(2)}) copy-start(bf16[2,384,384]{2,1,0:T(8,128)(2,1)S(1)} %collective-permute-done.refs_0_) | copy-start | bytes 1769476
  33.9 0.8 %copy-start.3 = (bf16[2,384,384]{2,1,0:T(8,128)(2,1)}, bf16[2,384,384]{2,1,0:T(8,128)(2,1)S(1)}, u32[]{:S(2)}) copy-start(bf16[2,384,384]{2,1,0:T(8,128)(2,1)S(1)} %collective-permute-done.1.refs_1_) | copy-start | bytes 1769476

commit v8 on v1

--- a/solution.py
+++ b/solution.py
@@ -1,8 +1,11 @@
+import functools
 import math
 
 import jax
 import jax.numpy as jnp
 from jax import lax
+from jax.experimental import pallas as pl
+from jax.experimental.pallas import tpu as pltpu
 from jax.sharding import PartitionSpec as P
 
 TS = 8
@@ -40,6 +43,95 @@
         "hqk,khd->hqd", weights, value_heads, preferred_element_type=jnp.float32
     )
     return (new_top, row_total, summed)
+
+
+def window_kernel(blocks, carry_in, finish, q_ref, *refs):
+    block_count = len(blocks)
+    source_refs = refs[:block_count]
+    keep_refs = refs[block_count : 2 * block_count]
+    rest = refs[2 * block_count :]
+    lane_width, tokens = q_ref.shape
+    head_count = lane_width // HEAD_DIM
+    keeps = [
+        jnp.concatenate([keep_refs[b][...]] * (tokens // 128), axis=1) > 0.5 for b in range(block_count)
+    ]
+    for h in range(head_count):
+        lanes = slice(h * HEAD_DIM, (h + 1) * HEAD_DIM)
+        query_t = q_ref[lanes, :]
+        scores, value_tiles = [], []
+        for b, (pair_form, key_at, value_at) in enumerate(blocks):
+            if pair_form:
+                key_tile = source_refs[b][key_at, :, lanes]
+                value_tile = source_refs[b][value_at, :, lanes]
+            else:
+                key_tile = source_refs[b][:, (key_at + h) * HEAD_DIM : (key_at + h + 1) * HEAD_DIM]
+                value_tile = source_refs[b][:, (value_at + h) * HEAD_DIM : (value_at + h + 1) * HEAD_DIM]
+            s = jnp.dot(key_tile, query_t, preferred_element_type=jnp.float32)
+            s = s * (1.0 / math.sqrt(HEAD_DIM))
+            scores.append(jnp.where(keeps[b], s, MASKED))
+            value_tiles.append(value_tile)
+        top = scores[0].max(axis=0, keepdims=True)
+        for s in scores[1:]:
+            top = jnp.maximum(top, s.max(axis=0, keepdims=True))
+        if carry_in:
+            top_in = rest[0][h : h + 1, :]
+            top = jnp.maximum(top, top_in)
+            scale_down = jnp.exp(top_in - top)
+            total = rest[0][head_count + h : head_count + h + 1, :] * scale_down
+            summed = rest[1][lanes, :] * scale_down
+        else:
+            total = jnp.zeros_like(top)
+            summed = None
+        for b in range(block_count):
+            terms = jnp.exp(scores[b] - top)
+            total = total + terms.sum(axis=0, keepdims=True)
+            part = lax.dot_general(
+                value_tiles[b],
+                terms.astype(jnp.bfloat16),
+                (((0,), (0,)), ((), ())),
+                preferred_element_type=jnp.float32,
+            )
+            summed = part if summed is None else summed + part
+        outs = rest[2:] if carry_in else rest
+        if finish:
+            outs[0][:, lanes] = jnp.transpose(summed / total).astype(outs[0].dtype)
+        else:
+            outs[0][h : h + 1, :] = top
+            outs[0][head_count + h : head_count + h + 1, :] = total
+            outs[1][lanes, :] = summed
+
+
+def window_attention(query_t, blocks, carry=None, finish=True):
+    lane_width, tokens = query_t.shape
+    head_count = lane_width // HEAD_DIM
+    layout, sources, keeps = [], [], []
+    key_total = 0
+    for source, key_at, value_at, keep in blocks:
+        key_total += keep.shape[0]
+        layout.append((source.ndim == 3, key_at, value_at))
+        sources.append(source)
+        keeps.append(keep)
+    stat_rows = -(-2 * head_count // 8) * 8
+    stat_shape = jax.ShapeDtypeStruct((stat_rows, tokens), jnp.float32)
+    if finish:
+        out_shape = jax.ShapeDtypeStruct((tokens, lane_width), jnp.bfloat16)
+        out_specs = pl.BlockSpec(memory_space=pltpu.VMEM)
+    else:
+        out_shape = (stat_shape, jax.ShapeDtypeStruct((lane_width, tokens), jnp.float32))
+        out_specs = tuple(pl.BlockSpec(memory_space=pltpu.VMEM) for _ in range(2))
+    carry_args = () if carry is None else tuple(carry)
+    operand_count = 1 + 2 * len(blocks) + len(carry_args)
+    flops = 4 * tokens * key_total * lane_width
+    moved = 2 * (2 * tokens * lane_width + 2 * key_total * lane_width) + 4 * 2 * tokens * (lane_width + 8)
+    return pl.pallas_call(
+        functools.partial(window_kernel, tuple(layout), carry is not None, finish),
+        out_shape=out_shape,
+        in_specs=[pl.BlockSpec(memory_space=pltpu.VMEM)] * operand_count,
+        out_specs=out_specs,
+        cost_estimate=pl.CostEstimate(
+            flops=flops, transcendentals=tokens * key_total * head_count, bytes_accessed=moved
+        ),
+    )(query_t, *sources, *keeps, *carry_args)
 
 
 def text_pieces(text_keys, text_values, text_mask, group_count, lane_width):
@@ -61,7 +153,7 @@
     )
     outgoing = jnp.tile(per_group, (count // group_count, 1, 1)).reshape(count * rows, 2 * lane_width + 128)
     got = lax.all_to_all(outgoing, "tile", 0, 0, tiled=True)
-    return got[:, :lane_width], got[:, lane_width : 2 * lane_width], got[:, 2 * lane_width] > 0.5
+    return got, got[:, 2 * lane_width] > 0.5
 
 
 def shards(queries, keys, values, text_keys, text_values, text_mask):
@@ -103,12 +195,23 @@
         jnp.zeros((head_count, tokens), jnp.float32),
         jnp.zeros((head_count, tokens, HEAD_DIM), jnp.float32),
     )
-    piece_keys, piece_values, text_keep = text_pieces(text_keys, text_values, text_mask, group_count, lane_width)
-    running = fold_block(running, query_heads, piece_keys, piece_values, text_keep)
-    running = fold_block(running, query_heads, own_pair[0], own_pair[1], keep_mask(0, 0, 0))
+    text_got, text_keep = text_pieces(text_keys, text_values, text_mask, group_count, lane_width)
     width_set = {0: own_pair}
     for off_width in (-1, 1):
         width_set[off_width] = passed_along(own_pair, "tile", -off_width * group_count)
+    if grid_h == 1 and grid_f == 1:
+        as_row = lambda keep: jnp.broadcast_to(keep.astype(jnp.float32)[:, None], (keep.shape[0], 128))
+        query_t = jnp.transpose(queries[0])
+        carry = window_attention(query_t, [(own_pair, 0, 1, as_row(keep_mask(0, 0, 0)))], finish=False)
+        carry = window_attention(
+            query_t, [(text_got, 0, head_count, as_row(text_keep))], carry=carry, finish=False
+        )
+        blocks = [(width_set[off_width], 0, 1, as_row(keep_mask(0, 0, off_width))) for off_width in (-1, 1)]
+        return window_attention(query_t, blocks, carry=carry)[None]
+    piece_keys = text_got[:, :lane_width]
+    piece_values = text_got[:, lane_width : 2 * lane_width]
+    running = fold_block(running, query_heads, piece_keys, piece_values, text_keep)
+    running = fold_block(running, query_heads, own_pair[0], own_pair[1], keep_mask(0, 0, 0))
     width_offsets = sorted(width_set)
     row_stack = jnp.stack([width_set[spot] for spot in width_offsets])
     height_set = {0: row_stack}

time: 45.6 us -> 41.2 us (0.904)
  the two profiles are of different devices: /device:TPU:18 before, /device:TPU:10 now
where the time goes in v8:
time: 41.2 us; the launch traced here: 40.7 us
  starting transfers between devices  12.3 us (30%)
  Pallas kernels  12.2 us (30%)
  waiting for transfers between devices  8.17 us (20%)
  local copies, waits for them, and re-layouts  6.97 us (17%)
  other arithmetic  0.89 us (2%)
    pallas_call x3, Pallas kernels, window_attention(): pl.pallas_call(functools.partial(window_kernel, tuple(layout), carry is n...  12.2 us
    ppermute x2, waiting for transfers between devices, passed_along(): lax.ppermute(value, axis, [(source, source + steps) for source in range(f...  8.17 us
    all_to_all x1, starting transfers between devices, text_pieces(): got = lax.all_to_all(outgoing, 'tile', 0, 0, tiled=True)  6.3 us
    ppermute x2, starting transfers between devices, passed_along(): lax.ppermute(value, axis, [(source, source + steps) for source in range(f...  6.01 us
    broadcast_in_dim x4, local copies, waits for them, and re-layouts, shards(): jnp.broadcast_to(keep.astype(jnp.float32)[:, None], (keep.shape[0], 128))  3.27 us
    slice x4, local copies, waits for them, and re-layouts, shards(): own_pair = jnp.stack([keys[0, :key_rows], values[0, :key_rows]])  1.04 us
    unnamed x11, local copies, waits for them, and re-layouts  0.96 us
    slice x1, local copies, waits for them, and re-layouts, text_pieces(): text_keys[:, g * lane_width:(g + 1) * lane_width]  0.84 us
  transfers between devices with their start and end apart: 3, of which 2 were waited for; matrix products, arithmetic and copies ran while one was open for 7% of the time, Pallas kernels for 17%

profile of v8, /device:TPU:10, one launch (start us, length us, event | category | flops | bytes accessed | tf_op | source)
XLA Modules:
  0.0 40.7 jit_solution(3863104189686409263)
XLA Ops:
  0.0 0.7 %convert_element_type.28 = bf16[16]{0:T(256)(128)(2,1)S(1)} convert(s32[16]{0:T(128)} %param.11) | non-fusion elementwise | flops 16 | bytes 96 | tf_op jit(solution)/shard_map/convert_element_type | solution.py:140
  0.7 0.8 %fusion.9 = (bf16[16,384]{1,0:T(8,128)(2,1)S(1)}, bf16[16,384]{1,0:T(8,128)(2,1)S(1)}, bf16[16,384]{1,0:T(8,128)(2,1)S(1)}, bf16[16,384]{1,0:T(8,128)(2,1)S(1)},...) fusion(bf16[16,1536]{1,0:T(8,128)(2,1)} %param.9, ...), kind=kLoop, calls=%fused_computation.23 | loop fusion | bytes 196608 | tf_op jit(solution)/shard_map/slice | solution.py:145
  1.5 0.1 broadcast_in_dim.19
  1.6 0.8 %tile.8 = bf16[4,4,16,896]{3,2,1,0:T(8,128)(2,1)} broadcast(bf16[4,16,896]{2,1,0:T(8,128)(2,1)S(1)} %pad_maximum_fusion.1), dimensions={1,2,3} | broadcast | bytes 573440 | tf_op jit(solution)/shard_map/tile | solution.py:154
  2.4 6.3 %all-to-all-start = ((bf16[16,16,896]{2,1,0:T(8,128)(2,1)}), bf16[16,16,896]{2,1,0:T(8,128)(2,1)S(1)}, u32[]{:S(2)}, u32[]{:S(2)}) async-start(bf16[16,16,896]{2,1,0:T(8,128)(2,1)} %bitcast.7), calls=%async_computation | async-start | bytes 917504 | tf_op jit(solution)/shard_map/all_to_all | solution.py:155
  8.7 0.0 slice-start
  8.7 0.0 slice-start.1
  8.7 0.9 %slice-done = bf16[1,384,384]{2,1,0:T(8,128)(2,1)S(1)} async-done(((bf16[1,512,384]{2,1,0:T(8,128)(2,1)}), bf16[1,384,384]{2,1,0:T(8,128)(2,1)S(1)}, s32[]{:S(2)}) %slice-start) | async-done | bytes 294936 | tf_op jit(solution)/shard_map/slice | solution.py:179
  9.7 0.1 slice-done.1
  9.8 0.0 copy-start.4
  9.8 0.1 pad_maximum_fusion.refs_0_
  9.8 0.0 copy-start
  9.9 3.5 %collective-permute-start = (bf16[2,384,384]{2,1,0:T(8,128)(2,1)S(1)}, bf16[2,384,384]{2,1,0:T(8,128)(2,1)S(1)}, u32[]{:S(2)}, u32[]{:S(2)}) collective-permute-start(bf16[2,384,384]{2,1,0:T(8,128)(2,1)S(1)} %pad_maximum_fusion.refs_0_), channel_id=1, source_target_pairs={{0,4},{1,5},{2,6},{3,7},{4,8},{5,9},{6,10},{7,11},{8,12},{9,13},{1... | collective-permute-start | bytes 1769480 | tf_op jit(solution)/shard_map/ppermute | solution.py:22
  13.4 2.5 %collective-permute-start.1 = (bf16[2,384,384]{2,1,0:T(8,128)(2,1)S(1)}, bf16[2,384,384]{2,1,0:T(8,128)(2,1)S(1)}, u32[]{:S(2)}, u32[]{:S(2)}) collective-permute-start(bf16[2,384,384]{2,1,0:T(8,128)(2,1)S(1)} %pad_maximum_fusion.refs_0_), channel_id=1, source_target_pairs={{4,0},{5,1},{6,2},{7,3},{8,4},{9,5},{10,6},{11,7},{12,8},{13,9},{1... | collective-permute-start | bytes 1769480 | tf_op jit(solution)/shard_map/ppermute | solution.py:22
  15.9 0.0 copy-done.4
  15.9 0.9 %copy.8 = bf16[1,512,384]{1,2,0:T(8,128)(2,1)} copy(bf16[1,512,384]{2,1,0:T(8,128)(2,1)S(1)} %copy-done.4) | data formatting | bytes 786432 | tf_op args[0]
  16.9 0.8 %broadcast_in_dim.44.refs_1_ = f32[384,128]{1,0:T(8,128)} broadcast(f32[384]{0:T(512)S(1)} %and_convert_fusion), dimensions={0} | broadcast | bytes 198144 | tf_op jit(solution)/shard_map/broadcast_in_dim | solution.py:203
  17.7 0.0 copy-done
  17.7 3.6 %shard_map.64 = (f32[8,512]{1,0:T(8,128)}, f32[384,512]{1,0:T(8,128)}) custom-call(bf16[384,512]{1,0:T(8,128)(2,1)} %bitcast.14, bf16[2,384,384]{2,1,0:T(8,128)(2,1)} %copy-done, f32[384,128]{1,0:T(8,128)} %broadcast_in_dim.44.refs_1_), custom_call_target="tpu_custom_call" | custom-call | flops 301989888 | bytes 2981888 | tf_op jit(solution)/shard_map/pallas_call | solution.py:126
  21.3 0.0 all-to-all-done
  21.3 0.0 copy-start.1
  21.3 0.1 convert_reduce_fusion
  21.4 0.8 %broadcast_in_dim.43.refs_1_ = f32[256,128]{1,0:T(8,128)} broadcast(f32[256]{0:T(256)S(1)} %convert_reduce_fusion), dimensions={0} | broadcast | bytes 132096 | tf_op jit(solution)/shard_map/broadcast_in_dim | solution.py:203
  22.2 0.0 copy-done.1
  22.2 3.5 %shard_map.65 = (f32[8,512]{1,0:T(8,128)}, f32[384,512]{1,0:T(8,128)}) custom-call(bf16[384,512]{1,0:T(8,128)(2,1)} %bitcast.15, bf16[256,896]{1,0:T(8,128)(2,1)} %bitcast.18, f32[256,128]{1,0:T(8,128)} %broadcast_in_dim.43.refs_1_, f32[8,512]{1,0:T(8,128)} %get-tuple-element.9.refs_2_, f32[384,512]{1,0:T(8,128)} %get-tuple-element.10.refs_3_), custom_call_target="tpu_custom_call" | custom-call | flops 201326592 | bytes 2785280 | tf_op jit(solution)/shard_map/pallas_call | solution.py:126
  25.7 6.3 %collective-permute-done.refs_0_ = bf16[2,384,384]{2,1,0:T(8,128)(2,1)S(1)} collective-permute-done((bf16[2,384,384]{2,1,0:T(8,128)(2,1)S(1)}, bf16[2,384,384]{2,1,0:T(8,128)(2,1)S(1)}, u32[]{:S(2)}, u32[]{:S(2)}) %collective-permute-start) | collective-permute-done | bytes 589856 | tf_op jit(solution)/shard_map/ppermute | solution.py:22
  32.0 0.0 copy-start.2
  32.0 1.9 %collective-permute-done.1.refs_1_ = bf16[2,384,384]{2,1,0:T(8,128)(2,1)S(1)} collective-permute-done((bf16[2,384,384]{2,1,0:T(8,128)(2,1)S(1)}, bf16[2,384,384]{2,1,0:T(8,128)(2,1)S(1)}, u32[]{:S(2)}, u32[]{:S(2)}) %collective-permute-start.1) | collective-permute-done | bytes 589856 | tf_op jit(solution)/shard_map/ppermute | solution.py:22
  33.9 0.0 copy-start.3
  33.9 0.9 %broadcast_in_dim.17.refs_2_ = f32[384,128]{1,0:T(8,128)} broadcast(f32[384]{0:T(512)S(1)} %get-tuple-element.26), dimensions={0} | broadcast | bytes 198144 | tf_op jit(solution)/shard_map/broadcast_in_dim | solution.py:203
  34.8 0.8 %broadcast_in_dim.18.refs_3_ = f32[384,128]{1,0:T(8,128)} broadcast(f32[384]{0:T(512)S(1)} %get-tuple-element.25), dimensions={0} | broadcast | bytes 198144 | tf_op jit(solution)/shard_map/broadcast_in_dim | solution.py:203
  35.6 0.0 copy-done.2
  35.6 0.0 copy-done.3
  35.6 5.2 %shard_map.66 = bf16[512,384]{1,0:T(8,128)(2,1)} custom-call(bf16[384,512]{1,0:T(8,128)(2,1)} %bitcast.16, bf16[2,384,384]{2,1,0:T(8,128)(2,1)} %copy-done.2, bf16[2,384,384]{2,1,0:T(8,128)(2,1)} %copy-done.3, f32[384,128]{1,0:T(8,128)} %broadcast_in_dim.17.refs_2_, f32[384,128]{1,0:T(8,128)} %broadcast_in_dim.18.refs_3_, ...), custom_call_target="tpu_custom_call" | custom-call | flops 603979776 | bytes 3571712 | tf_op jit(solution)/shard_map/pallas_call | solution.py:126
  (4 shorter events, 0.1 us)
Async XLA Ops:
  2.4 18.9 %all-to-all-start = ((bf16[16,16,896]{2,1,0:T(8,128)(2,1)}), bf16[16,16,896]{2,1,0:T(8,128)(2,1)S(1)}, u32[]{:S(2)}, u32[]{:S(2)}) async-start(bf16[16,16,896]{2,1,0:T(8,128)(2,1)} %bitcast.7), calls=%async_computation | async-start | bytes 917504 | tf_op jit(solution)/shard_map/all_to_all | solution.py:155
  8.7 1.0 %slice-start = ((bf16[1,512,384]{2,1,0:T(8,128)(2,1)}), bf16[1,384,384]{2,1,0:T(8,128)(2,1)S(1)}, s32[]{:S(2)}) async-start(bf16[1,512,384]{2,1,0:T(8,128)(2,1)} %param.7), calls=%async_computation.1 | async-start | bytes 589824 | tf_op jit(solution)/shard_map/slice | solution.py:179
  8.7 1.0 %slice-start.1 = ((bf16[1,512,384]{2,1,0:T(8,128)(2,1)}), bf16[1,384,384]{2,1,0:T(8,128)(2,1)S(1)}, s32[]{:S(2)}) async-start(bf16[1,512,384]{2,1,0:T(8,128)(2,1)} %param.8), calls=%async_computation.2 | async-start | bytes 589824 | tf_op jit(solution)/shard_map/slice | solution.py:179
  9.8 6.2 %copy-start.4 = (bf16[1,512,384]{2,1,0:T(8,128)(2,1)S(1)}, bf16[1,512,384]{2,1,0:T(8,128)(2,1)}, u32[]{:S(2)}) copy-start(bf16[1,512,384]{2,1,0:T(8,128)(2,1)} %param.6) | copy-start | bytes 1179652
  9.8 7.8 %copy-start = (bf16[2,384,384]{2,1,0:T(8,128)(2,1)}, bf16[2,384,384]{2,1,0:T(8,128)(2,1)S(1)}, u32[]{:S(2)}) copy-start(bf16[2,384,384]{2,1,0:T(8,128)(2,1)S(1)} %pad_maximum_fusion.refs_0_) | copy-start | bytes 1769476
  9.9 22.1 %collective-permute-start = (bf16[2,384,384]{2,1,0:T(8,128)(2,1)S(1)}, bf16[2,384,384]{2,1,0:T(8,128)(2,1)S(1)}, u32[]{:S(2)}, u32[]{:S(2)}) collective-permute-start(bf16[2,384,384]{2,1,0:T(8,128)(2,1)S(1)} %pad_maximum_fusion.refs_0_), channel_id=1, source_target_pairs={{0,4},{1,5},{2,6},{3,7},{4,8},{5,9},{6,10},{7,11},{8,12},{9,13},{1... | collective-permute-start | bytes 1769480 | tf_op jit(solution)/shard_map/ppermute | solution.py:22
  13.4 20.5 %collective-permute-start.1 = (bf16[2,384,384]{2,1,0:T(8,128)(2,1)S(1)}, bf16[2,384,384]{2,1,0:T(8,128)(2,1)S(1)}, u32[]{:S(2)}, u32[]{:S(2)}) collective-permute-start(bf16[2,384,384]{2,1,0:T(8,128)(2,1)S(1)} %pad_maximum_fusion.refs_0_), channel_id=1, source_target_pairs={{4,0},{5,1},{6,2},{7,3},{8,4},{9,5},{10,6},{11,7},{12,8},{13,9},{1... | collective-permute-start | bytes 1769480 | tf_op jit(solution)/shard_map/ppermute | solution.py:22
  21.3 0.9 %copy-start.1 = (bf16[16,16,896]{2,1,0:T(8,128)(2,1)}, bf16[16,16,896]{2,1,0:T(8,128)(2,1)S(1)}, u32[]{:S(2)}) copy-start(bf16[16,16,896]{2,1,0:T(8,128)(2,1)S(1)} %all-to-all-done) | copy-start | bytes 1376260
  32.0 3.6 %copy-start.2 = (bf16[2,384,384]{2,1,0:T(8,128)(2,1)}, bf16[2,384,384]{2,1,0:T(8,128)(2,1)S(1)}, u32[]{:S(2)}) copy-start(bf16[2,384,384]{2,1,0:T(8,128)(2,1)S(1)} %collective-permute-done.refs_0_) | copy-start | bytes 1769476
  33.9 1.7 %copy-start.3 = (bf16[2,384,384]{2,1,0:T(8,128)(2,1)}, bf16[2,384,384]{2,1,0:T(8,128)(2,1)S(1)}, u32[]{:S(2)}) copy-start(bf16[2,384,384]{2,1,0:T(8,128)(2,1)S(1)} %collective-permute-done.1.refs_1_) | copy-start | bytes 1769476

commit v9 on v8

--- a/solution.py
+++ b/solution.py
@@ -53,7 +53,7 @@
     lane_width, tokens = q_ref.shape
     head_count = lane_width // HEAD_DIM
     keeps = [
-        jnp.concatenate([keep_refs[b][...]] * (tokens // 128), axis=1) > 0.5 for b in range(block_count)
+        jnp.broadcast_to(keep_refs[b][...], (keep_refs[b].shape[0], tokens)) > 0.5 for b in range(block_count)
     ]
     for h in range(head_count):
         lanes = slice(h * HEAD_DIM, (h + 1) * HEAD_DIM)
@@ -200,7 +200,7 @@
     for off_width in (-1, 1):
         width_set[off_width] = passed_along(own_pair, "tile", -off_width * group_count)
     if grid_h == 1 and grid_f == 1:
-        as_row = lambda keep: jnp.broadcast_to(keep.astype(jnp.float32)[:, None], (keep.shape[0], 128))
+        as_row = lambda keep: keep.astype(jnp.float32)[:, None]
         query_t = jnp.transpose(queries[0])
         carry = window_attention(query_t, [(own_pair, 0, 1, as_row(keep_mask(0, 0, 0)))], finish=False)
         carry = window_attention(

time: 41.2 us -> 40.3 us (0.978)
  local copies, waits for them, and re-layouts: 6.97 us -> 4.63 us
  other arithmetic: 0.89 us -> 3.04 us
  waiting for transfers between devices: 8.17 us -> 7.46 us
    broadcast_in_dim x4 -> x0, local copies, waits for them, and re-layouts: 3.27 us -> none  [shards(): jnp.broadcast_to(keep.astype(jnp.float32)[:, None], (keep.shape[0], 128))]
    convert_element_type x2 -> x3, other arithmetic: 0.01 us -> 2.27 us  [shards(): as_row = lambda keep: keep.astype(jnp.float32)[:, None]]
    unnamed x11, local copies, waits for them, and re-layouts: 0.96 us -> 1.86 us
    ppermute x2, waiting for transfers between devices: 8.17 us -> 7.46 us  [passed_along(): lax.ppermute(value, axis, [(source, source + steps) for source in range(f...]
  transfers between devices with their start and end apart: 3 -> 3, of which waited for: 2 -> 2; matrix products, arithmetic and copies ran while one was open for 7% -> 8% of each run, Pallas kernels for 17% -> 18%
where the time goes in v9:
time: 40.3 us; the launch traced here: 39.9 us
  starting transfers between devices  12.3 us (31%)
  Pallas kernels  12.3 us (31%)
  waiting for transfers between devices  7.46 us (19%)
  local copies, waits for them, and re-layouts  4.63 us (11%)
  other arithmetic  3.04 us (8%)
    pallas_call x3, Pallas kernels, window_attention(): pl.pallas_call(functools.partial(window_kernel, tuple(layout), carry is n...  12.3 us
    ppermute x2, waiting for transfers between devices, passed_along(): lax.ppermute(value, axis, [(source, source + steps) for source in range(f...  7.46 us
    all_to_all x1, starting transfers between devices, text_pieces(): got = lax.all_to_all(outgoing, 'tile', 0, 0, tiled=True)  6.3 us
    ppermute x2, starting transfers between devices, passed_along(): lax.ppermute(value, axis, [(source, source + steps) for source in range(f...  6.01 us
    convert_element_type x3, other arithmetic, shards(): as_row = lambda keep: keep.astype(jnp.float32)[:, None]  2.27 us
    unnamed x11, local copies, waits for them, and re-layouts  1.86 us
    slice x4, local copies, waits for them, and re-layouts, shards(): own_pair = jnp.stack([keys[0, :key_rows], values[0, :key_rows]])  1.04 us
    slice x1, local copies, waits for them, and re-layouts, text_pieces(): text_keys[:, g * lane_width:(g + 1) * lane_width]  0.84 us
  transfers between devices with their start and end apart: 3, of which 2 were waited for; matrix products, arithmetic and copies ran while one was open for 8% of the time, Pallas kernels for 18%

profile of v9, /device:TPU:10, one launch (start us, length us, event | category | flops | bytes accessed | tf_op | source)
XLA Modules:
  0.0 39.9 jit_solution(6028469956710805841)
XLA Ops:
  0.0 0.7 %convert_element_type.39 = bf16[16]{0:T(256)(128)(2,1)S(1)} convert(s32[16]{0:T(128)} %param.11) | non-fusion elementwise | flops 16 | bytes 96 | tf_op jit(solution)/shard_map/convert_element_type | solution.py:140
  0.7 0.8 %fusion.9 = (bf16[16,384]{1,0:T(8,128)(2,1)S(1)}, bf16[16,384]{1,0:T(8,128)(2,1)S(1)}, bf16[16,384]{1,0:T(8,128)(2,1)S(1)}, bf16[16,384]{1,0:T(8,128)(2,1)S(1)},...) fusion(bf16[16,1536]{1,0:T(8,128)(2,1)} %param.9, ...), kind=kLoop, calls=%fused_computation.23 | loop fusion | bytes 196608 | tf_op jit(solution)/shard_map/slice | solution.py:145
  1.5 0.1 broadcast_in_dim.4
  1.6 0.8 %tile.8 = bf16[4,4,16,896]{3,2,1,0:T(8,128)(2,1)} broadcast(bf16[4,16,896]{2,1,0:T(8,128)(2,1)S(1)} %pad_maximum_fusion.1), dimensions={1,2,3} | broadcast | bytes 573440 | tf_op jit(solution)/shard_map/tile | solution.py:154
  2.4 6.3 %all-to-all-start = ((bf16[16,16,896]{2,1,0:T(8,128)(2,1)}), bf16[16,16,896]{2,1,0:T(8,128)(2,1)S(1)}, u32[]{:S(2)}, u32[]{:S(2)}) async-start(bf16[16,16,896]{2,1,0:T(8,128)(2,1)} %bitcast.7), calls=%async_computation | async-start | bytes 917504 | tf_op jit(solution)/shard_map/all_to_all | solution.py:155
  8.7 0.0 slice-start
  8.7 0.0 slice-start.1
  8.8 0.9 %slice-done = bf16[1,384,384]{2,1,0:T(8,128)(2,1)S(1)} async-done(((bf16[1,512,384]{2,1,0:T(8,128)(2,1)}), bf16[1,384,384]{2,1,0:T(8,128)(2,1)S(1)}, s32[]{:S(2)}) %slice-start) | async-done | bytes 294936 | tf_op jit(solution)/shard_map/slice | solution.py:179
  9.7 0.1 slice-done.1
  9.8 0.0 copy-start.4
  9.8 0.1 pad_maximum_fusion.refs_0_
  9.9 0.0 copy-start
  9.9 3.5 %collective-permute-start = (bf16[2,384,384]{2,1,0:T(8,128)(2,1)S(1)}, bf16[2,384,384]{2,1,0:T(8,128)(2,1)S(1)}, u32[]{:S(2)}, u32[]{:S(2)}) collective-permute-start(bf16[2,384,384]{2,1,0:T(8,128)(2,1)S(1)} %pad_maximum_fusion.refs_0_), channel_id=1, source_target_pairs={{0,4},{1,5},{2,6},{3,7},{4,8},{5,9},{6,10},{7,11},{8,12},{9,13},{1... | collective-permute-start | bytes 1769480 | tf_op jit(solution)/shard_map/ppermute | solution.py:22
  13.4 2.5 %collective-permute-start.1 = (bf16[2,384,384]{2,1,0:T(8,128)(2,1)S(1)}, bf16[2,384,384]{2,1,0:T(8,128)(2,1)S(1)}, u32[]{:S(2)}, u32[]{:S(2)}) collective-permute-start(bf16[2,384,384]{2,1,0:T(8,128)(2,1)S(1)} %pad_maximum_fusion.refs_0_), channel_id=1, source_target_pairs={{4,0},{5,1},{6,2},{7,3},{8,4},{9,5},{10,6},{11,7},{12,8},{13,9},{1... | collective-permute-start | bytes 1769480 | tf_op jit(solution)/shard_map/ppermute | solution.py:22
  16.0 0.0 copy-done.4
  16.0 0.9 %copy.8 = bf16[1,512,384]{1,2,0:T(8,128)(2,1)} copy(bf16[1,512,384]{2,1,0:T(8,128)(2,1)S(1)} %copy-done.4) | data formatting | bytes 786432 | tf_op args[0]
  16.9 0.7 %and_convert_fusion.refs_1_ = f32[384,1]{1,0:T(8,128)} fusion(s32[]{:T(128)S(6)} %mul.2, pred[]{:T(512)S(6)} %and.135), kind=kLoop, calls=%fused_computation.10 | loop fusion | flops 4608 | bytes 1541 | tf_op jit(solution)/shard_map/convert_element_type | solution.py:203
  17.6 0.0 copy-done
  17.6 3.6 %shard_map.64 = (f32[8,512]{1,0:T(8,128)}, f32[384,512]{1,0:T(8,128)}) custom-call(bf16[384,512]{1,0:T(8,128)(2,1)} %bitcast.14, bf16[2,384,384]{2,1,0:T(8,128)(2,1)} %copy-done, f32[384,1]{1,0:T(8,128)} %and_convert_fusion.refs_1_), custom_call_target="tpu_custom_call" | custom-call | flops 301989888 | bytes 2981888 | tf_op jit(solution)/shard_map/pallas_call | solution.py:126
  21.2 0.8 %and_convert_fusion.1 = (f32[384,1]{1,0:T(8,128)}, f32[384,1]{1,0:T(8,128)}) fusion(s32[]{:T(128)S(6)} %mul.2, pred[]{:T(512)S(6)} %and.131, pred[]{:T(512)S(6)} %and.126), kind=kLoop, calls=%fused_computation.11 | loop fusion | flops 5376 | bytes 3078 | tf_op jit(solution)/shard_map/convert_element_type | solution.py:203
  22.1 0.0 all-to-all-done
  22.1 0.0 copy-start.1
  22.1 0.7 %compare_convert_fusion.refs_1_ = f32[256,1]{1,0:T(8,128)} fusion(bf16[256,896]{1,0:T(8,128)(2,1)S(1)} %bitcast.17), kind=kLoop, calls=%fused_computation.13 | loop fusion | flops 512 | bytes 1536 | tf_op jit(solution)/shard_map/convert_element_type | solution.py:203
  22.8 0.1 copy-done.1
  22.9 3.5 %shard_map.65 = (f32[8,512]{1,0:T(8,128)}, f32[384,512]{1,0:T(8,128)}) custom-call(bf16[384,512]{1,0:T(8,128)(2,1)} %bitcast.15, bf16[256,896]{1,0:T(8,128)(2,1)} %bitcast.18, f32[256,1]{1,0:T(8,128)} %compare_convert_fusion.refs_1_, f32[8,512]{1,0:T(8,128)} %get-tuple-element.9.refs_2_, f32[384,512]{1,0:T(8,128)} %get-tuple-element.10.refs_3_), custom_call_target="tpu_custom_call" | custom-call | flops 201326592 | bytes 2785280 | tf_op jit(solution)/shard_map/pallas_call | solution.py:126
  26.4 5.6 %collective-permute-done.refs_0_ = bf16[2,384,384]{2,1,0:T(8,128)(2,1)S(1)} collective-permute-done((bf16[2,384,384]{2,1,0:T(8,128)(2,1)S(1)}, bf16[2,384,384]{2,1,0:T(8,128)(2,1)S(1)}, u32[]{:S(2)}, u32[]{:S(2)}) %collective-permute-start) | collective-permute-done | bytes 589856 | tf_op jit(solution)/shard_map/ppermute | solution.py:22
  32.0 0.0 copy-start.2
  32.0 1.9 %collective-permute-done.1.refs_1_ = bf16[2,384,384]{2,1,0:T(8,128)(2,1)S(1)} collective-permute-done((bf16[2,384,384]{2,1,0:T(8,128)(2,1)S(1)}, bf16[2,384,384]{2,1,0:T(8,128)(2,1)S(1)}, u32[]{:S(2)}, u32[]{:S(2)}) %collective-permute-start.1) | collective-permute-done | bytes 589856 | tf_op jit(solution)/shard_map/ppermute | solution.py:22
  33.9 0.0 copy-start.3
  33.9 0.0 copy-done.2
  33.9 0.8 %copy-done.3 = bf16[2,384,384]{2,1,0:T(8,128)(2,1)} copy-done((bf16[2,384,384]{2,1,0:T(8,128)(2,1)}, bf16[2,384,384]{2,1,0:T(8,128)(2,1)S(1)}, u32[]{:S(2)}) %copy-start.3) | copy-done | bytes 589848
  34.7 5.2 %shard_map.66 = bf16[512,384]{1,0:T(8,128)(2,1)} custom-call(bf16[384,512]{1,0:T(8,128)(2,1)} %bitcast.16, bf16[2,384,384]{2,1,0:T(8,128)(2,1)} %copy-done.2, bf16[2,384,384]{2,1,0:T(8,128)(2,1)} %copy-done.3, f32[384,1]{1,0:T(8,128)} %get-tuple-element.26.refs_2_, f32[384,1]{1,0:T(8,128)} %get-tuple-element.25.refs_3_, f32[8,512]{1,0:T(8,128)} %get-tuple-element.11.refs_4_, ...), custom_call_target="tpu_custom_call" | custom-call | flops 603979776 | bytes 3571712 | tf_op jit(solution)/shard_map/pallas_call | solution.py:126
  (2 shorter events, 0.0 us)
Async XLA Ops:
  2.4 19.6 %all-to-all-start = ((bf16[16,16,896]{2,1,0:T(8,128)(2,1)}), bf16[16,16,896]{2,1,0:T(8,128)(2,1)S(1)}, u32[]{:S(2)}, u32[]{:S(2)}) async-start(bf16[16,16,896]{2,1,0:T(8,128)(2,1)} %bitcast.7), calls=%async_computation | async-start | bytes 917504 | tf_op jit(solution)/shard_map/all_to_all | solution.py:155
  8.7 1.0 %slice-start = ((bf16[1,512,384]{2,1,0:T(8,128)(2,1)}), bf16[1,384,384]{2,1,0:T(8,128)(2,1)S(1)}, s32[]{:S(2)}) async-start(bf16[1,512,384]{2,1,0:T(8,128)(2,1)} %param.7), calls=%async_computation.1 | async-start | bytes 589824 | tf_op jit(solution)/shard_map/slice | solution.py:179
  8.7 1.0 %slice-start.1 = ((bf16[1,512,384]{2,1,0:T(8,128)(2,1)}), bf16[1,384,384]{2,1,0:T(8,128)(2,1)S(1)}, s32[]{:S(2)}) async-start(bf16[1,512,384]{2,1,0:T(8,128)(2,1)} %param.8), calls=%async_computation.2 | async-start | bytes 589824 | tf_op jit(solution)/shard_map/slice | solution.py:179
  9.8 6.2 %copy-start.4 = (bf16[1,512,384]{2,1,0:T(8,128)(2,1)S(1)}, bf16[1,512,384]{2,1,0:T(8,128)(2,1)}, u32[]{:S(2)}) copy-start(bf16[1,512,384]{2,1,0:T(8,128)(2,1)} %param.6) | copy-start | bytes 1179652
  9.9 7.8 %copy-start = (bf16[2,384,384]{2,1,0:T(8,128)(2,1)}, bf16[2,384,384]{2,1,0:T(8,128)(2,1)S(1)}, u32[]{:S(2)}) copy-start(bf16[2,384,384]{2,1,0:T(8,128)(2,1)S(1)} %pad_maximum_fusion.refs_0_) | copy-start | bytes 1769476
  9.9 22.1 %collective-permute-start = (bf16[2,384,384]{2,1,0:T(8,128)(2,1)S(1)}, bf16[2,384,384]{2,1,0:T(8,128)(2,1)S(1)}, u32[]{:S(2)}, u32[]{:S(2)}) collective-permute-start(bf16[2,384,384]{2,1,0:T(8,128)(2,1)S(1)} %pad_maximum_fusion.refs_0_), channel_id=1, source_target_pairs={{0,4},{1,5},{2,6},{3,7},{4,8},{5,9},{6,10},{7,11},{8,12},{9,13},{1... | collective-permute-start | bytes 1769480 | tf_op jit(solution)/shard_map/ppermute | solution.py:22
  13.4 20.5 %collective-permute-start.1 = (bf16[2,384,384]{2,1,0:T(8,128)(2,1)S(1)}, bf16[2,384,384]{2,1,0:T(8,128)(2,1)S(1)}, u32[]{:S(2)}, u32[]{:S(2)}) collective-permute-start(bf16[2,384,384]{2,1,0:T(8,128)(2,1)S(1)} %pad_maximum_fusion.refs_0_), channel_id=1, source_target_pairs={{4,0},{5,1},{6,2},{7,3},{8,4},{9,5},{10,6},{11,7},{12,8},{13,9},{1... | collective-permute-start | bytes 1769480 | tf_op jit(solution)/shard_map/ppermute | solution.py:22
  22.1 0.8 %copy-start.1 = (bf16[16,16,896]{2,1,0:T(8,128)(2,1)}, bf16[16,16,896]{2,1,0:T(8,128)(2,1)S(1)}, u32[]{:S(2)}) copy-start(bf16[16,16,896]{2,1,0:T(8,128)(2,1)S(1)} %all-to-all-done) | copy-start | bytes 1376260
  32.0 1.9 %copy-start.2 = (bf16[2,384,384]{2,1,0:T(8,128)(2,1)}, bf16[2,384,384]{2,1,0:T(8,128)(2,1)S(1)}, u32[]{:S(2)}) copy-start(bf16[2,384,384]{2,1,0:T(8,128)(2,1)S(1)} %collective-permute-done.refs_0_) | copy-start | bytes 1769476
  33.9 0.8 %copy-start.3 = (bf16[2,384,384]{2,1,0:T(8,128)(2,1)}, bf16[2,384,384]{2,1,0:T(8,128)(2,1)S(1)}, u32[]{:S(2)}) copy-start(bf16[2,384,384]{2,1,0:T(8,128)(2,1)S(1)} %collective-permute-done.1.refs_1_) | copy-start | bytes 1769476

commit v10 on v9

--- a/solution.py
+++ b/solution.py
@@ -14,6 +14,7 @@
 
 
 MASKED = -1e30
+EXP2_SCALE = math.log2(math.e) / math.sqrt(HEAD_DIM)
 
 
 def passed_along(value, axis, steps):
@@ -67,7 +68,6 @@
                 key_tile = source_refs[b][:, (key_at + h) * HEAD_DIM : (key_at + h + 1) * HEAD_DIM]
                 value_tile = source_refs[b][:, (value_at + h) * HEAD_DIM : (value_at + h + 1) * HEAD_DIM]
             s = jnp.dot(key_tile, query_t, preferred_element_type=jnp.float32)
-            s = s * (1.0 / math.sqrt(HEAD_DIM))
             scores.append(jnp.where(keeps[b], s, MASKED))
             value_tiles.append(value_tile)
         top = scores[0].max(axis=0, keepdims=True)
@@ -76,14 +76,14 @@
         if carry_in:
             top_in = rest[0][h : h + 1, :]
             top = jnp.maximum(top, top_in)
-            scale_down = jnp.exp(top_in - top)
+            scale_down = jnp.exp2((top_in - top) * EXP2_SCALE)
             total = rest[0][head_count + h : head_count + h + 1, :] * scale_down
             summed = rest[1][lanes, :] * scale_down
         else:
             total = jnp.zeros_like(top)
             summed = None
         for b in range(block_count):
-            terms = jnp.exp(scores[b] - top)
+            terms = jnp.exp2((scores[b] - top) * EXP2_SCALE)
             total = total + terms.sum(axis=0, keepdims=True)
             part = lax.dot_general(
                 value_tiles[b],

time: 40.3 us -> 40.1 us (level)
  no operation moved by 1% of the time
where the time goes in v10:
time: 40.1 us; the launch traced here: 39.7 us
  starting transfers between devices  12.3 us (31%)
  Pallas kernels  12.1 us (30%)
  waiting for transfers between devices  7.45 us (19%)
  local copies, waits for them, and re-layouts  4.63 us (12%)
  other arithmetic  3.04 us (8%)
    pallas_call x3, Pallas kernels, window_attention(): pl.pallas_call(functools.partial(window_kernel, tuple(layout), carry is n...  12.1 us
    ppermute x2, waiting for transfers between devices, passed_along(): lax.ppermute(value, axis, [(source, source + steps) for source in range(f...  7.45 us
    all_to_all x1, starting transfers between devices, text_pieces(): got = lax.all_to_all(outgoing, 'tile', 0, 0, tiled=True)  6.3 us
    ppermute x2, starting transfers between devices, passed_along(): lax.ppermute(value, axis, [(source, source + steps) for source in range(f...  6.01 us
    convert_element_type x3, other arithmetic, shards(): as_row = lambda keep: keep.astype(jnp.float32)[:, None]  2.27 us
    unnamed x11, local copies, waits for them, and re-layouts  1.86 us
    slice x4, local copies, waits for them, and re-layouts, shards(): own_pair = jnp.stack([keys[0, :key_rows], values[0, :key_rows]])  1.04 us
    slice x1, local copies, waits for them, and re-layouts, text_pieces(): text_keys[:, g * lane_width:(g + 1) * lane_width]  0.84 us
  transfers between devices with their start and end apart: 3, of which 2 were waited for; matrix products, arithmetic and copies ran while one was open for 8% of the time, Pallas kernels for 18%

profile of v10, /device:TPU:10, one launch (start us, length us, event | category | flops | bytes accessed | tf_op | source)
XLA Modules:
  0.0 39.7 jit_solution(4286508296458602204)
XLA Ops:
  0.0 0.7 %convert_element_type.39 = bf16[16]{0:T(256)(128)(2,1)S(1)} convert(s32[16]{0:T(128)} %param.11) | non-fusion elementwise | flops 16 | bytes 96 | tf_op jit(solution)/shard_map/convert_element_type | solution.py:140
  0.7 0.8 %fusion.9 = (bf16[16,384]{1,0:T(8,128)(2,1)S(1)}, bf16[16,384]{1,0:T(8,128)(2,1)S(1)}, bf16[16,384]{1,0:T(8,128)(2,1)S(1)}, bf16[16,384]{1,0:T(8,128)(2,1)S(1)},...) fusion(bf16[16,1536]{1,0:T(8,128)(2,1)} %param.9, ...), kind=kLoop, calls=%fused_computation.23 | loop fusion | bytes 196608 | tf_op jit(solution)/shard_map/slice | solution.py:145
  1.5 0.1 broadcast_in_dim.4
  1.6 0.8 %tile.8 = bf16[4,4,16,896]{3,2,1,0:T(8,128)(2,1)} broadcast(bf16[4,16,896]{2,1,0:T(8,128)(2,1)S(1)} %pad_maximum_fusion.1), dimensions={1,2,3} | broadcast | bytes 573440 | tf_op jit(solution)/shard_map/tile | solution.py:154
  2.4 6.3 %all-to-all-start = ((bf16[16,16,896]{2,1,0:T(8,128)(2,1)}), bf16[16,16,896]{2,1,0:T(8,128)(2,1)S(1)}, u32[]{:S(2)}, u32[]{:S(2)}) async-start(bf16[16,16,896]{2,1,0:T(8,128)(2,1)} %bitcast.7), calls=%async_computation | async-start | bytes 917504 | tf_op jit(solution)/shard_map/all_to_all | solution.py:155
  8.7 0.0 slice-start
  8.7 0.0 slice-start.1
  8.8 0.9 %slice-done = bf16[1,384,384]{2,1,0:T(8,128)(2,1)S(1)} async-done(((bf16[1,512,384]{2,1,0:T(8,128)(2,1)}), bf16[1,384,384]{2,1,0:T(8,128)(2,1)S(1)}, s32[]{:S(2)}) %slice-start) | async-done | bytes 294936 | tf_op jit(solution)/shard_map/slice | solution.py:179
  9.7 0.1 slice-done.1
  9.8 0.0 copy-start.4
  9.8 0.1 pad_maximum_fusion.refs_0_
  9.9 0.0 copy-start
  9.9 3.5 %collective-permute-start = (bf16[2,384,384]{2,1,0:T(8,128)(2,1)S(1)}, bf16[2,384,384]{2,1,0:T(8,128)(2,1)S(1)}, u32[]{:S(2)}, u32[]{:S(2)}) collective-permute-start(bf16[2,384,384]{2,1,0:T(8,128)(2,1)S(1)} %pad_maximum_fusion.refs_0_), channel_id=1, source_target_pairs={{0,4},{1,5},{2,6},{3,7},{4,8},{5,9},{6,10},{7,11},{8,12},{9,13},{1... | collective-permute-start | bytes 1769480 | tf_op jit(solution)/shard_map/ppermute | solution.py:23
  13.4 2.5 %collective-permute-start.1 = (bf16[2,384,384]{2,1,0:T(8,128)(2,1)S(1)}, bf16[2,384,384]{2,1,0:T(8,128)(2,1)S(1)}, u32[]{:S(2)}, u32[]{:S(2)}) collective-permute-start(bf16[2,384,384]{2,1,0:T(8,128)(2,1)S(1)} %pad_maximum_fusion.refs_0_), channel_id=1, source_target_pairs={{4,0},{5,1},{6,2},{7,3},{8,4},{9,5},{10,6},{11,7},{12,8},{13,9},{1... | collective-permute-start | bytes 1769480 | tf_op jit(solution)/shard_map/ppermute | solution.py:23
  16.0 0.0 copy-done.4
  16.0 0.9 %copy.8 = bf16[1,512,384]{1,2,0:T(8,128)(2,1)} copy(bf16[1,512,384]{2,1,0:T(8,128)(2,1)S(1)} %copy-done.4) | data formatting | bytes 786432 | tf_op args[0]
  16.9 0.7 %and_convert_fusion.refs_1_ = f32[384,1]{1,0:T(8,128)} fusion(s32[]{:T(128)S(6)} %mul.2, pred[]{:T(512)S(6)} %and.135), kind=kLoop, calls=%fused_computation.10 | loop fusion | flops 4608 | bytes 1541 | tf_op jit(solution)/shard_map/convert_element_type | solution.py:203
  17.6 0.0 copy-done
  17.6 3.6 %shard_map.64 = (f32[8,512]{1,0:T(8,128)}, f32[384,512]{1,0:T(8,128)}) custom-call(bf16[384,512]{1,0:T(8,128)(2,1)} %bitcast.14, bf16[2,384,384]{2,1,0:T(8,128)(2,1)} %copy-done, f32[384,1]{1,0:T(8,128)} %and_convert_fusion.refs_1_), custom_call_target="tpu_custom_call" | custom-call | flops 301989888 | bytes 2981888 | tf_op jit(solution)/shard_map/pallas_call | solution.py:126
  21.3 0.8 %and_convert_fusion.1 = (f32[384,1]{1,0:T(8,128)}, f32[384,1]{1,0:T(8,128)}) fusion(s32[]{:T(128)S(6)} %mul.2, pred[]{:T(512)S(6)} %and.131, pred[]{:T(512)S(6)} %and.126), kind=kLoop, calls=%fused_computation.11 | loop fusion | flops 5376 | bytes 3078 | tf_op jit(solution)/shard_map/convert_element_type | solution.py:203
  22.1 0.0 all-to-all-done
  22.1 0.0 copy-start.1
  22.1 0.7 %compare_convert_fusion.refs_1_ = f32[256,1]{1,0:T(8,128)} fusion(bf16[256,896]{1,0:T(8,128)(2,1)S(1)} %bitcast.17), kind=kLoop, calls=%fused_computation.13 | loop fusion | flops 512 | bytes 1536 | tf_op jit(solution)/shard_map/convert_element_type | solution.py:203
  22.8 0.1 copy-done.1
  22.9 3.5 %shard_map.65 = (f32[8,512]{1,0:T(8,128)}, f32[384,512]{1,0:T(8,128)}) custom-call(bf16[384,512]{1,0:T(8,128)(2,1)} %bitcast.15, bf16[256,896]{1,0:T(8,128)(2,1)} %bitcast.18, f32[256,1]{1,0:T(8,128)} %compare_convert_fusion.refs_1_, f32[8,512]{1,0:T(8,128)} %get-tuple-element.9.refs_2_, f32[384,512]{1,0:T(8,128)} %get-tuple-element.10.refs_3_), custom_call_target="tpu_custom_call" | custom-call | flops 201326592 | bytes 2785280 | tf_op jit(solution)/shard_map/pallas_call | solution.py:126
  26.4 5.6 %collective-permute-done.refs_0_ = bf16[2,384,384]{2,1,0:T(8,128)(2,1)S(1)} collective-permute-done((bf16[2,384,384]{2,1,0:T(8,128)(2,1)S(1)}, bf16[2,384,384]{2,1,0:T(8,128)(2,1)S(1)}, u32[]{:S(2)}, u32[]{:S(2)}) %collective-permute-start) | collective-permute-done | bytes 589856 | tf_op jit(solution)/shard_map/ppermute | solution.py:23
  32.0 0.0 copy-start.2
  32.0 1.9 %collective-permute-done.1.refs_1_ = bf16[2,384,384]{2,1,0:T(8,128)(2,1)S(1)} collective-permute-done((bf16[2,384,384]{2,1,0:T(8,128)(2,1)S(1)}, bf16[2,384,384]{2,1,0:T(8,128)(2,1)S(1)}, u32[]{:S(2)}, u32[]{:S(2)}) %collective-permute-start.1) | collective-permute-done | bytes 589856 | tf_op jit(solution)/shard_map/ppermute | solution.py:23
  33.9 0.0 copy-start.3
  33.9 0.0 copy-done.2
  33.9 0.8 %copy-done.3 = bf16[2,384,384]{2,1,0:T(8,128)(2,1)} copy-done((bf16[2,384,384]{2,1,0:T(8,128)(2,1)}, bf16[2,384,384]{2,1,0:T(8,128)(2,1)S(1)}, u32[]{:S(2)}) %copy-start.3) | copy-done | bytes 589848
  34.7 5.0 %shard_map.66 = bf16[512,384]{1,0:T(8,128)(2,1)} custom-call(bf16[384,512]{1,0:T(8,128)(2,1)} %bitcast.16, bf16[2,384,384]{2,1,0:T(8,128)(2,1)} %copy-done.2, bf16[2,384,384]{2,1,0:T(8,128)(2,1)} %copy-done.3, f32[384,1]{1,0:T(8,128)} %get-tuple-element.26.refs_2_, f32[384,1]{1,0:T(8,128)} %get-tuple-element.25.refs_3_, f32[8,512]{1,0:T(8,128)} %get-tuple-element.11.refs_4_, ...), custom_call_target="tpu_custom_call" | custom-call | flops 603979776 | bytes 3571712 | tf_op jit(solution)/shard_map/pallas_call | solution.py:126
  (2 shorter events, 0.0 us)
Async XLA Ops:
  2.4 19.6 %all-to-all-start = ((bf16[16,16,896]{2,1,0:T(8,128)(2,1)}), bf16[16,16,896]{2,1,0:T(8,128)(2,1)S(1)}, u32[]{:S(2)}, u32[]{:S(2)}) async-start(bf16[16,16,896]{2,1,0:T(8,128)(2,1)} %bitcast.7), calls=%async_computation | async-start | bytes 917504 | tf_op jit(solution)/shard_map/all_to_all | solution.py:155
  8.7 1.0 %slice-start = ((bf16[1,512,384]{2,1,0:T(8,128)(2,1)}), bf16[1,384,384]{2,1,0:T(8,128)(2,1)S(1)}, s32[]{:S(2)}) async-start(bf16[1,512,384]{2,1,0:T(8,128)(2,1)} %param.7), calls=%async_computation.1 | async-start | bytes 589824 | tf_op jit(solution)/shard_map/slice | solution.py:179
  8.7 1.0 %slice-start.1 = ((bf16[1,512,384]{2,1,0:T(8,128)(2,1)}), bf16[1,384,384]{2,1,0:T(8,128)(2,1)S(1)}, s32[]{:S(2)}) async-start(bf16[1,512,384]{2,1,0:T(8,128)(2,1)} %param.8), calls=%async_computation.2 | async-start | bytes 589824 | tf_op jit(solution)/shard_map/slice | solution.py:179
  9.8 6.2 %copy-start.4 = (bf16[1,512,384]{2,1,0:T(8,128)(2,1)S(1)}, bf16[1,512,384]{2,1,0:T(8,128)(2,1)}, u32[]{:S(2)}) copy-start(bf16[1,512,384]{2,1,0:T(8,128)(2,1)} %param.6) | copy-start | bytes 1179652
  9.9 7.8 %copy-start = (bf16[2,384,384]{2,1,0:T(8,128)(2,1)}, bf16[2,384,384]{2,1,0:T(8,128)(2,1)S(1)}, u32[]{:S(2)}) copy-start(bf16[2,384,384]{2,1,0:T(8,128)(2,1)S(1)} %pad_maximum_fusion.refs_0_) | copy-start | bytes 1769476
  9.9 22.1 %collective-permute-start = (bf16[2,384,384]{2,1,0:T(8,128)(2,1)S(1)}, bf16[2,384,384]{2,1,0:T(8,128)(2,1)S(1)}, u32[]{:S(2)}, u32[]{:S(2)}) collective-permute-start(bf16[2,384,384]{2,1,0:T(8,128)(2,1)S(1)} %pad_maximum_fusion.refs_0_), channel_id=1, source_target_pairs={{0,4},{1,5},{2,6},{3,7},{4,8},{5,9},{6,10},{7,11},{8,12},{9,13},{1... | collective-permute-start | bytes 1769480 | tf_op jit(solution)/shard_map/ppermute | solution.py:23
  13.4 20.5 %collective-permute-start.1 = (bf16[2,384,384]{2,1,0:T(8,128)(2,1)S(1)}, bf16[2,384,384]{2,1,0:T(8,128)(2,1)S(1)}, u32[]{:S(2)}, u32[]{:S(2)}) collective-permute-start(bf16[2,384,384]{2,1,0:T(8,128)(2,1)S(1)} %pad_maximum_fusion.refs_0_), channel_id=1, source_target_pairs={{4,0},{5,1},{6,2},{7,3},{8,4},{9,5},{10,6},{11,7},{12,8},{13,9},{1... | collective-permute-start | bytes 1769480 | tf_op jit(solution)/shard_map/ppermute | solution.py:23
  22.1 0.8 %copy-start.1 = (bf16[16,16,896]{2,1,0:T(8,128)(2,1)}, bf16[16,16,896]{2,1,0:T(8,128)(2,1)S(1)}, u32[]{:S(2)}) copy-start(bf16[16,16,896]{2,1,0:T(8,128)(2,1)S(1)} %all-to-all-done) | copy-start | bytes 1376260
  32.0 1.9 %copy-start.2 = (bf16[2,384,384]{2,1,0:T(8,128)(2,1)}, bf16[2,384,384]{2,1,0:T(8,128)(2,1)S(1)}, u32[]{:S(2)}) copy-start(bf16[2,384,384]{2,1,0:T(8,128)(2,1)S(1)} %collective-permute-done.refs_0_) | copy-start | bytes 1769476
  33.9 0.8 %copy-start.3 = (bf16[2,384,384]{2,1,0:T(8,128)(2,1)}, bf16[2,384,384]{2,1,0:T(8,128)(2,1)S(1)}, u32[]{:S(2)}) copy-start(bf16[2,384,384]{2,1,0:T(8,128)(2,1)S(1)} %collective-permute-done.1.refs_1_) | copy-start | bytes 1769476

commit v11 on v10

--- a/solution.py
+++ b/solution.py
@@ -46,11 +46,28 @@
     return (new_top, row_total, summed)
 
 
-def window_kernel(blocks, carry_in, finish, q_ref, *refs):
+def window_kernel(blocks, carry_in, finish, q_any, *refs):
     block_count = len(blocks)
-    source_refs = refs[:block_count]
+    source_anys = refs[:block_count]
     keep_refs = refs[block_count : 2 * block_count]
     rest = refs[2 * block_count :]
+    carry_anys = rest[:2] if carry_in else ()
+    rest = rest[2:] if carry_in else rest
+    out_count = 1 if finish else 2
+    outs = rest[:out_count]
+    rest = rest[out_count:]
+    q_ref = rest[0]
+    source_refs = rest[1 : 1 + block_count]
+    carry_refs = rest[1 + block_count : 1 + block_count + len(carry_anys)]
+    sems = rest[-1]
+    copies = [pltpu.make_async_copy(q_any, q_ref, sems.at[0])]
+    copies += [pltpu.make_async_copy(source_anys[b], source_refs[b], sems.at[1 + b]) for b in range(block_count)]
+    copies += [
+        pltpu.make_async_copy(carry_anys[i], carry_refs[i], sems.at[1 + block_count + i])
+        for i in range(len(carry_anys))
+    ]
+    for copy in copies:
+        copy.start()
     lane_width, tokens = q_ref.shape
     head_count = lane_width // HEAD_DIM
     keeps = [
@@ -58,9 +75,13 @@
     ]
     for h in range(head_count):
         lanes = slice(h * HEAD_DIM, (h + 1) * HEAD_DIM)
+        if h == 0:
+            copies[0].wait()
         query_t = q_ref[lanes, :]
         scores, value_tiles = [], []
         for b, (pair_form, key_at, value_at) in enumerate(blocks):
+            if h == 0:
+                copies[1 + b].wait()
             if pair_form:
                 key_tile = source_refs[b][key_at, :, lanes]
                 value_tile = source_refs[b][value_at, :, lanes]
@@ -74,11 +95,14 @@
         for s in scores[1:]:
             top = jnp.maximum(top, s.max(axis=0, keepdims=True))
         if carry_in:
-            top_in = rest[0][h : h + 1, :]
+            if h == 0:
+                for copy in copies[1 + block_count :]:
+                    copy.wait()
+            top_in = carry_refs[0][h : h + 1, :]
             top = jnp.maximum(top, top_in)
             scale_down = jnp.exp2((top_in - top) * EXP2_SCALE)
-            total = rest[0][head_count + h : head_count + h + 1, :] * scale_down
-            summed = rest[1][lanes, :] * scale_down
+            total = carry_refs[0][head_count + h : head_count + h + 1, :] * scale_down
+            summed = carry_refs[1][lanes, :] * scale_down
         else:
             total = jnp.zeros_like(top)
             summed = None
@@ -92,7 +116,6 @@
                 preferred_element_type=jnp.float32,
             )
             summed = part if summed is None else summed + part
-        outs = rest[2:] if carry_in else rest
         if finish:
             outs[0][:, lanes] = jnp.transpose(summed / total).astype(outs[0].dtype)
         else:
@@ -120,14 +143,21 @@
         out_shape = (stat_shape, jax.ShapeDtypeStruct((lane_width, tokens), jnp.float32))
         out_specs = tuple(pl.BlockSpec(memory_space=pltpu.VMEM) for _ in range(2))
     carry_args = () if carry is None else tuple(carry)
-    operand_count = 1 + 2 * len(blocks) + len(carry_args)
+    any_spec = pl.BlockSpec(memory_space=pl.ANY)
+    vmem_spec = pl.BlockSpec(memory_space=pltpu.VMEM)
+    in_specs = [any_spec] * (1 + len(sources)) + [vmem_spec] * len(keeps) + [any_spec] * len(carry_args)
+    scratch = [pltpu.VMEM(query_t.shape, query_t.dtype)]
+    scratch += [pltpu.VMEM(s.shape, s.dtype) for s in sources]
+    scratch += [pltpu.VMEM(c.shape, c.dtype) for c in carry_args]
+    scratch += [pltpu.SemaphoreType.DMA((1 + len(sources) + len(carry_args),))]
     flops = 4 * tokens * key_total * lane_width
     moved = 2 * (2 * tokens * lane_width + 2 * key_total * lane_width) + 4 * 2 * tokens * (lane_width + 8)
     return pl.pallas_call(
         functools.partial(window_kernel, tuple(layout), carry is not None, finish),
         out_shape=out_shape,
-        in_specs=[pl.BlockSpec(memory_space=pltpu.VMEM)] * operand_count,
+        in_specs=in_specs,
         out_specs=out_specs,
+        scratch_shapes=scratch,
         cost_estimate=pl.CostEstimate(
             flops=flops, transcendentals=tokens * key_total * head_count, bytes_accessed=moved
         ),

time: 40.1 us -> 40.7 us (1.015)
  Pallas kernels: 12.1 us -> 14.2 us
  waiting for transfers between devices: 7.45 us -> 5.86 us
    pallas_call x3, Pallas kernels: 12.1 us -> 14.2 us  [window_attention(): pl.pallas_call(functools.partial(window_kernel, tuple(layout), carry is n...]
    ppermute x2, waiting for transfers between devices: 7.45 us -> 5.86 us  [passed_along(): lax.ppermute(value, axis, [(source, source + steps) for source in range(f...]
  transfers between devices with their start and end apart: 3 -> 3, of which waited for: 2 -> 2; matrix products, arithmetic and copies ran while one was open for 8% -> 8% of each run, Pallas kernels for 18% -> 22%
where the time goes in v11:
time: 40.7 us; the launch traced here: 40.2 us
  Pallas kernels  14.2 us (35%)
  starting transfers between devices  12.3 us (30%)
  waiting for transfers between devices  5.86 us (14%)
  local copies, waits for them, and re-layouts  4.63 us (11%)
  other arithmetic  3.04 us (7%)
    pallas_call x3, Pallas kernels, window_attention(): pl.pallas_call(functools.partial(window_kernel, tuple(layout), carry is n...  14.2 us
    all_to_all x1, starting transfers between devices, text_pieces(): got = lax.all_to_all(outgoing, 'tile', 0, 0, tiled=True)  6.3 us
    ppermute x2, starting transfers between devices, passed_along(): lax.ppermute(value, axis, [(source, source + steps) for source in range(f...  6.01 us
    ppermute x2, waiting for transfers between devices, passed_along(): lax.ppermute(value, axis, [(source, source + steps) for source in range(f...  5.86 us
    convert_element_type x3, other arithmetic, shards(): as_row = lambda keep: keep.astype(jnp.float32)[:, None]  2.28 us
    unnamed x11, local copies, waits for them, and re-layouts  1.86 us
    slice x4, local copies, waits for them, and re-layouts, shards(): own_pair = jnp.stack([keys[0, :key_rows], values[0, :key_rows]])  1.04 us
    slice x1, local copies, waits for them, and re-layouts, text_pieces(): text_keys[:, g * lane_width:(g + 1) * lane_width]  0.84 us
  transfers between devices with their start and end apart: 3, of which 2 were waited for; matrix products, arithmetic and copies ran while one was open for 8% of the time, Pallas kernels for 22%

profile of v11, /device:TPU:10, one launch (start us, length us, event | category | flops | bytes accessed | tf_op | source)
XLA Modules:
  0.0 40.2 jit_solution(7323873712181310928)
XLA Ops:
  0.0 0.7 %convert_element_type.39 = bf16[16]{0:T(256)(128)(2,1)S(1)} convert(s32[16]{0:T(128)} %param.11) | non-fusion elementwise | flops 16 | bytes 96 | tf_op jit(solution)/shard_map/convert_element_type | solution.py:170
  0.7 0.8 %fusion.9 = (bf16[16,384]{1,0:T(8,128)(2,1)S(1)}, bf16[16,384]{1,0:T(8,128)(2,1)S(1)}, bf16[16,384]{1,0:T(8,128)(2,1)S(1)}, bf16[16,384]{1,0:T(8,128)(2,1)S(1)},...) fusion(bf16[16,1536]{1,0:T(8,128)(2,1)} %param.9, ...), kind=kLoop, calls=%fused_computation.23 | loop fusion | bytes 196608 | tf_op jit(solution)/shard_map/slice | solution.py:175
  1.5 0.1 broadcast_in_dim.4
  1.6 0.8 %tile.8 = bf16[4,4,16,896]{3,2,1,0:T(8,128)(2,1)} broadcast(bf16[4,16,896]{2,1,0:T(8,128)(2,1)S(1)} %pad_maximum_fusion.1), dimensions={1,2,3} | broadcast | bytes 573440 | tf_op jit(solution)/shard_map/tile | solution.py:184
  2.4 6.3 %all-to-all-start = ((bf16[16,16,896]{2,1,0:T(8,128)(2,1)}), bf16[16,16,896]{2,1,0:T(8,128)(2,1)S(1)}, u32[]{:S(2)}, u32[]{:S(2)}) async-start(bf16[16,16,896]{2,1,0:T(8,128)(2,1)} %bitcast.7), calls=%async_computation | async-start | bytes 917504 | tf_op jit(solution)/shard_map/all_to_all | solution.py:185
  8.7 0.0 slice-start
  8.7 0.0 slice-start.1
  8.8 0.9 %slice-done = bf16[1,384,384]{2,1,0:T(8,128)(2,1)S(1)} async-done(((bf16[1,512,384]{2,1,0:T(8,128)(2,1)}), bf16[1,384,384]{2,1,0:T(8,128)(2,1)S(1)}, s32[]{:S(2)}) %slice-start) | async-done | bytes 294936 | tf_op jit(solution)/shard_map/slice | solution.py:209
  9.7 0.1 slice-done.1
  9.8 0.0 copy-start.4
  9.8 0.1 pad_maximum_fusion.refs_0_
  9.9 0.0 copy-start
  9.9 3.5 %collective-permute-start = (bf16[2,384,384]{2,1,0:T(8,128)(2,1)S(1)}, bf16[2,384,384]{2,1,0:T(8,128)(2,1)S(1)}, u32[]{:S(2)}, u32[]{:S(2)}) collective-permute-start(bf16[2,384,384]{2,1,0:T(8,128)(2,1)S(1)} %pad_maximum_fusion.refs_0_), channel_id=1, source_target_pairs={{0,4},{1,5},{2,6},{3,7},{4,8},{5,9},{6,10},{7,11},{8,12},{9,13},{1... | collective-permute-start | bytes 1769480 | tf_op jit(solution)/shard_map/ppermute | solution.py:23
  13.4 2.5 %collective-permute-start.1 = (bf16[2,384,384]{2,1,0:T(8,128)(2,1)S(1)}, bf16[2,384,384]{2,1,0:T(8,128)(2,1)S(1)}, u32[]{:S(2)}, u32[]{:S(2)}) collective-permute-start(bf16[2,384,384]{2,1,0:T(8,128)(2,1)S(1)} %pad_maximum_fusion.refs_0_), channel_id=1, source_target_pairs={{4,0},{5,1},{6,2},{7,3},{8,4},{9,5},{10,6},{11,7},{12,8},{13,9},{1... | collective-permute-start | bytes 1769480 | tf_op jit(solution)/shard_map/ppermute | solution.py:23
  16.0 0.0 copy-done.4
  16.0 0.9 %copy.8 = bf16[1,512,384]{1,2,0:T(8,128)(2,1)} copy(bf16[1,512,384]{2,1,0:T(8,128)(2,1)S(1)} %copy-done.4) | data formatting | bytes 786432 | tf_op args[0]
  16.9 0.7 %and_convert_fusion.refs_1_ = f32[384,1]{1,0:T(8,128)} fusion(s32[]{:T(128)S(6)} %mul.2, pred[]{:T(512)S(6)} %and.135), kind=kLoop, calls=%fused_computation.10 | loop fusion | flops 4608 | bytes 1541 | tf_op jit(solution)/shard_map/convert_element_type | solution.py:233
  17.6 0.0 copy-done
  17.6 4.5 %shard_map.64 = (f32[8,512]{1,0:T(8,128)}, f32[384,512]{1,0:T(8,128)}) custom-call(bf16[384,512]{1,0:T(8,128)(2,1)} %bitcast.14, bf16[2,384,384]{2,1,0:T(8,128)(2,1)} %copy-done, f32[384,1]{1,0:T(8,128)} %and_convert_fusion.refs_1_), custom_call_target="tpu_custom_call" | custom-call | flops 301989888 | bytes 2981888 | tf_op jit(solution)/shard_map/pallas_call | solution.py:155
  22.2 0.8 %and_convert_fusion.1 = (f32[384,1]{1,0:T(8,128)}, f32[384,1]{1,0:T(8,128)}) fusion(s32[]{:T(128)S(6)} %mul.2, pred[]{:T(512)S(6)} %and.131, pred[]{:T(512)S(6)} %and.126), kind=kLoop, calls=%fused_computation.11 | loop fusion | flops 5376 | bytes 3078 | tf_op jit(solution)/shard_map/convert_element_type | solution.py:233
  23.0 0.0 all-to-all-done
  23.0 0.0 copy-start.1
  23.0 0.7 %compare_convert_fusion.refs_1_ = f32[256,1]{1,0:T(8,128)} fusion(bf16[256,896]{1,0:T(8,128)(2,1)S(1)} %bitcast.17), kind=kLoop, calls=%fused_computation.13 | loop fusion | flops 512 | bytes 1536 | tf_op jit(solution)/shard_map/convert_element_type | solution.py:233
  23.7 0.1 copy-done.1
  23.8 4.2 %shard_map.65 = (f32[8,512]{1,0:T(8,128)}, f32[384,512]{1,0:T(8,128)}) custom-call(bf16[384,512]{1,0:T(8,128)(2,1)} %bitcast.15, bf16[256,896]{1,0:T(8,128)(2,1)} %bitcast.18, f32[256,1]{1,0:T(8,128)} %compare_convert_fusion.refs_1_, f32[8,512]{1,0:T(8,128)} %get-tuple-element.9.refs_2_, f32[384,512]{1,0:T(8,128)} %get-tuple-element.10.refs_3_), custom_call_target="tpu_custom_call" | custom-call | flops 201326592 | bytes 2785280 | tf_op jit(solution)/shard_map/pallas_call | solution.py:155
  28.0 4.0 %collective-permute-done.refs_0_ = bf16[2,384,384]{2,1,0:T(8,128)(2,1)S(1)} collective-permute-done((bf16[2,384,384]{2,1,0:T(8,128)(2,1)S(1)}, bf16[2,384,384]{2,1,0:T(8,128)(2,1)S(1)}, u32[]{:S(2)}, u32[]{:S(2)}) %collective-permute-start) | collective-permute-done | bytes 589856 | tf_op jit(solution)/shard_map/ppermute | solution.py:23
  32.0 0.0 copy-start.2
  32.0 1.9 %collective-permute-done.1.refs_1_ = bf16[2,384,384]{2,1,0:T(8,128)(2,1)S(1)} collective-permute-done((bf16[2,384,384]{2,1,0:T(8,128)(2,1)S(1)}, bf16[2,384,384]{2,1,0:T(8,128)(2,1)S(1)}, u32[]{:S(2)}, u32[]{:S(2)}) %collective-permute-start.1) | collective-permute-done | bytes 589856 | tf_op jit(solution)/shard_map/ppermute | solution.py:23
  33.9 0.0 copy-start.3
  33.9 0.0 copy-done.2
  33.9 0.8 %copy-done.3 = bf16[2,384,384]{2,1,0:T(8,128)(2,1)} copy-done((bf16[2,384,384]{2,1,0:T(8,128)(2,1)}, bf16[2,384,384]{2,1,0:T(8,128)(2,1)S(1)}, u32[]{:S(2)}) %copy-start.3) | copy-done | bytes 589848
  34.7 5.5 %shard_map.66 = bf16[512,384]{1,0:T(8,128)(2,1)} custom-call(bf16[384,512]{1,0:T(8,128)(2,1)} %bitcast.16, bf16[2,384,384]{2,1,0:T(8,128)(2,1)} %copy-done.2, bf16[2,384,384]{2,1,0:T(8,128)(2,1)} %copy-done.3, f32[384,1]{1,0:T(8,128)} %get-tuple-element.26.refs_2_, f32[384,1]{1,0:T(8,128)} %get-tuple-element.25.refs_3_, f32[8,512]{1,0:T(8,128)} %get-tuple-element.11.refs_4_, ...), custom_call_target="tpu_custom_call" | custom-call | flops 603979776 | bytes 3571712 | tf_op jit(solution)/shard_map/pallas_call | solution.py:155
  (2 shorter events, 0.0 us)
Async XLA Ops:
  2.4 20.6 %all-to-all-start = ((bf16[16,16,896]{2,1,0:T(8,128)(2,1)}), bf16[16,16,896]{2,1,0:T(8,128)(2,1)S(1)}, u32[]{:S(2)}, u32[]{:S(2)}) async-start(bf16[16,16,896]{2,1,0:T(8,128)(2,1)} %bitcast.7), calls=%async_computation | async-start | bytes 917504 | tf_op jit(solution)/shard_map/all_to_all | solution.py:185
  8.7 1.0 %slice-start = ((bf16[1,512,384]{2,1,0:T(8,128)(2,1)}), bf16[1,384,384]{2,1,0:T(8,128)(2,1)S(1)}, s32[]{:S(2)}) async-start(bf16[1,512,384]{2,1,0:T(8,128)(2,1)} %param.7), calls=%async_computation.1 | async-start | bytes 589824 | tf_op jit(solution)/shard_map/slice | solution.py:209
  8.7 1.0 %slice-start.1 = ((bf16[1,512,384]{2,1,0:T(8,128)(2,1)}), bf16[1,384,384]{2,1,0:T(8,128)(2,1)S(1)}, s32[]{:S(2)}) async-start(bf16[1,512,384]{2,1,0:T(8,128)(2,1)} %param.8), calls=%async_computation.2 | async-start | bytes 589824 | tf_op jit(solution)/shard_map/slice | solution.py:209
  9.8 6.2 %copy-start.4 = (bf16[1,512,384]{2,1,0:T(8,128)(2,1)S(1)}, bf16[1,512,384]{2,1,0:T(8,128)(2,1)}, u32[]{:S(2)}) copy-start(bf16[1,512,384]{2,1,0:T(8,128)(2,1)} %param.6) | copy-start | bytes 1179652
  9.9 7.8 %copy-start = (bf16[2,384,384]{2,1,0:T(8,128)(2,1)}, bf16[2,384,384]{2,1,0:T(8,128)(2,1)S(1)}, u32[]{:S(2)}) copy-start(bf16[2,384,384]{2,1,0:T(8,128)(2,1)S(1)} %pad_maximum_fusion.refs_0_) | copy-start | bytes 1769476
  9.9 22.1 %collective-permute-start = (bf16[2,384,384]{2,1,0:T(8,128)(2,1)S(1)}, bf16[2,384,384]{2,1,0:T(8,128)(2,1)S(1)}, u32[]{:S(2)}, u32[]{:S(2)}) collective-permute-start(bf16[2,384,384]{2,1,0:T(8,128)(2,1)S(1)} %pad_maximum_fusion.refs_0_), channel_id=1, source_target_pairs={{0,4},{1,5},{2,6},{3,7},{4,8},{5,9},{6,10},{7,11},{8,12},{9,13},{1... | collective-permute-start | bytes 1769480 | tf_op jit(solution)/shard_map/ppermute | solution.py:23
  13.4 20.5 %collective-permute-start.1 = (bf16[2,384,384]{2,1,0:T(8,128)(2,1)S(1)}, bf16[2,384,384]{2,1,0:T(8,128)(2,1)S(1)}, u32[]{:S(2)}, u32[]{:S(2)}) collective-permute-start(bf16[2,384,384]{2,1,0:T(8,128)(2,1)S(1)} %pad_maximum_fusion.refs_0_), channel_id=1, source_target_pairs={{4,0},{5,1},{6,2},{7,3},{8,4},{9,5},{10,6},{11,7},{12,8},{13,9},{1... | collective-permute-start | bytes 1769480 | tf_op jit(solution)/shard_map/ppermute | solution.py:23
  23.0 0.8 %copy-start.1 = (bf16[16,16,896]{2,1,0:T(8,128)(2,1)}, bf16[16,16,896]{2,1,0:T(8,128)(2,1)S(1)}, u32[]{:S(2)}) copy-start(bf16[16,16,896]{2,1,0:T(8,128)(2,1)S(1)} %all-to-all-done) | copy-start | bytes 1376260
  32.0 1.9 %copy-start.2 = (bf16[2,384,384]{2,1,0:T(8,128)(2,1)}, bf16[2,384,384]{2,1,0:T(8,128)(2,1)S(1)}, u32[]{:S(2)}) copy-start(bf16[2,384,384]{2,1,0:T(8,128)(2,1)S(1)} %collective-permute-done.refs_0_) | copy-start | bytes 1769476
  33.9 0.8 %copy-start.3 = (bf16[2,384,384]{2,1,0:T(8,128)(2,1)}, bf16[2,384,384]{2,1,0:T(8,128)(2,1)S(1)}, u32[]{:S(2)}) copy-start(bf16[2,384,384]{2,1,0:T(8,128)(2,1)S(1)} %collective-permute-done.1.refs_1_) | copy-start | bytes 1769476

commit v12 on v10

--- a/solution.py
+++ b/solution.py
@@ -131,7 +131,7 @@
         cost_estimate=pl.CostEstimate(
             flops=flops, transcendentals=tokens * key_total * head_count, bytes_accessed=moved
         ),
-    )(query_t, *sources, *keeps, *carry_args)
+    )(query_t, *[pltpu.with_memory_space_constraint(s, pltpu.VMEM) for s in sources], *keeps, *carry_args)
 
 
 def text_pieces(text_keys, text_values, text_mask, group_count, lane_width):

time: 40.1 us -> 39 us (0.973)
  local copies, waits for them, and re-layouts: 4.63 us -> 3.7 us
  Pallas kernels: 12.1 us -> 11.5 us
  waiting for transfers between devices: 7.45 us -> 7.92 us
    unnamed x11 -> x3, local copies, waits for them, and re-layouts: 1.86 us -> 0.94 us
    pallas_call x3, Pallas kernels: 12.1 us -> 11.5 us  [window_attention(): pl.pallas_call(functools.partial(window_kernel, tuple(layout), carry is n...]
    ppermute x2, waiting for transfers between devices: 7.45 us -> 7.92 us  [passed_along(): lax.ppermute(value, axis, [(source, source + steps) for source in range(f...]
where the time goes in v12:
time: 39 us; the launch traced here: 38.5 us
  starting transfers between devices  12.3 us (32%)
  Pallas kernels  11.5 us (29%)
  waiting for transfers between devices  7.92 us (20%)
  local copies, waits for them, and re-layouts  3.7 us (9%)
  other arithmetic  2.96 us (8%)
    pallas_call x3, Pallas kernels, window_attention(): pl.pallas_call(functools.partial(window_kernel, tuple(layout), carry is n...  11.5 us
    ppermute x2, waiting for transfers between devices, passed_along(): lax.ppermute(value, axis, [(source, source + steps) for source in range(f...  7.92 us
    all_to_all x1, starting transfers between devices, text_pieces(): got = lax.all_to_all(outgoing, 'tile', 0, 0, tiled=True)  6.3 us
    ppermute x2, starting transfers between devices, passed_along(): lax.ppermute(value, axis, [(source, source + steps) for source in range(f...  6.01 us
    convert_element_type x3, other arithmetic, shards(): as_row = lambda keep: keep.astype(jnp.float32)[:, None]  2.2 us
    slice x4, local copies, waits for them, and re-layouts, shards(): own_pair = jnp.stack([keys[0, :key_rows], values[0, :key_rows]])  1.04 us
    unnamed x3, local copies, waits for them, and re-layouts  0.94 us
    slice x1, local copies, waits for them, and re-layouts, text_pieces(): text_keys[:, g * lane_width:(g + 1) * lane_width]  0.84 us
  transfers between devices with their start and end apart: 3, of which 2 were waited for; matrix products, arithmetic and copies ran while one was open for 8% of the time, Pallas kernels for 18%

profile of v12, /device:TPU:10, one launch (start us, length us, event | category | flops | bytes accessed | tf_op | source)
XLA Modules:
  0.0 38.5 jit_solution(10651582539426924439)
XLA Ops:
  0.0 0.7 %convert_element_type.39 = bf16[16]{0:T(256)(128)(2,1)S(1)} convert(s32[16]{0:T(128)} %param.11) | non-fusion elementwise | flops 16 | bytes 96 | tf_op jit(solution)/shard_map/convert_element_type | solution.py:140
  0.7 0.8 %fusion.9 = (bf16[16,384]{1,0:T(8,128)(2,1)S(1)}, bf16[16,384]{1,0:T(8,128)(2,1)S(1)}, bf16[16,384]{1,0:T(8,128)(2,1)S(1)}, bf16[16,384]{1,0:T(8,128)(2,1)S(1)},...) fusion(bf16[16,1536]{1,0:T(8,128)(2,1)} %param.9, ...), kind=kLoop, calls=%fused_computation.23 | loop fusion | bytes 196608 | tf_op jit(solution)/shard_map/slice | solution.py:145
  1.5 0.1 broadcast_in_dim.4
  1.6 0.8 %tile.8 = bf16[4,4,16,896]{3,2,1,0:T(8,128)(2,1)} broadcast(bf16[4,16,896]{2,1,0:T(8,128)(2,1)S(1)} %pad_maximum_fusion.1), dimensions={1,2,3} | broadcast | bytes 573440 | tf_op jit(solution)/shard_map/tile | solution.py:154
  2.4 6.3 %all-to-all-start = ((bf16[16,16,896]{2,1,0:T(8,128)(2,1)}), bf16[16,16,896]{2,1,0:T(8,128)(2,1)S(1)}, u32[]{:S(2)}, u32[]{:S(2)}) async-start(bf16[16,16,896]{2,1,0:T(8,128)(2,1)} %bitcast.7), calls=%async_computation | async-start | bytes 917504 | tf_op jit(solution)/shard_map/all_to_all | solution.py:155
  8.7 0.0 slice-start
  8.7 0.0 slice-start.1
  8.8 0.9 %slice-done = bf16[1,384,384]{2,1,0:T(8,128)(2,1)S(1)} async-done(((bf16[1,512,384]{2,1,0:T(8,128)(2,1)}), bf16[1,384,384]{2,1,0:T(8,128)(2,1)S(1)}, s32[]{:S(2)}) %slice-start) | async-done | bytes 294936 | tf_op jit(solution)/shard_map/slice | solution.py:179
  9.7 0.1 slice-done.1
  9.8 0.0 copy-start
  9.8 0.1 pad_maximum_fusion.refs_0_
  9.9 3.5 %collective-permute-start = (bf16[2,384,384]{2,1,0:T(8,128)(2,1)S(1)}, bf16[2,384,384]{2,1,0:T(8,128)(2,1)S(1)}, u32[]{:S(2)}, u32[]{:S(2)}) collective-permute-start(bf16[2,384,384]{2,1,0:T(8,128)(2,1)S(1)} %pad_maximum_fusion.refs_0_), channel_id=1, source_target_pairs={{0,4},{1,5},{2,6},{3,7},{4,8},{5,9},{6,10},{7,11},{8,12},{9,13},{1... | collective-permute-start | bytes 1769480 | tf_op jit(solution)/shard_map/ppermute | solution.py:23
  13.4 2.5 %collective-permute-start.1 = (bf16[2,384,384]{2,1,0:T(8,128)(2,1)S(1)}, bf16[2,384,384]{2,1,0:T(8,128)(2,1)S(1)}, u32[]{:S(2)}, u32[]{:S(2)}) collective-permute-start(bf16[2,384,384]{2,1,0:T(8,128)(2,1)S(1)} %pad_maximum_fusion.refs_0_), channel_id=1, source_target_pairs={{4,0},{5,1},{6,2},{7,3},{8,4},{9,5},{10,6},{11,7},{12,8},{13,9},{1... | collective-permute-start | bytes 1769480 | tf_op jit(solution)/shard_map/ppermute | solution.py:23
  15.9 0.0 copy-done
  15.9 0.9 %copy.8 = bf16[1,512,384]{1,2,0:T(8,128)(2,1)} copy(bf16[1,512,384]{2,1,0:T(8,128)(2,1)S(1)} %copy-done) | data formatting | bytes 786432 | tf_op args[0]
  16.9 0.7 %and_convert_fusion.refs_1_ = f32[384,1]{1,0:T(8,128)} fusion(s32[]{:T(128)S(6)} %mul.2, pred[]{:T(512)S(6)} %and.135), kind=kLoop, calls=%fused_computation.10 | loop fusion | flops 4608 | bytes 1541 | tf_op jit(solution)/shard_map/convert_element_type | solution.py:203
  17.6 3.4 %shard_map.64 = (f32[8,512]{1,0:T(8,128)}, f32[384,512]{1,0:T(8,128)}) custom-call(bf16[384,512]{1,0:T(8,128)(2,1)} %bitcast.16, bf16[2,384,384]{2,1,0:T(8,128)(2,1)S(1)} %pad_maximum_fusion.refs_0_, f32[384,1]{1,0:T(8,128)} %and_convert_fusion.refs_1_), custom_call_target="tpu_custom_call" | custom-call | flops 301989888 | bytes 2981888 | tf_op jit(solution)/shard_map/pallas_call | solution.py:126
  21.0 0.8 %and_convert_fusion.1 = (f32[384,1]{1,0:T(8,128)}, f32[384,1]{1,0:T(8,128)}) fusion(s32[]{:T(128)S(6)} %mul.2, pred[]{:T(512)S(6)} %and.131, pred[]{:T(512)S(6)} %and.126), kind=kLoop, calls=%fused_computation.11 | loop fusion | flops 5376 | bytes 3078 | tf_op jit(solution)/shard_map/convert_element_type | solution.py:203
  21.8 0.0 all-to-all-done
  21.8 0.7 %compare_convert_fusion.refs_1_ = f32[256,1]{1,0:T(8,128)} fusion(bf16[256,896]{1,0:T(8,128)(2,1)S(1)} %bitcast.14), kind=kLoop, calls=%fused_computation.13 | loop fusion | flops 512 | bytes 1536 | tf_op jit(solution)/shard_map/convert_element_type | solution.py:203
  22.5 3.4 %shard_map.65 = (f32[8,512]{1,0:T(8,128)}, f32[384,512]{1,0:T(8,128)}) custom-call(bf16[384,512]{1,0:T(8,128)(2,1)} %bitcast.17, bf16[256,896]{1,0:T(8,128)(2,1)S(1)} %bitcast.15, f32[256,1]{1,0:T(8,128)} %compare_convert_fusion.refs_1_, f32[8,512]{1,0:T(8,128)} %get-tuple-element.9.refs_2_, f32[384,512]{1,0:T(8,128)} %get-tuple-element.10.refs_3_), custom_call_target="tpu_custom_call" | custom-call | flops 201326592 | bytes 2785280 | tf_op jit(solution)/shard_map/pallas_call | solution.py:126
  25.9 6.0 %collective-permute-done.refs_0_ = bf16[2,384,384]{2,1,0:T(8,128)(2,1)S(1)} collective-permute-done((bf16[2,384,384]{2,1,0:T(8,128)(2,1)S(1)}, bf16[2,384,384]{2,1,0:T(8,128)(2,1)S(1)}, u32[]{:S(2)}, u32[]{:S(2)}) %collective-permute-start) | collective-permute-done | bytes 589856 | tf_op jit(solution)/shard_map/ppermute | solution.py:23
  32.0 1.9 %collective-permute-done.1.refs_1_ = bf16[2,384,384]{2,1,0:T(8,128)(2,1)S(1)} collective-permute-done((bf16[2,384,384]{2,1,0:T(8,128)(2,1)S(1)}, bf16[2,384,384]{2,1,0:T(8,128)(2,1)S(1)}, u32[]{:S(2)}, u32[]{:S(2)}) %collective-permute-start.1) | collective-permute-done | bytes 589856 | tf_op jit(solution)/shard_map/ppermute | solution.py:23
  33.9 4.7 %shard_map.66 = bf16[512,384]{1,0:T(8,128)(2,1)} custom-call(bf16[384,512]{1,0:T(8,128)(2,1)} %bitcast.18, bf16[2,384,384]{2,1,0:T(8,128)(2,1)S(1)} %collective-permute-done.refs_0_, bf16[2,384,384]{2,1,0:T(8,128)(2,1)S(1)} %collective-permute-done.1.refs_1_, f32[384,1]{1,0:T(8,128)} %get-tuple-element.26.refs_2_, f32[384,1]{1,0:T(8,128)} %get-tuple-element.25.refs_3_, ...), custom_call_target="tpu_custom_call" | custom-call | flops 603979776 | bytes 3571712 | tf_op jit(solution)/shard_map/pallas_call | solution.py:126
  (2 shorter events, 0.0 us)
Async XLA Ops:
  2.4 19.4 %all-to-all-start = ((bf16[16,16,896]{2,1,0:T(8,128)(2,1)}), bf16[16,16,896]{2,1,0:T(8,128)(2,1)S(1)}, u32[]{:S(2)}, u32[]{:S(2)}) async-start(bf16[16,16,896]{2,1,0:T(8,128)(2,1)} %bitcast.7), calls=%async_computation | async-start | bytes 917504 | tf_op jit(solution)/shard_map/all_to_all | solution.py:155
  8.7 1.0 %slice-start = ((bf16[1,512,384]{2,1,0:T(8,128)(2,1)}), bf16[1,384,384]{2,1,0:T(8,128)(2,1)S(1)}, s32[]{:S(2)}) async-start(bf16[1,512,384]{2,1,0:T(8,128)(2,1)} %param.7), calls=%async_computation.1 | async-start | bytes 589824 | tf_op jit(solution)/shard_map/slice | solution.py:179
  8.7 1.0 %slice-start.1 = ((bf16[1,512,384]{2,1,0:T(8,128)(2,1)}), bf16[1,384,384]{2,1,0:T(8,128)(2,1)S(1)}, s32[]{:S(2)}) async-start(bf16[1,512,384]{2,1,0:T(8,128)(2,1)} %param.8), calls=%async_computation.2 | async-start | bytes 589824 | tf_op jit(solution)/shard_map/slice | solution.py:179
  9.8 6.2 %copy-start = (bf16[1,512,384]{2,1,0:T(8,128)(2,1)S(1)}, bf16[1,512,384]{2,1,0:T(8,128)(2,1)}, u32[]{:S(2)}) copy-start(bf16[1,512,384]{2,1,0:T(8,128)(2,1)} %param.6) | copy-start | bytes 1179652
  9.9 22.1 %collective-permute-start = (bf16[2,384,384]{2,1,0:T(8,128)(2,1)S(1)}, bf16[2,384,384]{2,1,0:T(8,128)(2,1)S(1)}, u32[]{:S(2)}, u32[]{:S(2)}) collective-permute-start(bf16[2,384,384]{2,1,0:T(8,128)(2,1)S(1)} %pad_maximum_fusion.refs_0_), channel_id=1, source_target_pairs={{0,4},{1,5},{2,6},{3,7},{4,8},{5,9},{6,10},{7,11},{8,12},{9,13},{1... | collective-permute-start | bytes 1769480 | tf_op jit(solution)/shard_map/ppermute | solution.py:23
  13.4 20.5 %collective-permute-start.1 = (bf16[2,384,384]{2,1,0:T(8,128)(2,1)S(1)}, bf16[2,384,384]{2,1,0:T(8,128)(2,1)S(1)}, u32[]{:S(2)}, u32[]{:S(2)}) collective-permute-start(bf16[2,384,384]{2,1,0:T(8,128)(2,1)S(1)} %pad_maximum_fusion.refs_0_), channel_id=1, source_target_pairs={{4,0},{5,1},{6,2},{7,3},{8,4},{9,5},{10,6},{11,7},{12,8},{13,9},{1... | collective-permute-start | bytes 1769480 | tf_op jit(solution)/shard_map/ppermute | solution.py:23

commit v13 on v12

--- a/solution.py
+++ b/solution.py
@@ -131,7 +131,7 @@
         cost_estimate=pl.CostEstimate(
             flops=flops, transcendentals=tokens * key_total * head_count, bytes_accessed=moved
         ),
-    )(query_t, *[pltpu.with_memory_space_constraint(s, pltpu.VMEM) for s in sources], *keeps, *carry_args)
+    )(*[pltpu.with_memory_space_constraint(a, pltpu.VMEM) for a in (query_t, *sources, *keeps)], *carry_args)
 
 
 def text_pieces(text_keys, text_values, text_mask, group_count, lane_width):

time: 39 us -> 38.6 us (0.990)
  waiting for transfers between devices: 7.92 us -> 11.9 us
  other arithmetic: 2.96 us -> 0.9 us
  Pallas kernels: 11.5 us -> 10 us
  local copies, waits for them, and re-layouts: 3.7 us -> 2.95 us
    all_to_all x1, waiting for transfers between devices: 0.01 us -> 2.28 us  [text_pieces(): got = lax.all_to_all(outgoing, 'tile', 0, 0, tiled=True)]
    convert_element_type x3, other arithmetic: 2.2 us -> 0.14 us  [shards(): as_row = lambda keep: keep.astype(jnp.float32)[:, None]]
    ppermute x2, waiting for transfers between devices: 7.92 us -> 9.63 us  [passed_along(): lax.ppermute(value, axis, [(source, source + steps) for source in range(f...]
    pallas_call x3, Pallas kernels: 11.5 us -> 10 us  [window_attention(): pl.pallas_call(functools.partial(window_kernel, tuple(layout), carry is n...]
    unnamed x3, local copies, waits for them, and re-layouts: 0.94 us -> 0.19 us
  transfers between devices with their start and end apart: 3 -> 3, of which waited for: 2 -> 3; matrix products, arithmetic and copies ran while one was open for 8% -> 1% of each run, Pallas kernels for 18% -> 15%
where the time goes in v13:
time: 38.6 us; the launch traced here: 38.2 us
  starting transfers between devices  12.3 us (32%)
  waiting for transfers between devices  11.9 us (31%)
  Pallas kernels  10 us (26%)
  local copies, waits for them, and re-layouts  2.95 us (8%)
  other arithmetic  0.9 us (2%)
    pallas_call x3, Pallas kernels, window_attention(): pl.pallas_call(functools.partial(window_kernel, tuple(layout), carry is n...  10 us
    ppermute x2, waiting for transfers between devices, passed_along(): lax.ppermute(value, axis, [(source, source + steps) for source in range(f...  9.63 us
    all_to_all x1, starting transfers between devices, text_pieces(): got = lax.all_to_all(outgoing, 'tile', 0, 0, tiled=True)  6.3 us
    ppermute x2, starting transfers between devices, passed_along(): lax.ppermute(value, axis, [(source, source + steps) for source in range(f...  6.01 us
    all_to_all x1, waiting for transfers between devices, text_pieces(): got = lax.all_to_all(outgoing, 'tile', 0, 0, tiled=True)  2.28 us
    slice x4, local copies, waits for them, and re-layouts, shards(): own_pair = jnp.stack([keys[0, :key_rows], values[0, :key_rows]])  1.04 us
    slice x1, local copies, waits for them, and re-layouts, text_pieces(): text_keys[:, g * lane_width:(g + 1) * lane_width]  0.84 us
    another operation x1, local copies, waits for them, and re-layouts, text_pieces(): jnp.tile(per_group, (count // group_count, 1, 1))  0.81 us
  transfers between devices with their start and end apart: 3, of which 3 were waited for; matrix products, arithmetic and copies ran while one was open for 1% of the time, Pallas kernels for 15%

profile of v13, /device:TPU:10, one launch (start us, length us, event | category | flops | bytes accessed | tf_op | source)
XLA Modules:
  0.0 38.2 jit_solution(18274982066064354607)
XLA Ops:
  0.0 0.7 %convert_element_type.39 = bf16[16]{0:T(256)(128)(2,1)S(1)} convert(s32[16]{0:T(128)} %param.11) | non-fusion elementwise | flops 16 | bytes 96 | tf_op jit(solution)/shard_map/convert_element_type | solution.py:140
  0.7 0.8 %fusion.9 = (bf16[16,384]{1,0:T(8,128)(2,1)S(1)}, bf16[16,384]{1,0:T(8,128)(2,1)S(1)}, bf16[16,384]{1,0:T(8,128)(2,1)S(1)}, bf16[16,384]{1,0:T(8,128)(2,1)S(1)},...) fusion(bf16[16,1536]{1,0:T(8,128)(2,1)} %param.9, ...), kind=kLoop, calls=%fused_computation.23 | loop fusion | bytes 196608 | tf_op jit(solution)/shard_map/slice | solution.py:145
  1.5 0.1 broadcast_in_dim.4
  1.6 0.8 %tile.8 = bf16[4,4,16,896]{3,2,1,0:T(8,128)(2,1)} broadcast(bf16[4,16,896]{2,1,0:T(8,128)(2,1)S(1)} %pad_maximum_fusion.1), dimensions={1,2,3} | broadcast | bytes 573440 | tf_op jit(solution)/shard_map/tile | solution.py:154
  2.4 6.3 %all-to-all-start = ((bf16[16,16,896]{2,1,0:T(8,128)(2,1)}), bf16[16,16,896]{2,1,0:T(8,128)(2,1)S(1)}, u32[]{:S(2)}, u32[]{:S(2)}) async-start(bf16[16,16,896]{2,1,0:T(8,128)(2,1)} %bitcast.7), calls=%async_computation | async-start | bytes 917504 | tf_op jit(solution)/shard_map/all_to_all | solution.py:155
  8.7 0.0 slice-start
  8.7 0.0 slice-start.1
  8.8 0.9 %slice-done = bf16[1,384,384]{2,1,0:T(8,128)(2,1)S(1)} async-done(((bf16[1,512,384]{2,1,0:T(8,128)(2,1)}), bf16[1,384,384]{2,1,0:T(8,128)(2,1)S(1)}, s32[]{:S(2)}) %slice-start) | async-done | bytes 294936 | tf_op jit(solution)/shard_map/slice | solution.py:179
  9.7 0.1 slice-done.1
  9.8 0.0 copy-start
  9.8 0.1 pad_maximum_fusion.refs_0_
  9.9 3.5 %collective-permute-start = (bf16[2,384,384]{2,1,0:T(8,128)(2,1)S(1)}, bf16[2,384,384]{2,1,0:T(8,128)(2,1)S(1)}, u32[]{:S(2)}, u32[]{:S(2)}) collective-permute-start(bf16[2,384,384]{2,1,0:T(8,128)(2,1)S(1)} %pad_maximum_fusion.refs_0_), channel_id=1, source_target_pairs={{0,4},{1,5},{2,6},{3,7},{4,8},{5,9},{6,10},{7,11},{8,12},{9,13},{1... | collective-permute-start | bytes 1769480 | tf_op jit(solution)/shard_map/ppermute | solution.py:23
  13.4 2.5 %collective-permute-start.1 = (bf16[2,384,384]{2,1,0:T(8,128)(2,1)S(1)}, bf16[2,384,384]{2,1,0:T(8,128)(2,1)S(1)}, u32[]{:S(2)}, u32[]{:S(2)}) collective-permute-start(bf16[2,384,384]{2,1,0:T(8,128)(2,1)S(1)} %pad_maximum_fusion.refs_0_), channel_id=1, source_target_pairs={{4,0},{5,1},{6,2},{7,3},{8,4},{9,5},{10,6},{11,7},{12,8},{13,9},{1... | collective-permute-start | bytes 1769480 | tf_op jit(solution)/shard_map/ppermute | solution.py:23
  15.9 0.0 copy-done
  15.9 0.2 copy.8
  16.2 0.1 and_convert_fusion.refs_1_
  16.2 2.4 %shard_map.64 = (f32[8,512]{1,0:T(8,128)}, f32[384,512]{1,0:T(8,128)}) custom-call(bf16[384,512]{1,0:T(8,128)(2,1)S(1)} %bitcast.14, bf16[2,384,384]{2,1,0:T(8,128)(2,1)S(1)} %pad_maximum_fusion.refs_0_, f32[384,1]{1,0:T(8,128)S(1)} %and_convert_fusion.refs_1_), custom_call_target="tpu_custom_call" | custom-call | flops 301989888 | bytes 2981888 | tf_op jit(solution)/shard_map/pallas_call | solution.py:126
  18.6 0.1 and_convert_fusion.1
  18.7 2.3 %all-to-all-done = bf16[16,16,896]{2,1,0:T(8,128)(2,1)S(1)} async-done(((bf16[16,16,896]{2,1,0:T(8,128)(2,1)}), bf16[16,16,896]{2,1,0:T(8,128)(2,1)S(1)}, u32[]{:S(2)}, u32[]{:S(2)}) %all-to-all-start) | async-done | bytes 458784 | tf_op jit(solution)/shard_map/all_to_all | solution.py:155
  21.0 3.2 %shard_map.65 = (f32[8,512]{1,0:T(8,128)}, f32[384,512]{1,0:T(8,128)}) custom-call(bf16[384,512]{1,0:T(8,128)(2,1)S(1)} %bitcast.15, bf16[256,896]{1,0:T(8,128)(2,1)S(1)} %bitcast.18, f32[256,1]{1,0:T(8,128)S(1)} %compare_convert_fusion.refs_1_, f32[8,512]{1,0:T(8,128)} %get-tuple-element.9.refs_2_, f32[384,512]{1,0:T(8,128)} %get-tuple-element.10.refs_3_), custom_call_target="tpu_custom_call" | custom-call | flops 201326592 | bytes 2785280 | tf_op jit(solution)/shard_map/pallas_call | solution.py:126
  24.2 7.8 %collective-permute-done.refs_0_ = bf16[2,384,384]{2,1,0:T(8,128)(2,1)S(1)} collective-permute-done((bf16[2,384,384]{2,1,0:T(8,128)(2,1)S(1)}, bf16[2,384,384]{2,1,0:T(8,128)(2,1)S(1)}, u32[]{:S(2)}, u32[]{:S(2)}) %collective-permute-start) | collective-permute-done | bytes 589856 | tf_op jit(solution)/shard_map/ppermute | solution.py:23
  32.0 1.9 %collective-permute-done.1.refs_1_ = bf16[2,384,384]{2,1,0:T(8,128)(2,1)S(1)} collective-permute-done((bf16[2,384,384]{2,1,0:T(8,128)(2,1)S(1)}, bf16[2,384,384]{2,1,0:T(8,128)(2,1)S(1)}, u32[]{:S(2)}, u32[]{:S(2)}) %collective-permute-start.1) | collective-permute-done | bytes 589856 | tf_op jit(solution)/shard_map/ppermute | solution.py:23
  33.9 4.4 %shard_map.66 = bf16[512,384]{1,0:T(8,128)(2,1)} custom-call(bf16[384,512]{1,0:T(8,128)(2,1)S(1)} %bitcast.16, bf16[2,384,384]{2,1,0:T(8,128)(2,1)S(1)} %collective-permute-done.refs_0_, bf16[2,384,384]{2,1,0:T(8,128)(2,1)S(1)} %collective-permute-done.1.refs_1_, f32[384,1]{1,0:T(8,128)S(1)} %get-tuple-element.26.refs_2_, ...), custom_call_target="tpu_custom_call" | custom-call | flops 603979776 | bytes 3571712 | tf_op jit(solution)/shard_map/pallas_call | solution.py:126
  (3 shorter events, 0.1 us)
Async XLA Ops:
  2.4 18.5 %all-to-all-start = ((bf16[16,16,896]{2,1,0:T(8,128)(2,1)}), bf16[16,16,896]{2,1,0:T(8,128)(2,1)S(1)}, u32[]{:S(2)}, u32[]{:S(2)}) async-start(bf16[16,16,896]{2,1,0:T(8,128)(2,1)} %bitcast.7), calls=%async_computation | async-start | bytes 917504 | tf_op jit(solution)/shard_map/all_to_all | solution.py:155
  8.7 1.0 %slice-start = ((bf16[1,512,384]{2,1,0:T(8,128)(2,1)}), bf16[1,384,384]{2,1,0:T(8,128)(2,1)S(1)}, s32[]{:S(2)}) async-start(bf16[1,512,384]{2,1,0:T(8,128)(2,1)} %param.7), calls=%async_computation.1 | async-start | bytes 589824 | tf_op jit(solution)/shard_map/slice | solution.py:179
  8.7 1.0 %slice-start.1 = ((bf16[1,512,384]{2,1,0:T(8,128)(2,1)}), bf16[1,384,384]{2,1,0:T(8,128)(2,1)S(1)}, s32[]{:S(2)}) async-start(bf16[1,512,384]{2,1,0:T(8,128)(2,1)} %param.8), calls=%async_computation.2 | async-start | bytes 589824 | tf_op jit(solution)/shard_map/slice | solution.py:179
  9.8 6.2 %copy-start = (bf16[1,512,384]{2,1,0:T(8,128)(2,1)S(1)}, bf16[1,512,384]{2,1,0:T(8,128)(2,1)}, u32[]{:S(2)}) copy-start(bf16[1,512,384]{2,1,0:T(8,128)(2,1)} %param.6) | copy-start | bytes 1179652
  9.9 22.1 %collective-permute-start = (bf16[2,384,384]{2,1,0:T(8,128)(2,1)S(1)}, bf16[2,384,384]{2,1,0:T(8,128)(2,1)S(1)}, u32[]{:S(2)}, u32[]{:S(2)}) collective-permute-start(bf16[2,384,384]{2,1,0:T(8,128)(2,1)S(1)} %pad_maximum_fusion.refs_0_), channel_id=1, source_target_pairs={{0,4},{1,5},{2,6},{3,7},{4,8},{5,9},{6,10},{7,11},{8,12},{9,13},{1... | collective-permute-start | bytes 1769480 | tf_op jit(solution)/shard_map/ppermute | solution.py:23
  13.4 20.5 %collective-permute-start.1 = (bf16[2,384,384]{2,1,0:T(8,128)(2,1)S(1)}, bf16[2,384,384]{2,1,0:T(8,128)(2,1)S(1)}, u32[]{:S(2)}, u32[]{:S(2)}) collective-permute-start(bf16[2,384,384]{2,1,0:T(8,128)(2,1)S(1)} %pad_maximum_fusion.refs_0_), channel_id=1, source_target_pairs={{4,0},{5,1},{6,2},{7,3},{8,4},{9,5},{10,6},{11,7},{12,8},{13,9},{1... | collective-permute-start | bytes 1769480 | tf_op jit(solution)/shard_map/ppermute | solution.py:23

commit v14 on v13

--- a/solution.py
+++ b/solution.py
@@ -117,7 +117,10 @@
         out_shape = jax.ShapeDtypeStruct((tokens, lane_width), jnp.bfloat16)
         out_specs = pl.BlockSpec(memory_space=pltpu.VMEM)
     else:
-        out_shape = (stat_shape, jax.ShapeDtypeStruct((lane_width, tokens), jnp.float32))
+        out_shape = (
+            pltpu.VMEM(stat_shape.shape, stat_shape.dtype),
+            pltpu.VMEM((lane_width, tokens), jnp.float32),
+        )
         out_specs = tuple(pl.BlockSpec(memory_space=pltpu.VMEM) for _ in range(2))
     carry_args = () if carry is None else tuple(carry)
     operand_count = 1 + 2 * len(blocks) + len(carry_args)
@@ -131,7 +134,8 @@
         cost_estimate=pl.CostEstimate(
             flops=flops, transcendentals=tokens * key_total * head_count, bytes_accessed=moved
         ),
-    )(*[pltpu.with_memory_space_constraint(a, pltpu.VMEM) for a in (query_t, *sources, *keeps)], *carry_args)
+        compiler_params=pltpu.CompilerParams(vmem_limit_bytes=16 * 1024 * 1024),
+    )(*[pltpu.with_memory_space_constraint(a, pltpu.VMEM) for a in (query_t, *sources, *keeps, *carry_args)])
 
 
 def text_pieces(text_keys, text_values, text_mask, group_count, lane_width):

time: 38.6 us -> 38.7 us (level)
  waiting for transfers between devices: 11.9 us -> 15 us
  Pallas kernels: 10 us -> 6.94 us
    pallas_call x3, Pallas kernels: 10 us -> 6.94 us  [window_attention(): pl.pallas_call(functools.partial(window_kernel, tuple(layout), carry is n...]
    ppermute x2, waiting for transfers between devices: 9.63 us -> 11.8 us  [passed_along(): lax.ppermute(value, axis, [(source, source + steps) for source in range(f...]
    all_to_all x1, waiting for transfers between devices: 2.28 us -> 3.16 us  [text_pieces(): got = lax.all_to_all(outgoing, 'tile', 0, 0, tiled=True)]
  transfers between devices with their start and end apart: 3 -> 3, of which waited for: 3 -> 3; matrix products, arithmetic and copies ran while one was open for 1% -> 1% of each run, Pallas kernels for 15% -> 7%
where the time goes in v14:
time: 38.7 us; the launch traced here: 38.3 us
  waiting for transfers between devices  15 us (39%)
  starting transfers between devices  12.3 us (32%)
  Pallas kernels  6.94 us (18%)
  local copies, waits for them, and re-layouts  2.95 us (8%)
  other arithmetic  0.9 us (2%)
    ppermute x2, waiting for transfers between devices, passed_along(): lax.ppermute(value, axis, [(source, source + steps) for source in range(f...  11.8 us
    pallas_call x3, Pallas kernels, window_attention(): pl.pallas_call(functools.partial(window_kernel, tuple(layout), carry is n...  6.94 us
    all_to_all x1, starting transfers between devices, text_pieces(): got = lax.all_to_all(outgoing, 'tile', 0, 0, tiled=True)  6.3 us
    ppermute x2, starting transfers between devices, passed_along(): lax.ppermute(value, axis, [(source, source + steps) for source in range(f...  6.01 us
    all_to_all x1, waiting for transfers between devices, text_pieces(): got = lax.all_to_all(outgoing, 'tile', 0, 0, tiled=True)  3.16 us
    slice x4, local copies, waits for them, and re-layouts, shards(): own_pair = jnp.stack([keys[0, :key_rows], values[0, :key_rows]])  1.04 us
    slice x1, local copies, waits for them, and re-layouts, text_pieces(): text_keys[:, g * lane_width:(g + 1) * lane_width]  0.84 us
    another operation x1, local copies, waits for them, and re-layouts, text_pieces(): jnp.tile(per_group, (count // group_count, 1, 1))  0.81 us
  transfers between devices with their start and end apart: 3, of which 3 were waited for; matrix products, arithmetic and copies ran while one was open for 1% of the time, Pallas kernels for 7%

profile of v14, /device:TPU:10, one launch (start us, length us, event | category | flops | bytes accessed | tf_op | source)
XLA Modules:
  0.0 38.3 jit_solution(9626734191801563076)
XLA Ops:
  0.0 0.7 %convert_element_type.39 = bf16[16]{0:T(256)(128)(2,1)S(1)} convert(s32[16]{0:T(128)} %param.11) | non-fusion elementwise | flops 16 | bytes 96 | tf_op jit(solution)/shard_map/convert_element_type | solution.py:144
  0.7 0.8 %fusion.9 = (bf16[16,384]{1,0:T(8,128)(2,1)S(1)}, bf16[16,384]{1,0:T(8,128)(2,1)S(1)}, bf16[16,384]{1,0:T(8,128)(2,1)S(1)}, bf16[16,384]{1,0:T(8,128)(2,1)S(1)},...) fusion(bf16[16,1536]{1,0:T(8,128)(2,1)} %param.9, ...), kind=kLoop, calls=%fused_computation.23 | loop fusion | bytes 196608 | tf_op jit(solution)/shard_map/slice | solution.py:149
  1.5 0.1 broadcast_in_dim.4
  1.6 0.8 %tile.8 = bf16[4,4,16,896]{3,2,1,0:T(8,128)(2,1)} broadcast(bf16[4,16,896]{2,1,0:T(8,128)(2,1)S(1)} %pad_maximum_fusion.1), dimensions={1,2,3} | broadcast | bytes 573440 | tf_op jit(solution)/shard_map/tile | solution.py:158
  2.4 6.3 %all-to-all-start = ((bf16[16,16,896]{2,1,0:T(8,128)(2,1)}), bf16[16,16,896]{2,1,0:T(8,128)(2,1)S(1)}, u32[]{:S(2)}, u32[]{:S(2)}) async-start(bf16[16,16,896]{2,1,0:T(8,128)(2,1)} %bitcast.7), calls=%async_computation | async-start | bytes 917504 | tf_op jit(solution)/shard_map/all_to_all | solution.py:159
  8.7 0.0 slice-start
  8.7 0.0 slice-start.1
  8.7 0.9 %slice-done = bf16[1,384,384]{2,1,0:T(8,128)(2,1)S(1)} async-done(((bf16[1,512,384]{2,1,0:T(8,128)(2,1)}), bf16[1,384,384]{2,1,0:T(8,128)(2,1)S(1)}, s32[]{:S(2)}) %slice-start) | async-done | bytes 294936 | tf_op jit(solution)/shard_map/slice | solution.py:183
  9.7 0.1 slice-done.1
  9.8 0.0 copy-start
  9.8 0.1 pad_maximum_fusion.refs_0_
  9.9 3.5 %collective-permute-start = (bf16[2,384,384]{2,1,0:T(8,128)(2,1)S(1)}, bf16[2,384,384]{2,1,0:T(8,128)(2,1)S(1)}, u32[]{:S(2)}, u32[]{:S(2)}) collective-permute-start(bf16[2,384,384]{2,1,0:T(8,128)(2,1)S(1)} %pad_maximum_fusion.refs_0_), channel_id=1, source_target_pairs={{0,4},{1,5},{2,6},{3,7},{4,8},{5,9},{6,10},{7,11},{8,12},{9,13},{1... | collective-permute-start | bytes 1769480 | tf_op jit(solution)/shard_map/ppermute | solution.py:23
  13.4 2.5 %collective-permute-start.1 = (bf16[2,384,384]{2,1,0:T(8,128)(2,1)S(1)}, bf16[2,384,384]{2,1,0:T(8,128)(2,1)}, u32[]{:S(2)}, u32[]{:S(2)}) collective-permute-start(bf16[2,384,384]{2,1,0:T(8,128)(2,1)S(1)} %pad_maximum_fusion.refs_0_), channel_id=1, source_target_pairs={{4,0},{5,1},{6,2},{7,3},{8,4},{9,5},{10,6},{11,7},{12,8},{13,9},{1... | collective-permute-start | bytes 1769480 | tf_op jit(solution)/shard_map/ppermute | solution.py:23
  15.9 0.0 copy-done
  15.9 0.2 copy.8
  16.2 0.1 and_convert_fusion.refs_1_
  16.2 1.5 %shard_map.64 = (f32[8,512]{1,0:T(8,128)S(1)}, f32[384,512]{1,0:T(8,128)S(1)}) custom-call(bf16[384,512]{1,0:T(8,128)(2,1)S(1)} %bitcast.14, bf16[2,384,384]{2,1,0:T(8,128)(2,1)S(1)} %pad_maximum_fusion.refs_0_, f32[384,1]{1,0:T(8,128)S(1)} %and_convert_fusion.refs_1_), custom_call_target="tpu_custom_call" | custom-call | flops 301989888 | bytes 2981888 | tf_op jit(solution)/shard_map/pallas_call | solution.py:129
  17.7 0.1 and_convert_fusion.1
  17.8 3.2 %all-to-all-done = bf16[16,16,896]{2,1,0:T(8,128)(2,1)S(1)} async-done(((bf16[16,16,896]{2,1,0:T(8,128)(2,1)}), bf16[16,16,896]{2,1,0:T(8,128)(2,1)S(1)}, u32[]{:S(2)}, u32[]{:S(2)}) %all-to-all-start) | async-done | bytes 458784 | tf_op jit(solution)/shard_map/all_to_all | solution.py:159
  21.0 1.2 %shard_map.65 = (f32[8,512]{1,0:T(8,128)S(1)}, f32[384,512]{1,0:T(8,128)S(1)}) custom-call(bf16[384,512]{1,0:T(8,128)(2,1)S(1)} %bitcast.15, bf16[256,896]{1,0:T(8,128)(2,1)S(1)} %bitcast.18, f32[256,1]{1,0:T(8,128)S(1)} %compare_convert_fusion.refs_1_, f32[8,512]{1,0:T(8,128)S(1)} %get-tuple-element.9.refs_2_, f32[384,512]{1,0:T(8,128)S(1)} %get-tuple-element.10.refs_3_), custom_call_target="tpu_custom_call" | custom-call | flops 201326592 | bytes 2785280 | tf_op jit(solution)/shard_map/pallas_call | solution.py:129
  22.2 9.8 %collective-permute-done.refs_0_ = bf16[2,384,384]{2,1,0:T(8,128)(2,1)S(1)} collective-permute-done((bf16[2,384,384]{2,1,0:T(8,128)(2,1)S(1)}, bf16[2,384,384]{2,1,0:T(8,128)(2,1)S(1)}, u32[]{:S(2)}, u32[]{:S(2)}) %collective-permute-start) | collective-permute-done | bytes 589856 | tf_op jit(solution)/shard_map/ppermute | solution.py:23
  32.0 2.0 %collective-permute-done.1.refs_1_ = bf16[2,384,384]{2,1,0:T(8,128)(2,1)} collective-permute-done((bf16[2,384,384]{2,1,0:T(8,128)(2,1)S(1)}, bf16[2,384,384]{2,1,0:T(8,128)(2,1)}, u32[]{:S(2)}, u32[]{:S(2)}) %collective-permute-start.1) | collective-permute-done | bytes 589856 | tf_op jit(solution)/shard_map/ppermute | solution.py:23
  34.0 4.3 %shard_map.66 = bf16[512,384]{1,0:T(8,128)(2,1)} custom-call(bf16[384,512]{1,0:T(8,128)(2,1)S(1)} %bitcast.16, bf16[2,384,384]{2,1,0:T(8,128)(2,1)S(1)} %collective-permute-done.refs_0_, bf16[2,384,384]{2,1,0:T(8,128)(2,1)} %collective-permute-done.1.refs_1_, f32[384,1]{1,0:T(8,128)S(1)} %get-tuple-element.26.refs_2_, ...), custom_call_target="tpu_custom_call" | custom-call | flops 603979776 | bytes 3571712 | tf_op jit(solution)/shard_map/pallas_call | solution.py:129
  (3 shorter events, 0.1 us)
Async XLA Ops:
  2.4 18.5 %all-to-all-start = ((bf16[16,16,896]{2,1,0:T(8,128)(2,1)}), bf16[16,16,896]{2,1,0:T(8,128)(2,1)S(1)}, u32[]{:S(2)}, u32[]{:S(2)}) async-start(bf16[16,16,896]{2,1,0:T(8,128)(2,1)} %bitcast.7), calls=%async_computation | async-start | bytes 917504 | tf_op jit(solution)/shard_map/all_to_all | solution.py:159
  8.7 1.0 %slice-start = ((bf16[1,512,384]{2,1,0:T(8,128)(2,1)}), bf16[1,384,384]{2,1,0:T(8,128)(2,1)S(1)}, s32[]{:S(2)}) async-start(bf16[1,512,384]{2,1,0:T(8,128)(2,1)} %param.7), calls=%async_computation.1 | async-start | bytes 589824 | tf_op jit(solution)/shard_map/slice | solution.py:183
  8.7 1.0 %slice-start.1 = ((bf16[1,512,384]{2,1,0:T(8,128)(2,1)}), bf16[1,384,384]{2,1,0:T(8,128)(2,1)S(1)}, s32[]{:S(2)}) async-start(bf16[1,512,384]{2,1,0:T(8,128)(2,1)} %param.8), calls=%async_computation.2 | async-start | bytes 589824 | tf_op jit(solution)/shard_map/slice | solution.py:183
  9.8 6.2 %copy-start = (bf16[1,512,384]{2,1,0:T(8,128)(2,1)S(1)}, bf16[1,512,384]{2,1,0:T(8,128)(2,1)}, u32[]{:S(2)}) copy-start(bf16[1,512,384]{2,1,0:T(8,128)(2,1)} %param.6) | copy-start | bytes 1179652
  9.9 22.1 %collective-permute-start = (bf16[2,384,384]{2,1,0:T(8,128)(2,1)S(1)}, bf16[2,384,384]{2,1,0:T(8,128)(2,1)S(1)}, u32[]{:S(2)}, u32[]{:S(2)}) collective-permute-start(bf16[2,384,384]{2,1,0:T(8,128)(2,1)S(1)} %pad_maximum_fusion.refs_0_), channel_id=1, source_target_pairs={{0,4},{1,5},{2,6},{3,7},{4,8},{5,9},{6,10},{7,11},{8,12},{9,13},{1... | collective-permute-start | bytes 1769480 | tf_op jit(solution)/shard_map/ppermute | solution.py:23
  13.4 20.6 %collective-permute-start.1 = (bf16[2,384,384]{2,1,0:T(8,128)(2,1)S(1)}, bf16[2,384,384]{2,1,0:T(8,128)(2,1)}, u32[]{:S(2)}, u32[]{:S(2)}) collective-permute-start(bf16[2,384,384]{2,1,0:T(8,128)(2,1)S(1)} %pad_maximum_fusion.refs_0_), channel_id=1, source_target_pairs={{4,0},{5,1},{6,2},{7,3},{8,4},{9,5},{10,6},{11,7},{12,8},{13,9},{1... | collective-permute-start | bytes 1769480 | tf_op jit(solution)/shard_map/ppermute | solution.py:23

commit v15 on v14

--- a/solution.py
+++ b/solution.py
@@ -210,7 +210,9 @@
         carry = window_attention(
             query_t, [(text_got, 0, head_count, as_row(text_keep))], carry=carry, finish=False
         )
-        blocks = [(width_set[off_width], 0, 1, as_row(keep_mask(0, 0, off_width))) for off_width in (-1, 1)]
+        blocks = [(width_set[-1], 0, 1, as_row(keep_mask(0, 0, -1)))]
+        carry = window_attention(query_t, blocks, carry=carry, finish=False)
+        blocks = [(width_set[1], 0, 1, as_row(keep_mask(0, 0, 1)))]
         return window_attention(query_t, blocks, carry=carry)[None]
     piece_keys = text_got[:, :lane_width]
     piece_values = text_got[:, lane_width : 2 * lane_width]

time: 38.7 us -> 38.3 us (0.990)
  the two profiles are of different devices: /device:TPU:10 before, /device:TPU:16 now
where the time goes in v15:
time: 38.3 us; the launch traced here: 37.9 us
  waiting for transfers between devices  14.1 us (37%)
  starting transfers between devices  12.2 us (32%)
  Pallas kernels  7.57 us (20%)
  local copies, waits for them, and re-layouts  2.95 us (8%)
  other arithmetic  0.94 us (2%)
    ppermute x2, waiting for transfers between devices, passed_along(): lax.ppermute(value, axis, [(source, source + steps) for source in range(f...  10.4 us
    pallas_call x4, Pallas kernels, window_attention(): pl.pallas_call(functools.partial(window_kernel, tuple(layout), carry is n...  7.57 us
    all_to_all x1, starting transfers between devices, text_pieces(): got = lax.all_to_all(outgoing, 'tile', 0, 0, tiled=True)  6.18 us
    ppermute x2, starting transfers between devices, passed_along(): lax.ppermute(value, axis, [(source, source + steps) for source in range(f...  5.98 us
    all_to_all x1, waiting for transfers between devices, text_pieces(): got = lax.all_to_all(outgoing, 'tile', 0, 0, tiled=True)  3.74 us
    slice x4, local copies, waits for them, and re-layouts, shards(): own_pair = jnp.stack([keys[0, :key_rows], values[0, :key_rows]])  1.04 us
    slice x1, local copies, waits for them, and re-layouts, text_pieces(): text_keys[:, g * lane_width:(g + 1) * lane_width]  0.84 us
    another operation x1, local copies, waits for them, and re-layouts, text_pieces(): jnp.tile(per_group, (count // group_count, 1, 1))  0.81 us
  transfers between devices with their start and end apart: 3, of which 2 were waited for; matrix products, arithmetic and copies ran while one was open for 1% of the time, Pallas kernels for 14%

profile of v15, /device:TPU:16, one launch (start us, length us, event | category | flops | bytes accessed | tf_op | source)
XLA Modules:
  0.0 37.9 jit_solution(14601956045481928156)
XLA Ops:
  0.0 0.7 %convert_element_type.39 = bf16[16]{0:T(256)(128)(2,1)S(1)} convert(s32[16]{0:T(128)} %param.11) | non-fusion elementwise | flops 16 | bytes 96 | tf_op jit(solution)/shard_map/convert_element_type | solution.py:144
  0.7 0.8 %fusion.9 = (bf16[16,384]{1,0:T(8,128)(2,1)S(1)}, bf16[16,384]{1,0:T(8,128)(2,1)S(1)}, bf16[16,384]{1,0:T(8,128)(2,1)S(1)}, bf16[16,384]{1,0:T(8,128)(2,1)S(1)},...) fusion(bf16[16,1536]{1,0:T(8,128)(2,1)} %param.9, ...), kind=kLoop, calls=%fused_computation.23 | loop fusion | bytes 196608 | tf_op jit(solution)/shard_map/slice | solution.py:149
  1.5 0.1 broadcast_in_dim.4
  1.6 0.8 %tile.8 = bf16[4,4,16,896]{3,2,1,0:T(8,128)(2,1)} broadcast(bf16[4,16,896]{2,1,0:T(8,128)(2,1)S(1)} %pad_maximum_fusion.1), dimensions={1,2,3} | broadcast | bytes 573440 | tf_op jit(solution)/shard_map/tile | solution.py:158
  2.4 6.2 %all-to-all-start = ((bf16[16,16,896]{2,1,0:T(8,128)(2,1)}), bf16[16,16,896]{2,1,0:T(8,128)(2,1)S(1)}, u32[]{:S(2)}, u32[]{:S(2)}) async-start(bf16[16,16,896]{2,1,0:T(8,128)(2,1)} %bitcast.7), calls=%async_computation | async-start | bytes 917504 | tf_op jit(solution)/shard_map/all_to_all | solution.py:159
  8.6 0.0 slice-start
  8.6 0.0 slice-start.1
  8.6 0.9 %slice-done = bf16[1,384,384]{2,1,0:T(8,128)(2,1)S(1)} async-done(((bf16[1,512,384]{2,1,0:T(8,128)(2,1)}), bf16[1,384,384]{2,1,0:T(8,128)(2,1)S(1)}, s32[]{:S(2)}) %slice-start) | async-done | bytes 294936 | tf_op jit(solution)/shard_map/slice | solution.py:183
  9.6 0.1 slice-done.1
  9.7 0.0 copy-start
  9.7 0.1 pad_maximum_fusion.refs_0_
  9.7 3.5 %collective-permute-start.1 = (bf16[2,384,384]{2,1,0:T(8,128)(2,1)S(1)}, bf16[2,384,384]{2,1,0:T(8,128)(2,1)}, u32[]{:S(2)}, u32[]{:S(2)}) collective-permute-start(bf16[2,384,384]{2,1,0:T(8,128)(2,1)S(1)} %pad_maximum_fusion.refs_0_), channel_id=1, source_target_pairs={{0,4},{1,5},{2,6},{3,7},{4,8},{5,9},{6,10},{7,11},{8,12},{9,13},{1... | collective-permute-start | bytes 1769480 | tf_op jit(solution)/shard_map/ppermute | solution.py:23
  13.3 2.5 %collective-permute-start = (bf16[2,384,384]{2,1,0:T(8,128)(2,1)S(1)}, bf16[2,384,384]{2,1,0:T(8,128)(2,1)S(1)}, u32[]{:S(2)}, u32[]{:S(2)}) collective-permute-start(bf16[2,384,384]{2,1,0:T(8,128)(2,1)S(1)} %pad_maximum_fusion.refs_0_), channel_id=1, source_target_pairs={{4,0},{5,1},{6,2},{7,3},{8,4},{9,5},{10,6},{11,7},{12,8},{13,9},{1... | collective-permute-start | bytes 1769480 | tf_op jit(solution)/shard_map/ppermute | solution.py:23
  15.8 0.1 and_convert_fusion.refs_1_
  15.9 0.0 copy-done
  15.9 0.2 copy.8
  16.1 1.5 %shard_map.64 = (f32[8,512]{1,0:T(8,128)S(1)}, f32[384,512]{1,0:T(8,128)S(1)}) custom-call(bf16[384,512]{1,0:T(8,128)(2,1)S(1)} %bitcast.14, bf16[2,384,384]{2,1,0:T(8,128)(2,1)S(1)} %pad_maximum_fusion.refs_0_, f32[384,1]{1,0:T(8,128)S(1)} %and_convert_fusion.refs_1_), custom_call_target="tpu_custom_call" | custom-call | flops 301989888 | bytes 2981888 | tf_op jit(solution)/shard_map/pallas_call | solution.py:129
  17.6 0.1 and_convert_fusion.1.refs_1_
  17.6 0.1 and_convert_fusion.2.refs_1_
  17.7 3.7 %all-to-all-done = bf16[16,16,896]{2,1,0:T(8,128)(2,1)S(1)} async-done(((bf16[16,16,896]{2,1,0:T(8,128)(2,1)}), bf16[16,16,896]{2,1,0:T(8,128)(2,1)S(1)}, u32[]{:S(2)}, u32[]{:S(2)}) %all-to-all-start) | async-done | bytes 458784 | tf_op jit(solution)/shard_map/all_to_all | solution.py:159
  21.5 1.2 %shard_map.65 = (f32[8,512]{1,0:T(8,128)S(1)}, f32[384,512]{1,0:T(8,128)S(1)}) custom-call(bf16[384,512]{1,0:T(8,128)(2,1)S(1)} %bitcast.15, bf16[256,896]{1,0:T(8,128)(2,1)S(1)} %bitcast.19, f32[256,1]{1,0:T(8,128)S(1)} %compare_convert_fusion.refs_1_, f32[8,512]{1,0:T(8,128)S(1)} %get-tuple-element.11.refs_2_, f32[384,512]{1,0:T(8,128)S(1)} %get-tuple-element.12.refs_3_), custom_call_target="tpu_custom_call" | custom-call | flops 201326592 | bytes 2785280 | tf_op jit(solution)/shard_map/pallas_call | solution.py:129
  22.6 10.4 %collective-permute-done.1.refs_0_ = bf16[2,384,384]{2,1,0:T(8,128)(2,1)} collective-permute-done((bf16[2,384,384]{2,1,0:T(8,128)(2,1)S(1)}, bf16[2,384,384]{2,1,0:T(8,128)(2,1)}, u32[]{:S(2)}, u32[]{:S(2)}) %collective-permute-start.1) | collective-permute-done | bytes 589856 | tf_op jit(solution)/shard_map/ppermute | solution.py:23
  33.0 2.6 %shard_map.66 = (f32[8,512]{1,0:T(8,128)S(1)}, f32[384,512]{1,0:T(8,128)S(1)}) custom-call(bf16[384,512]{1,0:T(8,128)(2,1)S(1)} %bitcast.16, bf16[2,384,384]{2,1,0:T(8,128)(2,1)} %collective-permute-done.1.refs_0_, f32[384,1]{1,0:T(8,128)S(1)} %and_convert_fusion.1.refs_1_, f32[8,512]{1,0:T(8,128)S(1)} %get-tuple-element.13.refs_2_, ...), custom_call_target="tpu_custom_call" | custom-call | flops 301989888 | bytes 2981888 | tf_op jit(solution)/shard_map/pallas_call | solution.py:129
  35.6 0.0 collective-permute-done.refs_0_
  35.6 2.3 %shard_map.67 = bf16[512,384]{1,0:T(8,128)(2,1)} custom-call(bf16[384,512]{1,0:T(8,128)(2,1)S(1)} %bitcast.17, bf16[2,384,384]{2,1,0:T(8,128)(2,1)S(1)} %collective-permute-done.refs_0_, f32[384,1]{1,0:T(8,128)S(1)} %and_convert_fusion.2.refs_1_, f32[8,512]{1,0:T(8,128)S(1)} %get-tuple-element.15.refs_2_, f32[384,512]{1,0:T(8,128)S(1)} %get-tuple-element.16.refs_3_), custom_call_target="tpu_custom_call" | custom-call | flops 301989888 | bytes 2981888 | tf_op jit(solution)/shard_map/pallas_call | solution.py:129
  (3 shorter events, 0.1 us)
Async XLA Ops:
  2.4 19.0 %all-to-all-start = ((bf16[16,16,896]{2,1,0:T(8,128)(2,1)}), bf16[16,16,896]{2,1,0:T(8,128)(2,1)S(1)}, u32[]{:S(2)}, u32[]{:S(2)}) async-start(bf16[16,16,896]{2,1,0:T(8,128)(2,1)} %bitcast.7), calls=%async_computation | async-start | bytes 917504 | tf_op jit(solution)/shard_map/all_to_all | solution.py:159
  8.6 1.0 %slice-start = ((bf16[1,512,384]{2,1,0:T(8,128)(2,1)}), bf16[1,384,384]{2,1,0:T(8,128)(2,1)S(1)}, s32[]{:S(2)}) async-start(bf16[1,512,384]{2,1,0:T(8,128)(2,1)} %param.7), calls=%async_computation.1 | async-start | bytes 589824 | tf_op jit(solution)/shard_map/slice | solution.py:183
  8.6 1.0 %slice-start.1 = ((bf16[1,512,384]{2,1,0:T(8,128)(2,1)}), bf16[1,384,384]{2,1,0:T(8,128)(2,1)S(1)}, s32[]{:S(2)}) async-start(bf16[1,512,384]{2,1,0:T(8,128)(2,1)} %param.8), calls=%async_computation.2 | async-start | bytes 589824 | tf_op jit(solution)/shard_map/slice | solution.py:183
  9.7 6.2 %copy-start = (bf16[1,512,384]{2,1,0:T(8,128)(2,1)S(1)}, bf16[1,512,384]{2,1,0:T(8,128)(2,1)}, u32[]{:S(2)}) copy-start(bf16[1,512,384]{2,1,0:T(8,128)(2,1)} %param.6) | copy-start | bytes 1179652
  9.7 23.3 %collective-permute-start.1 = (bf16[2,384,384]{2,1,0:T(8,128)(2,1)S(1)}, bf16[2,384,384]{2,1,0:T(8,128)(2,1)}, u32[]{:S(2)}, u32[]{:S(2)}) collective-permute-start(bf16[2,384,384]{2,1,0:T(8,128)(2,1)S(1)} %pad_maximum_fusion.refs_0_), channel_id=1, source_target_pairs={{0,4},{1,5},{2,6},{3,7},{4,8},{5,9},{6,10},{7,11},{8,12},{9,13},{1... | collective-permute-start | bytes 1769480 | tf_op jit(solution)/shard_map/ppermute | solution.py:23
  13.3 22.4 %collective-permute-start = (bf16[2,384,384]{2,1,0:T(8,128)(2,1)S(1)}, bf16[2,384,384]{2,1,0:T(8,128)(2,1)S(1)}, u32[]{:S(2)}, u32[]{:S(2)}) collective-permute-start(bf16[2,384,384]{2,1,0:T(8,128)(2,1)S(1)} %pad_maximum_fusion.refs_0_), channel_id=1, source_target_pairs={{4,0},{5,1},{6,2},{7,3},{8,4},{9,5},{10,6},{11,7},{12,8},{13,9},{1... | collective-permute-start | bytes 1769480 | tf_op jit(solution)/shard_map/ppermute | solution.py:23

commit v16 on v15

--- a/solution.py
+++ b/solution.py
@@ -141,21 +141,13 @@
 def text_pieces(text_keys, text_values, text_mask, group_count, lane_width):
     count = lax.axis_size("tile")
     rows = text_keys.shape[0]
-    flags = jnp.broadcast_to(text_mask.astype(jnp.bfloat16)[:, None], (rows, 128))
-    per_group = jnp.stack(
-        [
-            jnp.concatenate(
-                [
-                    text_keys[:, g * lane_width : (g + 1) * lane_width],
-                    text_values[:, g * lane_width : (g + 1) * lane_width],
-                    flags,
-                ],
-                axis=1,
-            )
-            for g in range(group_count)
-        ]
-    )
-    outgoing = jnp.tile(per_group, (count // group_count, 1, 1)).reshape(count * rows, 2 * lane_width + 128)
+    shape = (rows, group_count, lane_width)
+    flags = jnp.broadcast_to(text_mask.astype(jnp.bfloat16)[:, None, None], (rows, group_count, 128))
+    per_group = jnp.concatenate([text_keys.reshape(shape), text_values.reshape(shape), flags], axis=2)
+    per_group = jnp.transpose(per_group, (1, 0, 2))
+    width = 2 * lane_width + 128
+    outgoing = jnp.broadcast_to(per_group[None], (count // group_count, group_count, rows, width))
+    outgoing = outgoing.reshape(count * rows, width)
     got = lax.all_to_all(outgoing, "tile", 0, 0, tiled=True)
     return got, got[:, 2 * lane_width] > 0.5
 

time: 38.3 us -> 38.4 us (level)
  the two profiles are of different devices: /device:TPU:16 before, /device:TPU:18 now
where the time goes in v16:
time: 38.4 us; the launch traced here: 38 us
  waiting for transfers between devices  14.1 us (37%)
  starting transfers between devices  12.2 us (32%)
  Pallas kernels  7.57 us (20%)
  local copies, waits for them, and re-layouts  3.61 us (9%)
    ppermute x2, waiting for transfers between devices, passed_along(): lax.ppermute(value, axis, [(source, source + steps) for source in range(f...  10.4 us
    pallas_call x4, Pallas kernels, window_attention(): pl.pallas_call(functools.partial(window_kernel, tuple(layout), carry is n...  7.57 us
    all_to_all x1, starting transfers between devices, text_pieces(): got = lax.all_to_all(outgoing, 'tile', 0, 0, tiled=True)  6.18 us
    ppermute x2, starting transfers between devices, passed_along(): lax.ppermute(value, axis, [(source, source + steps) for source in range(f...  5.98 us
    all_to_all x1, waiting for transfers between devices, text_pieces(): got = lax.all_to_all(outgoing, 'tile', 0, 0, tiled=True)  3.74 us
    slice x4, local copies, waits for them, and re-layouts, shards(): own_pair = jnp.stack([keys[0, :key_rows], values[0, :key_rows]])  1.04 us
    unnamed x7, local copies, waits for them, and re-layouts  0.82 us
    reshape x1, local copies, waits for them, and re-layouts, text_pieces(): text_keys.reshape(shape)  0.82 us
  transfers between devices with their start and end apart: 3, of which 2 were waited for; matrix products, arithmetic and copies ran while one was open for 1% of the time, Pallas kernels for 14%

profile of v16, /device:TPU:18, one launch (start us, length us, event | category | flops | bytes accessed | tf_op | source)
XLA Modules:
  0.0 38.0 jit_solution(18259488389701801172)
XLA Ops:
  0.0 0.0 copy-start.1
  0.0 0.8 %reshape.72 = bf16[16,4,384]{2,1,0:T(4,128)(2,1)S(1)} reshape(bf16[16,1536]{1,0:T(8,128)(2,1)} %param.9) | data formatting | bytes 98304 | tf_op jit(solution)/shard_map/reshape | solution.py:146
  0.8 0.0 copy-done.1
  0.8 0.0 copy-start.2
  0.9 0.6 %copy-done.2 = s32[16]{0:T(128)S(1)} copy-done((s32[16]{0:T(128)S(1)}, s32[16]{0:T(128)}, u32[]{:S(2)}) %copy-start.2) | copy-done | bytes 88
  1.5 0.1 broadcast_in_dim.6
  1.6 0.1 maximum_bitcast_fusion
  1.7 0.8 %broadcast_in_dim.7 = bf16[4,4,16,896]{3,2,1,0:T(8,128)(2,1)} broadcast(bf16[4,16,896]{2,1,0:T(8,128)(2,1)S(1)} %copy.11), dimensions={1,2,3} | broadcast | bytes 573440 | tf_op jit(solution)/shard_map/broadcast_in_dim | solution.py:149
  2.5 6.2 %all-to-all-start = ((bf16[16,16,896]{2,1,0:T(8,128)(2,1)}), bf16[16,16,896]{2,1,0:T(8,128)(2,1)S(1)}, u32[]{:S(2)}, u32[]{:S(2)}) async-start(bf16[16,16,896]{2,1,0:T(8,128)(2,1)} %bitcast.4), calls=%async_computation | async-start | bytes 917504 | tf_op jit(solution)/shard_map/all_to_all | solution.py:151
  8.7 0.0 slice-start
  8.7 0.0 slice-start.1
  8.7 0.9 %slice-done = bf16[1,384,384]{2,1,0:T(8,128)(2,1)S(1)} async-done(((bf16[1,512,384]{2,1,0:T(8,128)(2,1)}), bf16[1,384,384]{2,1,0:T(8,128)(2,1)S(1)}, s32[]{:S(2)}) %slice-start) | async-done | bytes 294936 | tf_op jit(solution)/shard_map/slice | solution.py:175
  9.6 0.1 slice-done.1
  9.7 0.0 copy-start
  9.7 0.1 pad_maximum_fusion.refs_0_
  9.8 3.5 %collective-permute-start.1 = (bf16[2,384,384]{2,1,0:T(8,128)(2,1)S(1)}, bf16[2,384,384]{2,1,0:T(8,128)(2,1)}, u32[]{:S(2)}, u32[]{:S(2)}) collective-permute-start(bf16[2,384,384]{2,1,0:T(8,128)(2,1)S(1)} %pad_maximum_fusion.refs_0_), channel_id=1, source_target_pairs={{0,4},{1,5},{2,6},{3,7},{4,8},{5,9},{6,10},{7,11},{8,12},{9,13},{1... | collective-permute-start | bytes 1769480 | tf_op jit(solution)/shard_map/ppermute | solution.py:23
  13.3 2.5 %collective-permute-start = (bf16[2,384,384]{2,1,0:T(8,128)(2,1)S(1)}, bf16[2,384,384]{2,1,0:T(8,128)(2,1)S(1)}, u32[]{:S(2)}, u32[]{:S(2)}) collective-permute-start(bf16[2,384,384]{2,1,0:T(8,128)(2,1)S(1)} %pad_maximum_fusion.refs_0_), channel_id=1, source_target_pairs={{4,0},{5,1},{6,2},{7,3},{8,4},{9,5},{10,6},{11,7},{12,8},{13,9},{1... | collective-permute-start | bytes 1769480 | tf_op jit(solution)/shard_map/ppermute | solution.py:23
  15.8 0.1 and_convert_fusion.refs_1_
  15.9 0.0 copy-done
  15.9 0.2 copy.9
  16.1 1.5 %shard_map.64 = (f32[8,512]{1,0:T(8,128)S(1)}, f32[384,512]{1,0:T(8,128)S(1)}) custom-call(bf16[384,512]{1,0:T(8,128)(2,1)S(1)} %bitcast.8, bf16[2,384,384]{2,1,0:T(8,128)(2,1)S(1)} %pad_maximum_fusion.refs_0_, f32[384,1]{1,0:T(8,128)S(1)} %and_convert_fusion.refs_1_), custom_call_target="tpu_custom_call" | custom-call | flops 301989888 | bytes 2981888 | tf_op jit(solution)/shard_map/pallas_call | solution.py:129
  17.6 0.1 and_convert_fusion.1.refs_1_
  17.7 0.1 and_convert_fusion.2.refs_1_
  17.7 3.7 %all-to-all-done = bf16[16,16,896]{2,1,0:T(8,128)(2,1)S(1)} async-done(((bf16[16,16,896]{2,1,0:T(8,128)(2,1)}), bf16[16,16,896]{2,1,0:T(8,128)(2,1)S(1)}, u32[]{:S(2)}, u32[]{:S(2)}) %all-to-all-start) | async-done | bytes 458784 | tf_op jit(solution)/shard_map/all_to_all | solution.py:151
  21.5 1.2 %shard_map.65 = (f32[8,512]{1,0:T(8,128)S(1)}, f32[384,512]{1,0:T(8,128)S(1)}) custom-call(bf16[384,512]{1,0:T(8,128)(2,1)S(1)} %bitcast.9, bf16[256,896]{1,0:T(8,128)(2,1)S(1)} %bitcast.13, f32[256,1]{1,0:T(8,128)S(1)} %compare_convert_fusion.refs_1_, f32[8,512]{1,0:T(8,128)S(1)} %get-tuple-element.11.refs_2_, f32[384,512]{1,0:T(8,128)S(1)} %get-tuple-element.12.refs_3_), custom_call_target="tpu_custom_call" | custom-call | flops 201326592 | bytes 2785280 | tf_op jit(solution)/shard_map/pallas_call | solution.py:129
  22.7 10.4 %collective-permute-done.1.refs_0_ = bf16[2,384,384]{2,1,0:T(8,128)(2,1)} collective-permute-done((bf16[2,384,384]{2,1,0:T(8,128)(2,1)S(1)}, bf16[2,384,384]{2,1,0:T(8,128)(2,1)}, u32[]{:S(2)}, u32[]{:S(2)}) %collective-permute-start.1) | collective-permute-done | bytes 589856 | tf_op jit(solution)/shard_map/ppermute | solution.py:23
  33.0 2.6 %shard_map.66 = (f32[8,512]{1,0:T(8,128)S(1)}, f32[384,512]{1,0:T(8,128)S(1)}) custom-call(bf16[384,512]{1,0:T(8,128)(2,1)S(1)} %bitcast.10, bf16[2,384,384]{2,1,0:T(8,128)(2,1)} %collective-permute-done.1.refs_0_, f32[384,1]{1,0:T(8,128)S(1)} %and_convert_fusion.1.refs_1_, f32[8,512]{1,0:T(8,128)S(1)} %get-tuple-element.13.refs_2_, ...), custom_call_target="tpu_custom_call" | custom-call | flops 301989888 | bytes 2981888 | tf_op jit(solution)/shard_map/pallas_call | solution.py:129
  35.7 0.0 collective-permute-done.refs_0_
  35.7 2.3 %shard_map.67 = bf16[512,384]{1,0:T(8,128)(2,1)} custom-call(bf16[384,512]{1,0:T(8,128)(2,1)S(1)} %bitcast.11, bf16[2,384,384]{2,1,0:T(8,128)(2,1)S(1)} %collective-permute-done.refs_0_, f32[384,1]{1,0:T(8,128)S(1)} %and_convert_fusion.2.refs_1_, f32[8,512]{1,0:T(8,128)S(1)} %get-tuple-element.15.refs_2_, f32[384,512]{1,0:T(8,128)S(1)} %get-tuple-element.16.refs_3_), custom_call_target="tpu_custom_call" | custom-call | flops 301989888 | bytes 2981888 | tf_op jit(solution)/shard_map/pallas_call | solution.py:129
  (4 shorter events, 0.1 us)
Async XLA Ops:
  0.0 0.8 %copy-start.1 = (bf16[16,1536]{1,0:T(8,128)(2,1)S(1)}, bf16[16,1536]{1,0:T(8,128)(2,1)}, u32[]{:S(2)}) copy-start(bf16[16,1536]{1,0:T(8,128)(2,1)} %param.10) | copy-start | bytes 147460
  0.8 0.7 %copy-start.2 = (s32[16]{0:T(128)S(1)}, s32[16]{0:T(128)}, u32[]{:S(2)}) copy-start(s32[16]{0:T(128)} %param.11) | copy-start | bytes 196
  2.5 19.0 %all-to-all-start = ((bf16[16,16,896]{2,1,0:T(8,128)(2,1)}), bf16[16,16,896]{2,1,0:T(8,128)(2,1)S(1)}, u32[]{:S(2)}, u32[]{:S(2)}) async-start(bf16[16,16,896]{2,1,0:T(8,128)(2,1)} %bitcast.4), calls=%async_computation | async-start | bytes 917504 | tf_op jit(solution)/shard_map/all_to_all | solution.py:151
  8.7 1.0 %slice-start = ((bf16[1,512,384]{2,1,0:T(8,128)(2,1)}), bf16[1,384,384]{2,1,0:T(8,128)(2,1)S(1)}, s32[]{:S(2)}) async-start(bf16[1,512,384]{2,1,0:T(8,128)(2,1)} %param.8), calls=%async_computation.1 | async-start | bytes 589824 | tf_op jit(solution)/shard_map/slice | solution.py:175
  8.7 1.0 %slice-start.1 = ((bf16[1,512,384]{2,1,0:T(8,128)(2,1)}), bf16[1,384,384]{2,1,0:T(8,128)(2,1)S(1)}, s32[]{:S(2)}) async-start(bf16[1,512,384]{2,1,0:T(8,128)(2,1)} %param.7), calls=%async_computation.2 | async-start | bytes 589824 | tf_op jit(solution)/shard_map/slice | solution.py:175
  9.7 6.2 %copy-start = (bf16[1,512,384]{2,1,0:T(8,128)(2,1)S(1)}, bf16[1,512,384]{2,1,0:T(8,128)(2,1)}, u32[]{:S(2)}) copy-start(bf16[1,512,384]{2,1,0:T(8,128)(2,1)} %param.6) | copy-start | bytes 1179652
  9.8 23.3 %collective-permute-start.1 = (bf16[2,384,384]{2,1,0:T(8,128)(2,1)S(1)}, bf16[2,384,384]{2,1,0:T(8,128)(2,1)}, u32[]{:S(2)}, u32[]{:S(2)}) collective-permute-start(bf16[2,384,384]{2,1,0:T(8,128)(2,1)S(1)} %pad_maximum_fusion.refs_0_), channel_id=1, source_target_pairs={{0,4},{1,5},{2,6},{3,7},{4,8},{5,9},{6,10},{7,11},{8,12},{9,13},{1... | collective-permute-start | bytes 1769480 | tf_op jit(solution)/shard_map/ppermute | solution.py:23
  13.3 22.4 %collective-permute-start = (bf16[2,384,384]{2,1,0:T(8,128)(2,1)S(1)}, bf16[2,384,384]{2,1,0:T(8,128)(2,1)S(1)}, u32[]{:S(2)}, u32[]{:S(2)}) collective-permute-start(bf16[2,384,384]{2,1,0:T(8,128)(2,1)S(1)} %pad_maximum_fusion.refs_0_), channel_id=1, source_target_pairs={{4,0},{5,1},{6,2},{7,3},{8,4},{9,5},{10,6},{11,7},{12,8},{13,9},{1... | collective-permute-start | bytes 1769480 | tf_op jit(solution)/shard_map/ppermute | solution.py:23

commit v17 on v16

--- a/solution.py
+++ b/solution.py
@@ -138,7 +138,7 @@
     )(*[pltpu.with_memory_space_constraint(a, pltpu.VMEM) for a in (query_t, *sources, *keeps, *carry_args)])
 
 
-def text_pieces(text_keys, text_values, text_mask, group_count, lane_width):
+def text_pieces(text_keys, text_values, text_mask, group_count, lane_width, after=None):
     count = lax.axis_size("tile")
     rows = text_keys.shape[0]
     shape = (rows, group_count, lane_width)
@@ -148,6 +148,8 @@
     width = 2 * lane_width + 128
     outgoing = jnp.broadcast_to(per_group[None], (count // group_count, group_count, rows, width))
     outgoing = outgoing.reshape(count * rows, width)
+    if after is not None:
+        outgoing = lax.optimization_barrier((outgoing, after))[0]
     got = lax.all_to_all(outgoing, "tile", 0, 0, tiled=True)
     return got, got[:, 2 * lane_width] > 0.5
 
@@ -191,7 +193,7 @@
         jnp.zeros((head_count, tokens), jnp.float32),
         jnp.zeros((head_count, tokens, HEAD_DIM), jnp.float32),
     )
-    text_got, text_keep = text_pieces(text_keys, text_values, text_mask, group_count, lane_width)
+    text_got, text_keep = text_pieces(text_keys, text_values, text_mask, group_count, lane_width, own_pair)
     width_set = {0: own_pair}
     for off_width in (-1, 1):
         width_set[off_width] = passed_along(own_pair, "tile", -off_width * group_count)

time: 38.4 us -> 38.8 us (1.010)
  the two profiles are of different devices: /device:TPU:18 before, /device:TPU:16 now
where the time goes in v17:
time: 38.8 us; the launch traced here: 38.4 us
  waiting for transfers between devices  15.4 us (40%)
  starting transfers between devices  12.1 us (31%)
  Pallas kernels  7.57 us (20%)
  local copies, waits for them, and re-layouts  2.74 us (7%)
    ppermute x2, waiting for transfers between devices, passed_along(): lax.ppermute(value, axis, [(source, source + steps) for source in range(f...  10.4 us
    pallas_call x4, Pallas kernels, window_attention(): pl.pallas_call(functools.partial(window_kernel, tuple(layout), carry is n...  7.57 us
    all_to_all x1, starting transfers between devices, text_pieces(): got = lax.all_to_all(outgoing, 'tile', 0, 0, tiled=True)  6.32 us
    ppermute x2, starting transfers between devices, passed_along(): lax.ppermute(value, axis, [(source, source + steps) for source in range(f...  5.83 us
    all_to_all x1, waiting for transfers between devices, text_pieces(): got = lax.all_to_all(outgoing, 'tile', 0, 0, tiled=True)  5.01 us
    unnamed x9, local copies, waits for them, and re-layouts  0.99 us
    broadcast_in_dim x1, local copies, waits for them, and re-layouts, text_pieces(): jnp.broadcast_to(per_group[None], (count // group_count, group_count, row...  0.82 us
    slice x4, local copies, waits for them, and re-layouts, shards(): own_pair = jnp.stack([keys[0, :key_rows], values[0, :key_rows]])  0.8 us
  transfers between devices with their start and end apart: 3, of which 2 were waited for; matrix products, arithmetic and copies ran while one was open for 1% of the time, Pallas kernels for 14%

profile of v17, /device:TPU:16, one launch (start us, length us, event | category | flops | bytes accessed | tf_op | source)
XLA Modules:
  0.0 38.4 jit_solution(16651771453857104273)
XLA Ops:
  0.0 0.0 copy-start.1
  0.0 0.0 copy-start.2
  0.0 0.0 copy-start.3
  0.0 0.8 %copy-done.1 = bf16[16,1536]{1,0:T(8,128)(2,1)S(1)} copy-done((bf16[16,1536]{1,0:T(8,128)(2,1)S(1)}, bf16[16,1536]{1,0:T(8,128)(2,1)}, u32[]{:S(2)}) %copy-start.1) | copy-done | bytes 49176
  0.8 0.0 slice-start.1
  0.8 0.0 copy-done.2
  0.8 0.0 slice-start
  0.9 0.0 copy-done.3
  0.9 0.1 broadcast_in_dim.6
  1.0 0.1 maximum_bitcast_fusion
  1.1 0.7 %slice-done.1 = bf16[1,384,384]{2,1,0:T(8,128)(2,1)S(1)} async-done(((bf16[1,512,384]{2,1,0:T(8,128)(2,1)}), bf16[1,384,384]{2,1,0:T(8,128)(2,1)S(1)}, s32[]{:S(2)}) %slice-start.1) | async-done | bytes 294936 | tf_op jit(solution)/shard_map/slice | solution.py:177
  1.8 0.1 slice-done
  1.9 0.1 pad_maximum_fusion.refs_0_
  1.9 0.8 %broadcast_in_dim.7 = bf16[4,4,16,896]{3,2,1,0:T(8,128)(2,1)} broadcast(bf16[4,16,896]{2,1,0:T(8,128)(2,1)S(1)} %copy.11), dimensions={1,2,3} | broadcast | bytes 573440 | tf_op jit(solution)/shard_map/broadcast_in_dim | solution.py:149
  2.7 0.0 copy-start
  2.8 6.3 %all-to-all-start = ((bf16[16,16,896]{2,1,0:T(8,128)(2,1)}), bf16[16,16,896]{2,1,0:T(8,128)(2,1)S(1)}, u32[]{:S(2)}, u32[]{:S(2)}) async-start(bf16[16,16,896]{2,1,0:T(8,128)(2,1)} %bitcast.5), calls=%async_computation | async-start | bytes 917504 | tf_op jit(solution)/shard_map/all_to_all | solution.py:153
  9.1 3.4 %collective-permute-start.1 = (bf16[2,384,384]{2,1,0:T(8,128)(2,1)S(1)}, bf16[2,384,384]{2,1,0:T(8,128)(2,1)}, u32[]{:S(2)}, u32[]{:S(2)}) collective-permute-start(bf16[2,384,384]{2,1,0:T(8,128)(2,1)S(1)} %pad_maximum_fusion.refs_0_), channel_id=1, source_target_pairs={{0,4},{1,5},{2,6},{3,7},{4,8},{5,9},{6,10},{7,11},{8,12},{9,13},{1... | collective-permute-start | bytes 1769480 | tf_op jit(solution)/shard_map/ppermute | solution.py:23
  12.4 2.5 %collective-permute-start = (bf16[2,384,384]{2,1,0:T(8,128)(2,1)S(1)}, bf16[2,384,384]{2,1,0:T(8,128)(2,1)S(1)}, u32[]{:S(2)}, u32[]{:S(2)}) collective-permute-start(bf16[2,384,384]{2,1,0:T(8,128)(2,1)S(1)} %pad_maximum_fusion.refs_0_), channel_id=1, source_target_pairs={{4,0},{5,1},{6,2},{7,3},{8,4},{9,5},{10,6},{11,7},{12,8},{13,9},{1... | collective-permute-start | bytes 1769480 | tf_op jit(solution)/shard_map/ppermute | solution.py:23
  15.0 0.1 and_convert_fusion.refs_1_
  15.0 0.0 copy-done
  15.1 0.2 copy.9
  15.3 1.5 %shard_map.64 = (f32[8,512]{1,0:T(8,128)S(1)}, f32[384,512]{1,0:T(8,128)S(1)}) custom-call(bf16[384,512]{1,0:T(8,128)(2,1)S(1)} %bitcast.9, bf16[2,384,384]{2,1,0:T(8,128)(2,1)S(1)} %pad_maximum_fusion.refs_0_, f32[384,1]{1,0:T(8,128)S(1)} %and_convert_fusion.refs_1_), custom_call_target="tpu_custom_call" | custom-call | flops 301989888 | bytes 2981888 | tf_op jit(solution)/shard_map/pallas_call | solution.py:129
  16.8 0.1 and_convert_fusion.1.refs_1_
  16.8 0.1 and_convert_fusion.2.refs_1_
  16.9 5.0 %all-to-all-done = bf16[16,16,896]{2,1,0:T(8,128)(2,1)S(1)} async-done(((bf16[16,16,896]{2,1,0:T(8,128)(2,1)}), bf16[16,16,896]{2,1,0:T(8,128)(2,1)S(1)}, u32[]{:S(2)}, u32[]{:S(2)}) %all-to-all-start) | async-done | bytes 458784 | tf_op jit(solution)/shard_map/all_to_all | solution.py:153
  21.9 1.2 %shard_map.65 = (f32[8,512]{1,0:T(8,128)S(1)}, f32[384,512]{1,0:T(8,128)S(1)}) custom-call(bf16[384,512]{1,0:T(8,128)(2,1)S(1)} %bitcast.10, bf16[256,896]{1,0:T(8,128)(2,1)S(1)} %bitcast.14, f32[256,1]{1,0:T(8,128)S(1)} %compare_convert_fusion.refs_1_, f32[8,512]{1,0:T(8,128)S(1)} %get-tuple-element.13.refs_2_, f32[384,512]{1,0:T(8,128)S(1)} %get-tuple-element.14.refs_3_), custom_call_target="tpu_custom_call" | custom-call | flops 201326592 | bytes 2785280 | tf_op jit(solution)/shard_map/pallas_call | solution.py:129
  23.1 10.4 %collective-permute-done.1.refs_0_ = bf16[2,384,384]{2,1,0:T(8,128)(2,1)} collective-permute-done((bf16[2,384,384]{2,1,0:T(8,128)(2,1)S(1)}, bf16[2,384,384]{2,1,0:T(8,128)(2,1)}, u32[]{:S(2)}, u32[]{:S(2)}) %collective-permute-start.1) | collective-permute-done | bytes 589856 | tf_op jit(solution)/shard_map/ppermute | solution.py:23
  33.4 2.6 %shard_map.66 = (f32[8,512]{1,0:T(8,128)S(1)}, f32[384,512]{1,0:T(8,128)S(1)}) custom-call(bf16[384,512]{1,0:T(8,128)(2,1)S(1)} %bitcast.11, bf16[2,384,384]{2,1,0:T(8,128)(2,1)} %collective-permute-done.1.refs_0_, f32[384,1]{1,0:T(8,128)S(1)} %and_convert_fusion.1.refs_1_, f32[8,512]{1,0:T(8,128)S(1)} %get-tuple-element.15.refs_2_, ...), custom_call_target="tpu_custom_call" | custom-call | flops 301989888 | bytes 2981888 | tf_op jit(solution)/shard_map/pallas_call | solution.py:129
  36.1 0.0 collective-permute-done.refs_0_
  36.1 2.3 %shard_map.67 = bf16[512,384]{1,0:T(8,128)(2,1)} custom-call(bf16[384,512]{1,0:T(8,128)(2,1)S(1)} %bitcast.12, bf16[2,384,384]{2,1,0:T(8,128)(2,1)S(1)} %collective-permute-done.refs_0_, f32[384,1]{1,0:T(8,128)S(1)} %and_convert_fusion.2.refs_1_, f32[8,512]{1,0:T(8,128)S(1)} %get-tuple-element.17.refs_2_, f32[384,512]{1,0:T(8,128)S(1)} %get-tuple-element.18.refs_3_), custom_call_target="tpu_custom_call" | custom-call | flops 301989888 | bytes 2981888 | tf_op jit(solution)/shard_map/pallas_call | solution.py:129
  (5 shorter events, 0.1 us)
Async XLA Ops:
  0.0 0.8 %copy-start.1 = (bf16[16,1536]{1,0:T(8,128)(2,1)S(1)}, bf16[16,1536]{1,0:T(8,128)(2,1)}, u32[]{:S(2)}) copy-start(bf16[16,1536]{1,0:T(8,128)(2,1)} %param.9) | copy-start | bytes 147460
  0.0 0.8 %copy-start.2 = (bf16[16,1536]{1,0:T(8,128)(2,1)S(1)}, bf16[16,1536]{1,0:T(8,128)(2,1)}, u32[]{:S(2)}) copy-start(bf16[16,1536]{1,0:T(8,128)(2,1)} %param.10) | copy-start | bytes 147460
  0.0 0.9 %copy-start.3 = (s32[16]{0:T(128)S(1)}, s32[16]{0:T(128)}, u32[]{:S(2)}) copy-start(s32[16]{0:T(128)} %param.11) | copy-start | bytes 196
  0.8 1.0 %slice-start.1 = ((bf16[1,512,384]{2,1,0:T(8,128)(2,1)}), bf16[1,384,384]{2,1,0:T(8,128)(2,1)S(1)}, s32[]{:S(2)}) async-start(bf16[1,512,384]{2,1,0:T(8,128)(2,1)} %param.7), calls=%async_computation.2 | async-start | bytes 589824 | tf_op jit(solution)/shard_map/slice | solution.py:177
  0.8 1.0 %slice-start = ((bf16[1,512,384]{2,1,0:T(8,128)(2,1)}), bf16[1,384,384]{2,1,0:T(8,128)(2,1)S(1)}, s32[]{:S(2)}) async-start(bf16[1,512,384]{2,1,0:T(8,128)(2,1)} %param.8), calls=%async_computation.1 | async-start | bytes 589824 | tf_op jit(solution)/shard_map/slice | solution.py:177
  2.7 12.3 %copy-start = (bf16[1,512,384]{2,1,0:T(8,128)(2,1)S(1)}, bf16[1,512,384]{2,1,0:T(8,128)(2,1)}, u32[]{:S(2)}) copy-start(bf16[1,512,384]{2,1,0:T(8,128)(2,1)} %param.6) | copy-start | bytes 1179652
  2.8 19.1 %all-to-all-start = ((bf16[16,16,896]{2,1,0:T(8,128)(2,1)}), bf16[16,16,896]{2,1,0:T(8,128)(2,1)S(1)}, u32[]{:S(2)}, u32[]{:S(2)}) async-start(bf16[16,16,896]{2,1,0:T(8,128)(2,1)} %bitcast.5), calls=%async_computation | async-start | bytes 917504 | tf_op jit(solution)/shard_map/all_to_all | solution.py:153
  9.1 24.4 %collective-permute-start.1 = (bf16[2,384,384]{2,1,0:T(8,128)(2,1)S(1)}, bf16[2,384,384]{2,1,0:T(8,128)(2,1)}, u32[]{:S(2)}, u32[]{:S(2)}) collective-permute-start(bf16[2,384,384]{2,1,0:T(8,128)(2,1)S(1)} %pad_maximum_fusion.refs_0_), channel_id=1, source_target_pairs={{0,4},{1,5},{2,6},{3,7},{4,8},{5,9},{6,10},{7,11},{8,12},{9,13},{1... | collective-permute-start | bytes 1769480 | tf_op jit(solution)/shard_map/ppermute | solution.py:23
  12.4 23.6 %collective-permute-start = (bf16[2,384,384]{2,1,0:T(8,128)(2,1)S(1)}, bf16[2,384,384]{2,1,0:T(8,128)(2,1)S(1)}, u32[]{:S(2)}, u32[]{:S(2)}) collective-permute-start(bf16[2,384,384]{2,1,0:T(8,128)(2,1)S(1)} %pad_maximum_fusion.refs_0_), channel_id=1, source_target_pairs={{4,0},{5,1},{6,2},{7,3},{8,4},{9,5},{10,6},{11,7},{12,8},{13,9},{1... | collective-permute-start | bytes 1769480 | tf_op jit(solution)/shard_map/ppermute | solution.py:23

commit v18 on v14

--- a/solution.py
+++ b/solution.py
@@ -200,18 +200,31 @@
         jnp.zeros((head_count, tokens, HEAD_DIM), jnp.float32),
     )
     text_got, text_keep = text_pieces(text_keys, text_values, text_mask, group_count, lane_width)
+    if grid_h == 1 and grid_f == 1:
+        pieces = 2 if key_rows % 32 == 0 else 1
+        step = key_rows // pieces
+        spans = [(p * step, (p + 1) * step) for p in range(pieces)]
+        own_parts = [jnp.stack([keys[0, a:b], values[0, a:b]]) for a, b in spans]
+        as_row = lambda keep: keep.astype(jnp.float32)[:, None]
+
+        def part_blocks(parts, off_width):
+            keep = keep_mask(0, 0, off_width)
+            return [(part, 0, 1, as_row(keep[a:b])) for part, (a, b) in zip(parts, spans)]
+
+        got_parts = {
+            off_width: [passed_along(part, "tile", -off_width * group_count) for part in own_parts]
+            for off_width in (-1, 1)
+        }
+        query_t = jnp.transpose(queries[0])
+        carry = window_attention(query_t, part_blocks(own_parts, 0), finish=False)
+        carry = window_attention(
+            query_t, [(text_got, 0, head_count, as_row(text_keep))], carry=carry, finish=False
+        )
+        carry = window_attention(query_t, part_blocks(got_parts[-1], -1), carry=carry, finish=False)
+        return window_attention(query_t, part_blocks(got_parts[1], 1), carry=carry)[None]
     width_set = {0: own_pair}
     for off_width in (-1, 1):
         width_set[off_width] = passed_along(own_pair, "tile", -off_width * group_count)
-    if grid_h == 1 and grid_f == 1:
-        as_row = lambda keep: keep.astype(jnp.float32)[:, None]
-        query_t = jnp.transpose(queries[0])
-        carry = window_attention(query_t, [(own_pair, 0, 1, as_row(keep_mask(0, 0, 0)))], finish=False)
-        carry = window_attention(
-            query_t, [(text_got, 0, head_count, as_row(text_keep))], carry=carry, finish=False
-        )
-        blocks = [(width_set[off_width], 0, 1, as_row(keep_mask(0, 0, off_width))) for off_width in (-1, 1)]
-        return window_attention(query_t, blocks, carry=carry)[None]
     piece_keys = text_got[:, :lane_width]
     piece_values = text_got[:, lane_width : 2 * lane_width]
     running = fold_block(running, query_heads, piece_keys, piece_values, text_keep)

time: 38.7 us -> 41.3 us (1.067)
  the two profiles are of different devices: /device:TPU:10 before, /device:TPU:0 now
where the time goes in v18:
time: 41.3 us; the launch traced here: 41 us
  starting transfers between devices  19.2 us (46%)
  waiting for transfers between devices  10.4 us (25%)
  Pallas kernels  7.56 us (18%)
  local copies, waits for them, and re-layouts  3 us (7%)
    ppermute x4, starting transfers between devices, passed_along(): lax.ppermute(value, axis, [(source, source + steps) for source in range(f...  13.5 us
    all_to_all x1, waiting for transfers between devices, text_pieces(): got = lax.all_to_all(outgoing, 'tile', 0, 0, tiled=True)  10.4 us
    pallas_call x4, Pallas kernels, window_attention(): pl.pallas_call(functools.partial(window_kernel, tuple(layout), carry is n...  7.56 us
    all_to_all x1, starting transfers between devices, text_pieces(): got = lax.all_to_all(outgoing, 'tile', 0, 0, tiled=True)  5.76 us
    slice x1, local copies, waits for them, and re-layouts, shards(): own_parts = [jnp.stack([keys[0, a:b], values[0, a:b]]) for a, b in spans]  1.18 us
  transfers between devices with their start and end apart: 5, of which 1 were waited for; matrix products, arithmetic and copies ran while one was open for 5% of the time, Pallas kernels for 13%

profile of v18, /device:TPU:0, one launch (start us, length us, event | category | flops | bytes accessed | tf_op | source)
XLA Modules:
  0.0 41.0 jit_solution(2074537606259529952)
XLA Ops:
  0.0 1.2 %fusion.9 = (bf16[1,192,384]{2,1,0:T(8,128)(2,1)S(1)}, bf16[1,192,384]{2,1,0:T(8,128)(2,1)S(1)}, bf16[1,192,384]{2,1,0:T(8,128)(2,1)S(1)}, bf16[1,192,384]{2,1,0:T(8,128)(2,1)S(1)}) fusion(bf16[1,512,384]{2,1,0:T(8,128)(2,1)} %param.7, bf16[1,512,384]{2,1,0:T(8,128)(2,1)} %param.8), kind=kLoop, calls=%fused_computation.30 | loop fusion | bytes 1179648 | tf_op jit(solution)/shard_map/slice | solution.py:207
  1.2 5.7 %collective-permute-start.3 = (bf16[2,192,384]{2,1,0:T(8,128)(2,1)S(1)}, bf16[2,192,384]{2,1,0:T(8,128)(2,1)}, u32[]{:S(2)}, u32[]{:S(2)}) collective-permute-start(bf16[2,192,384]{2,1,0:T(8,128)(2,1)S(1)} %pad_maximum_fusion.1.refs_1_), channel_id=1, source_target_pairs={{0,4},{1,5},{2,6},{3,7},{4,8},{5,9},{6,10},{7,11},{8,12},{9,13},{1... | collective-permute-start | bytes 884744 | tf_op jit(solution)/shard_map/ppermute | solution.py:23
  6.9 1.3 %collective-permute-start.1 = (bf16[2,192,384]{2,1,0:T(8,128)(2,1)S(1)}, bf16[2,192,384]{2,1,0:T(8,128)(2,1)S(1)}, u32[]{:S(2)}, u32[]{:S(2)}) collective-permute-start(bf16[2,192,384]{2,1,0:T(8,128)(2,1)S(1)} %pad_maximum_fusion.1.refs_1_), channel_id=1, source_target_pairs={{4,0},{5,1},{6,2},{7,3},{8,4},{9,5},{10,6},{11,7},{12,8},{13,9},{1... | collective-permute-start | bytes 884744 | tf_op jit(solution)/shard_map/ppermute | solution.py:23
  8.2 0.0 copy-start.3
  8.2 0.0 copy-start.1
  8.2 0.0 copy-start.2
  8.3 5.3 %collective-permute-start.2 = (bf16[2,192,384]{2,1,0:T(8,128)(2,1)S(1)}, bf16[2,192,384]{2,1,0:T(8,128)(2,1)}, u32[]{:S(2)}, u32[]{:S(2)}) collective-permute-start(bf16[2,192,384]{2,1,0:T(8,128)(2,1)S(1)} %pad_maximum_fusion.refs_0_), channel_id=1, source_target_pairs={{0,4},{1,5},{2,6},{3,7},{4,8},{5,9},{6,10},{7,11},{8,12},{9,13},{1... | collective-permute-start | bytes 884744 | tf_op jit(solution)/shard_map/ppermute | solution.py:23
  13.5 1.3 %collective-permute-start = (bf16[2,192,384]{2,1,0:T(8,128)(2,1)S(1)}, bf16[2,192,384]{2,1,0:T(8,128)(2,1)S(1)}, u32[]{:S(2)}, u32[]{:S(2)}) collective-permute-start(bf16[2,192,384]{2,1,0:T(8,128)(2,1)S(1)} %pad_maximum_fusion.refs_0_), channel_id=1, source_target_pairs={{4,0},{5,1},{6,2},{7,3},{8,4},{9,5},{10,6},{11,7},{12,8},{13,9},{1... | collective-permute-start | bytes 884744 | tf_op jit(solution)/shard_map/ppermute | solution.py:23
  14.8 0.0 copy-done.3
  14.8 0.0 copy-done.1
  14.8 0.0 copy-done.2
  14.9 0.1 broadcast_in_dim.48
  15.0 0.8 %tile.8 = bf16[4,4,16,896]{3,2,1,0:T(8,128)(2,1)} broadcast(bf16[4,16,896]{2,1,0:T(8,128)(2,1)S(1)} %pad_maximum_fusion.2), dimensions={1,2,3} | broadcast | bytes 573440 | tf_op jit(solution)/shard_map/tile | solution.py:158
  15.8 0.0 copy-start
  15.8 5.8 %all-to-all-start = ((bf16[16,16,896]{2,1,0:T(8,128)(2,1)}), bf16[16,16,896]{2,1,0:T(8,128)(2,1)S(1)}, u32[]{:S(2)}, u32[]{:S(2)}) async-start(bf16[16,16,896]{2,1,0:T(8,128)(2,1)} %bitcast.11), calls=%async_computation | async-start | bytes 917504 | tf_op jit(solution)/shard_map/all_to_all | solution.py:159
  21.7 0.1 slice_convert_fusion
  21.8 0.1 slice_convert_fusion.2
  21.8 0.1 slice_convert_fusion.4
  21.9 0.1 copy.10.refs_3_
  22.0 0.1 copy.9.refs_2_
  22.2 0.0 copy-done
  22.2 0.2 copy.8
  22.4 0.1 copy.11.refs_2_
  22.5 0.1 copy.12.refs_3_
  22.6 0.1 copy.13.refs_2_
  22.7 0.1 copy.14.refs_3_
  22.9 1.5 %shard_map.64 = (f32[8,512]{1,0:T(8,128)S(1)}, f32[384,512]{1,0:T(8,128)S(1)}) custom-call(bf16[384,512]{1,0:T(8,128)(2,1)S(1)} %bitcast.20, bf16[2,192,384]{2,1,0:T(8,128)(2,1)S(1)} %pad_maximum_fusion.refs_0_, bf16[2,192,384]{2,1,0:T(8,128)(2,1)S(1)} %pad_maximum_fusion.1.refs_1_, f32[192,1]{1,0:T(8,128)S(1)} %copy.9.refs_2_, f32[192,1]{1,0:T(8,128)S(1)} %copy.10.refs_3_), custom_call_target="tpu_custom_call" | custom-call | flops 301989888 | bytes 2981888 | tf_op jit(solution)/shard_map/pallas_call | solution.py:129
  24.4 10.4 %all-to-all-done = bf16[16,16,896]{2,1,0:T(8,128)(2,1)S(1)} async-done(((bf16[16,16,896]{2,1,0:T(8,128)(2,1)}), bf16[16,16,896]{2,1,0:T(8,128)(2,1)S(1)}, u32[]{:S(2)}, u32[]{:S(2)}) %all-to-all-start) | async-done | bytes 458784 | tf_op jit(solution)/shard_map/all_to_all | solution.py:159
  34.8 1.2 %shard_map.65 = (f32[8,512]{1,0:T(8,128)S(1)}, f32[384,512]{1,0:T(8,128)S(1)}) custom-call(bf16[384,512]{1,0:T(8,128)(2,1)S(1)} %bitcast.21, bf16[256,896]{1,0:T(8,128)(2,1)S(1)} %bitcast.25, f32[256,1]{1,0:T(8,128)S(1)} %compare_convert_fusion.refs_1_, f32[8,512]{1,0:T(8,128)S(1)} %get-tuple-element.11.refs_2_, f32[384,512]{1,0:T(8,128)S(1)} %get-tuple-element.12.refs_3_), custom_call_target="tpu_custom_call" | custom-call | flops 201326592 | bytes 2785280 | tf_op jit(solution)/shard_map/pallas_call | solution.py:129
  36.0 0.0 collective-permute-done.3.refs_1_
  36.0 0.0 collective-permute-done.2.refs_0_
  36.0 2.6 %shard_map.66 = (f32[8,512]{1,0:T(8,128)S(1)}, f32[384,512]{1,0:T(8,128)S(1)}) custom-call(bf16[384,512]{1,0:T(8,128)(2,1)S(1)} %bitcast.22, bf16[2,192,384]{2,1,0:T(8,128)(2,1)} %collective-permute-done.2.refs_0_, bf16[2,192,384]{2,1,0:T(8,128)(2,1)} %collective-permute-done.3.refs_1_, f32[192,1]{1,0:T(8,128)S(1)} %copy.11.refs_2_, ...), custom_call_target="tpu_custom_call" | custom-call | flops 301989888 | bytes 2981888 | tf_op jit(solution)/shard_map/pallas_call | solution.py:129
  38.6 0.0 collective-permute-done.1.refs_1_
  38.7 0.0 collective-permute-done.refs_0_
  38.7 2.3 %shard_map.67 = bf16[512,384]{1,0:T(8,128)(2,1)} custom-call(bf16[384,512]{1,0:T(8,128)(2,1)S(1)} %bitcast.23, bf16[2,192,384]{2,1,0:T(8,128)(2,1)S(1)} %collective-permute-done.refs_0_, bf16[2,192,384]{2,1,0:T(8,128)(2,1)S(1)} %collective-permute-done.1.refs_1_, f32[192,1]{1,0:T(8,128)S(1)} %copy.13.refs_2_, f32[192,1]{1,0:T(8,128)S(1)} %copy.14.refs_3_, ...), custom_call_target="tpu_custom_call" | custom-call | flops 301989888 | bytes 2981888 | tf_op jit(solution)/shard_map/pallas_call | solution.py:129
  (9 shorter events, 0.2 us)
Async XLA Ops:
  1.2 34.8 %collective-permute-start.3 = (bf16[2,192,384]{2,1,0:T(8,128)(2,1)S(1)}, bf16[2,192,384]{2,1,0:T(8,128)(2,1)}, u32[]{:S(2)}, u32[]{:S(2)}) collective-permute-start(bf16[2,192,384]{2,1,0:T(8,128)(2,1)S(1)} %pad_maximum_fusion.1.refs_1_), channel_id=1, source_target_pairs={{0,4},{1,5},{2,6},{3,7},{4,8},{5,9},{6,10},{7,11},{8,12},{9,13},{1... | collective-permute-start | bytes 884744 | tf_op jit(solution)/shard_map/ppermute | solution.py:23
  6.9 31.8 %collective-permute-start.1 = (bf16[2,192,384]{2,1,0:T(8,128)(2,1)S(1)}, bf16[2,192,384]{2,1,0:T(8,128)(2,1)S(1)}, u32[]{:S(2)}, u32[]{:S(2)}) collective-permute-start(bf16[2,192,384]{2,1,0:T(8,128)(2,1)S(1)} %pad_maximum_fusion.1.refs_1_), channel_id=1, source_target_pairs={{4,0},{5,1},{6,2},{7,3},{8,4},{9,5},{10,6},{11,7},{12,8},{13,9},{1... | collective-permute-start | bytes 884744 | tf_op jit(solution)/shard_map/ppermute | solution.py:23
  8.2 6.6 %copy-start.3 = (s32[16]{0:T(128)S(1)}, s32[16]{0:T(128)}, u32[]{:S(2)}) copy-start(s32[16]{0:T(128)} %param.11) | copy-start | bytes 196
  8.2 6.6 %copy-start.1 = (bf16[16,1536]{1,0:T(8,128)(2,1)S(1)}, bf16[16,1536]{1,0:T(8,128)(2,1)}, u32[]{:S(2)}) copy-start(bf16[16,1536]{1,0:T(8,128)(2,1)} %param.9) | copy-start | bytes 147460
  8.2 6.6 %copy-start.2 = (bf16[16,1536]{1,0:T(8,128)(2,1)S(1)}, bf16[16,1536]{1,0:T(8,128)(2,1)}, u32[]{:S(2)}) copy-start(bf16[16,1536]{1,0:T(8,128)(2,1)} %param.10) | copy-start | bytes 147460
  8.3 27.8 %collective-permute-start.2 = (bf16[2,192,384]{2,1,0:T(8,128)(2,1)S(1)}, bf16[2,192,384]{2,1,0:T(8,128)(2,1)}, u32[]{:S(2)}, u32[]{:S(2)}) collective-permute-start(bf16[2,192,384]{2,1,0:T(8,128)(2,1)S(1)} %pad_maximum_fusion.refs_0_), channel_id=1, source_target_pairs={{0,4},{1,5},{2,6},{3,7},{4,8},{5,9},{6,10},{7,11},{8,12},{9,13},{1... | collective-permute-start | bytes 884744 | tf_op jit(solution)/shard_map/ppermute | solution.py:23
  13.5 25.1 %collective-permute-start = (bf16[2,192,384]{2,1,0:T(8,128)(2,1)S(1)}, bf16[2,192,384]{2,1,0:T(8,128)(2,1)S(1)}, u32[]{:S(2)}, u32[]{:S(2)}) collective-permute-start(bf16[2,192,384]{2,1,0:T(8,128)(2,1)S(1)} %pad_maximum_fusion.refs_0_), channel_id=1, source_target_pairs={{4,0},{5,1},{6,2},{7,3},{8,4},{9,5},{10,6},{11,7},{12,8},{13,9},{1... | collective-permute-start | bytes 884744 | tf_op jit(solution)/shard_map/ppermute | solution.py:23
  15.8 6.4 %copy-start = (bf16[1,512,384]{2,1,0:T(8,128)(2,1)S(1)}, bf16[1,512,384]{2,1,0:T(8,128)(2,1)}, u32[]{:S(2)}) copy-start(bf16[1,512,384]{2,1,0:T(8,128)(2,1)} %param.6) | copy-start | bytes 1179652
  15.8 19.0 %all-to-all-start = ((bf16[16,16,896]{2,1,0:T(8,128)(2,1)}), bf16[16,16,896]{2,1,0:T(8,128)(2,1)S(1)}, u32[]{:S(2)}, u32[]{:S(2)}) async-start(bf16[16,16,896]{2,1,0:T(8,128)(2,1)} %bitcast.11), calls=%async_computation | async-start | bytes 917504 | tf_op jit(solution)/shard_map/all_to_all | solution.py:159

commit v19 on v16

--- a/solution.py
+++ b/solution.py
@@ -138,16 +138,34 @@
     )(*[pltpu.with_memory_space_constraint(a, pltpu.VMEM) for a in (query_t, *sources, *keeps, *carry_args)])
 
 
+def payload_kernel(group_count, lane_width, mask_ref, key_ref, value_ref, out_ref):
+    rows = key_ref.shape[0]
+    row_at = lax.broadcasted_iota(jnp.int32, (rows, 128), 0)
+    flags = jnp.zeros((rows, 128), jnp.float32)
+    for r in range(rows):
+        flags = jnp.where(row_at == r, mask_ref[r].astype(jnp.float32), flags)
+    flags = flags.astype(out_ref.dtype)
+    for j in range(out_ref.shape[0]):
+        g = j % group_count
+        out_ref[j, :, :lane_width] = key_ref[:, g * lane_width : (g + 1) * lane_width]
+        out_ref[j, :, lane_width : 2 * lane_width] = value_ref[:, g * lane_width : (g + 1) * lane_width]
+        out_ref[j, :, 2 * lane_width :] = flags
+
+
 def text_pieces(text_keys, text_values, text_mask, group_count, lane_width):
     count = lax.axis_size("tile")
     rows = text_keys.shape[0]
-    shape = (rows, group_count, lane_width)
-    flags = jnp.broadcast_to(text_mask.astype(jnp.bfloat16)[:, None, None], (rows, group_count, 128))
-    per_group = jnp.concatenate([text_keys.reshape(shape), text_values.reshape(shape), flags], axis=2)
-    per_group = jnp.transpose(per_group, (1, 0, 2))
     width = 2 * lane_width + 128
-    outgoing = jnp.broadcast_to(per_group[None], (count // group_count, group_count, rows, width))
-    outgoing = outgoing.reshape(count * rows, width)
+    outgoing = pl.pallas_call(
+        functools.partial(payload_kernel, group_count, lane_width),
+        out_shape=jax.ShapeDtypeStruct((count, rows, width), jnp.bfloat16),
+        in_specs=[
+            pl.BlockSpec(memory_space=pltpu.SMEM),
+            pl.BlockSpec(memory_space=pltpu.VMEM),
+            pl.BlockSpec(memory_space=pltpu.VMEM),
+        ],
+        out_specs=pl.BlockSpec(memory_space=pltpu.VMEM),
+    )(text_mask, text_keys, text_values).reshape(count * rows, width)
     got = lax.all_to_all(outgoing, "tile", 0, 0, tiled=True)
     return got, got[:, 2 * lane_width] > 0.5
 

time: 38.4 us -> 37.5 us (0.977)
  the two profiles are of different devices: /device:TPU:18 before, /device:TPU:16 now
where the time goes in v19:
time: 37.5 us; the launch traced here: 37.1 us
  waiting for transfers between devices  14.1 us (38%)
  starting transfers between devices  12.2 us (33%)
  Pallas kernels  9.2 us (25%)
  local copies, waits for them, and re-layouts  1.23 us (3%)
    ppermute x2, waiting for transfers between devices, passed_along(): lax.ppermute(value, axis, [(source, source + steps) for source in range(f...  10.4 us
    pallas_call x4, Pallas kernels, window_attention(): pl.pallas_call(functools.partial(window_kernel, tuple(layout), carry is n...  7.56 us
    all_to_all x1, starting transfers between devices, text_pieces(): got = lax.all_to_all(outgoing, 'tile', 0, 0, tiled=True)  6.18 us
    ppermute x2, starting transfers between devices, passed_along(): lax.ppermute(value, axis, [(source, source + steps) for source in range(f...  5.98 us
    all_to_all x1, waiting for transfers between devices, text_pieces(): got = lax.all_to_all(outgoing, 'tile', 0, 0, tiled=True)  3.74 us
    pallas_call x1, Pallas kernels, text_pieces(): pl.pallas_call(functools.partial(payload_kernel, group_count, lane_width)...  1.64 us
    slice x4, local copies, waits for them, and re-layouts, shards(): own_pair = jnp.stack([keys[0, :key_rows], values[0, :key_rows]])  1.04 us
  transfers between devices with their start and end apart: 3, of which 2 were waited for; matrix products, arithmetic and copies ran while one was open for 1% of the time, Pallas kernels for 14%

profile of v19, /device:TPU:16, one launch (start us, length us, event | category | flops | bytes accessed | tf_op | source)
XLA Modules:
  0.0 37.1 jit_solution(18307040506298979489)
XLA Ops:
  0.0 1.6 %shard_map.64 = bf16[16,16,896]{2,1,0:T(8,128)(2,1)} custom-call(s32[16]{0:T(128)} %mask_ref.1, bf16[16,1536]{1,0:T(8,128)(2,1)} %key_ref.1, bf16[16,1536]{1,0:T(8,128)(2,1)} %value_ref.1), custom_call_target="tpu_custom_call" | custom-call | tf_op jit(solution)/shard_map/pallas_call | solution.py:159
  1.6 6.2 %all-to-all-start = ((bf16[16,16,896]{2,1,0:T(8,128)(2,1)}), bf16[16,16,896]{2,1,0:T(8,128)(2,1)S(1)}, u32[]{:S(2)}, u32[]{:S(2)}) async-start(bf16[16,16,896]{2,1,0:T(8,128)(2,1)} %shard_map.64), calls=%async_computation | async-start | bytes 917504 | tf_op jit(solution)/shard_map/all_to_all | solution.py:169
  7.8 0.0 slice-start
  7.8 0.0 slice-start.1
  7.8 0.9 %slice-done = bf16[1,384,384]{2,1,0:T(8,128)(2,1)S(1)} async-done(((bf16[1,512,384]{2,1,0:T(8,128)(2,1)}), bf16[1,384,384]{2,1,0:T(8,128)(2,1)S(1)}, s32[]{:S(2)}) %slice-start) | async-done | bytes 294936 | tf_op jit(solution)/shard_map/slice | solution.py:193
  8.8 0.1 slice-done.1
  8.9 0.0 copy-start
  8.9 0.1 pad_maximum_fusion.refs_0_
  8.9 3.5 %collective-permute-start.1 = (bf16[2,384,384]{2,1,0:T(8,128)(2,1)S(1)}, bf16[2,384,384]{2,1,0:T(8,128)(2,1)}, u32[]{:S(2)}, u32[]{:S(2)}) collective-permute-start(bf16[2,384,384]{2,1,0:T(8,128)(2,1)S(1)} %pad_maximum_fusion.refs_0_), channel_id=1, source_target_pairs={{0,4},{1,5},{2,6},{3,7},{4,8},{5,9},{6,10},{7,11},{8,12},{9,13},{1... | collective-permute-start | bytes 1769480 | tf_op jit(solution)/shard_map/ppermute | solution.py:23
  12.5 2.5 %collective-permute-start = (bf16[2,384,384]{2,1,0:T(8,128)(2,1)S(1)}, bf16[2,384,384]{2,1,0:T(8,128)(2,1)S(1)}, u32[]{:S(2)}, u32[]{:S(2)}) collective-permute-start(bf16[2,384,384]{2,1,0:T(8,128)(2,1)S(1)} %pad_maximum_fusion.refs_0_), channel_id=1, source_target_pairs={{4,0},{5,1},{6,2},{7,3},{8,4},{9,5},{10,6},{11,7},{12,8},{13,9},{1... | collective-permute-start | bytes 1769480 | tf_op jit(solution)/shard_map/ppermute | solution.py:23
  15.0 0.1 and_convert_fusion.refs_1_
  15.1 0.0 copy-done
  15.1 0.2 copy.8
  15.3 1.5 %shard_map.65 = (f32[8,512]{1,0:T(8,128)S(1)}, f32[384,512]{1,0:T(8,128)S(1)}) custom-call(bf16[384,512]{1,0:T(8,128)(2,1)S(1)} %bitcast.5, bf16[2,384,384]{2,1,0:T(8,128)(2,1)S(1)} %pad_maximum_fusion.refs_0_, f32[384,1]{1,0:T(8,128)S(1)} %and_convert_fusion.refs_1_), custom_call_target="tpu_custom_call" | custom-call | flops 301989888 | bytes 2981888 | tf_op jit(solution)/shard_map/pallas_call | solution.py:129
  16.8 0.1 and_convert_fusion.1.refs_1_
  16.8 0.1 and_convert_fusion.2.refs_1_
  16.9 3.7 %all-to-all-done = bf16[16,16,896]{2,1,0:T(8,128)(2,1)S(1)} async-done(((bf16[16,16,896]{2,1,0:T(8,128)(2,1)}), bf16[16,16,896]{2,1,0:T(8,128)(2,1)S(1)}, u32[]{:S(2)}, u32[]{:S(2)}) %all-to-all-start) | async-done | bytes 458784 | tf_op jit(solution)/shard_map/all_to_all | solution.py:169
  20.7 1.2 %shard_map.66 = (f32[8,512]{1,0:T(8,128)S(1)}, f32[384,512]{1,0:T(8,128)S(1)}) custom-call(bf16[384,512]{1,0:T(8,128)(2,1)S(1)} %bitcast.6, bf16[256,896]{1,0:T(8,128)(2,1)S(1)} %bitcast.10, f32[256,1]{1,0:T(8,128)S(1)} %compare_convert_fusion.refs_1_, f32[8,512]{1,0:T(8,128)S(1)} %get-tuple-element.11.refs_2_, f32[384,512]{1,0:T(8,128)S(1)} %get-tuple-element.12.refs_3_), custom_call_target="tpu_custom_call" | custom-call | flops 201326592 | bytes 2785280 | tf_op jit(solution)/shard_map/pallas_call | solution.py:129
  21.8 10.4 %collective-permute-done.1.refs_0_ = bf16[2,384,384]{2,1,0:T(8,128)(2,1)} collective-permute-done((bf16[2,384,384]{2,1,0:T(8,128)(2,1)S(1)}, bf16[2,384,384]{2,1,0:T(8,128)(2,1)}, u32[]{:S(2)}, u32[]{:S(2)}) %collective-permute-start.1) | collective-permute-done | bytes 589856 | tf_op jit(solution)/shard_map/ppermute | solution.py:23
  32.2 2.6 %shard_map.67 = (f32[8,512]{1,0:T(8,128)S(1)}, f32[384,512]{1,0:T(8,128)S(1)}) custom-call(bf16[384,512]{1,0:T(8,128)(2,1)S(1)} %bitcast.7, bf16[2,384,384]{2,1,0:T(8,128)(2,1)} %collective-permute-done.1.refs_0_, f32[384,1]{1,0:T(8,128)S(1)} %and_convert_fusion.1.refs_1_, f32[8,512]{1,0:T(8,128)S(1)} %get-tuple-element.13.refs_2_, ...), custom_call_target="tpu_custom_call" | custom-call | flops 301989888 | bytes 2981888 | tf_op jit(solution)/shard_map/pallas_call | solution.py:129
  34.8 0.0 collective-permute-done.refs_0_
  34.8 2.3 %shard_map.68 = bf16[512,384]{1,0:T(8,128)(2,1)} custom-call(bf16[384,512]{1,0:T(8,128)(2,1)S(1)} %bitcast.8, bf16[2,384,384]{2,1,0:T(8,128)(2,1)S(1)} %collective-permute-done.refs_0_, f32[384,1]{1,0:T(8,128)S(1)} %and_convert_fusion.2.refs_1_, f32[8,512]{1,0:T(8,128)S(1)} %get-tuple-element.15.refs_2_, f32[384,512]{1,0:T(8,128)S(1)} %get-tuple-element.16.refs_3_), custom_call_target="tpu_custom_call" | custom-call | flops 301989888 | bytes 2981888 | tf_op jit(solution)/shard_map/pallas_call | solution.py:129
  (1 shorter events, 0.0 us)
Async XLA Ops:
  1.6 19.0 %all-to-all-start = ((bf16[16,16,896]{2,1,0:T(8,128)(2,1)}), bf16[16,16,896]{2,1,0:T(8,128)(2,1)S(1)}, u32[]{:S(2)}, u32[]{:S(2)}) async-start(bf16[16,16,896]{2,1,0:T(8,128)(2,1)} %shard_map.64), calls=%async_computation | async-start | bytes 917504 | tf_op jit(solution)/shard_map/all_to_all | solution.py:169
  7.8 1.0 %slice-start = ((bf16[1,512,384]{2,1,0:T(8,128)(2,1)}), bf16[1,384,384]{2,1,0:T(8,128)(2,1)S(1)}, s32[]{:S(2)}) async-start(bf16[1,512,384]{2,1,0:T(8,128)(2,1)} %param.8), calls=%async_computation.1 | async-start | bytes 589824 | tf_op jit(solution)/shard_map/slice | solution.py:193
  7.8 1.0 %slice-start.1 = ((bf16[1,512,384]{2,1,0:T(8,128)(2,1)}), bf16[1,384,384]{2,1,0:T(8,128)(2,1)S(1)}, s32[]{:S(2)}) async-start(bf16[1,512,384]{2,1,0:T(8,128)(2,1)} %param.7), calls=%async_computation.2 | async-start | bytes 589824 | tf_op jit(solution)/shard_map/slice | solution.py:193
  8.9 6.2 %copy-start = (bf16[1,512,384]{2,1,0:T(8,128)(2,1)S(1)}, bf16[1,512,384]{2,1,0:T(8,128)(2,1)}, u32[]{:S(2)}) copy-start(bf16[1,512,384]{2,1,0:T(8,128)(2,1)} %param.6) | copy-start | bytes 1179652
  8.9 23.3 %collective-permute-start.1 = (bf16[2,384,384]{2,1,0:T(8,128)(2,1)S(1)}, bf16[2,384,384]{2,1,0:T(8,128)(2,1)}, u32[]{:S(2)}, u32[]{:S(2)}) collective-permute-start(bf16[2,384,384]{2,1,0:T(8,128)(2,1)S(1)} %pad_maximum_fusion.refs_0_), channel_id=1, source_target_pairs={{0,4},{1,5},{2,6},{3,7},{4,8},{5,9},{6,10},{7,11},{8,12},{9,13},{1... | collective-permute-start | bytes 1769480 | tf_op jit(solution)/shard_map/ppermute | solution.py:23
  12.5 22.4 %collective-permute-start = (bf16[2,384,384]{2,1,0:T(8,128)(2,1)S(1)}, bf16[2,384,384]{2,1,0:T(8,128)(2,1)S(1)}, u32[]{:S(2)}, u32[]{:S(2)}) collective-permute-start(bf16[2,384,384]{2,1,0:T(8,128)(2,1)S(1)} %pad_maximum_fusion.refs_0_), channel_id=1, source_target_pairs={{4,0},{5,1},{6,2},{7,3},{8,4},{9,5},{10,6},{11,7},{12,8},{13,9},{1... | collective-permute-start | bytes 1769480 | tf_op jit(solution)/shard_map/ppermute | solution.py:23

commit v20 on v19

--- a/solution.py
+++ b/solution.py
@@ -138,7 +138,13 @@
     )(*[pltpu.with_memory_space_constraint(a, pltpu.VMEM) for a in (query_t, *sources, *keeps, *carry_args)])
 
 
-def payload_kernel(group_count, lane_width, mask_ref, key_ref, value_ref, out_ref):
+def payload_kernel(group_count, lane_width, mask_ref, key_ref, value_ref, *refs):
+    if len(refs) == 4:
+        own_keys, own_values, out_ref, pair_ref = refs
+        pair_ref[0] = own_keys[: pair_ref.shape[1], :]
+        pair_ref[1] = own_values[: pair_ref.shape[1], :]
+    else:
+        (out_ref,) = refs
     rows = key_ref.shape[0]
     row_at = lax.broadcasted_iota(jnp.int32, (rows, 128), 0)
     flags = jnp.zeros((rows, 128), jnp.float32)
@@ -152,21 +158,30 @@
         out_ref[j, :, 2 * lane_width :] = flags
 
 
-def text_pieces(text_keys, text_values, text_mask, group_count, lane_width):
+def text_pieces(text_keys, text_values, text_mask, group_count, lane_width, own=None):
     count = lax.axis_size("tile")
     rows = text_keys.shape[0]
     width = 2 * lane_width + 128
-    outgoing = pl.pallas_call(
+    vmem = pl.BlockSpec(memory_space=pltpu.VMEM)
+    out_shape = jax.ShapeDtypeStruct((count, rows, width), jnp.bfloat16)
+    extra = ()
+    if own is not None:
+        own_keys, own_values, key_rows = own
+        extra = (own_keys, own_values)
+        out_shape = (out_shape, jax.ShapeDtypeStruct((2, key_rows, own_keys.shape[1]), own_keys.dtype))
+    made = pl.pallas_call(
         functools.partial(payload_kernel, group_count, lane_width),
-        out_shape=jax.ShapeDtypeStruct((count, rows, width), jnp.bfloat16),
-        in_specs=[
-            pl.BlockSpec(memory_space=pltpu.SMEM),
-            pl.BlockSpec(memory_space=pltpu.VMEM),
-            pl.BlockSpec(memory_space=pltpu.VMEM),
-        ],
-        out_specs=pl.BlockSpec(memory_space=pltpu.VMEM),
-    )(text_mask, text_keys, text_values).reshape(count * rows, width)
+        out_shape=out_shape,
+        in_specs=[pl.BlockSpec(memory_space=pltpu.SMEM)] + [vmem] * (2 + len(extra)),
+        out_specs=vmem if own is None else (vmem, vmem),
+    )(text_mask, text_keys, text_values, *extra)
+    own_pair = None
+    if own is not None:
+        made, own_pair = made
+    outgoing = made.reshape(count * rows, width)
     got = lax.all_to_all(outgoing, "tile", 0, 0, tiled=True)
+    if own is not None:
+        return got, got[:, 2 * lane_width] > 0.5, own_pair
     return got, got[:, 2 * lane_width] > 0.5
 
 
@@ -209,7 +224,12 @@
         jnp.zeros((head_count, tokens), jnp.float32),
         jnp.zeros((head_count, tokens, HEAD_DIM), jnp.float32),
     )
-    text_got, text_keep = text_pieces(text_keys, text_values, text_mask, group_count, lane_width)
+    if grid_h == 1 and grid_f == 1:
+        text_got, text_keep, own_pair = text_pieces(
+            text_keys, text_values, text_mask, group_count, lane_width, (keys[0], values[0], key_rows)
+        )
+    else:
+        text_got, text_keep = text_pieces(text_keys, text_values, text_mask, group_count, lane_width)
     width_set = {0: own_pair}
     for off_width in (-1, 1):
         width_set[off_width] = passed_along(own_pair, "tile", -off_width * group_count)

time: 37.5 us -> 38.2 us (1.019)
  waiting for transfers between devices: 14.1 us -> 15.4 us
  local copies, waits for them, and re-layouts: 1.23 us -> 0.2 us
  Pallas kernels: 9.2 us -> 9.77 us
    all_to_all x1, waiting for transfers between devices: 3.74 us -> 4.99 us  [text_pieces(): got = lax.all_to_all(outgoing, 'tile', 0, 0, tiled=True)]
    slice x4 -> x0, local copies, waits for them, and re-layouts: 1.04 us -> none  [shards(): own_pair = jnp.stack([keys[0, :key_rows], values[0, :key_rows]])]
    pallas_call x1, Pallas kernels: 1.64 us -> 2.21 us  [text_pieces(): pl.pallas_call(functools.partial(payload_kernel, group_count, lane_width)...]
where the time goes in v20:
time: 38.2 us; the launch traced here: 37.9 us
  waiting for transfers between devices  15.4 us (40%)
  starting transfers between devices  12.2 us (32%)
  Pallas kernels  9.77 us (26%)
    ppermute x2, waiting for transfers between devices, passed_along(): lax.ppermute(value, axis, [(source, source + steps) for source in range(f...  10.4 us
    pallas_call x4, Pallas kernels, window_attention(): pl.pallas_call(functools.partial(window_kernel, tuple(layout), carry is n...  7.56 us
    all_to_all x1, starting transfers between devices, text_pieces(): got = lax.all_to_all(outgoing, 'tile', 0, 0, tiled=True)  6.32 us
    ppermute x2, starting transfers between devices, passed_along(): lax.ppermute(value, axis, [(source, source + steps) for source in range(f...  5.84 us
    all_to_all x1, waiting for transfers between devices, text_pieces(): got = lax.all_to_all(outgoing, 'tile', 0, 0, tiled=True)  4.99 us
    pallas_call x1, Pallas kernels, text_pieces(): pl.pallas_call(functools.partial(payload_kernel, group_count, lane_width)...  2.21 us
  transfers between devices with their start and end apart: 3, of which 2 were waited for; matrix products, arithmetic and copies ran while one was open for 1% of the time, Pallas kernels for 14%

profile of v20, /device:TPU:16, one launch (start us, length us, event | category | flops | bytes accessed | tf_op | source)
XLA Modules:
  0.0 37.9 jit_solution(757047005522319682)
XLA Ops:
  0.0 2.2 %shard_map.64 = (bf16[16,16,896]{2,1,0:T(8,128)(2,1)}, bf16[2,384,384]{2,1,0:T(8,128)(2,1)}) custom-call(s32[16]{0:T(128)} %mask_ref.1, bf16[16,1536]{1,0:T(8,128)(2,1)} %key_ref.1, bf16[16,1536]{1,0:T(8,128)(2,1)} %value_ref.1, bf16[512,384]{1,0:T(8,128)(2,1)} %bitcast.13, bf16[512,384]{1,0:T(8,128)(2,1)} %bitcast.14), custom_call_target="tpu_custom_call" | custom-call | tf_op jit(solution)/shard_map/pallas_call | solution.py:172
  2.2 0.0 copy-start
  2.2 0.0 copy-start.1
  2.2 6.3 %all-to-all-start = ((bf16[16,16,896]{2,1,0:T(8,128)(2,1)}), bf16[16,16,896]{2,1,0:T(8,128)(2,1)S(1)}, u32[]{:S(2)}, u32[]{:S(2)}) async-start(bf16[16,16,896]{2,1,0:T(8,128)(2,1)} %get-tuple-element.14), calls=%async_computation | async-start | bytes 917504 | tf_op jit(solution)/shard_map/all_to_all | solution.py:182
  8.5 0.0 copy-done
  8.5 3.4 %collective-permute-start.1 = (bf16[2,384,384]{2,1,0:T(8,128)(2,1)S(1)}, bf16[2,384,384]{2,1,0:T(8,128)(2,1)}, u32[]{:S(2)}, u32[]{:S(2)}) collective-permute-start(bf16[2,384,384]{2,1,0:T(8,128)(2,1)S(1)} %copy-done), channel_id=1, source_target_pairs={{0,4},{1,5},{2,6},{3,7},{4,8},{5,9},{6,10},{7,11},{8,12},{9,13},{1... | collective-permute-start | bytes 1769480 | tf_op jit(solution)/shard_map/ppermute | solution.py:23
  11.9 2.5 %collective-permute-start = (bf16[2,384,384]{2,1,0:T(8,128)(2,1)S(1)}, bf16[2,384,384]{2,1,0:T(8,128)(2,1)S(1)}, u32[]{:S(2)}, u32[]{:S(2)}) collective-permute-start(bf16[2,384,384]{2,1,0:T(8,128)(2,1)S(1)} %copy-done), channel_id=1, source_target_pairs={{4,0},{5,1},{6,2},{7,3},{8,4},{9,5},{10,6},{11,7},{12,8},{13,9},{1... | collective-permute-start | bytes 1769480 | tf_op jit(solution)/shard_map/ppermute | solution.py:23
  14.5 0.1 and_convert_fusion.refs_1_
  14.5 0.0 copy-done.1
  14.5 0.2 copy.8
  14.8 1.5 %shard_map.65 = (f32[8,512]{1,0:T(8,128)S(1)}, f32[384,512]{1,0:T(8,128)S(1)}) custom-call(bf16[384,512]{1,0:T(8,128)(2,1)S(1)} %bitcast.7, bf16[2,384,384]{2,1,0:T(8,128)(2,1)S(1)} %copy-done, f32[384,1]{1,0:T(8,128)S(1)} %and_convert_fusion.refs_1_), custom_call_target="tpu_custom_call" | custom-call | flops 301989888 | bytes 2981888 | tf_op jit(solution)/shard_map/pallas_call | solution.py:129
  16.3 0.1 and_convert_fusion.1.refs_1_
  16.3 0.1 and_convert_fusion.2.refs_1_
  16.4 5.0 %all-to-all-done = bf16[16,16,896]{2,1,0:T(8,128)(2,1)S(1)} async-done(((bf16[16,16,896]{2,1,0:T(8,128)(2,1)}), bf16[16,16,896]{2,1,0:T(8,128)(2,1)S(1)}, u32[]{:S(2)}, u32[]{:S(2)}) %all-to-all-start) | async-done | bytes 458784 | tf_op jit(solution)/shard_map/all_to_all | solution.py:182
  21.4 1.2 %shard_map.66 = (f32[8,512]{1,0:T(8,128)S(1)}, f32[384,512]{1,0:T(8,128)S(1)}) custom-call(bf16[384,512]{1,0:T(8,128)(2,1)S(1)} %bitcast.8, bf16[256,896]{1,0:T(8,128)(2,1)S(1)} %bitcast.12, f32[256,1]{1,0:T(8,128)S(1)} %compare_convert_fusion.refs_1_, f32[8,512]{1,0:T(8,128)S(1)} %get-tuple-element.15.refs_2_, f32[384,512]{1,0:T(8,128)S(1)} %get-tuple-element.16.refs_3_), custom_call_target="tpu_custom_call" | custom-call | flops 201326592 | bytes 2785280 | tf_op jit(solution)/shard_map/pallas_call | solution.py:129
  22.6 10.4 %collective-permute-done.1.refs_0_ = bf16[2,384,384]{2,1,0:T(8,128)(2,1)} collective-permute-done((bf16[2,384,384]{2,1,0:T(8,128)(2,1)S(1)}, bf16[2,384,384]{2,1,0:T(8,128)(2,1)}, u32[]{:S(2)}, u32[]{:S(2)}) %collective-permute-start.1) | collective-permute-done | bytes 589856 | tf_op jit(solution)/shard_map/ppermute | solution.py:23
  32.9 2.6 %shard_map.67 = (f32[8,512]{1,0:T(8,128)S(1)}, f32[384,512]{1,0:T(8,128)S(1)}) custom-call(bf16[384,512]{1,0:T(8,128)(2,1)S(1)} %bitcast.9, bf16[2,384,384]{2,1,0:T(8,128)(2,1)} %collective-permute-done.1.refs_0_, f32[384,1]{1,0:T(8,128)S(1)} %and_convert_fusion.1.refs_1_, f32[8,512]{1,0:T(8,128)S(1)} %get-tuple-element.17.refs_2_, ...), custom_call_target="tpu_custom_call" | custom-call | flops 301989888 | bytes 2981888 | tf_op jit(solution)/shard_map/pallas_call | solution.py:129
  35.5 0.0 collective-permute-done.refs_0_
  35.5 2.3 %shard_map.68 = bf16[512,384]{1,0:T(8,128)(2,1)} custom-call(bf16[384,512]{1,0:T(8,128)(2,1)S(1)} %bitcast.10, bf16[2,384,384]{2,1,0:T(8,128)(2,1)S(1)} %collective-permute-done.refs_0_, f32[384,1]{1,0:T(8,128)S(1)} %and_convert_fusion.2.refs_1_, f32[8,512]{1,0:T(8,128)S(1)} %get-tuple-element.19.refs_2_, f32[384,512]{1,0:T(8,128)S(1)} %get-tuple-element.20.refs_3_), custom_call_target="tpu_custom_call" | custom-call | flops 301989888 | bytes 2981888 | tf_op jit(solution)/shard_map/pallas_call | solution.py:129
  (1 shorter events, 0.0 us)
Async XLA Ops:
  2.2 6.3 %copy-start = (bf16[2,384,384]{2,1,0:T(8,128)(2,1)S(1)}, bf16[2,384,384]{2,1,0:T(8,128)(2,1)}, u32[]{:S(2)}) copy-start(bf16[2,384,384]{2,1,0:T(8,128)(2,1)} %get-tuple-element.13.refs_0_) | copy-start | bytes 1769476
  2.2 12.3 %copy-start.1 = (bf16[1,512,384]{2,1,0:T(8,128)(2,1)S(1)}, bf16[1,512,384]{2,1,0:T(8,128)(2,1)}, u32[]{:S(2)}) copy-start(bf16[1,512,384]{2,1,0:T(8,128)(2,1)} %param.6) | copy-start | bytes 1179652
  2.2 19.1 %all-to-all-start = ((bf16[16,16,896]{2,1,0:T(8,128)(2,1)}), bf16[16,16,896]{2,1,0:T(8,128)(2,1)S(1)}, u32[]{:S(2)}, u32[]{:S(2)}) async-start(bf16[16,16,896]{2,1,0:T(8,128)(2,1)} %get-tuple-element.14), calls=%async_computation | async-start | bytes 917504 | tf_op jit(solution)/shard_map/all_to_all | solution.py:182
  8.5 24.4 %collective-permute-start.1 = (bf16[2,384,384]{2,1,0:T(8,128)(2,1)S(1)}, bf16[2,384,384]{2,1,0:T(8,128)(2,1)}, u32[]{:S(2)}, u32[]{:S(2)}) collective-permute-start(bf16[2,384,384]{2,1,0:T(8,128)(2,1)S(1)} %copy-done), channel_id=1, source_target_pairs={{0,4},{1,5},{2,6},{3,7},{4,8},{5,9},{6,10},{7,11},{8,12},{9,13},{1... | collective-permute-start | bytes 1769480 | tf_op jit(solution)/shard_map/ppermute | solution.py:23
  11.9 23.6 %collective-permute-start = (bf16[2,384,384]{2,1,0:T(8,128)(2,1)S(1)}, bf16[2,384,384]{2,1,0:T(8,128)(2,1)S(1)}, u32[]{:S(2)}, u32[]{:S(2)}) collective-permute-start(bf16[2,384,384]{2,1,0:T(8,128)(2,1)S(1)} %copy-done), channel_id=1, source_target_pairs={{4,0},{5,1},{6,2},{7,3},{8,4},{9,5},{10,6},{11,7},{12,8},{13,9},{1... | collective-permute-start | bytes 1769480 | tf_op jit(solution)/shard_map/ppermute | solution.py:23

commit v21 on v19

--- a/solution.py
+++ b/solution.py
@@ -94,7 +94,14 @@
             summed = part if summed is None else summed + part
         outs = rest[2:] if carry_in else rest
         if finish:
-            outs[0][:, lanes] = jnp.transpose(summed / total).astype(outs[0].dtype)
+            staged, sems = rest[-2], rest[-1]
+            staged[:, lanes] = jnp.transpose(summed / total).astype(staged.dtype)
+            copy = pltpu.make_async_copy(staged.at[:, lanes], outs[0].at[:, lanes], sems.at[h])
+            copy.start()
+            if h == head_count - 1:
+                for k in range(head_count):
+                    done = slice(k * HEAD_DIM, (k + 1) * HEAD_DIM)
+                    pltpu.make_async_copy(staged.at[:, done], outs[0].at[:, done], sems.at[k]).wait()
         else:
             outs[0][h : h + 1, :] = top
             outs[0][head_count + h : head_count + h + 1, :] = total
@@ -113,9 +120,11 @@
         keeps.append(keep)
     stat_rows = -(-2 * head_count // 8) * 8
     stat_shape = jax.ShapeDtypeStruct((stat_rows, tokens), jnp.float32)
+    scratch = []
     if finish:
         out_shape = jax.ShapeDtypeStruct((tokens, lane_width), jnp.bfloat16)
-        out_specs = pl.BlockSpec(memory_space=pltpu.VMEM)
+        out_specs = pl.BlockSpec(memory_space=pl.ANY)
+        scratch = [pltpu.VMEM((tokens, lane_width), jnp.bfloat16), pltpu.SemaphoreType.DMA((head_count,))]
     else:
         out_shape = (
             pltpu.VMEM(stat_shape.shape, stat_shape.dtype),
@@ -131,6 +140,7 @@
         out_shape=out_shape,
         in_specs=[pl.BlockSpec(memory_space=pltpu.VMEM)] * operand_count,
         out_specs=out_specs,
+        scratch_shapes=scratch,
         cost_estimate=pl.CostEstimate(
             flops=flops, transcendentals=tokens * key_total * head_count, bytes_accessed=moved
         ),

time: 37.5 us -> 37.4 us (level)
  the two profiles are of different devices: /device:TPU:16 before, /device:TPU:18 now
where the time goes in v21:
time: 37.4 us; the launch traced here: 37.1 us
  waiting for transfers between devices  14.1 us (38%)
  starting transfers between devices  12.2 us (33%)
  Pallas kernels  9.13 us (24%)
  local copies, waits for them, and re-layouts  1.23 us (3%)
    ppermute x2, waiting for transfers between devices, passed_along(): lax.ppermute(value, axis, [(source, source + steps) for source in range(f...  10.4 us
    pallas_call x4, Pallas kernels, window_attention(): pl.pallas_call(functools.partial(window_kernel, tuple(layout), carry is n...  7.5 us
    all_to_all x1, starting transfers between devices, text_pieces(): got = lax.all_to_all(outgoing, 'tile', 0, 0, tiled=True)  6.18 us
    ppermute x2, starting transfers between devices, passed_along(): lax.ppermute(value, axis, [(source, source + steps) for source in range(f...  5.98 us
    all_to_all x1, waiting for transfers between devices, text_pieces(): got = lax.all_to_all(outgoing, 'tile', 0, 0, tiled=True)  3.74 us
    pallas_call x1, Pallas kernels, text_pieces(): pl.pallas_call(functools.partial(payload_kernel, group_count, lane_width)...  1.64 us
    slice x4, local copies, waits for them, and re-layouts, shards(): own_pair = jnp.stack([keys[0, :key_rows], values[0, :key_rows]])  1.04 us
  transfers between devices with their start and end apart: 3, of which 2 were waited for; matrix products, arithmetic and copies ran while one was open for 1% of the time, Pallas kernels for 14%

profile of v21, /device:TPU:18, one launch (start us, length us, event | category | flops | bytes accessed | tf_op | source)
XLA Modules:
  0.0 37.1 jit_solution(3356686493995754288)
XLA Ops:
  0.0 1.6 %shard_map.64 = bf16[16,16,896]{2,1,0:T(8,128)(2,1)} custom-call(s32[16]{0:T(128)} %mask_ref.1, bf16[16,1536]{1,0:T(8,128)(2,1)} %key_ref.1, bf16[16,1536]{1,0:T(8,128)(2,1)} %value_ref.1), custom_call_target="tpu_custom_call" | custom-call | tf_op jit(solution)/shard_map/pallas_call | solution.py:169
  1.6 6.2 %all-to-all-start = ((bf16[16,16,896]{2,1,0:T(8,128)(2,1)}), bf16[16,16,896]{2,1,0:T(8,128)(2,1)S(1)}, u32[]{:S(2)}, u32[]{:S(2)}) async-start(bf16[16,16,896]{2,1,0:T(8,128)(2,1)} %shard_map.64), calls=%async_computation | async-start | bytes 917504 | tf_op jit(solution)/shard_map/all_to_all | solution.py:179
  7.8 0.0 slice-start
  7.8 0.0 slice-start.1
  7.8 0.9 %slice-done = bf16[1,384,384]{2,1,0:T(8,128)(2,1)S(1)} async-done(((bf16[1,512,384]{2,1,0:T(8,128)(2,1)}), bf16[1,384,384]{2,1,0:T(8,128)(2,1)S(1)}, s32[]{:S(2)}) %slice-start) | async-done | bytes 294936 | tf_op jit(solution)/shard_map/slice | solution.py:203
  8.8 0.1 slice-done.1
  8.9 0.0 copy-start
  8.9 0.1 pad_maximum_fusion.refs_0_
  8.9 3.5 %collective-permute-start.1 = (bf16[2,384,384]{2,1,0:T(8,128)(2,1)S(1)}, bf16[2,384,384]{2,1,0:T(8,128)(2,1)}, u32[]{:S(2)}, u32[]{:S(2)}) collective-permute-start(bf16[2,384,384]{2,1,0:T(8,128)(2,1)S(1)} %pad_maximum_fusion.refs_0_), channel_id=1, source_target_pairs={{0,4},{1,5},{2,6},{3,7},{4,8},{5,9},{6,10},{7,11},{8,12},{9,13},{1... | collective-permute-start | bytes 1769480 | tf_op jit(solution)/shard_map/ppermute | solution.py:23
  12.5 2.5 %collective-permute-start = (bf16[2,384,384]{2,1,0:T(8,128)(2,1)S(1)}, bf16[2,384,384]{2,1,0:T(8,128)(2,1)S(1)}, u32[]{:S(2)}, u32[]{:S(2)}) collective-permute-start(bf16[2,384,384]{2,1,0:T(8,128)(2,1)S(1)} %pad_maximum_fusion.refs_0_), channel_id=1, source_target_pairs={{4,0},{5,1},{6,2},{7,3},{8,4},{9,5},{10,6},{11,7},{12,8},{13,9},{1... | collective-permute-start | bytes 1769480 | tf_op jit(solution)/shard_map/ppermute | solution.py:23
  15.0 0.1 and_convert_fusion.refs_1_
  15.1 0.0 copy-done
  15.1 0.2 copy.8
  15.3 1.5 %shard_map.65 = (f32[8,512]{1,0:T(8,128)S(1)}, f32[384,512]{1,0:T(8,128)S(1)}) custom-call(bf16[384,512]{1,0:T(8,128)(2,1)S(1)} %bitcast.5, bf16[2,384,384]{2,1,0:T(8,128)(2,1)S(1)} %pad_maximum_fusion.refs_0_, f32[384,1]{1,0:T(8,128)S(1)} %and_convert_fusion.refs_1_), custom_call_target="tpu_custom_call" | custom-call | flops 301989888 | bytes 2981888 | tf_op jit(solution)/shard_map/pallas_call | solution.py:138
  16.8 0.1 and_convert_fusion.1.refs_1_
  16.8 0.1 and_convert_fusion.2.refs_1_
  16.9 3.7 %all-to-all-done = bf16[16,16,896]{2,1,0:T(8,128)(2,1)S(1)} async-done(((bf16[16,16,896]{2,1,0:T(8,128)(2,1)}), bf16[16,16,896]{2,1,0:T(8,128)(2,1)S(1)}, u32[]{:S(2)}, u32[]{:S(2)}) %all-to-all-start) | async-done | bytes 458784 | tf_op jit(solution)/shard_map/all_to_all | solution.py:179
  20.7 1.2 %shard_map.66 = (f32[8,512]{1,0:T(8,128)S(1)}, f32[384,512]{1,0:T(8,128)S(1)}) custom-call(bf16[384,512]{1,0:T(8,128)(2,1)S(1)} %bitcast.6, bf16[256,896]{1,0:T(8,128)(2,1)S(1)} %bitcast.10, f32[256,1]{1,0:T(8,128)S(1)} %compare_convert_fusion.refs_1_, f32[8,512]{1,0:T(8,128)S(1)} %get-tuple-element.11.refs_2_, f32[384,512]{1,0:T(8,128)S(1)} %get-tuple-element.12.refs_3_), custom_call_target="tpu_custom_call" | custom-call | flops 201326592 | bytes 2785280 | tf_op jit(solution)/shard_map/pallas_call | solution.py:138
  21.8 10.4 %collective-permute-done.1.refs_0_ = bf16[2,384,384]{2,1,0:T(8,128)(2,1)} collective-permute-done((bf16[2,384,384]{2,1,0:T(8,128)(2,1)S(1)}, bf16[2,384,384]{2,1,0:T(8,128)(2,1)}, u32[]{:S(2)}, u32[]{:S(2)}) %collective-permute-start.1) | collective-permute-done | bytes 589856 | tf_op jit(solution)/shard_map/ppermute | solution.py:23
  32.2 2.6 %shard_map.67 = (f32[8,512]{1,0:T(8,128)S(1)}, f32[384,512]{1,0:T(8,128)S(1)}) custom-call(bf16[384,512]{1,0:T(8,128)(2,1)S(1)} %bitcast.7, bf16[2,384,384]{2,1,0:T(8,128)(2,1)} %collective-permute-done.1.refs_0_, f32[384,1]{1,0:T(8,128)S(1)} %and_convert_fusion.1.refs_1_, f32[8,512]{1,0:T(8,128)S(1)} %get-tuple-element.13.refs_2_, ...), custom_call_target="tpu_custom_call" | custom-call | flops 301989888 | bytes 2981888 | tf_op jit(solution)/shard_map/pallas_call | solution.py:138
  34.8 0.0 collective-permute-done.refs_0_
  34.8 2.2 %shard_map.68 = bf16[512,384]{1,0:T(8,128)(2,1)} custom-call(bf16[384,512]{1,0:T(8,128)(2,1)S(1)} %bitcast.8, bf16[2,384,384]{2,1,0:T(8,128)(2,1)S(1)} %collective-permute-done.refs_0_, f32[384,1]{1,0:T(8,128)S(1)} %and_convert_fusion.2.refs_1_, f32[8,512]{1,0:T(8,128)S(1)} %get-tuple-element.15.refs_2_, f32[384,512]{1,0:T(8,128)S(1)} %get-tuple-element.16.refs_3_), custom_call_target="tpu_custom_call" | custom-call | flops 301989888 | bytes 2981888 | tf_op jit(solution)/shard_map/pallas_call | solution.py:138
  (1 shorter events, 0.0 us)
Async XLA Ops:
  1.6 19.0 %all-to-all-start = ((bf16[16,16,896]{2,1,0:T(8,128)(2,1)}), bf16[16,16,896]{2,1,0:T(8,128)(2,1)S(1)}, u32[]{:S(2)}, u32[]{:S(2)}) async-start(bf16[16,16,896]{2,1,0:T(8,128)(2,1)} %shard_map.64), calls=%async_computation | async-start | bytes 917504 | tf_op jit(solution)/shard_map/all_to_all | solution.py:179
  7.8 1.0 %slice-start = ((bf16[1,512,384]{2,1,0:T(8,128)(2,1)}), bf16[1,384,384]{2,1,0:T(8,128)(2,1)S(1)}, s32[]{:S(2)}) async-start(bf16[1,512,384]{2,1,0:T(8,128)(2,1)} %param.8), calls=%async_computation.1 | async-start | bytes 589824 | tf_op jit(solution)/shard_map/slice | solution.py:203
  7.8 1.0 %slice-start.1 = ((bf16[1,512,384]{2,1,0:T(8,128)(2,1)}), bf16[1,384,384]{2,1,0:T(8,128)(2,1)S(1)}, s32[]{:S(2)}) async-start(bf16[1,512,384]{2,1,0:T(8,128)(2,1)} %param.7), calls=%async_computation.2 | async-start | bytes 589824 | tf_op jit(solution)/shard_map/slice | solution.py:203
  8.9 6.2 %copy-start = (bf16[1,512,384]{2,1,0:T(8,128)(2,1)S(1)}, bf16[1,512,384]{2,1,0:T(8,128)(2,1)}, u32[]{:S(2)}) copy-start(bf16[1,512,384]{2,1,0:T(8,128)(2,1)} %param.6) | copy-start | bytes 1179652
  8.9 23.3 %collective-permute-start.1 = (bf16[2,384,384]{2,1,0:T(8,128)(2,1)S(1)}, bf16[2,384,384]{2,1,0:T(8,128)(2,1)}, u32[]{:S(2)}, u32[]{:S(2)}) collective-permute-start(bf16[2,384,384]{2,1,0:T(8,128)(2,1)S(1)} %pad_maximum_fusion.refs_0_), channel_id=1, source_target_pairs={{0,4},{1,5},{2,6},{3,7},{4,8},{5,9},{6,10},{7,11},{8,12},{9,13},{1... | collective-permute-start | bytes 1769480 | tf_op jit(solution)/shard_map/ppermute | solution.py:23
  12.5 22.4 %collective-permute-start = (bf16[2,384,384]{2,1,0:T(8,128)(2,1)S(1)}, bf16[2,384,384]{2,1,0:T(8,128)(2,1)S(1)}, u32[]{:S(2)}, u32[]{:S(2)}) collective-permute-start(bf16[2,384,384]{2,1,0:T(8,128)(2,1)S(1)} %pad_maximum_fusion.refs_0_), channel_id=1, source_target_pairs={{4,0},{5,1},{6,2},{7,3},{8,4},{9,5},{10,6},{11,7},{12,8},{13,9},{1... | collective-permute-start | bytes 1769480 | tf_op jit(solution)/shard_map/ppermute | solution.py:23

commit v22 on v19

--- a/solution.py
+++ b/solution.py
@@ -158,7 +158,7 @@
     width = 2 * lane_width + 128
     outgoing = pl.pallas_call(
         functools.partial(payload_kernel, group_count, lane_width),
-        out_shape=jax.ShapeDtypeStruct((count, rows, width), jnp.bfloat16),
+        out_shape=pltpu.VMEM((count, rows, width), jnp.bfloat16),
         in_specs=[
             pl.BlockSpec(memory_space=pltpu.SMEM),
             pl.BlockSpec(memory_space=pltpu.VMEM),

time: 37.5 us -> 37.5 us (level)
  no operation moved by 1% of the time
where the time goes in v22:
time: 37.5 us; the launch traced here: 37.1 us
  waiting for transfers between devices  14.1 us (38%)
  starting transfers between devices  12.2 us (33%)
  Pallas kernels  9.2 us (25%)
  local copies, waits for them, and re-layouts  1.23 us (3%)
    ppermute x2, waiting for transfers between devices, passed_along(): lax.ppermute(value, axis, [(source, source + steps) for source in range(f...  10.4 us
    pallas_call x4, Pallas kernels, window_attention(): pl.pallas_call(functools.partial(window_kernel, tuple(layout), carry is n...  7.56 us
    all_to_all x1, starting transfers between devices, text_pieces(): got = lax.all_to_all(outgoing, 'tile', 0, 0, tiled=True)  6.18 us
    ppermute x2, starting transfers between devices, passed_along(): lax.ppermute(value, axis, [(source, source + steps) for source in range(f...  5.98 us
    all_to_all x1, waiting for transfers between devices, text_pieces(): got = lax.all_to_all(outgoing, 'tile', 0, 0, tiled=True)  3.74 us
    pallas_call x1, Pallas kernels, text_pieces(): pl.pallas_call(functools.partial(payload_kernel, group_count, lane_width)...  1.64 us
    slice x4, local copies, waits for them, and re-layouts, shards(): own_pair = jnp.stack([keys[0, :key_rows], values[0, :key_rows]])  1.04 us
  transfers between devices with their start and end apart: 3, of which 2 were waited for; matrix products, arithmetic and copies ran while one was open for 1% of the time, Pallas kernels for 14%

profile of v22, /device:TPU:16, one launch (start us, length us, event | category | flops | bytes accessed | tf_op | source)
XLA Modules:
  0.0 37.1 jit_solution(4339923476667926315)
XLA Ops:
  0.0 1.6 %shard_map.64 = bf16[16,16,896]{2,1,0:T(8,128)(2,1)} custom-call(s32[16]{0:T(128)} %mask_ref.1, bf16[16,1536]{1,0:T(8,128)(2,1)} %key_ref.1, bf16[16,1536]{1,0:T(8,128)(2,1)} %value_ref.1), custom_call_target="tpu_custom_call" | custom-call | tf_op jit(solution)/shard_map/pallas_call | solution.py:159
  1.6 6.2 %all-to-all-start = ((bf16[16,16,896]{2,1,0:T(8,128)(2,1)}), bf16[16,16,896]{2,1,0:T(8,128)(2,1)S(1)}, u32[]{:S(2)}, u32[]{:S(2)}) async-start(bf16[16,16,896]{2,1,0:T(8,128)(2,1)} %shard_map.64), calls=%async_computation | async-start | bytes 917504 | tf_op jit(solution)/shard_map/all_to_all | solution.py:169
  7.8 0.0 slice-start
  7.8 0.0 slice-start.1
  7.8 0.9 %slice-done = bf16[1,384,384]{2,1,0:T(8,128)(2,1)S(1)} async-done(((bf16[1,512,384]{2,1,0:T(8,128)(2,1)}), bf16[1,384,384]{2,1,0:T(8,128)(2,1)S(1)}, s32[]{:S(2)}) %slice-start) | async-done | bytes 294936 | tf_op jit(solution)/shard_map/slice | solution.py:193
  8.8 0.1 slice-done.1
  8.9 0.0 copy-start
  8.9 0.1 pad_maximum_fusion.refs_0_
  8.9 3.5 %collective-permute-start.1 = (bf16[2,384,384]{2,1,0:T(8,128)(2,1)S(1)}, bf16[2,384,384]{2,1,0:T(8,128)(2,1)}, u32[]{:S(2)}, u32[]{:S(2)}) collective-permute-start(bf16[2,384,384]{2,1,0:T(8,128)(2,1)S(1)} %pad_maximum_fusion.refs_0_), channel_id=1, source_target_pairs={{0,4},{1,5},{2,6},{3,7},{4,8},{5,9},{6,10},{7,11},{8,12},{9,13},{1... | collective-permute-start | bytes 1769480 | tf_op jit(solution)/shard_map/ppermute | solution.py:23
  12.5 2.5 %collective-permute-start = (bf16[2,384,384]{2,1,0:T(8,128)(2,1)S(1)}, bf16[2,384,384]{2,1,0:T(8,128)(2,1)S(1)}, u32[]{:S(2)}, u32[]{:S(2)}) collective-permute-start(bf16[2,384,384]{2,1,0:T(8,128)(2,1)S(1)} %pad_maximum_fusion.refs_0_), channel_id=1, source_target_pairs={{4,0},{5,1},{6,2},{7,3},{8,4},{9,5},{10,6},{11,7},{12,8},{13,9},{1... | collective-permute-start | bytes 1769480 | tf_op jit(solution)/shard_map/ppermute | solution.py:23
  15.0 0.1 and_convert_fusion.refs_1_
  15.1 0.0 copy-done
  15.1 0.2 copy.8
  15.3 1.5 %shard_map.65 = (f32[8,512]{1,0:T(8,128)S(1)}, f32[384,512]{1,0:T(8,128)S(1)}) custom-call(bf16[384,512]{1,0:T(8,128)(2,1)S(1)} %bitcast.5, bf16[2,384,384]{2,1,0:T(8,128)(2,1)S(1)} %pad_maximum_fusion.refs_0_, f32[384,1]{1,0:T(8,128)S(1)} %and_convert_fusion.refs_1_), custom_call_target="tpu_custom_call" | custom-call | flops 301989888 | bytes 2981888 | tf_op jit(solution)/shard_map/pallas_call | solution.py:129
  16.8 0.1 and_convert_fusion.1.refs_1_
  16.8 0.1 and_convert_fusion.2.refs_1_
  16.9 3.7 %all-to-all-done = bf16[16,16,896]{2,1,0:T(8,128)(2,1)S(1)} async-done(((bf16[16,16,896]{2,1,0:T(8,128)(2,1)}), bf16[16,16,896]{2,1,0:T(8,128)(2,1)S(1)}, u32[]{:S(2)}, u32[]{:S(2)}) %all-to-all-start) | async-done | bytes 458784 | tf_op jit(solution)/shard_map/all_to_all | solution.py:169
  20.7 1.2 %shard_map.66 = (f32[8,512]{1,0:T(8,128)S(1)}, f32[384,512]{1,0:T(8,128)S(1)}) custom-call(bf16[384,512]{1,0:T(8,128)(2,1)S(1)} %bitcast.6, bf16[256,896]{1,0:T(8,128)(2,1)S(1)} %bitcast.10, f32[256,1]{1,0:T(8,128)S(1)} %compare_convert_fusion.refs_1_, f32[8,512]{1,0:T(8,128)S(1)} %get-tuple-element.11.refs_2_, f32[384,512]{1,0:T(8,128)S(1)} %get-tuple-element.12.refs_3_), custom_call_target="tpu_custom_call" | custom-call | flops 201326592 | bytes 2785280 | tf_op jit(solution)/shard_map/pallas_call | solution.py:129
  21.8 10.4 %collective-permute-done.1.refs_0_ = bf16[2,384,384]{2,1,0:T(8,128)(2,1)} collective-permute-done((bf16[2,384,384]{2,1,0:T(8,128)(2,1)S(1)}, bf16[2,384,384]{2,1,0:T(8,128)(2,1)}, u32[]{:S(2)}, u32[]{:S(2)}) %collective-permute-start.1) | collective-permute-done | bytes 589856 | tf_op jit(solution)/shard_map/ppermute | solution.py:23
  32.2 2.6 %shard_map.67 = (f32[8,512]{1,0:T(8,128)S(1)}, f32[384,512]{1,0:T(8,128)S(1)}) custom-call(bf16[384,512]{1,0:T(8,128)(2,1)S(1)} %bitcast.7, bf16[2,384,384]{2,1,0:T(8,128)(2,1)} %collective-permute-done.1.refs_0_, f32[384,1]{1,0:T(8,128)S(1)} %and_convert_fusion.1.refs_1_, f32[8,512]{1,0:T(8,128)S(1)} %get-tuple-element.13.refs_2_, ...), custom_call_target="tpu_custom_call" | custom-call | flops 301989888 | bytes 2981888 | tf_op jit(solution)/shard_map/pallas_call | solution.py:129
  34.8 0.0 collective-permute-done.refs_0_
  34.8 2.3 %shard_map.68 = bf16[512,384]{1,0:T(8,128)(2,1)} custom-call(bf16[384,512]{1,0:T(8,128)(2,1)S(1)} %bitcast.8, bf16[2,384,384]{2,1,0:T(8,128)(2,1)S(1)} %collective-permute-done.refs_0_, f32[384,1]{1,0:T(8,128)S(1)} %and_convert_fusion.2.refs_1_, f32[8,512]{1,0:T(8,128)S(1)} %get-tuple-element.15.refs_2_, f32[384,512]{1,0:T(8,128)S(1)} %get-tuple-element.16.refs_3_), custom_call_target="tpu_custom_call" | custom-call | flops 301989888 | bytes 2981888 | tf_op jit(solution)/shard_map/pallas_call | solution.py:129
  (1 shorter events, 0.0 us)
Async XLA Ops:
  1.6 19.0 %all-to-all-start = ((bf16[16,16,896]{2,1,0:T(8,128)(2,1)}), bf16[16,16,896]{2,1,0:T(8,128)(2,1)S(1)}, u32[]{:S(2)}, u32[]{:S(2)}) async-start(bf16[16,16,896]{2,1,0:T(8,128)(2,1)} %shard_map.64), calls=%async_computation | async-start | bytes 917504 | tf_op jit(solution)/shard_map/all_to_all | solution.py:169
  7.8 1.0 %slice-start = ((bf16[1,512,384]{2,1,0:T(8,128)(2,1)}), bf16[1,384,384]{2,1,0:T(8,128)(2,1)S(1)}, s32[]{:S(2)}) async-start(bf16[1,512,384]{2,1,0:T(8,128)(2,1)} %param.8), calls=%async_computation.1 | async-start | bytes 589824 | tf_op jit(solution)/shard_map/slice | solution.py:193
  7.8 1.0 %slice-start.1 = ((bf16[1,512,384]{2,1,0:T(8,128)(2,1)}), bf16[1,384,384]{2,1,0:T(8,128)(2,1)S(1)}, s32[]{:S(2)}) async-start(bf16[1,512,384]{2,1,0:T(8,128)(2,1)} %param.7), calls=%async_computation.2 | async-start | bytes 589824 | tf_op jit(solution)/shard_map/slice | solution.py:193
  8.9 6.2 %copy-start = (bf16[1,512,384]{2,1,0:T(8,128)(2,1)S(1)}, bf16[1,512,384]{2,1,0:T(8,128)(2,1)}, u32[]{:S(2)}) copy-start(bf16[1,512,384]{2,1,0:T(8,128)(2,1)} %param.6) | copy-start | bytes 1179652
  8.9 23.3 %collective-permute-start.1 = (bf16[2,384,384]{2,1,0:T(8,128)(2,1)S(1)}, bf16[2,384,384]{2,1,0:T(8,128)(2,1)}, u32[]{:S(2)}, u32[]{:S(2)}) collective-permute-start(bf16[2,384,384]{2,1,0:T(8,128)(2,1)S(1)} %pad_maximum_fusion.refs_0_), channel_id=1, source_target_pairs={{0,4},{1,5},{2,6},{3,7},{4,8},{5,9},{6,10},{7,11},{8,12},{9,13},{1... | collective-permute-start | bytes 1769480 | tf_op jit(solution)/shard_map/ppermute | solution.py:23
  12.5 22.4 %collective-permute-start = (bf16[2,384,384]{2,1,0:T(8,128)(2,1)S(1)}, bf16[2,384,384]{2,1,0:T(8,128)(2,1)S(1)}, u32[]{:S(2)}, u32[]{:S(2)}) collective-permute-start(bf16[2,384,384]{2,1,0:T(8,128)(2,1)S(1)} %pad_maximum_fusion.refs_0_), channel_id=1, source_target_pairs={{4,0},{5,1},{6,2},{7,3},{8,4},{9,5},{10,6},{11,7},{12,8},{13,9},{1... | collective-permute-start | bytes 1769480 | tf_op jit(solution)/shard_map/ppermute | solution.py:23

commit v23 on v20

--- a/solution.py
+++ b/solution.py
@@ -163,12 +163,12 @@
     rows = text_keys.shape[0]
     width = 2 * lane_width + 128
     vmem = pl.BlockSpec(memory_space=pltpu.VMEM)
-    out_shape = jax.ShapeDtypeStruct((count, rows, width), jnp.bfloat16)
+    out_shape = pltpu.VMEM((count, rows, width), jnp.bfloat16)
     extra = ()
     if own is not None:
         own_keys, own_values, key_rows = own
         extra = (own_keys, own_values)
-        out_shape = (out_shape, jax.ShapeDtypeStruct((2, key_rows, own_keys.shape[1]), own_keys.dtype))
+        out_shape = (out_shape, pltpu.VMEM((2, key_rows, own_keys.shape[1]), own_keys.dtype))
     made = pl.pallas_call(
         functools.partial(payload_kernel, group_count, lane_width),
         out_shape=out_shape,

time: 38.2 us -> 38 us (level)
  no operation moved by 1% of the time
where the time goes in v23:
time: 38 us; the launch traced here: 37.6 us
  waiting for transfers between devices  15.4 us (41%)
  starting transfers between devices  12.1 us (32%)
  Pallas kernels  9.56 us (25%)
    ppermute x2, waiting for transfers between devices, passed_along(): lax.ppermute(value, axis, [(source, source + steps) for source in range(f...  10.4 us
    pallas_call x4, Pallas kernels, window_attention(): pl.pallas_call(functools.partial(window_kernel, tuple(layout), carry is n...  7.56 us
    all_to_all x1, starting transfers between devices, text_pieces(): got = lax.all_to_all(outgoing, 'tile', 0, 0, tiled=True)  6.32 us
    ppermute x2, starting transfers between devices, passed_along(): lax.ppermute(value, axis, [(source, source + steps) for source in range(f...  5.83 us
    all_to_all x1, waiting for transfers between devices, text_pieces(): got = lax.all_to_all(outgoing, 'tile', 0, 0, tiled=True)  5.01 us
    pallas_call x1, Pallas kernels, text_pieces(): pl.pallas_call(functools.partial(payload_kernel, group_count, lane_width)...  2 us
  transfers between devices with their start and end apart: 3, of which 2 were waited for; matrix products, arithmetic and copies ran while one was open for 1% of the time, Pallas kernels for 14%

profile of v23, /device:TPU:16, one launch (start us, length us, event | category | flops | bytes accessed | tf_op | source)
XLA Modules:
  0.0 37.6 jit_solution(13529482707065282020)
XLA Ops:
  0.0 2.0 %shard_map.64 = (bf16[16,16,896]{2,1,0:T(8,128)(2,1)}, bf16[2,384,384]{2,1,0:T(8,128)(2,1)S(1)}) custom-call(s32[16]{0:T(128)} %mask_ref.1, bf16[16,1536]{1,0:T(8,128)(2,1)} %key_ref.1, bf16[16,1536]{1,0:T(8,128)(2,1)} %value_ref.1, bf16[512,384]{1,0:T(8,128)(2,1)} %bitcast.13, bf16[512,384]{1,0:T(8,128)(2,1)} %bitcast.14), custom_call_target="tpu_custom_call" | custom-call | tf_op jit(solution)/shard_map/pallas_call | solution.py:172
  2.0 0.0 copy-start
  2.0 6.3 %all-to-all-start = ((bf16[16,16,896]{2,1,0:T(8,128)(2,1)}), bf16[16,16,896]{2,1,0:T(8,128)(2,1)S(1)}, u32[]{:S(2)}, u32[]{:S(2)}) async-start(bf16[16,16,896]{2,1,0:T(8,128)(2,1)} %get-tuple-element.14), calls=%async_computation | async-start | bytes 917504 | tf_op jit(solution)/shard_map/all_to_all | solution.py:182
  8.3 3.4 %collective-permute-start.1 = (bf16[2,384,384]{2,1,0:T(8,128)(2,1)S(1)}, bf16[2,384,384]{2,1,0:T(8,128)(2,1)}, u32[]{:S(2)}, u32[]{:S(2)}) collective-permute-start(bf16[2,384,384]{2,1,0:T(8,128)(2,1)S(1)} %get-tuple-element.13.refs_0_), channel_id=1, source_target_pairs={{0,4},{1,5},{2,6},{3,7},{4,8},{5,9},{6,10},{7,11},{8,12},{9,13},{1... | collective-permute-start | bytes 1769480 | tf_op jit(solution)/shard_map/ppermute | solution.py:23
  11.7 2.5 %collective-permute-start = (bf16[2,384,384]{2,1,0:T(8,128)(2,1)S(1)}, bf16[2,384,384]{2,1,0:T(8,128)(2,1)S(1)}, u32[]{:S(2)}, u32[]{:S(2)}) collective-permute-start(bf16[2,384,384]{2,1,0:T(8,128)(2,1)S(1)} %get-tuple-element.13.refs_0_), channel_id=1, source_target_pairs={{4,0},{5,1},{6,2},{7,3},{8,4},{9,5},{10,6},{11,7},{12,8},{13,9},{1... | collective-permute-start | bytes 1769480 | tf_op jit(solution)/shard_map/ppermute | solution.py:23
  14.2 0.1 and_convert_fusion.refs_1_
  14.3 0.0 copy-done
  14.3 0.2 copy.8
  14.5 1.5 %shard_map.65 = (f32[8,512]{1,0:T(8,128)S(1)}, f32[384,512]{1,0:T(8,128)S(1)}) custom-call(bf16[384,512]{1,0:T(8,128)(2,1)S(1)} %bitcast.7, bf16[2,384,384]{2,1,0:T(8,128)(2,1)S(1)} %get-tuple-element.13.refs_0_, f32[384,1]{1,0:T(8,128)S(1)} %and_convert_fusion.refs_1_), custom_call_target="tpu_custom_call" | custom-call | flops 301989888 | bytes 2981888 | tf_op jit(solution)/shard_map/pallas_call | solution.py:129
  16.0 0.1 and_convert_fusion.1.refs_1_
  16.1 0.1 and_convert_fusion.2.refs_1_
  16.1 5.0 %all-to-all-done = bf16[16,16,896]{2,1,0:T(8,128)(2,1)S(1)} async-done(((bf16[16,16,896]{2,1,0:T(8,128)(2,1)}), bf16[16,16,896]{2,1,0:T(8,128)(2,1)S(1)}, u32[]{:S(2)}, u32[]{:S(2)}) %all-to-all-start) | async-done | bytes 458784 | tf_op jit(solution)/shard_map/all_to_all | solution.py:182
  21.2 1.2 %shard_map.66 = (f32[8,512]{1,0:T(8,128)S(1)}, f32[384,512]{1,0:T(8,128)S(1)}) custom-call(bf16[384,512]{1,0:T(8,128)(2,1)S(1)} %bitcast.8, bf16[256,896]{1,0:T(8,128)(2,1)S(1)} %bitcast.12, f32[256,1]{1,0:T(8,128)S(1)} %compare_convert_fusion.refs_1_, f32[8,512]{1,0:T(8,128)S(1)} %get-tuple-element.15.refs_2_, f32[384,512]{1,0:T(8,128)S(1)} %get-tuple-element.16.refs_3_), custom_call_target="tpu_custom_call" | custom-call | flops 201326592 | bytes 2785280 | tf_op jit(solution)/shard_map/pallas_call | solution.py:129
  22.3 10.4 %collective-permute-done.1.refs_0_ = bf16[2,384,384]{2,1,0:T(8,128)(2,1)} collective-permute-done((bf16[2,384,384]{2,1,0:T(8,128)(2,1)S(1)}, bf16[2,384,384]{2,1,0:T(8,128)(2,1)}, u32[]{:S(2)}, u32[]{:S(2)}) %collective-permute-start.1) | collective-permute-done | bytes 589856 | tf_op jit(solution)/shard_map/ppermute | solution.py:23
  32.7 2.6 %shard_map.67 = (f32[8,512]{1,0:T(8,128)S(1)}, f32[384,512]{1,0:T(8,128)S(1)}) custom-call(bf16[384,512]{1,0:T(8,128)(2,1)S(1)} %bitcast.9, bf16[2,384,384]{2,1,0:T(8,128)(2,1)} %collective-permute-done.1.refs_0_, f32[384,1]{1,0:T(8,128)S(1)} %and_convert_fusion.1.refs_1_, f32[8,512]{1,0:T(8,128)S(1)} %get-tuple-element.17.refs_2_, ...), custom_call_target="tpu_custom_call" | custom-call | flops 301989888 | bytes 2981888 | tf_op jit(solution)/shard_map/pallas_call | solution.py:129
  35.3 0.0 collective-permute-done.refs_0_
  35.3 2.3 %shard_map.68 = bf16[512,384]{1,0:T(8,128)(2,1)} custom-call(bf16[384,512]{1,0:T(8,128)(2,1)S(1)} %bitcast.10, bf16[2,384,384]{2,1,0:T(8,128)(2,1)S(1)} %collective-permute-done.refs_0_, f32[384,1]{1,0:T(8,128)S(1)} %and_convert_fusion.2.refs_1_, f32[8,512]{1,0:T(8,128)S(1)} %get-tuple-element.19.refs_2_, f32[384,512]{1,0:T(8,128)S(1)} %get-tuple-element.20.refs_3_), custom_call_target="tpu_custom_call" | custom-call | flops 301989888 | bytes 2981888 | tf_op jit(solution)/shard_map/pallas_call | solution.py:129
  (1 shorter events, 0.0 us)
Async XLA Ops:
  2.0 12.3 %copy-start = (bf16[1,512,384]{2,1,0:T(8,128)(2,1)S(1)}, bf16[1,512,384]{2,1,0:T(8,128)(2,1)}, u32[]{:S(2)}) copy-start(bf16[1,512,384]{2,1,0:T(8,128)(2,1)} %param.6) | copy-start | bytes 1179652
  2.0 19.1 %all-to-all-start = ((bf16[16,16,896]{2,1,0:T(8,128)(2,1)}), bf16[16,16,896]{2,1,0:T(8,128)(2,1)S(1)}, u32[]{:S(2)}, u32[]{:S(2)}) async-start(bf16[16,16,896]{2,1,0:T(8,128)(2,1)} %get-tuple-element.14), calls=%async_computation | async-start | bytes 917504 | tf_op jit(solution)/shard_map/all_to_all | solution.py:182
  8.3 24.4 %collective-permute-start.1 = (bf16[2,384,384]{2,1,0:T(8,128)(2,1)S(1)}, bf16[2,384,384]{2,1,0:T(8,128)(2,1)}, u32[]{:S(2)}, u32[]{:S(2)}) collective-permute-start(bf16[2,384,384]{2,1,0:T(8,128)(2,1)S(1)} %get-tuple-element.13.refs_0_), channel_id=1, source_target_pairs={{0,4},{1,5},{2,6},{3,7},{4,8},{5,9},{6,10},{7,11},{8,12},{9,13},{1... | collective-permute-start | bytes 1769480 | tf_op jit(solution)/shard_map/ppermute | solution.py:23
  11.7 23.6 %collective-permute-start = (bf16[2,384,384]{2,1,0:T(8,128)(2,1)S(1)}, bf16[2,384,384]{2,1,0:T(8,128)(2,1)S(1)}, u32[]{:S(2)}, u32[]{:S(2)}) collective-permute-start(bf16[2,384,384]{2,1,0:T(8,128)(2,1)S(1)} %get-tuple-element.13.refs_0_), channel_id=1, source_target_pairs={{4,0},{5,1},{6,2},{7,3},{8,4},{9,5},{10,6},{11,7},{12,8},{13,9},{1... | collective-permute-start | bytes 1769480 | tf_op jit(solution)/shard_map/ppermute | solution.py:23
